TPU v7x, 128 devices: a whole 4x4x4 slice. The times are simulated.
128 devices in a mesh: fsdp: 32 (over z, y, core), fac: 4 (over x).
Axes of the slice: x: 4, y: 4, z: 4, core: 2. Of those that a mesh axis runs over, the one named last changes fastest.
Arguments:
- activations: bfloat16 [32768, 3072], P('fsdp'), may hold values from -6 to 6
- out_grads: bfloat16 [32768, 3072], P('fsdp', 'fac'), may hold values from -12 to 12
- token_ids: int32 [32768], P('fsdp'), may hold values from 0 to 32767
- forget_mask: int32 [32768], P('fsdp'), may hold values 0 or 1
- importance: float32 [32768], replicated, may hold values from 0.3 to 3
- in_inverse: bfloat16 [3072, 3072], P('fsdp'), may hold values from -1 to 3, as said below
- out_inverse: bfloat16 [3072, 3072], P(None, 'fac'), may hold values from -1 to 3, as said below
Outputs:
- newton_step: float32 [3072, 3072], P('fsdp', 'fac')
- residual: float32 [3072, 3072], P('fsdp', 'fac')
Inputs may be any that keep to these rules, and one draw needn't show every extreme that they name: `in_inverse`: symmetric and positive definite. `out_inverse`: symmetric and positive definite.
All inputs are finite; a program needn't handle non-finite values. No bound on the sum of `forget_mask` on one device may be relied on, other than what follows from the above.
Results may differ from a plain program's by a relative error of at most 0.03.
Values may be sent and summed in bfloat16 or wider, within the bound.
No kernel may reach another device: no remote copies, remote signals or barrier semaphores. Data moves between devices by JAX's collectives and lax.ppermute only.
A program may use at most 64 MiB of HBM per device.

v0:
```python
import math

import jax
import jax.numpy as jnp
from jax import lax
from jax.sharding import PartitionSpec as P

ITERS = 2


damping = 0.3


def add_columns(matrix, piece):
    return jnp.dot(matrix, piece, preferred_element_type=jnp.float32)


def transposed_term(matrix, right):
    return lax.dot_general(
        matrix, right, (((0,), (0,)), ((), ())), preferred_element_type=jnp.float32
    )


def body(activations, out_grads, token_ids, forget_mask, importance, in_inverse, out_inverse):
    tok_rows = activations.shape[0]
    total = tok_rows * lax.axis_size("fsdp")
    keep = 1.0 - forget_mask.astype(jnp.float32)
    weights = importance[token_ids] * keep / total
    forget_grads = out_grads * forget_mask.astype(jnp.bfloat16)[:, None]
    grad_scale = 1.0 / math.sqrt(total)
    gradient = lax.psum_scatter(
        (transposed_term(activations, forget_grads) * grad_scale).astype(jnp.bfloat16),
        "fsdp",
        scatter_dimension=0,
        tiled=True,
    ).astype(jnp.float32)

    def precondition(matrix):
        matrix_low = matrix.astype(jnp.bfloat16)
        mixed = add_columns(in_inverse, lax.all_gather(matrix_low, "fsdp", axis=0, tiled=True))
        mixed_low = mixed.astype(jnp.bfloat16)
        return jnp.dot(
            lax.all_gather(mixed_low, "fac", axis=1, tiled=True),
            out_inverse,
            preferred_element_type=jnp.float32,
        )

    def inner_sum(left, right):
        return lax.psum(jnp.sum(left * right), ("fsdp", "fac"))

    newton_step = jnp.zeros(gradient.shape, jnp.float32)
    residual = -gradient
    precond = precondition(residual)
    direction = precond
    inner_now = inner_sum(residual, precond)
    for iteration in range(ITERS):
        curvature_matrix_low = direction.astype(jnp.bfloat16)
        tok_out = add_columns(
            activations, lax.all_gather(curvature_matrix_low, "fsdp", axis=0, tiled=True)
        )
        scaled = (tok_out * weights[:, None]).astype(jnp.bfloat16)
        image = (
            lax.psum_scatter(
                transposed_term(activations, scaled).astype(jnp.bfloat16),
                "fsdp",
                scatter_dimension=0,
                tiled=True,
            ).astype(jnp.float32)
            + damping * direction
        )
        energy = lax.psum(jnp.sum(direction * image), ("fsdp", "fac"))
        image, energy = (image, energy)
        alpha = inner_now / energy
        newton_step = newton_step + alpha * direction
        residual = residual - alpha * image
        if iteration + 1 < ITERS:
            precond = precondition(residual)
            inner_next = inner_sum(residual, precond)
            direction = precond + inner_next / inner_now * direction
            inner_now = inner_next
    return (newton_step, residual)


def solution(mesh):
    placed = (
        P("fsdp", None),
        P("fsdp", "fac"),
        P("fsdp"),
        P("fsdp"),
        P(),
        P("fsdp", None),
        P(None, "fac"),
    )
    return jax.shard_map(
        body,
        mesh=mesh,
        in_specs=placed,
        out_specs=(P("fsdp", "fac"), P("fsdp", "fac")),
        check_vma=False,
    )
```

profile of v0, /device:TPU:1, one launch (start us, length us, event | category | flops | bytes accessed | tf_op | source)
XLA Modules:
  0.0 761.0 jit_solution(16423299963666644336)
XLA Ops:
  8.0 9.3 %fusion.2 = bf16[3072,768]{0,1:T(8,128)(2,1)} fusion(bf16[1024,3072]{1,0:T(8,128)(2,1)} %param.7, bf16[1024,768]{1,0:T(8,128)(2,1)} %param.8, bf16[1024]{0:T(1024)(128)(2,1)S(1)} %convert_element_type.65), kind=kOutput, calls=%fused_computation.6 | convolution fusion | flops 4837343232 | bytes 12584960 | tf_op jit(solution)/shard_map/dot_general | solution.py:19
  17.3 6.6 copy.30
  24.0 85.4 %reduce-scatter.10.cloned.1.call-done = bf16[96,768]{1,0:T(8,128)(2,1)} async-done(((bf16[3072,768]{1,0:T(8,128)(2,1)}), bf16[96,768]{1,0:T(8,128)(2,1)}) %reduce-scatter.10.cloned.1.call-update) | async-done | bytes 147472 | tf_op jit(solution)/shard_map/reduce_scatter | solution.py:31
  111.1 49.7 %all-gather.5.cloned.1.call-done = bf16[3072,768]{1,0:T(8,128)(2,1)} async-done(((bf16[96,768]{1,0:T(8,128)(2,1)}), bf16[3072,768]{1,0:T(8,128)(2,1)}) %all-gather.5.cloned.1.call-update) | async-done | bytes 4718608 | tf_op jit(solution)/shard_map/all_gather | solution.py:40
  160.8 3.2 fusion.4
  164.0 11.3 %all_gather.19 = bf16[96,3072]{1,0:T(8,128)(2,1)S(1)} all-gather(bf16[96,768]{1,0:T(8,128)(2,1)S(1)} %fusion.4), channel_id=1, replica_groups=mesh['fsdp'=32,'fac'=4] {'fac'}, dimensions={1}, use_global_device_ids=true | all-gather | bytes 737280 | tf_op jit(solution)/shard_map/all_gather | solution.py:43
  175.4 3.9 fusion.11
  179.4 6.2 gather_fusion
  185.5 42.3 %all-gather.7.cloned.1.call-done = bf16[3072,768]{1,0:T(8,128)(2,1)} async-done(((bf16[96,768]{1,0:T(8,128)(2,1)}), bf16[3072,768]{1,0:T(8,128)(2,1)}) %all-gather.7.cloned.1.call-update) | async-done | bytes 4718608 | tf_op jit(solution)/shard_map/all_gather | solution.py:59
  227.8 17.5 %fusion = bf16[3072,768]{0,1:T(8,128)(2,1)} fusion(bf16[1024,3072]{1,0:T(8,128)(2,1)} %param.7, bf16[3072,768]{1,0:T(8,128)(2,1)} %all-gather.7.cloned.1.call-done, f32[1024]{0:T(1024)S(1)} %multiply_multiply_fusion), kind=kOutput, calls=%fused_computation.4 | convolution fusion | flops 9667608576 | bytes 15732736 | tf_op jit(solution)/shard_map/dot_general | solution.py:19
  245.3 6.7 copy.32
  252.1 81.0 %reduce-scatter.12.cloned.1.call-done = bf16[96,768]{1,0:T(8,128)(2,1)} async-done(((bf16[3072,768]{1,0:T(8,128)(2,1)}), bf16[96,768]{1,0:T(8,128)(2,1)}) %reduce-scatter.12.cloned.1.call-update) | async-done | bytes 147472 | tf_op jit(solution)/shard_map/reduce_scatter | solution.py:63
  334.7 65.9 %all-reduce = (f32[]{:T(128)}, f32[]{:T(128)}) all-reduce(f32[]{:T(128)} %get-tuple-element.7, f32[]{:T(128)} %get-tuple-element.6), channel_id=1, replica_groups=mesh['fsdp'=32,'fac'=4] {'fsdp','fac'}, use_global_device_ids=true, to_apply=%region_2.0 | all-reduce | flops 2 | bytes 16 | tf_op jit(solution)/shard_map/psum | solution.py:49
  403.8 43.8 %all-gather.9.cloned.1.call-done = bf16[3072,768]{1,0:T(8,128)(2,1)} async-done(((bf16[96,768]{1,0:T(8,128)(2,1)}), bf16[3072,768]{1,0:T(8,128)(2,1)}) %all-gather.9.cloned.1.call-update) | async-done | bytes 4718608 | tf_op jit(solution)/shard_map/all_gather | solution.py:40
  447.6 3.2 fusion.5
  450.8 11.3 %all_gather.22 = bf16[96,3072]{1,0:T(8,128)(2,1)S(1)} all-gather(bf16[96,768]{1,0:T(8,128)(2,1)S(1)} %fusion.5), channel_id=1, replica_groups=mesh['fsdp'=32,'fac'=4] {'fac'}, dimensions={1}, use_global_device_ids=true | all-gather | bytes 737280 | tf_op jit(solution)/shard_map/all_gather | solution.py:43
  462.1 3.9 multiply_reduce_fusion.1
  466.0 66.2 %psum.30 = f32[]{:T(128)} all-reduce(f32[]{:T(128)} %get-tuple-element.18), channel_id=1, replica_groups=mesh['fsdp'=32,'fac'=4] {'fsdp','fac'}, use_global_device_ids=true, to_apply=%region_7.0 | all-reduce | flops 1 | bytes 8 | tf_op jit(solution)/shard_map/psum | solution.py:49
  534.3 44.0 %all-gather.11.cloned.1.call-done = bf16[3072,768]{1,0:T(8,128)(2,1)} async-done(((bf16[96,768]{1,0:T(8,128)(2,1)}), bf16[3072,768]{1,0:T(8,128)(2,1)}) %all-gather.11.cloned.1.call-update) | async-done | bytes 4718608 | tf_op jit(solution)/shard_map/all_gather | solution.py:59
  578.2 17.5 %fusion.1 = bf16[3072,768]{0,1:T(8,128)(2,1)} fusion(bf16[1024,3072]{1,0:T(8,128)(2,1)} %param.7, bf16[3072,768]{1,0:T(8,128)(2,1)} %all-gather.11.cloned.1.call-done, f32[1024]{0:T(1024)S(1)} %multiply_multiply_fusion), kind=kOutput, calls=%fused_computation.5 | convolution fusion | flops 9667608576 | bytes 15732736 | tf_op jit(solution)/shard_map/dot_general | solution.py:19
  595.7 6.7 copy.34
  602.4 81.1 %reduce-scatter.14.cloned.1.call-done = bf16[96,768]{1,0:T(8,128)(2,1)} async-done(((bf16[3072,768]{1,0:T(8,128)(2,1)}), bf16[96,768]{1,0:T(8,128)(2,1)}) %reduce-scatter.14.cloned.1.call-update) | async-done | bytes 147472 | tf_op jit(solution)/shard_map/reduce_scatter | solution.py:63
  685.1 65.9 %psum.31 = f32[]{:T(128)} all-reduce(f32[]{:T(128)} %multiply_reduce_fusion), channel_id=1, replica_groups=mesh['fsdp'=32,'fac'=4] {'fsdp','fac'}, use_global_device_ids=true, to_apply=%region_10.0 | all-reduce | flops 1 | bytes 8 | tf_op jit(solution)/shard_map/psum | solution.py:71
  752.3 1.8 multiply_subtract_fusion
  (32 shorter events, 8.5 us)
Async XLA Ops:
  7.2 153.7 %copy-start = (bf16[96,3072]{1,0:T(8,128)(2,1)S(1)}, bf16[96,3072]{1,0:T(8,128)(2,1)}, u32[]{:S(2)}) copy-start(bf16[96,3072]{1,0:T(8,128)(2,1)} %param.12) | copy-start | bytes 1769476
  7.2 102.3 %reduce-scatter.10.cloned.1.call-start = ((), (), s32[]{:S(2)}) async-start(), calls=%async_computation.7 | async-start | bytes 4866048 | tf_op jit(solution)/shard_map/reduce_scatter | solution.py:31
  24.0 136.9 %all-gather.5.cloned.1.call-start = ((), (), s32[]{:S(2)}) async-start(), calls=%async_computation.3 | async-start | bytes 4866048 | tf_op jit(solution)/shard_map/all_gather | solution.py:40
  111.1 68.3 %copy-start.4 = (s32[1024]{0:T(1024)S(1)}, s32[1024]{0:T(1024)}, u32[]{:S(2)}) copy-start(s32[1024]{0:T(1024)} %param.9) | copy-start | bytes 12292
  111.1 68.3 %copy-start.1 = (f32[32768]{0:T(1024)S(1)}, f32[32768]{0:T(1024)}, u32[]{:S(2)}) copy-start(f32[32768]{0:T(1024)} %param.11) | copy-start | bytes 393220
  111.1 116.7 %all-gather.7.cloned.1.call-start = ((), (), s32[]{:S(2)}) async-start(), calls=%async_computation.4 | async-start | bytes 4866048 | tf_op jit(solution)/shard_map/all_gather | solution.py:59
  175.4 10.2 %copy-start.3 = (s32[1024]{0:T(1024)S(1)}, s32[1024]{0:T(1024)}, u32[]{:S(2)}) copy-start(s32[1024]{0:T(1024)} %param.10) | copy-start | bytes 12292
  179.3 153.8 %reduce-scatter.12.cloned.1.call-start = ((), (), s32[]{:S(2)}) async-start(), calls=%async_computation.8 | async-start | bytes 4866048 | tf_op jit(solution)/shard_map/reduce_scatter | solution.py:63
  252.0 81.1 %copy-start.2 = (bf16[96,768]{1,0:T(8,128)(2,1)S(1)}, bf16[96,768]{1,0:T(8,128)(2,1)}, u32[]{:S(2)}) copy-start(bf16[96,768]{1,0:T(8,128)(2,1)} %reduce-scatter.10.cloned.1.call-done) | copy-start | bytes 442372
  252.0 195.6 %all-gather.9.cloned.1.call-start = ((), (), s32[]{:S(2)}) async-start(), calls=%async_computation.5 | async-start | bytes 4866048 | tf_op jit(solution)/shard_map/all_gather | solution.py:40
  403.6 174.6 %all-gather.11.cloned.1.call-start = ((), (), s32[]{:S(2)}) async-start(), calls=%async_computation.6 | async-start | bytes 4866048 | tf_op jit(solution)/shard_map/all_gather | solution.py:59
  534.2 149.3 %reduce-scatter.14.cloned.1.call-start = ((), (), s32[]{:S(2)}) async-start(), calls=%async_computation.9 | async-start | bytes 4866048 | tf_op jit(solution)/shard_map/reduce_scatter | solution.py:63
Sparse Core Ops, SparseCore 0:
  24.1 85.3 reduce-scatter.9
  112.5 48.2 all-gather.4
  179.4 48.3 all-gather.6
  252.1 80.9 reduce-scatter.11
  403.7 43.8 all-gather.8
  534.3 43.8 all-gather.10
  602.6 80.9 reduce-scatter.13
where the time goes:
time: 762 us; the launch traced here: 761 us
  waiting for transfers between devices  427 us (56%)
  blocking collectives  221 us (29%)
  matrix products  58.5 us (8%)
  local copies, waits for them, and re-layouts  26.2 us (3%)
  between operations  18.2 us (2%)
  other arithmetic  9.7 us (1%)
    reduce_scatter x2, waiting for transfers between devices, body(): lax.psum_scatter(transposed_term(activations, scaled).astype(jnp.bfloat16...  162 us
    psum x2, blocking collectives, inner_sum(): return lax.psum(jnp.sum(left * right), ('fsdp', 'fac'))  132 us
    all_gather x2, waiting for transfers between devices, precondition(): lax.all_gather(matrix_low, 'fsdp', axis=0, tiled=True)  93.4 us
    all_gather x2, waiting for transfers between devices, body(): lax.all_gather(curvature_matrix_low, 'fsdp', axis=0, tiled=True)  86.2 us
    reduce_scatter x1, waiting for transfers between devices, body(): lax.psum_scatter((transposed_term(activations, forget_grads) * grad_scale...  85.4 us
    psum x1, blocking collectives, body(): energy = lax.psum(jnp.sum(direction * image), ('fsdp', 'fac'))  65.9 us
    dot_general x3, matrix products, transposed_term(): lax.dot_general(matrix, right, (((0,), (0,)), ((), ())), preferred_elemen...  44.3 us
    all_gather x2, blocking collectives, precondition(): lax.all_gather(mixed_low, 'fac', axis=1, tiled=True)  22.6 us
  transfers between devices with their start and end apart: 7, of which 7 were waited for; matrix products, arithmetic and copies ran while one was open for 1% of the time, Pallas kernels for 0%

commit v1 on v0

--- a/solution.py
+++ b/solution.py
@@ -21,6 +21,21 @@
     )
 
 
+def scatter_sum(partial):
+    parts = lax.axis_size("fsdp")
+    blocks = partial.reshape(parts, partial.shape[0] // parts, partial.shape[1])
+    received = lax.all_to_all(blocks, "fsdp", 0, 0, tiled=False)
+    return jnp.sum(received.astype(jnp.float32), axis=0)
+
+
+def global_sums(*partials):
+    devices = lax.axis_size("fsdp") * lax.axis_size("fac")
+    stacked = jnp.broadcast_to(jnp.stack(partials)[None, :], (devices, len(partials)))
+    received = lax.all_to_all(stacked, ("fsdp", "fac"), 0, 0, tiled=True)
+    total = jnp.sum(received, axis=0)
+    return tuple(total[i] for i in range(len(partials)))
+
+
 def body(activations, out_grads, token_ids, forget_mask, importance, in_inverse, out_inverse):
     tok_rows = activations.shape[0]
     total = tok_rows * lax.axis_size("fsdp")
@@ -28,12 +43,9 @@
     weights = importance[token_ids] * keep / total
     forget_grads = out_grads * forget_mask.astype(jnp.bfloat16)[:, None]
     grad_scale = 1.0 / math.sqrt(total)
-    gradient = lax.psum_scatter(
-        (transposed_term(activations, forget_grads) * grad_scale).astype(jnp.bfloat16),
-        "fsdp",
-        scatter_dimension=0,
-        tiled=True,
-    ).astype(jnp.float32)
+    gradient = scatter_sum(
+        (transposed_term(activations, forget_grads) * grad_scale).astype(jnp.bfloat16)
+    )
 
     def precondition(matrix):
         matrix_low = matrix.astype(jnp.bfloat16)
@@ -45,14 +57,14 @@
             preferred_element_type=jnp.float32,
         )
 
-    def inner_sum(left, right):
-        return lax.psum(jnp.sum(left * right), ("fsdp", "fac"))
+    def inner_part(left, right):
+        return jnp.sum(left * right)
 
     newton_step = jnp.zeros(gradient.shape, jnp.float32)
     residual = -gradient
     precond = precondition(residual)
     direction = precond
-    inner_now = inner_sum(residual, precond)
+    inner_part_now = inner_part(residual, precond)
     for iteration in range(ITERS):
         curvature_matrix_low = direction.astype(jnp.bfloat16)
         tok_out = add_columns(
@@ -60,22 +72,19 @@
         )
         scaled = (tok_out * weights[:, None]).astype(jnp.bfloat16)
         image = (
-            lax.psum_scatter(
-                transposed_term(activations, scaled).astype(jnp.bfloat16),
-                "fsdp",
-                scatter_dimension=0,
-                tiled=True,
-            ).astype(jnp.float32)
+            scatter_sum(transposed_term(activations, scaled).astype(jnp.bfloat16))
             + damping * direction
         )
-        energy = lax.psum(jnp.sum(direction * image), ("fsdp", "fac"))
-        image, energy = (image, energy)
+        if iteration == 0:
+            inner_now, energy = global_sums(inner_part_now, inner_part(direction, image))
+        else:
+            (energy,) = global_sums(inner_part(direction, image))
         alpha = inner_now / energy
         newton_step = newton_step + alpha * direction
         residual = residual - alpha * image
         if iteration + 1 < ITERS:
             precond = precondition(residual)
-            inner_next = inner_sum(residual, precond)
+            (inner_next,) = global_sums(inner_part(residual, precond))
             direction = precond + inner_next / inner_now * direction
             inner_now = inner_next
     return (newton_step, residual)

time: 762 us -> 552 us (0.72)
  waiting for transfers between devices: 427 us -> 174 us
  blocking collectives: 221 us -> 262 us
    reduce_scatter x3 -> x0, waiting for transfers between devices: 248 us -> none  [the longest x2 162 us: body(): lax.psum_scatter(transposed_term(activations, scaled).astype(jnp.bfloat16...]
    all_to_all x0 -> x6, blocking collectives: none -> 239 us  [the longest x3 190 us: scatter_sum(): received = lax.all_to_all(blocks, 'fsdp', 0, 0, tiled=False)]
    psum x3 -> x0, blocking collectives: 198 us -> none  [the longest x2 132 us: inner_sum(): return lax.psum(jnp.sum(left * right), ('fsdp', 'fac'))]
    convert_element_type x0 -> x3, local copies, waits for them, and re-layouts: none -> 20.1 us  [the longest x2 13.4 us: body(): transposed_term(activations, scaled).astype(jnp.bfloat16)]
    unnamed x13 -> x8, local copies, waits for them, and re-layouts: 20.1 us -> 0.03 us
  transfers between devices with their start and end apart: 7 -> 4, of which waited for: 7 -> 4; matrix products, arithmetic and copies ran while one was open for 1% -> 1% of each run, Pallas kernels for 0% -> 0%
where the time goes in v1:
time: 552 us; the launch traced here: 551 us
  blocking collectives  262 us (47%)
  waiting for transfers between devices  174 us (32%)
  matrix products  58.3 us (11%)
  local copies, waits for them, and re-layouts  28.3 us (5%)
  between operations  17.9 us (3%)
  other arithmetic  10.1 us (2%)
    all_to_all x3, blocking collectives, scatter_sum(): received = lax.all_to_all(blocks, 'fsdp', 0, 0, tiled=False)  190 us
    all_gather x2, waiting for transfers between devices, precondition(): lax.all_gather(matrix_low, 'fsdp', axis=0, tiled=True)  88.7 us
    all_gather x2, waiting for transfers between devices, body(): lax.all_gather(curvature_matrix_low, 'fsdp', axis=0, tiled=True)  85.7 us
    all_to_all x3, blocking collectives, global_sums(): received = lax.all_to_all(stacked, ('fsdp', 'fac'), 0, 0, tiled=True)  49.5 us
    dot_general x3, matrix products, transposed_term(): lax.dot_general(matrix, right, (((0,), (0,)), ((), ())), preferred_elemen...  44.1 us
    all_gather x2, blocking collectives, precondition(): lax.all_gather(mixed_low, 'fac', axis=1, tiled=True)  22.8 us
    convert_element_type x2, local copies, waits for them, and re-layouts, body(): transposed_term(activations, scaled).astype(jnp.bfloat16)  13.4 us
  transfers between devices with their start and end apart: 4, of which 4 were waited for; matrix products, arithmetic and copies ran while one was open for 1% of the time, Pallas kernels for 0%

profile of v1, /device:TPU:1, one launch (start us, length us, event | category | flops | bytes accessed | tf_op | source)
XLA Modules:
  0.0 551.1 jit_solution(4985250210493842964)
XLA Ops:
  8.0 9.3 %fusion.2 = bf16[3072,768]{0,1:T(8,128)(2,1)} fusion(bf16[1024,3072]{1,0:T(8,128)(2,1)} %param.7, bf16[1024,768]{1,0:T(8,128)(2,1)} %param.8, bf16[1024]{0:T(1024)(128)(2,1)S(1)} %convert_element_type.65), kind=kOutput, calls=%fused_computation.9 | convolution fusion | flops 4837343232 | bytes 12584960 | tf_op jit(solution)/shard_map/dot_general | solution.py:19
  17.3 6.7 %copy.15 = bf16[3072,768]{1,0:T(8,128)(2,1)} copy(bf16[3072,768]{0,1:T(8,128)(2,1)} %fusion.2) | data formatting | bytes 9437184 | tf_op jit(solution)/shard_map/convert_element_type | solution.py:47
  24.0 66.1 %all_to_all.33 = bf16[32,96,768]{2,1,0:T(8,128)(2,1)S(1)} all-to-all(bf16[32,96,768]{2,1,0:T(8,128)(2,1)} %bitcast.50), channel_id=1, replica_groups=mesh['fsdp'=32,'fac'=4] {'fsdp'}, dimensions={0} | all-to-all | bytes 9437184 | tf_op jit(solution)/shard_map/all_to_all | solution.py:27
  91.5 45.2 %all-gather.5.cloned.1.call-done = bf16[3072,768]{1,0:T(8,128)(2,1)} async-done(((bf16[96,768]{1,0:T(8,128)(2,1)}), bf16[3072,768]{1,0:T(8,128)(2,1)}) %all-gather.5.cloned.1.call-update) | async-done | bytes 4718608 | tf_op jit(solution)/shard_map/all_gather | solution.py:52
  136.7 3.2 fusion.4
  139.9 11.4 %all_gather.19 = bf16[96,3072]{1,0:T(8,128)(2,1)S(1)} all-gather(bf16[96,768]{1,0:T(8,128)(2,1)S(1)} %fusion.4), channel_id=1, replica_groups=mesh['fsdp'=32,'fac'=4] {'fac'}, dimensions={1}, use_global_device_ids=true | all-gather | bytes 737280 | tf_op jit(solution)/shard_map/all_gather | solution.py:55
  151.3 3.9 fusion.11
  155.3 6.2 %gather_fusion = f32[1024]{0:T(1024)S(1)} fusion(f32[32768]{0:T(1024)S(1)} %copy-done.1, s32[1024]{0:T(1024)S(1)} %fusion.7), kind=kCustom, calls=%fused_computation | custom fusion | bytes 12288 | tf_op jit(solution)/shard_map/gather | solution.py:43
  161.5 42.2 %all-gather.7.cloned.1.call-done = bf16[3072,768]{1,0:T(8,128)(2,1)} async-done(((bf16[96,768]{1,0:T(8,128)(2,1)}), bf16[3072,768]{1,0:T(8,128)(2,1)}) %all-gather.7.cloned.1.call-update) | async-done | bytes 4718608 | tf_op jit(solution)/shard_map/all_gather | solution.py:71
  203.7 17.4 %fusion = bf16[3072,768]{0,1:T(8,128)(2,1)} fusion(bf16[1024,3072]{1,0:T(8,128)(2,1)} %param.7, bf16[3072,768]{1,0:T(8,128)(2,1)} %all-gather.7.cloned.1.call-done, f32[1024]{0:T(1024)S(1)} %multiply_multiply_fusion), kind=kOutput, calls=%fused_computation.7 | convolution fusion | flops 9667608576 | bytes 15732736 | tf_op jit(solution)/shard_map/dot_general | solution.py:19
  221.1 6.7 %copy.16 = bf16[3072,768]{1,0:T(8,128)(2,1)} copy(bf16[3072,768]{0,1:T(8,128)(2,1)} %fusion) | data formatting | bytes 9437184 | tf_op jit(solution)/shard_map/convert_element_type | solution.py:75
  227.8 61.8 %all_to_all.34 = bf16[32,96,768]{2,1,0:T(8,128)(2,1)S(1)} all-to-all(bf16[32,96,768]{2,1,0:T(8,128)(2,1)} %bitcast.51), channel_id=1, replica_groups=mesh['fsdp'=32,'fac'=4] {'fsdp'}, dimensions={0} | all-to-all | bytes 9437184 | tf_op jit(solution)/shard_map/all_to_all | solution.py:27
  290.9 1.4 pad_maximum_fusion
  292.3 15.4 %all_to_all.35 = f32[128,1,2]{2,1,0:T(1,128)S(1)} all-to-all(f32[128,1,2]{2,1,0:T(1,128)S(1)} %broadcast_in_dim.9), channel_id=1, replica_groups=mesh['fsdp'=32,'fac'=4] {'fsdp','fac'}, dimensions={0} | all-to-all | bytes 2048 | tf_op jit(solution)/shard_map/all_to_all | solution.py:34
  310.6 43.5 %all-gather.9.cloned.1.call-done = bf16[3072,768]{1,0:T(8,128)(2,1)} async-done(((bf16[96,768]{1,0:T(8,128)(2,1)}), bf16[3072,768]{1,0:T(8,128)(2,1)}) %all-gather.9.cloned.1.call-update) | async-done | bytes 4718608 | tf_op jit(solution)/shard_map/all_gather | solution.py:52
  354.1 3.2 fusion.5
  357.3 11.4 %all_gather.22 = bf16[96,3072]{1,0:T(8,128)(2,1)S(1)} all-gather(bf16[96,768]{1,0:T(8,128)(2,1)S(1)} %fusion.5), channel_id=1, replica_groups=mesh['fsdp'=32,'fac'=4] {'fac'}, dimensions={1}, use_global_device_ids=true | all-gather | bytes 737280 | tf_op jit(solution)/shard_map/all_gather | solution.py:55
  368.7 3.9 multiply_reduce_fusion.1
  373.3 18.6 %all_to_all.36 = f32[128,1,1]{2,1,0:T(1,128)S(1)} all-to-all(f32[128,1,1]{2,1,0:T(1,128)S(1)} %broadcast_in_dim.10), channel_id=1, replica_groups=mesh['fsdp'=32,'fac'=4] {'fsdp','fac'}, dimensions={0} | all-to-all | bytes 1024 | tf_op jit(solution)/shard_map/all_to_all | solution.py:34
  394.8 43.6 %all-gather.11.cloned.1.call-done = bf16[3072,768]{1,0:T(8,128)(2,1)} async-done(((bf16[96,768]{1,0:T(8,128)(2,1)}), bf16[3072,768]{1,0:T(8,128)(2,1)}) %all-gather.11.cloned.1.call-update) | async-done | bytes 4718608 | tf_op jit(solution)/shard_map/all_gather | solution.py:71
  438.3 17.4 %fusion.1 = bf16[3072,768]{0,1:T(8,128)(2,1)} fusion(bf16[1024,3072]{1,0:T(8,128)(2,1)} %param.7, bf16[3072,768]{1,0:T(8,128)(2,1)} %all-gather.11.cloned.1.call-done, f32[1024]{0:T(1024)S(1)} %multiply_multiply_fusion), kind=kOutput, calls=%fused_computation.8 | convolution fusion | flops 9667608576 | bytes 15732736 | tf_op jit(solution)/shard_map/dot_general | solution.py:19
  455.7 6.7 %copy.19 = bf16[3072,768]{1,0:T(8,128)(2,1)} copy(bf16[3072,768]{0,1:T(8,128)(2,1)} %fusion.1) | data formatting | bytes 9437184 | tf_op jit(solution)/shard_map/convert_element_type | solution.py:75
  462.4 61.8 %all_to_all.37 = bf16[32,96,768]{2,1,0:T(8,128)(2,1)S(1)} all-to-all(bf16[32,96,768]{2,1,0:T(8,128)(2,1)} %bitcast.52), channel_id=1, replica_groups=mesh['fsdp'=32,'fac'=4] {'fsdp'}, dimensions={0} | all-to-all | bytes 9437184 | tf_op jit(solution)/shard_map/all_to_all | solution.py:27
  526.2 15.4 %all_to_all.38 = f32[128,1,1]{2,1,0:T(1,128)S(1)} all-to-all(f32[128,1,1]{2,1,0:T(1,128)S(1)} %broadcast_in_dim.11), channel_id=1, replica_groups=mesh['fsdp'=32,'fac'=4] {'fsdp','fac'}, dimensions={0} | all-to-all | bytes 1024 | tf_op jit(solution)/shard_map/all_to_all | solution.py:34
  (35 shorter events, 11.0 us)
Async XLA Ops:
  7.2 129.5 %copy-start = (bf16[96,3072]{1,0:T(8,128)(2,1)S(1)}, bf16[96,3072]{1,0:T(8,128)(2,1)}, u32[]{:S(2)}) copy-start(bf16[96,3072]{1,0:T(8,128)(2,1)} %param.12) | copy-start | bytes 1769476
  7.2 129.5 %all-gather.5.cloned.1.call-start = ((), (), s32[]{:S(2)}) async-start(), calls=%async_computation.6 | async-start | bytes 4866048 | tf_op jit(solution)/shard_map/all_gather | solution.py:52
  91.4 63.8 %copy-start.3 = (s32[1024]{0:T(1024)S(1)}, s32[1024]{0:T(1024)}, u32[]{:S(2)}) copy-start(s32[1024]{0:T(1024)} %param.9) | copy-start | bytes 12292
  91.5 63.9 %copy-start.1 = (f32[32768]{0:T(1024)S(1)}, f32[32768]{0:T(1024)}, u32[]{:S(2)}) copy-start(f32[32768]{0:T(1024)} %param.11) | copy-start | bytes 393220
  91.5 112.2 %all-gather.7.cloned.1.call-start = ((), (), s32[]{:S(2)}) async-start(), calls=%async_computation.7 | async-start | bytes 4866048 | tf_op jit(solution)/shard_map/all_gather | solution.py:71
  151.3 10.2 %copy-start.2 = (s32[1024]{0:T(1024)S(1)}, s32[1024]{0:T(1024)}, u32[]{:S(2)}) copy-start(s32[1024]{0:T(1024)} %param.10) | copy-start | bytes 12292
  155.2 198.9 %all-gather.9.cloned.1.call-start = ((), (), s32[]{:S(2)}) async-start(), calls=%async_computation.8 | async-start | bytes 4866048 | tf_op jit(solution)/shard_map/all_gather | solution.py:52
  310.6 127.7 %all-gather.11.cloned.1.call-start = ((), (), s32[]{:S(2)}) async-start(), calls=%async_computation.9 | async-start | bytes 4866048 | tf_op jit(solution)/shard_map/all_gather | solution.py:71
Sparse Core Ops, SparseCore 0:
  91.6 45.0 all-gather.4
  155.4 48.2 all-gather.6
  310.7 43.3 all-gather.8
  394.9 43.3 all-gather.10

commit v2 on v1

--- a/solution.py
+++ b/solution.py
@@ -37,14 +37,25 @@
 
 
 def body(activations, out_grads, token_ids, forget_mask, importance, in_inverse, out_inverse):
-    tok_rows = activations.shape[0]
+    tok_rows, d_in = activations.shape
     total = tok_rows * lax.axis_size("fsdp")
     keep = 1.0 - forget_mask.astype(jnp.float32)
     weights = importance[token_ids] * keep / total
     forget_grads = out_grads * forget_mask.astype(jnp.bfloat16)[:, None]
     grad_scale = 1.0 / math.sqrt(total)
-    gradient = scatter_sum(
-        (transposed_term(activations, forget_grads) * grad_scale).astype(jnp.bfloat16)
+    d_out_part = out_grads.shape[1]
+
+    gram_cols = d_in // lax.axis_size("fac")
+    own_cols = lax.dynamic_slice_in_dim(
+        activations, lax.axis_index("fac") * gram_cols, gram_cols, axis=1
+    )
+    weighted = (own_cols * weights[:, None]).astype(jnp.bfloat16)
+    grad_part = (transposed_term(activations, forget_grads) * grad_scale).astype(jnp.bfloat16)
+    gram_part = transposed_term(activations, weighted).astype(jnp.bfloat16)
+    summed = scatter_sum(jnp.concatenate([grad_part, gram_part], axis=1))
+    gradient = summed[:, :d_out_part]
+    gram_rows = lax.all_gather(
+        summed[:, d_out_part:].astype(jnp.bfloat16), "fac", axis=1, tiled=True
     )
 
     def precondition(matrix):
@@ -57,6 +68,11 @@
             preferred_element_type=jnp.float32,
         )
 
+    def curvature(matrix):
+        matrix_low = matrix.astype(jnp.bfloat16)
+        gathered = lax.all_gather(matrix_low, "fsdp", axis=0, tiled=True)
+        return add_columns(gram_rows, gathered) + damping * matrix
+
     def inner_part(left, right):
         return jnp.sum(left * right)
 
@@ -66,15 +82,7 @@
     direction = precond
     inner_part_now = inner_part(residual, precond)
     for iteration in range(ITERS):
-        curvature_matrix_low = direction.astype(jnp.bfloat16)
-        tok_out = add_columns(
-            activations, lax.all_gather(curvature_matrix_low, "fsdp", axis=0, tiled=True)
-        )
-        scaled = (tok_out * weights[:, None]).astype(jnp.bfloat16)
-        image = (
-            scatter_sum(transposed_term(activations, scaled).astype(jnp.bfloat16))
-            + damping * direction
-        )
+        image = curvature(direction)
         if iteration == 0:
             inner_now, energy = global_sums(inner_part_now, inner_part(direction, image))
         else:

time: 552 us -> 462 us (0.84)
  blocking collectives: 262 us -> 201 us
  matrix products: 58.3 us -> 35.6 us
  local copies, waits for them, and re-layouts: 28.3 us -> 20.7 us
    all_to_all x3 -> x1, blocking collectives: 190 us -> 117 us  [scatter_sum(): received = lax.all_to_all(blocks, 'fsdp', 0, 0, tiled=False)]
    dot_general x3 -> x2, matrix products: 44.1 us -> 13.8 us  [transposed_term(): lax.dot_general(matrix, right, (((0,), (0,)), ((), ())), preferred_elemen...]
    convert_element_type x3 -> x0, local copies, waits for them, and re-layouts: 20.1 us -> none  [the longest x2 13.4 us: body(): transposed_term(activations, scaled).astype(jnp.bfloat16)]
    concatenate x0 -> x1, local copies, waits for them, and re-layouts: none -> 12.7 us  [body(): summed = scatter_sum(jnp.concatenate([grad_part, gram_part], axis=1))]
    all_gather x0 -> x1, blocking collectives: none -> 10 us  [body(): lax.all_gather(summed[:, d_out_part:].astype(jnp.bfloat16), 'fac', axis=1...]
    dot_general x2 -> x4, matrix products: 6.43 us -> 14.1 us  [add_columns(): return jnp.dot(matrix, piece, preferred_element_type=jnp.float32)]
  transfers between devices with their start and end apart: 4 -> 4, of which waited for: 4 -> 4; matrix products, arithmetic and copies ran while one was open for 1% -> 0% of each run, Pallas kernels for 0% -> 0%
where the time goes in v2:
time: 462 us; the launch traced here: 461 us
  blocking collectives  201 us (44%)
  waiting for transfers between devices  171 us (37%)
  matrix products  35.6 us (8%)
  local copies, waits for them, and re-layouts  20.7 us (4%)
  between operations  17.7 us (4%)
  other arithmetic  13.8 us (3%)
    all_to_all x1, blocking collectives, scatter_sum(): received = lax.all_to_all(blocks, 'fsdp', 0, 0, tiled=False)  117 us
    all_gather x2, waiting for transfers between devices, precondition(): lax.all_gather(matrix_low, 'fsdp', axis=0, tiled=True)  89.4 us
    all_gather x2, waiting for transfers between devices, curvature(): gathered = lax.all_gather(matrix_low, 'fsdp', axis=0, tiled=True)  81.9 us
    all_to_all x3, blocking collectives, global_sums(): received = lax.all_to_all(stacked, ('fsdp', 'fac'), 0, 0, tiled=True)  51.9 us
    all_gather x2, blocking collectives, precondition(): lax.all_gather(mixed_low, 'fac', axis=1, tiled=True)  22.8 us
    dot_general x4, matrix products, add_columns(): return jnp.dot(matrix, piece, preferred_element_type=jnp.float32)  14.1 us
    dot_general x2, matrix products, transposed_term(): lax.dot_general(matrix, right, (((0,), (0,)), ((), ())), preferred_elemen...  13.8 us
    concatenate x1, local copies, waits for them, and re-layouts, body(): summed = scatter_sum(jnp.concatenate([grad_part, gram_part], axis=1))  12.7 us
  transfers between devices with their start and end apart: 4, of which 4 were waited for; matrix products, arithmetic and copies ran while one was open for 0% of the time, Pallas kernels for 0%

profile of v2, /device:TPU:1, one launch (start us, length us, event | category | flops | bytes accessed | tf_op | source)
XLA Modules:
  0.0 460.9 jit_solution(6206840054525495741)
XLA Ops:
  8.7 5.9 %gather_fusion = f32[1024]{0:T(1024)S(1)} fusion(f32[32768]{0:T(1024)} %param.11, s32[1024]{0:T(1024)S(1)} %fusion.9), kind=kCustom, calls=%fused_computation | custom fusion | bytes 12288 | tf_op jit(solution)/shard_map/gather | solution.py:43
  15.3 8.0 %fusion = bf16[3072,768]{0,1:T(8,128)(2,1)S(1)} fusion(bf16[1024,3072]{1,0:T(8,128)(2,1)} %param.7, f32[1024]{0:T(1024)S(1)} %multiply_multiply_fusion, s32[]{:T(128)S(6)} %select_n.6), kind=kOutput, calls=%fused_computation.5 | convolution fusion | flops 4836556800 | bytes 12587012 | tf_op jit(solution)/shard_map/dot_general | solution.py:19
  23.4 5.7 %fusion.1 = bf16[3072,768]{0,1:T(8,128)(2,1)S(1)} fusion(bf16[1024,3072]{1,0:T(8,128)(2,1)S(1)} %copy-done.1, bf16[1024,768]{1,0:T(8,128)(2,1)S(1)} %copy-done.2, bf16[1024]{0:T(1024)(128)(2,1)S(1)} %convert_element_type.52), kind=kOutput, calls=%fused_computation.6 | convolution fusion | flops 4837343232 | bytes 12584960 | tf_op jit(solution)/shard_map/dot_general | solution.py:19
  29.1 4.3 pad_maximum_fusion
  33.4 12.7 %copy.11 = bf16[3072,1536]{1,0:T(8,128)(2,1)} copy(bf16[3072,1536]{0,1:T(8,128)(2,1)} %pad_maximum_fusion) | data formatting | bytes 18874368 | tf_op jit(solution)/shard_map/concatenate | solution.py:55
  46.1 116.7 %all_to_all.23 = bf16[32,96,1536]{2,1,0:T(8,128)(2,1)S(1)} all-to-all(bf16[32,96,1536]{2,1,0:T(8,128)(2,1)} %bitcast.27), channel_id=1, replica_groups=mesh['fsdp'=32,'fac'=4] {'fsdp'}, dimensions={0} | all-to-all | bytes 18874368 | tf_op jit(solution)/shard_map/all_to_all | solution.py:27
  162.8 1.5 convert_reduce_fusion
  165.0 46.1 %all-gather.5.cloned.1.call-done = bf16[3072,768]{1,0:T(8,128)(2,1)} async-done(((bf16[96,768]{1,0:T(8,128)(2,1)}), bf16[3072,768]{1,0:T(8,128)(2,1)}) %all-gather.5.cloned.1.call-update) | async-done | bytes 4718608 | tf_op jit(solution)/shard_map/all_gather | solution.py:63
  211.1 3.2 fusion.5
  214.3 11.4 %all_gather.22 = bf16[96,3072]{1,0:T(8,128)(2,1)S(1)} all-gather(bf16[96,768]{1,0:T(8,128)(2,1)S(1)} %fusion.5), channel_id=1, replica_groups=mesh['fsdp'=32,'fac'=4] {'fac'}, dimensions={1}, use_global_device_ids=true | all-gather | bytes 737280 | tf_op jit(solution)/shard_map/all_gather | solution.py:66
  225.7 3.9 fusion.14
  229.7 10.0 %all_gather.23 = bf16[96,3072]{1,0:T(8,128)(2,1)S(1)} all-gather(bf16[96,768]{1,0:T(8,128)(2,1)S(1)} %slice.29), channel_id=1, replica_groups=mesh['fsdp'=32,'fac'=4] {'fac'}, dimensions={1}, use_global_device_ids=true | all-gather | bytes 737280 | tf_op jit(solution)/shard_map/all_gather | solution.py:57
  239.7 38.4 %all-gather.7.cloned.1.call-done = bf16[3072,768]{1,0:T(8,128)(2,1)} async-done(((bf16[96,768]{1,0:T(8,128)(2,1)}), bf16[3072,768]{1,0:T(8,128)(2,1)}) %all-gather.7.cloned.1.call-update) | async-done | bytes 4718608 | tf_op jit(solution)/shard_map/all_gather | solution.py:73
  278.1 3.9 multiply_reduce_fusion.3
  281.9 1.4 pad_maximum_fusion.1
  283.3 16.6 %all_to_all.24 = f32[128,1,2]{2,1,0:T(1,128)S(1)} all-to-all(f32[128,1,2]{2,1,0:T(1,128)S(1)} %broadcast_in_dim.9), channel_id=1, replica_groups=mesh['fsdp'=32,'fac'=4] {'fsdp','fac'}, dimensions={0} | all-to-all | bytes 2048 | tf_op jit(solution)/shard_map/all_to_all | solution.py:34
  303.0 43.3 %all-gather.9.cloned.1.call-done = bf16[3072,768]{1,0:T(8,128)(2,1)} async-done(((bf16[96,768]{1,0:T(8,128)(2,1)}), bf16[3072,768]{1,0:T(8,128)(2,1)}) %all-gather.9.cloned.1.call-update) | async-done | bytes 4718608 | tf_op jit(solution)/shard_map/all_gather | solution.py:63
  346.3 3.2 fusion.6
  349.5 11.4 %all_gather.26 = bf16[96,3072]{1,0:T(8,128)(2,1)S(1)} all-gather(bf16[96,768]{1,0:T(8,128)(2,1)S(1)} %fusion.6), channel_id=1, replica_groups=mesh['fsdp'=32,'fac'=4] {'fac'}, dimensions={1}, use_global_device_ids=true | all-gather | bytes 737280 | tf_op jit(solution)/shard_map/all_gather | solution.py:66
  360.9 3.9 multiply_reduce_fusion.1
  365.5 18.7 %all_to_all.25 = f32[128,1,1]{2,1,0:T(1,128)S(1)} all-to-all(f32[128,1,1]{2,1,0:T(1,128)S(1)} %broadcast_in_dim.10), channel_id=1, replica_groups=mesh['fsdp'=32,'fac'=4] {'fsdp','fac'}, dimensions={0} | all-to-all | bytes 1024 | tf_op jit(solution)/shard_map/all_to_all | solution.py:34
  386.8 43.6 %all-gather.11.cloned.1.call-done = bf16[3072,768]{1,0:T(8,128)(2,1)} async-done(((bf16[96,768]{1,0:T(8,128)(2,1)}), bf16[3072,768]{1,0:T(8,128)(2,1)}) %all-gather.11.cloned.1.call-update) | async-done | bytes 4718608 | tf_op jit(solution)/shard_map/all_gather | solution.py:73
  430.3 3.9 multiply_reduce_fusion
  434.9 16.6 %all_to_all.26 = f32[128,1,1]{2,1,0:T(1,128)S(1)} all-to-all(f32[128,1,1]{2,1,0:T(1,128)S(1)} %broadcast_in_dim.11), channel_id=1, replica_groups=mesh['fsdp'=32,'fac'=4] {'fsdp','fac'}, dimensions={0} | all-to-all | bytes 1024 | tf_op jit(solution)/shard_map/all_to_all | solution.py:34
  (29 shorter events, 9.1 us)
Async XLA Ops:
  7.2 203.9 %copy-start = (bf16[96,3072]{1,0:T(8,128)(2,1)S(1)}, bf16[96,3072]{1,0:T(8,128)(2,1)}, u32[]{:S(2)}) copy-start(bf16[96,3072]{1,0:T(8,128)(2,1)} %param.12) | copy-start | bytes 1769476
  7.2 203.9 %all-gather.5.cloned.1.call-start = ((), (), s32[]{:S(2)}) async-start(), calls=%async_computation.4 | async-start | bytes 4866048 | tf_op jit(solution)/shard_map/all_gather | solution.py:63
  15.3 8.1 %copy-start.1 = (bf16[1024,3072]{1,0:T(8,128)(2,1)S(1)}, bf16[1024,3072]{1,0:T(8,128)(2,1)}, u32[]{:S(2)}) copy-start(bf16[1024,3072]{1,0:T(8,128)(2,1)} %param.7) | copy-start | bytes 18874372
  15.3 8.1 %copy-start.2 = (bf16[1024,768]{1,0:T(8,128)(2,1)S(1)}, bf16[1024,768]{1,0:T(8,128)(2,1)}, u32[]{:S(2)}) copy-start(bf16[1024,768]{1,0:T(8,128)(2,1)} %param.8) | copy-start | bytes 4718596
  164.9 113.1 %all-gather.7.cloned.1.call-start = ((), (), s32[]{:S(2)}) async-start(), calls=%async_computation.5 | async-start | bytes 4866048 | tf_op jit(solution)/shard_map/all_gather | solution.py:73
  229.6 116.7 %all-gather.9.cloned.1.call-start = ((), (), s32[]{:S(2)}) async-start(), calls=%async_computation.6 | async-start | bytes 4866048 | tf_op jit(solution)/shard_map/all_gather | solution.py:63
  302.7 127.6 %all-gather.11.cloned.1.call-start = ((), (), s32[]{:S(2)}) async-start(), calls=%async_computation.7 | async-start | bytes 4866048 | tf_op jit(solution)/shard_map/all_gather | solution.py:73
Sparse Core Ops, SparseCore 0:
  165.1 45.9 all-gather.4
  229.7 48.2 all-gather.6
  302.9 43.3 all-gather.8
  386.9 43.3 all-gather.10

commit v3 on v1

--- a/solution.py
+++ b/solution.py
@@ -37,12 +37,13 @@
 
 
 def body(activations, out_grads, token_ids, forget_mask, importance, in_inverse, out_inverse):
-    tok_rows = activations.shape[0]
+    tok_rows, d_in = activations.shape
     total = tok_rows * lax.axis_size("fsdp")
     keep = 1.0 - forget_mask.astype(jnp.float32)
     weights = importance[token_ids] * keep / total
     forget_grads = out_grads * forget_mask.astype(jnp.bfloat16)[:, None]
     grad_scale = 1.0 / math.sqrt(total)
+
     gradient = scatter_sum(
         (transposed_term(activations, forget_grads) * grad_scale).astype(jnp.bfloat16)
     )
@@ -60,33 +61,46 @@
     def inner_part(left, right):
         return jnp.sum(left * right)
 
-    newton_step = jnp.zeros(gradient.shape, jnp.float32)
     residual = -gradient
     precond = precondition(residual)
+
+    gram_cols = d_in // lax.axis_size("fac")
+    own_cols = lax.dynamic_slice_in_dim(
+        activations, lax.axis_index("fac") * gram_cols, gram_cols, axis=1
+    )
+    weighted = (own_cols * weights[:, None]).astype(jnp.bfloat16)
+    gram_part = transposed_term(activations, weighted).astype(jnp.bfloat16)
+    gram_rows = lax.all_gather(
+        scatter_sum(gram_part).astype(jnp.bfloat16), "fac", axis=1, tiled=True
+    )
+
+    def curvature(matrix):
+        matrix_low = matrix.astype(jnp.bfloat16)
+        gathered = lax.all_gather(matrix_low, "fsdp", axis=0, tiled=True)
+        return add_columns(gram_rows, gathered) + damping * matrix
+
     direction = precond
-    inner_part_now = inner_part(residual, precond)
-    for iteration in range(ITERS):
-        curvature_matrix_low = direction.astype(jnp.bfloat16)
-        tok_out = add_columns(
-            activations, lax.all_gather(curvature_matrix_low, "fsdp", axis=0, tiled=True)
-        )
-        scaled = (tok_out * weights[:, None]).astype(jnp.bfloat16)
-        image = (
-            scatter_sum(transposed_term(activations, scaled).astype(jnp.bfloat16))
-            + damping * direction
-        )
-        if iteration == 0:
-            inner_now, energy = global_sums(inner_part_now, inner_part(direction, image))
-        else:
-            (energy,) = global_sums(inner_part(direction, image))
-        alpha = inner_now / energy
-        newton_step = newton_step + alpha * direction
-        residual = residual - alpha * image
-        if iteration + 1 < ITERS:
-            precond = precondition(residual)
-            (inner_next,) = global_sums(inner_part(residual, precond))
-            direction = precond + inner_next / inner_now * direction
-            inner_now = inner_next
+    image = curvature(direction)
+    inner_now, energy = global_sums(inner_part(residual, precond), inner_part(direction, image))
+    alpha = inner_now / energy
+    newton_step = alpha * direction
+    residual = residual - alpha * image
+
+    precond = precondition(residual)
+    precond_image = curvature(precond)
+    inner_next, z_hz, z_hd, d_hz = global_sums(
+        inner_part(residual, precond),
+        inner_part(precond, precond_image),
+        inner_part(precond, image),
+        inner_part(direction, precond_image),
+    )
+    beta = inner_next / inner_now
+    direction = precond + beta * direction
+    image = precond_image + beta * image
+    energy = z_hz + beta * (z_hd + d_hz) + beta * beta * energy
+    alpha = inner_next / energy
+    newton_step = newton_step + alpha * direction
+    residual = residual - alpha * image
     return (newton_step, residual)
 
 

time: 552 us -> 438 us (0.79)
  blocking collectives: 262 us -> 208 us
  waiting for transfers between devices: 174 us -> 137 us
  matrix products: 58.3 us -> 40.7 us
  local copies, waits for them, and re-layouts: 28.3 us -> 20.9 us
    all_to_all x3 -> x2, blocking collectives: 190 us -> 139 us  [scatter_sum(): received = lax.all_to_all(blocks, 'fsdp', 0, 0, tiled=False)]
    all_gather x2, waiting for transfers between devices: 85.7 us -> 48.5 us  [curvature(): gathered = lax.all_gather(matrix_low, 'fsdp', axis=0, tiled=True)]
    dot_general x3 -> x2, matrix products: 44.1 us -> 18.7 us  [transposed_term(): lax.dot_general(matrix, right, (((0,), (0,)), ((), ())), preferred_elemen...]
    all_to_all x3 -> x2, blocking collectives: 49.5 us -> 33.8 us  [global_sums(): received = lax.all_to_all(stacked, ('fsdp', 'fac'), 0, 0, tiled=True)]
    all_gather x0 -> x1, blocking collectives: none -> 11.7 us  [body(): lax.all_gather(scatter_sum(gram_part).astype(jnp.bfloat16), 'fac', axis=1...]
    dot_general x2 -> x4, matrix products: 6.43 us -> 14.2 us  [add_columns(): return jnp.dot(matrix, piece, preferred_element_type=jnp.float32)]
    convert_element_type x2 -> x1, local copies, waits for them, and re-layouts: 13.4 us -> 6.72 us  [body(): gram_part = transposed_term(activations, weighted).astype(jnp.bfloat16)]
  transfers between devices with their start and end apart: 4 -> 4, of which waited for: 4 -> 3; matrix products, arithmetic and copies ran while one was open for 1% -> 6% of each run, Pallas kernels for 0% -> 0%
where the time goes in v3:
time: 438 us; the launch traced here: 437 us
  blocking collectives  208 us (47%)
  waiting for transfers between devices  137 us (31%)
  matrix products  40.7 us (9%)
  local copies, waits for them, and re-layouts  20.9 us (5%)
  between operations  19.5 us (4%)
  other arithmetic  11 us (3%)
    all_to_all x2, blocking collectives, scatter_sum(): received = lax.all_to_all(blocks, 'fsdp', 0, 0, tiled=False)  139 us
    all_gather x2, waiting for transfers between devices, precondition(): lax.all_gather(matrix_low, 'fsdp', axis=0, tiled=True)  88.7 us
    all_gather x2, waiting for transfers between devices, curvature(): gathered = lax.all_gather(matrix_low, 'fsdp', axis=0, tiled=True)  48.5 us
    all_to_all x2, blocking collectives, global_sums(): received = lax.all_to_all(stacked, ('fsdp', 'fac'), 0, 0, tiled=True)  33.8 us
    all_gather x2, blocking collectives, precondition(): lax.all_gather(mixed_low, 'fac', axis=1, tiled=True)  22.8 us
    dot_general x2, matrix products, transposed_term(): lax.dot_general(matrix, right, (((0,), (0,)), ((), ())), preferred_elemen...  18.7 us
    dot_general x4, matrix products, add_columns(): return jnp.dot(matrix, piece, preferred_element_type=jnp.float32)  14.2 us
    all_gather x1, blocking collectives, body(): lax.all_gather(scatter_sum(gram_part).astype(jnp.bfloat16), 'fac', axis=1...  11.7 us
  transfers between devices with their start and end apart: 4, of which 3 were waited for; matrix products, arithmetic and copies ran while one was open for 6% of the time, Pallas kernels for 0%

profile of v3, /device:TPU:1, one launch (start us, length us, event | category | flops | bytes accessed | tf_op | source)
XLA Modules:
  0.0 437.1 jit_solution(545364215922132036)
XLA Ops:
  8.0 9.3 %fusion.1 = bf16[3072,768]{0,1:T(8,128)(2,1)} fusion(bf16[1024,3072]{1,0:T(8,128)(2,1)} %param.7, bf16[1024,768]{1,0:T(8,128)(2,1)} %param.8, bf16[1024]{0:T(1024)(128)(2,1)S(1)} %convert_element_type.53), kind=kOutput, calls=%fused_computation.5 | convolution fusion | flops 4837343232 | bytes 12584960 | tf_op jit(solution)/shard_map/dot_general | solution.py:19
  17.3 6.7 %copy.13 = bf16[3072,768]{1,0:T(8,128)(2,1)} copy(bf16[3072,768]{0,1:T(8,128)(2,1)} %fusion.1) | data formatting | bytes 9437184 | tf_op jit(solution)/shard_map/convert_element_type | solution.py:48
  24.0 66.1 %all_to_all.22 = bf16[32,96,768]{2,1,0:T(8,128)(2,1)S(1)} all-to-all(bf16[32,96,768]{2,1,0:T(8,128)(2,1)} %bitcast.35), channel_id=1, replica_groups=mesh['fsdp'=32,'fac'=4] {'fsdp'}, dimensions={0} | all-to-all | bytes 9437184 | tf_op jit(solution)/shard_map/all_to_all | solution.py:27
  91.5 45.2 %all-gather.5.cloned.1.call-done = bf16[3072,768]{1,0:T(8,128)(2,1)} async-done(((bf16[96,768]{1,0:T(8,128)(2,1)}), bf16[3072,768]{1,0:T(8,128)(2,1)}) %all-gather.5.cloned.1.call-update) | async-done | bytes 4718608 | tf_op jit(solution)/shard_map/all_gather | solution.py:53
  136.7 3.2 fusion.5
  139.9 11.4 %all_gather.22 = bf16[96,3072]{1,0:T(8,128)(2,1)S(1)} all-gather(bf16[96,768]{1,0:T(8,128)(2,1)S(1)} %fusion.5), channel_id=1, replica_groups=mesh['fsdp'=32,'fac'=4] {'fac'}, dimensions={1}, use_global_device_ids=true | all-gather | bytes 737280 | tf_op jit(solution)/shard_map/all_gather | solution.py:56
  151.3 3.9 fusion.13
  155.3 6.2 %gather_fusion = f32[1024]{0:T(1024)S(1)} fusion(f32[32768]{0:T(1024)S(1)} %copy-done.1, s32[1024]{0:T(1024)S(1)} %fusion.9), kind=kCustom, calls=%fused_computation | custom fusion | bytes 12288 | tf_op jit(solution)/shard_map/gather | solution.py:43
  161.5 9.4 %fusion = bf16[3072,768]{0,1:T(8,128)(2,1)} fusion(bf16[1024,3072]{1,0:T(8,128)(2,1)} %param.7, f32[1024]{0:T(1024)S(1)} %multiply_multiply_fusion, s32[]{:T(128)S(6)} %select_n.6), kind=kOutput, calls=%fused_computation.4 | convolution fusion | flops 4836556800 | bytes 12587012 | tf_op jit(solution)/shard_map/dot_general | solution.py:19
  170.9 6.7 %copy.14 = bf16[3072,768]{1,0:T(8,128)(2,1)} copy(bf16[3072,768]{0,1:T(8,128)(2,1)} %fusion) | data formatting | bytes 9437184 | tf_op jit(solution)/shard_map/convert_element_type | solution.py:72
  177.6 73.2 %all_to_all.23 = bf16[32,96,768]{2,1,0:T(8,128)(2,1)} all-to-all(bf16[32,96,768]{2,1,0:T(8,128)(2,1)} %bitcast.36), channel_id=1, replica_groups=mesh['fsdp'=32,'fac'=4] {'fsdp'}, dimensions={0} | all-to-all | bytes 9437184 | tf_op jit(solution)/shard_map/all_to_all | solution.py:27
  250.8 3.0 reduce_sum.95
  253.9 11.7 %all_gather.23 = bf16[96,3072]{1,0:T(8,128)(2,1)S(1)} all-gather(bf16[96,768]{1,0:T(8,128)(2,1)S(1)} %reduce_sum.95), channel_id=1, replica_groups=mesh['fsdp'=32,'fac'=4] {'fac'}, dimensions={1}, use_global_device_ids=true | all-gather | bytes 737280 | tf_op jit(solution)/shard_map/all_gather | solution.py:73
  265.6 3.9 multiply_reduce_fusion.5
  269.5 1.4 pad_maximum_fusion
  270.9 17.2 %all_to_all.24 = f32[128,1,2]{2,1,0:T(1,128)S(1)} all-to-all(f32[128,1,2]{2,1,0:T(1,128)S(1)} %broadcast_in_dim.7), channel_id=1, replica_groups=mesh['fsdp'=32,'fac'=4] {'fsdp','fac'}, dimensions={0} | all-to-all | bytes 2048 | tf_op jit(solution)/shard_map/all_to_all | solution.py:34
  290.8 43.5 %all-gather.9.cloned.1.call-done = bf16[3072,768]{1,0:T(8,128)(2,1)} async-done(((bf16[96,768]{1,0:T(8,128)(2,1)}), bf16[3072,768]{1,0:T(8,128)(2,1)}) %all-gather.9.cloned.1.call-update) | async-done | bytes 4718608 | tf_op jit(solution)/shard_map/all_gather | solution.py:53
  334.3 3.2 fusion.6
  337.5 11.4 %all_gather.26 = bf16[96,3072]{1,0:T(8,128)(2,1)S(1)} all-gather(bf16[96,768]{1,0:T(8,128)(2,1)S(1)} %fusion.6), channel_id=1, replica_groups=mesh['fsdp'=32,'fac'=4] {'fac'}, dimensions={1}, use_global_device_ids=true | all-gather | bytes 737280 | tf_op jit(solution)/shard_map/all_gather | solution.py:56
  348.9 3.9 fusion.14
  352.8 48.5 %all-gather.11.cloned.1.call-done = bf16[3072,768]{1,0:T(8,128)(2,1)} async-done(((bf16[96,768]{1,0:T(8,128)(2,1)}), bf16[3072,768]{1,0:T(8,128)(2,1)}) %all-gather.11.cloned.1.call-update) | async-done | bytes 4718608 | tf_op jit(solution)/shard_map/all_gather | solution.py:79
  401.3 3.9 multiply_reduce_fusion.3
  405.2 2.6 pad_maximum_fusion.1
  407.8 16.6 %all_to_all.25 = f32[128,1,4]{2,1,0:T(1,128)S(1)} all-to-all(f32[128,1,4]{2,1,0:T(1,128)S(1)} %broadcast_in_dim.8), channel_id=1, replica_groups=mesh['fsdp'=32,'fac'=4] {'fsdp','fac'}, dimensions={0} | all-to-all | bytes 4096 | tf_op jit(solution)/shard_map/all_to_all | solution.py:34
  (30 shorter events, 5.6 us)
Async XLA Ops:
  7.2 129.5 %copy-start = (bf16[96,3072]{1,0:T(8,128)(2,1)S(1)}, bf16[96,3072]{1,0:T(8,128)(2,1)}, u32[]{:S(2)}) copy-start(bf16[96,3072]{1,0:T(8,128)(2,1)} %param.12) | copy-start | bytes 1769476
  7.2 129.5 %all-gather.5.cloned.1.call-start = ((), (), s32[]{:S(2)}) async-start(), calls=%async_computation.4 | async-start | bytes 4866048 | tf_op jit(solution)/shard_map/all_gather | solution.py:53
  91.4 63.8 %copy-start.3 = (s32[1024]{0:T(1024)S(1)}, s32[1024]{0:T(1024)}, u32[]{:S(2)}) copy-start(s32[1024]{0:T(1024)} %param.9) | copy-start | bytes 12292
  91.5 63.9 %copy-start.1 = (f32[32768]{0:T(1024)S(1)}, f32[32768]{0:T(1024)}, u32[]{:S(2)}) copy-start(f32[32768]{0:T(1024)} %param.11) | copy-start | bytes 393220
  91.5 174.1 %all-gather.7.cloned.1.call-start = ((), (), s32[]{:S(2)}) async-start(), calls=%async_computation.5 | async-start | bytes 4866048 | tf_op jit(solution)/shard_map/all_gather | solution.py:79
  151.3 10.2 %copy-start.2 = (s32[1024]{0:T(1024)S(1)}, s32[1024]{0:T(1024)}, u32[]{:S(2)}) copy-start(s32[1024]{0:T(1024)} %param.10) | copy-start | bytes 12292
  155.2 179.1 %all-gather.9.cloned.1.call-start = ((), (), s32[]{:S(2)}) async-start(), calls=%async_computation.6 | async-start | bytes 4866048 | tf_op jit(solution)/shard_map/all_gather | solution.py:53
  290.7 110.5 %all-gather.11.cloned.1.call-start = ((), (), s32[]{:S(2)}) async-start(), calls=%async_computation.7 | async-start | bytes 4866048 | tf_op jit(solution)/shard_map/all_gather | solution.py:79
Sparse Core Ops, SparseCore 0:
  91.6 45.0 all-gather.4
  155.4 85.9 all-gather.6
  290.9 43.3 all-gather.8
  352.9 48.2 all-gather.10

commit v4 on v3

--- a/solution.py
+++ b/solution.py
@@ -48,9 +48,11 @@
         (transposed_term(activations, forget_grads) * grad_scale).astype(jnp.bfloat16)
     )
 
-    def precondition(matrix):
-        matrix_low = matrix.astype(jnp.bfloat16)
-        mixed = add_columns(in_inverse, lax.all_gather(matrix_low, "fsdp", axis=0, tiled=True))
+    def gather_rows(matrix):
+        return lax.all_gather(matrix.astype(jnp.bfloat16), "fsdp", axis=0, tiled=True)
+
+    def precondition(gathered):
+        mixed = add_columns(in_inverse, gathered)
         mixed_low = mixed.astype(jnp.bfloat16)
         return jnp.dot(
             lax.all_gather(mixed_low, "fac", axis=1, tiled=True),
@@ -62,7 +64,7 @@
         return jnp.sum(left * right)
 
     residual = -gradient
-    precond = precondition(residual)
+    residual_rows = gather_rows(residual)
 
     gram_cols = d_in // lax.axis_size("fac")
     own_cols = lax.dynamic_slice_in_dim(
@@ -70,23 +72,27 @@
     )
     weighted = (own_cols * weights[:, None]).astype(jnp.bfloat16)
     gram_part = transposed_term(activations, weighted).astype(jnp.bfloat16)
+    residual_rows, gram_part = lax.optimization_barrier((residual_rows, gram_part))
+    precond = precondition(residual_rows)
     gram_rows = lax.all_gather(
         scatter_sum(gram_part).astype(jnp.bfloat16), "fac", axis=1, tiled=True
     )
 
     def curvature(matrix):
-        matrix_low = matrix.astype(jnp.bfloat16)
-        gathered = lax.all_gather(matrix_low, "fsdp", axis=0, tiled=True)
-        return add_columns(gram_rows, gathered) + damping * matrix
+        return add_columns(gram_rows, gather_rows(matrix)) + damping * matrix
 
     direction = precond
     image = curvature(direction)
+    image_rows = gather_rows(image)
     inner_now, energy = global_sums(inner_part(residual, precond), inner_part(direction, image))
     alpha = inner_now / energy
     newton_step = alpha * direction
     residual = residual - alpha * image
+    next_rows = (
+        residual_rows.astype(jnp.float32) - alpha * image_rows.astype(jnp.float32)
+    ).astype(jnp.bfloat16)
 
-    precond = precondition(residual)
+    precond = precondition(next_rows)
     precond_image = curvature(precond)
     inner_next, z_hz, z_hd, d_hz = global_sums(
         inner_part(residual, precond),

time: 438 us -> 409 us (0.934)
  waiting for transfers between devices: 137 us -> 105 us
    all_gather x4, waiting for transfers between devices: 137 us -> 105 us  [gather_rows(): lax.all_gather(matrix.astype(jnp.bfloat16), 'fsdp', axis=0, tiled=True)]
    convert_element_type x1 -> x0, local copies, waits for them, and re-layouts: 6.72 us -> none  [body(): gram_part = transposed_term(activations, weighted).astype(jnp.bfloat16)]
    optimization_barrier x0 -> x1, local copies, waits for them, and re-layouts: none -> 6.71 us  [body(): lax.optimization_barrier((residual_rows, gram_part))]
  transfers between devices with their start and end apart: 4 -> 4, of which waited for: 3 -> 3; matrix products, arithmetic and copies ran while one was open for 6% -> 7% of each run, Pallas kernels for 0% -> 0%
where the time goes in v4:
time: 409 us; the launch traced here: 408 us
  blocking collectives  209 us (51%)
  waiting for transfers between devices  105 us (26%)
  matrix products  43.7 us (11%)
  local copies, waits for them, and re-layouts  20.9 us (5%)
  between operations  19.7 us (5%)
  other arithmetic  10.3 us (3%)
    all_to_all x2, blocking collectives, scatter_sum(): received = lax.all_to_all(blocks, 'fsdp', 0, 0, tiled=False)  140 us
    all_gather x4, waiting for transfers between devices, gather_rows(): lax.all_gather(matrix.astype(jnp.bfloat16), 'fsdp', axis=0, tiled=True)  105 us
    all_to_all x2, blocking collectives, global_sums(): received = lax.all_to_all(stacked, ('fsdp', 'fac'), 0, 0, tiled=True)  34.4 us
    all_gather x2, blocking collectives, precondition(): lax.all_gather(mixed_low, 'fac', axis=1, tiled=True)  22.7 us
    dot_general x2, matrix products, transposed_term(): lax.dot_general(matrix, right, (((0,), (0,)), ((), ())), preferred_elemen...  18.8 us
    dot_general x4, matrix products, add_columns(): return jnp.dot(matrix, piece, preferred_element_type=jnp.float32)  17.2 us
    all_gather x1, blocking collectives, body(): lax.all_gather(scatter_sum(gram_part).astype(jnp.bfloat16), 'fac', axis=1...  11.3 us
  transfers between devices with their start and end apart: 4, of which 3 were waited for; matrix products, arithmetic and copies ran while one was open for 7% of the time, Pallas kernels for 0%

profile of v4, /device:TPU:1, one launch (start us, length us, event | category | flops | bytes accessed | tf_op | source)
XLA Modules:
  0.0 408.1 jit_solution(8710928332919497214)
XLA Ops:
  8.0 9.3 %fusion.3 = bf16[3072,768]{0,1:T(8,128)(2,1)} fusion(bf16[1024,3072]{1,0:T(8,128)(2,1)} %param.7, bf16[1024,768]{1,0:T(8,128)(2,1)} %param.8, bf16[1024]{0:T(1024)(128)(2,1)S(1)} %convert_element_type.62), kind=kOutput, calls=%fused_computation.8 | convolution fusion | flops 4837343232 | bytes 12584960 | tf_op jit(solution)/shard_map/dot_general | solution.py:19
  17.3 6.7 %copy.13 = bf16[3072,768]{1,0:T(8,128)(2,1)} copy(bf16[3072,768]{0,1:T(8,128)(2,1)} %fusion.3) | data formatting | bytes 9437184 | tf_op jit(solution)/shard_map/convert_element_type | solution.py:48
  24.0 66.1 %all_to_all.22 = bf16[32,96,768]{2,1,0:T(8,128)(2,1)S(1)} all-to-all(bf16[32,96,768]{2,1,0:T(8,128)(2,1)} %bitcast.34), channel_id=1, replica_groups=mesh['fsdp'=32,'fac'=4] {'fsdp'}, dimensions={0} | all-to-all | bytes 9437184 | tf_op jit(solution)/shard_map/all_to_all | solution.py:27
  91.5 6.2 %gather_fusion = f32[1024]{0:T(1024)S(1)} fusion(f32[32768]{0:T(1024)S(1)} %copy-done.1, s32[1024]{0:T(1024)S(1)} %fusion.11), kind=kCustom, calls=%fused_computation | custom fusion | bytes 12288 | tf_op jit(solution)/shard_map/gather | solution.py:43
  97.7 9.5 %fusion.2 = bf16[3072,768]{0,1:T(8,128)(2,1)} fusion(bf16[1024,3072]{1,0:T(8,128)(2,1)} %param.7, f32[1024]{0:T(1024)S(1)} %multiply_multiply_fusion, s32[]{:T(128)S(6)} %select_n.6), kind=kOutput, calls=%fused_computation.7 | convolution fusion | flops 4836556800 | bytes 12587012 | tf_op jit(solution)/shard_map/dot_general | solution.py:19
  107.2 29.5 %all-gather.5.cloned.1.call-done = bf16[3072,768]{1,0:T(8,128)(2,1)} async-done(((bf16[96,768]{1,0:T(8,128)(2,1)}), bf16[3072,768]{1,0:T(8,128)(2,1)}) %all-gather.5.cloned.1.call-update) | async-done | bytes 4718608 | tf_op jit(solution)/shard_map/all_gather | solution.py:52
  136.7 3.2 fusion.8
  139.9 11.4 %all_gather.22 = bf16[96,3072]{1,0:T(8,128)(2,1)S(1)} all-gather(bf16[96,768]{1,0:T(8,128)(2,1)S(1)} %fusion.8), channel_id=1, replica_groups=mesh['fsdp'=32,'fac'=4] {'fac'}, dimensions={1}, use_global_device_ids=true | all-gather | bytes 737280 | tf_op jit(solution)/shard_map/all_gather | solution.py:58
  151.3 3.9 fusion.15
  155.3 6.7 %copy.14 = bf16[3072,768]{1,0:T(8,128)(2,1)} copy(bf16[3072,768]{0,1:T(8,128)(2,1)} %fusion.2) | data formatting | bytes 9437184 | tf_op jit(solution)/shard_map/optimization_barrier | solution.py:75
  162.0 74.3 %all_to_all.23 = bf16[32,96,768]{2,1,0:T(8,128)(2,1)} all-to-all(bf16[32,96,768]{2,1,0:T(8,128)(2,1)} %bitcast.35), channel_id=1, replica_groups=mesh['fsdp'=32,'fac'=4] {'fsdp'}, dimensions={0} | all-to-all | bytes 9437184 | tf_op jit(solution)/shard_map/all_to_all | solution.py:27
  236.2 3.0 reduce_sum.95
  239.3 11.3 %all_gather.23 = bf16[96,3072]{1,0:T(8,128)(2,1)S(1)} all-gather(bf16[96,768]{1,0:T(8,128)(2,1)S(1)} %reduce_sum.95), channel_id=1, replica_groups=mesh['fsdp'=32,'fac'=4] {'fac'}, dimensions={1}, use_global_device_ids=true | all-gather | bytes 737280 | tf_op jit(solution)/shard_map/all_gather | solution.py:77
  250.6 4.5 %multiply_reduce_fusion.5 = (f32[]{:T(128)}, f32[]{:T(128)}, bf16[96,768]{1,0:T(8,128)(2,1)}, f32[96,768]{1,0:T(8,128)S(1)}) fusion(f32[96,768]{1,0:T(8,128)S(1)} %get-tuple-element.20, f32[96,768]{1,0:T(8,128)S(1)} %convert_reduce_fusion, bf16[96,3072]{1,0:T(8,128)(2,1)S(1)} %all_gather.23, bf16[3072,768]{1,0:T(8,128)(2,1)} %all-gather.7.cloned.1.call-done), kind=kOutput, calls=%fused_computation.28 | convolution fusion | flops 453574656 | bytes 6340616 | tf_op jit(solution)/shard_map/dot_general | solution.py:15
  255.2 1.3 pad_maximum_fusion
  256.6 17.8 %all_to_all.24 = f32[128,1,2]{2,1,0:T(1,128)S(1)} all-to-all(f32[128,1,2]{2,1,0:T(1,128)S(1)} %broadcast_in_dim.7), channel_id=1, replica_groups=mesh['fsdp'=32,'fac'=4] {'fsdp','fac'}, dimensions={0} | all-to-all | bytes 2048 | tf_op jit(solution)/shard_map/all_to_all | solution.py:34
  276.4 26.5 %all-gather.9.cloned.1.call-done = bf16[3072,768]{1,0:T(8,128)(2,1)} async-done(((bf16[96,768]{1,0:T(8,128)(2,1)}), bf16[3072,768]{1,0:T(8,128)(2,1)}) %all-gather.9.cloned.1.call-update) | async-done | bytes 4718608 | tf_op jit(solution)/shard_map/all_gather | solution.py:52
  302.9 5.5 %fusion.9 = bf16[96,768]{1,0:T(8,128)(2,1)S(1)} fusion(bf16[96,3072]{1,0:T(8,128)(2,1)S(1)} %copy-done, bf16[3072,768]{1,0:T(8,128)(2,1)} %all-gather.9.cloned.1.call-done, bf16[3072,768]{1,0:T(8,128)(2,1)} %all-gather.5.cloned.1.call-done, f32[]{:T(128)S(6)} %div.17), kind=kOutput, calls=%fused_computation.18 | convolution fusion | flops 464855040 | bytes 10174468 | tf_op jit(solution)/shard_map/dot_general | solution.py:15
  308.4 11.3 %all_gather.26 = bf16[96,3072]{1,0:T(8,128)(2,1)S(1)} all-gather(bf16[96,768]{1,0:T(8,128)(2,1)S(1)} %fusion.9), channel_id=1, replica_groups=mesh['fsdp'=32,'fac'=4] {'fac'}, dimensions={1}, use_global_device_ids=true | all-gather | bytes 737280 | tf_op jit(solution)/shard_map/all_gather | solution.py:58
  319.7 3.9 fusion.16
  323.6 48.6 %all-gather.11.cloned.1.call-done = bf16[3072,768]{1,0:T(8,128)(2,1)} async-done(((bf16[96,768]{1,0:T(8,128)(2,1)}), bf16[3072,768]{1,0:T(8,128)(2,1)}) %all-gather.11.cloned.1.call-update) | async-done | bytes 4718608 | tf_op jit(solution)/shard_map/all_gather | solution.py:52
  372.2 3.9 multiply_reduce_fusion.3
  376.1 2.6 pad_maximum_fusion.1
  378.7 16.6 %all_to_all.25 = f32[128,1,4]{2,1,0:T(1,128)S(1)} all-to-all(f32[128,1,4]{2,1,0:T(1,128)S(1)} %broadcast_in_dim.8), channel_id=1, replica_groups=mesh['fsdp'=32,'fac'=4] {'fsdp','fac'}, dimensions={0} | all-to-all | bytes 4096 | tf_op jit(solution)/shard_map/all_to_all | solution.py:34
  (29 shorter events, 4.9 us)
Async XLA Ops:
  7.2 129.6 %copy-start = (bf16[96,3072]{1,0:T(8,128)(2,1)S(1)}, bf16[96,3072]{1,0:T(8,128)(2,1)}, u32[]{:S(2)}) copy-start(bf16[96,3072]{1,0:T(8,128)(2,1)} %param.12) | copy-start | bytes 1769476
  7.2 129.5 %all-gather.5.cloned.1.call-start = ((), (), s32[]{:S(2)}) async-start(), calls=%async_computation.4 | async-start | bytes 4866048 | tf_op jit(solution)/shard_map/all_gather | solution.py:52
  90.1 1.4 copy-start.3
  90.1 1.4 copy-start.1
  90.1 7.6 %copy-start.2 = (s32[1024]{0:T(1024)S(1)}, s32[1024]{0:T(1024)}, u32[]{:S(2)}) copy-start(s32[1024]{0:T(1024)} %param.10) | copy-start | bytes 12292
  91.5 159.1 %all-gather.7.cloned.1.call-start = ((), (), s32[]{:S(2)}) async-start(), calls=%async_computation.5 | async-start | bytes 4866048 | tf_op jit(solution)/shard_map/all_gather | solution.py:52
  155.2 147.7 %all-gather.9.cloned.1.call-start = ((), (), s32[]{:S(2)}) async-start(), calls=%async_computation.6 | async-start | bytes 4866048 | tf_op jit(solution)/shard_map/all_gather | solution.py:52
  255.2 117.0 %all-gather.11.cloned.1.call-start = ((), (), s32[]{:S(2)}) async-start(), calls=%async_computation.7 | async-start | bytes 4866048 | tf_op jit(solution)/shard_map/all_gather | solution.py:52
Sparse Core Ops, SparseCore 0:
  91.6 45.0 all-gather.4
  155.3 80.5 all-gather.6
  255.3 47.5 all-gather.8
  323.7 48.3 all-gather.10

commit v5 on v4

--- a/solution.py
+++ b/solution.py
@@ -25,7 +25,7 @@
     parts = lax.axis_size("fsdp")
     blocks = partial.reshape(parts, partial.shape[0] // parts, partial.shape[1])
     received = lax.all_to_all(blocks, "fsdp", 0, 0, tiled=False)
-    return jnp.sum(received.astype(jnp.float32), axis=0)
+    return lax.optimization_barrier(jnp.sum(received.astype(jnp.float32), axis=0))
 
 
 def global_sums(*partials):
@@ -71,12 +71,13 @@
         activations, lax.axis_index("fac") * gram_cols, gram_cols, axis=1
     )
     weighted = (own_cols * weights[:, None]).astype(jnp.bfloat16)
-    gram_part = transposed_term(activations, weighted).astype(jnp.bfloat16)
-    residual_rows, gram_part = lax.optimization_barrier((residual_rows, gram_part))
+    half = gram_cols // 2
+    gram_first = transposed_term(activations, weighted[:, :half]).astype(jnp.bfloat16)
+    gram_second = transposed_term(activations, weighted[:, half:]).astype(jnp.bfloat16)
+    residual_rows, first_rows = lax.optimization_barrier((residual_rows, scatter_sum(gram_first)))
     precond = precondition(residual_rows)
-    gram_rows = lax.all_gather(
-        scatter_sum(gram_part).astype(jnp.bfloat16), "fac", axis=1, tiled=True
-    )
+    gram_own = jnp.concatenate([first_rows, scatter_sum(gram_second)], axis=1)
+    gram_rows = lax.all_gather(gram_own.astype(jnp.bfloat16), "fac", axis=1, tiled=True)
 
     def curvature(matrix):
         return add_columns(gram_rows, gather_rows(matrix)) + damping * matrix

time: 409 us -> 395 us (0.966)
  waiting for transfers between devices: 105 us -> 75.1 us
  blocking collectives: 209 us -> 219 us
  matrix products: 43.7 us -> 48.1 us
    all_gather x4, waiting for transfers between devices: 105 us -> 75 us  [gather_rows(): lax.all_gather(matrix.astype(jnp.bfloat16), 'fsdp', axis=0, tiled=True)]
    all_to_all x2 -> x3, blocking collectives: 140 us -> 152 us  [scatter_sum(): received = lax.all_to_all(blocks, 'fsdp', 0, 0, tiled=False)]
    optimization_barrier x1 -> x0, local copies, waits for them, and re-layouts: 6.71 us -> none  [body(): lax.optimization_barrier((residual_rows, gram_part))]
    convert_element_type x0 -> x2, local copies, waits for them, and re-layouts: none -> 6.02 us  [the longest x1 3.01 us: body(): transposed_term(activations, weighted[:, half:]).astype(jnp.bfloat16)]
    dot_general x2 -> x3, matrix products: 18.8 us -> 23 us  [transposed_term(): lax.dot_general(matrix, right, (((0,), (0,)), ((), ())), preferred_elemen...]
  transfers between devices with their start and end apart: 4 -> 4, of which waited for: 3 -> 2; matrix products, arithmetic and copies ran while one was open for 7% -> 8% of each run, Pallas kernels for 0% -> 0%
where the time goes in v5:
time: 395 us; the launch traced here: 394 us
  blocking collectives  219 us (55%)
  waiting for transfers between devices  75.1 us (19%)
  matrix products  48.1 us (12%)
  local copies, waits for them, and re-layouts  21.4 us (5%)
  between operations  19.7 us (5%)
  other arithmetic  10.3 us (3%)
    all_to_all x3, blocking collectives, scatter_sum(): received = lax.all_to_all(blocks, 'fsdp', 0, 0, tiled=False)  152 us
    all_gather x4, waiting for transfers between devices, gather_rows(): lax.all_gather(matrix.astype(jnp.bfloat16), 'fsdp', axis=0, tiled=True)  75 us
    all_to_all x2, blocking collectives, global_sums(): received = lax.all_to_all(stacked, ('fsdp', 'fac'), 0, 0, tiled=True)  33 us
    dot_general x3, matrix products, transposed_term(): lax.dot_general(matrix, right, (((0,), (0,)), ((), ())), preferred_elemen...  23 us
    all_gather x2, blocking collectives, precondition(): lax.all_gather(mixed_low, 'fac', axis=1, tiled=True)  22.7 us
    dot_general x4, matrix products, add_columns(): return jnp.dot(matrix, piece, preferred_element_type=jnp.float32)  17.3 us
    all_gather x1, blocking collectives, body(): lax.all_gather(gram_own.astype(jnp.bfloat16), 'fac', axis=1, tiled=True)  12 us
  transfers between devices with their start and end apart: 4, of which 2 were waited for; matrix products, arithmetic and copies ran while one was open for 8% of the time, Pallas kernels for 0%

profile of v5, /device:TPU:1, one launch (start us, length us, event | category | flops | bytes accessed | tf_op | source)
XLA Modules:
  0.0 394.4 jit_solution(3237199469966427775)
XLA Ops:
  8.0 9.3 %fusion.2 = bf16[3072,768]{0,1:T(8,128)(2,1)} fusion(bf16[1024,3072]{1,0:T(8,128)(2,1)} %param.7, bf16[1024,768]{1,0:T(8,128)(2,1)} %param.8, bf16[1024]{0:T(1024)(128)(2,1)S(1)} %convert_element_type.73), kind=kOutput, calls=%fused_computation.8 | convolution fusion | flops 4837343232 | bytes 12584960 | tf_op jit(solution)/shard_map/dot_general | solution.py:19
  17.3 6.7 %copy.15 = bf16[3072,768]{1,0:T(8,128)(2,1)} copy(bf16[3072,768]{0,1:T(8,128)(2,1)} %fusion.2) | data formatting | bytes 9437184 | tf_op jit(solution)/shard_map/convert_element_type | solution.py:48
  24.0 66.1 %all_to_all.27 = bf16[32,96,768]{2,1,0:T(8,128)(2,1)S(1)} all-to-all(bf16[32,96,768]{2,1,0:T(8,128)(2,1)} %bitcast.38), channel_id=1, replica_groups=mesh['fsdp'=32,'fac'=4] {'fsdp'}, dimensions={0} | all-to-all | bytes 9437184 | tf_op jit(solution)/shard_map/all_to_all | solution.py:27
  91.5 6.2 %gather_fusion = f32[1024]{0:T(1024)S(1)} fusion(f32[32768]{0:T(1024)S(1)} %copy-done.1, s32[1024]{0:T(1024)S(1)} %fusion.12), kind=kCustom, calls=%fused_computation | custom fusion | bytes 12288 | tf_op jit(solution)/shard_map/gather | solution.py:43
  100.7 6.9 %fusion.3 = bf16[3072,384]{0,1:T(8,128)(2,1)} fusion(bf16[1024,3072]{1,0:T(8,128)(2,1)} %param.7, bf16[1024,768]{1,0:T(8,128)(2,1)S(1)} %multiply_convert_fusion.1), kind=kOutput, calls=%fused_computation.11 | convolution fusion | flops 2417098752 | bytes 9437184 | tf_op jit(solution)/shard_map/dot_general | solution.py:19
  107.6 3.0 copy.16
  110.6 44.8 %all_to_all.28 = bf16[32,96,384]{2,1,0:T(8,128)(2,1)S(1)} all-to-all(bf16[32,96,384]{2,1,0:T(8,128)(2,1)S(1)} %bitcast.39), channel_id=1, replica_groups=mesh['fsdp'=32,'fac'=4] {'fsdp'}, dimensions={0} | all-to-all | bytes 4718592 | tf_op jit(solution)/shard_map/all_to_all | solution.py:27
  156.3 3.3 fusion.7
  159.7 11.4 %all_gather.22 = bf16[96,3072]{1,0:T(8,128)(2,1)S(1)} all-gather(bf16[96,768]{1,0:T(8,128)(2,1)S(1)} %fusion.7), channel_id=1, replica_groups=mesh['fsdp'=32,'fac'=4] {'fac'}, dimensions={1}, use_global_device_ids=true | all-gather | bytes 737280 | tf_op jit(solution)/shard_map/all_gather | solution.py:58
  171.1 3.9 fusion.15
  175.2 6.8 %fusion.4 = bf16[3072,384]{0,1:T(8,128)(2,1)} fusion(bf16[1024,3072]{1,0:T(8,128)(2,1)} %param.7, bf16[1024,768]{1,0:T(8,128)(2,1)S(1)} %copy-done.3), kind=kOutput, calls=%fused_computation.12 | convolution fusion | flops 2417098752 | bytes 9437184 | tf_op jit(solution)/shard_map/dot_general | solution.py:19
  182.1 3.0 copy.17
  185.1 40.9 %all_to_all.29 = bf16[32,96,384]{2,1,0:T(8,128)(2,1)S(1)} all-to-all(bf16[32,96,384]{2,1,0:T(8,128)(2,1)S(1)} %bitcast.40), channel_id=1, replica_groups=mesh['fsdp'=32,'fac'=4] {'fsdp'}, dimensions={0} | all-to-all | bytes 4718592 | tf_op jit(solution)/shard_map/all_to_all | solution.py:27
  226.3 12.0 %all_gather.23 = bf16[96,3072]{1,0:T(8,128)(2,1)S(1)} all-gather(bf16[96,768]{1,0:T(8,128)(2,1)S(1)} %pad_maximum_fusion), channel_id=1, replica_groups=mesh['fsdp'=32,'fac'=4] {'fac'}, dimensions={1}, use_global_device_ids=true | all-gather | bytes 737280 | tf_op jit(solution)/shard_map/all_gather | solution.py:80
  238.4 4.5 %multiply_reduce_fusion.5 = (f32[]{:T(128)}, f32[]{:T(128)}, bf16[96,768]{1,0:T(8,128)(2,1)}, f32[96,768]{1,0:T(8,128)S(1)}) fusion(f32[96,768]{1,0:T(8,128)S(1)} %get-tuple-element.20, f32[96,768]{1,0:T(8,128)S(1)} %convert_reduce_fusion, bf16[96,3072]{1,0:T(8,128)(2,1)S(1)} %all_gather.23, bf16[3072,768]{1,0:T(8,128)(2,1)} %all-gather.7.cloned.1.call-done), kind=kOutput, calls=%fused_computation.32 | convolution fusion | flops 453574656 | bytes 6340616 | tf_op jit(solution)/shard_map/dot_general | solution.py:15
  244.4 16.4 %all_to_all.30 = f32[128,1,2]{2,1,0:T(1,128)S(1)} all-to-all(f32[128,1,2]{2,1,0:T(1,128)S(1)} %broadcast_in_dim.7), channel_id=1, replica_groups=mesh['fsdp'=32,'fac'=4] {'fsdp','fac'}, dimensions={0} | all-to-all | bytes 2048 | tf_op jit(solution)/shard_map/all_to_all | solution.py:34
  262.8 26.5 %all-gather.9.cloned.1.call-done = bf16[3072,768]{1,0:T(8,128)(2,1)} async-done(((bf16[96,768]{1,0:T(8,128)(2,1)}), bf16[3072,768]{1,0:T(8,128)(2,1)}) %all-gather.9.cloned.1.call-update) | async-done | bytes 4718608 | tf_op jit(solution)/shard_map/all_gather | solution.py:52
  289.3 5.5 %fusion.8 = bf16[96,768]{1,0:T(8,128)(2,1)S(1)} fusion(bf16[96,3072]{1,0:T(8,128)(2,1)S(1)} %copy-done, bf16[3072,768]{1,0:T(8,128)(2,1)} %all-gather.9.cloned.1.call-done, bf16[3072,768]{1,0:T(8,128)(2,1)} %all-gather.5.cloned.1.call-done, f32[]{:T(128)S(6)} %div.17), kind=kOutput, calls=%fused_computation.20 | convolution fusion | flops 464855040 | bytes 10174468 | tf_op jit(solution)/shard_map/dot_general | solution.py:15
  294.8 11.3 %all_gather.26 = bf16[96,3072]{1,0:T(8,128)(2,1)S(1)} all-gather(bf16[96,768]{1,0:T(8,128)(2,1)S(1)} %fusion.8), channel_id=1, replica_groups=mesh['fsdp'=32,'fac'=4] {'fac'}, dimensions={1}, use_global_device_ids=true | all-gather | bytes 737280 | tf_op jit(solution)/shard_map/all_gather | solution.py:58
  306.0 3.9 fusion.16
  310.0 48.6 %all-gather.11.cloned.1.call-done = bf16[3072,768]{1,0:T(8,128)(2,1)} async-done(((bf16[96,768]{1,0:T(8,128)(2,1)}), bf16[3072,768]{1,0:T(8,128)(2,1)}) %all-gather.11.cloned.1.call-update) | async-done | bytes 4718608 | tf_op jit(solution)/shard_map/all_gather | solution.py:52
  358.5 3.9 multiply_reduce_fusion.3
  362.4 2.6 pad_maximum_fusion.2
  365.1 16.6 %all_to_all.31 = f32[128,1,4]{2,1,0:T(1,128)S(1)} all-to-all(f32[128,1,4]{2,1,0:T(1,128)S(1)} %broadcast_in_dim.8), channel_id=1, replica_groups=mesh['fsdp'=32,'fac'=4] {'fsdp','fac'}, dimensions={0} | all-to-all | bytes 4096 | tf_op jit(solution)/shard_map/all_to_all | solution.py:34
  (41 shorter events, 10.7 us)
Async XLA Ops:
  7.2 149.2 %copy-start = (bf16[96,3072]{1,0:T(8,128)(2,1)S(1)}, bf16[96,3072]{1,0:T(8,128)(2,1)}, u32[]{:S(2)}) copy-start(bf16[96,3072]{1,0:T(8,128)(2,1)} %param.12) | copy-start | bytes 1769476
  7.2 149.2 %all-gather.5.cloned.1.call-start = ((), (), s32[]{:S(2)}) async-start(), calls=%async_computation.5 | async-start | bytes 4866048 | tf_op jit(solution)/shard_map/all_gather | solution.py:52
  90.1 1.4 copy-start.6
  90.1 1.4 copy-start.1
  90.1 7.6 %copy-start.5 = (s32[1024]{0:T(1024)S(1)}, s32[1024]{0:T(1024)}, u32[]{:S(2)}) copy-start(s32[1024]{0:T(1024)} %param.10) | copy-start | bytes 12292
  91.5 146.9 %all-gather.7.cloned.1.call-start = ((), (), s32[]{:S(2)}) async-start(), calls=%async_computation.6 | async-start | bytes 4866048 | tf_op jit(solution)/shard_map/all_gather | solution.py:52
  99.5 1.2 copy-start.2
  156.3 18.9 %copy-start.3 = (bf16[1024,768]{1,0:T(8,128)(2,1)S(1)}, bf16[1024,768]{1,0:T(8,128)(2,1)}, u32[]{:S(2)}) copy-start(bf16[1024,768]{1,0:T(8,128)(2,1)} %copy-done.2) | copy-start | bytes 4718596
  175.0 114.3 %all-gather.9.cloned.1.call-start = ((), (), s32[]{:S(2)}) async-start(), calls=%async_computation.7 | async-start | bytes 4866048 | tf_op jit(solution)/shard_map/all_gather | solution.py:52
  185.1 41.2 %copy-start.4 = (bf16[96,384]{1,0:T(8,128)(2,1)S(1)}, bf16[96,384]{1,0:T(8,128)(2,1)}, u32[]{:S(2)}) copy-start(bf16[96,384]{1,0:T(8,128)(2,1)} %convert_reduce_fusion.2) | copy-start | bytes 221188
  242.9 115.6 %all-gather.11.cloned.1.call-start = ((), (), s32[]{:S(2)}) async-start(), calls=%async_computation.8 | async-start | bytes 4866048 | tf_op jit(solution)/shard_map/all_gather | solution.py:52
Sparse Core Ops, SparseCore 0:
  91.6 62.9 all-gather.4
  175.1 58.5 all-gather.6
  243.0 46.1 all-gather.8
  310.1 48.3 all-gather.10

commit v6 on v5

--- a/solution.py
+++ b/solution.py
@@ -21,24 +21,29 @@
     )
 
 
+FSDP = ("pairs", "core")
+
+
 def scatter_sum(partial):
-    parts = lax.axis_size("fsdp")
-    blocks = partial.reshape(parts, partial.shape[0] // parts, partial.shape[1])
-    received = lax.all_to_all(blocks, "fsdp", 0, 0, tiled=False)
+    pairs, cores = lax.axis_size("pairs"), lax.axis_size("core")
+    blocks = partial.reshape(pairs, cores, partial.shape[0] // (pairs * cores), partial.shape[1])
+    on_chip = lax.all_to_all(blocks, "core", 1, 1, tiled=False)
+    chip_sum = jnp.sum(on_chip.astype(jnp.float32), axis=1).astype(jnp.bfloat16)
+    received = lax.all_to_all(chip_sum, "pairs", 0, 0, tiled=False)
     return lax.optimization_barrier(jnp.sum(received.astype(jnp.float32), axis=0))
 
 
 def global_sums(*partials):
-    devices = lax.axis_size("fsdp") * lax.axis_size("fac")
+    devices = lax.axis_size("pairs") * lax.axis_size("core") * lax.axis_size("fac")
     stacked = jnp.broadcast_to(jnp.stack(partials)[None, :], (devices, len(partials)))
-    received = lax.all_to_all(stacked, ("fsdp", "fac"), 0, 0, tiled=True)
+    received = lax.all_to_all(stacked, FSDP + ("fac",), 0, 0, tiled=True)
     total = jnp.sum(received, axis=0)
     return tuple(total[i] for i in range(len(partials)))
 
 
 def body(activations, out_grads, token_ids, forget_mask, importance, in_inverse, out_inverse):
     tok_rows, d_in = activations.shape
-    total = tok_rows * lax.axis_size("fsdp")
+    total = tok_rows * lax.axis_size("pairs") * lax.axis_size("core")
     keep = 1.0 - forget_mask.astype(jnp.float32)
     weights = importance[token_ids] * keep / total
     forget_grads = out_grads * forget_mask.astype(jnp.bfloat16)[:, None]
@@ -49,7 +54,7 @@
     )
 
     def gather_rows(matrix):
-        return lax.all_gather(matrix.astype(jnp.bfloat16), "fsdp", axis=0, tiled=True)
+        return lax.all_gather(matrix.astype(jnp.bfloat16), FSDP, axis=0, tiled=True)
 
     def precondition(gathered):
         mixed = add_columns(in_inverse, gathered)
@@ -112,19 +117,24 @@
 
 
 def solution(mesh):
+    cores = 2
+    split = jax.sharding.Mesh(
+        mesh.devices.reshape(mesh.shape["fsdp"] // cores, cores, mesh.shape["fac"]),
+        ("pairs", "core", "fac"),
+    )
     placed = (
-        P("fsdp", None),
-        P("fsdp", "fac"),
-        P("fsdp"),
-        P("fsdp"),
+        P(FSDP, None),
+        P(FSDP, "fac"),
+        P(FSDP),
+        P(FSDP),
         P(),
-        P("fsdp", None),
+        P(FSDP, None),
         P(None, "fac"),
     )
     return jax.shard_map(
         body,
-        mesh=mesh,
+        mesh=split,
         in_specs=placed,
-        out_specs=(P("fsdp", "fac"), P("fsdp", "fac")),
+        out_specs=(P(FSDP, "fac"), P(FSDP, "fac")),
         check_vma=False,
     )

time: 395 us -> 375 us (0.949)
  blocking collectives: 219 us -> 188 us
  other arithmetic: 10.3 us -> 17.5 us
    all_to_all x5 -> x8, blocking collectives: 185 us -> 154 us  [the longest x3 93.9 us: scatter_sum(): received = lax.all_to_all(chip_sum, 'pairs', 0, 0, tiled=False)]
    reduce_sum x0 -> x3, other arithmetic: none -> 7.05 us  [scatter_sum(): chip_sum = jnp.sum(on_chip.astype(jnp.float32), axis=1).astype(jnp.bfloat16)]
  transfers between devices with their start and end apart: 4 -> 4, of which waited for: 2 -> 2; matrix products, arithmetic and copies ran while one was open for 8% -> 10% of each run, Pallas kernels for 0% -> 0%
where the time goes in v6:
time: 375 us; the launch traced here: 373 us
  blocking collectives  188 us (50%)
  waiting for transfers between devices  75.1 us (20%)
  matrix products  48.1 us (13%)
  local copies, waits for them, and re-layouts  24.5 us (7%)
  between operations  19.8 us (5%)
  other arithmetic  17.5 us (5%)
    all_to_all x3, blocking collectives, scatter_sum(): received = lax.all_to_all(chip_sum, 'pairs', 0, 0, tiled=False)  93.9 us
    all_gather x4, waiting for transfers between devices, gather_rows(): return lax.all_gather(matrix.astype(jnp.bfloat16), FSDP, axis=0, tiled=True)  75 us
    all_to_all x2, blocking collectives, global_sums(): received = lax.all_to_all(stacked, FSDP + ('fac',), 0, 0, tiled=True)  36.4 us
    all_to_all x3, blocking collectives, scatter_sum(): on_chip = lax.all_to_all(blocks, 'core', 1, 1, tiled=False)  24 us
    all_gather x2, blocking collectives, precondition(): lax.all_gather(mixed_low, 'fac', axis=1, tiled=True)  23.1 us
    dot_general x3, matrix products, transposed_term(): lax.dot_general(matrix, right, (((0,), (0,)), ((), ())), preferred_elemen...  23 us
    dot_general x4, matrix products, add_columns(): return jnp.dot(matrix, piece, preferred_element_type=jnp.float32)  17.3 us
    all_gather x1, blocking collectives, body(): lax.all_gather(gram_own.astype(jnp.bfloat16), 'fac', axis=1, tiled=True)  10.8 us
  transfers between devices with their start and end apart: 4, of which 2 were waited for; matrix products, arithmetic and copies ran while one was open for 10% of the time, Pallas kernels for 0%

profile of v6, /device:TPU:1, one launch (start us, length us, event | category | flops | bytes accessed | tf_op | source)
XLA Modules:
  0.0 373.5 jit_solution(16601365555449277453)
XLA Ops:
  8.0 9.3 %fusion.2 = bf16[3072,768]{0,1:T(8,128)(2,1)} fusion(bf16[1024,3072]{1,0:T(8,128)(2,1)} %param.7, bf16[1024,768]{1,0:T(8,128)(2,1)} %param.8, bf16[1024]{0:T(1024)(128)(2,1)S(1)} %convert_element_type.79), kind=kOutput, calls=%fused_computation.6 | convolution fusion | flops 4837343232 | bytes 12584960 | tf_op jit(solution)/shard_map/dot_general | solution.py:19
  17.3 6.7 %copy.24 = bf16[3072,768]{1,0:T(8,128)(2,1)} copy(bf16[3072,768]{0,1:T(8,128)(2,1)} %fusion.2) | data formatting | bytes 9437184 | tf_op jit(solution)/shard_map/convert_element_type | solution.py:53
  26.7 9.7 %all_to_all.42 = bf16[16,2,96,768]{3,2,0,1:T(8,128)(2,1)} all-to-all(bf16[16,2,96,768]{3,2,0,1:T(8,128)(2,1)S(1)} %copy.25), channel_id=1, replica_groups=mesh['pairs'=16,'core'=2,'fac'=4] {'core'}, dimensions={1} | all-to-all | bytes 9437184 | tf_op jit(solution)/shard_map/all_to_all | solution.py:30
  36.3 3.5 reduce_sum.135
  39.8 38.5 %all_to_all.43 = bf16[16,96,768]{2,1,0:T(8,128)(2,1)S(1)} all-to-all(bf16[16,96,768]{2,1,0:T(8,128)(2,1)S(1)} %reduce_sum.135), channel_id=1, replica_groups=mesh['pairs'=16,'core'=2,'fac'=4] {'pairs'}, dimensions={0} | all-to-all | bytes 4718592 | tf_op jit(solution)/shard_map/all_to_all | solution.py:32
  79.4 6.2 %gather_fusion = f32[1024]{0:T(1024)S(1)} fusion(f32[32768]{0:T(1024)S(1)} %copy-done.1, s32[1024]{0:T(1024)S(1)} %fusion.12), kind=kCustom, calls=%fused_computation | custom fusion | bytes 12288 | tf_op jit(solution)/shard_map/gather | solution.py:48
  88.5 6.9 %fusion.3 = bf16[3072,384]{0,1:T(8,128)(2,1)} fusion(bf16[1024,3072]{1,0:T(8,128)(2,1)} %param.7, bf16[1024,768]{1,0:T(8,128)(2,1)S(1)} %multiply_convert_fusion.1), kind=kOutput, calls=%fused_computation.9 | convolution fusion | flops 2417098752 | bytes 9437184 | tf_op jit(solution)/shard_map/dot_general | solution.py:19
  98.6 6.8 %all_to_all.44 = bf16[16,2,96,384]{3,2,0,1:T(8,128)(2,1)S(1)} all-to-all(bf16[16,2,96,384]{3,2,0,1:T(8,128)(2,1)S(1)} %copy.27), channel_id=1, replica_groups=mesh['pairs'=16,'core'=2,'fac'=4] {'core'}, dimensions={1} | all-to-all | bytes 4718592 | tf_op jit(solution)/shard_map/all_to_all | solution.py:30
  107.2 28.5 %all_to_all.45 = bf16[16,96,384]{2,1,0:T(8,128)(2,1)S(1)} all-to-all(bf16[16,96,384]{2,1,0:T(8,128)(2,1)} %reduce_sum.137), channel_id=1, replica_groups=mesh['pairs'=16,'core'=2,'fac'=4] {'pairs'}, dimensions={0} | all-to-all | bytes 2359296 | tf_op jit(solution)/shard_map/all_to_all | solution.py:32
  139.8 11.8 %all_gather.22 = bf16[96,3072]{1,0:T(8,128)(2,1)S(1)} all-gather(bf16[96,768]{1,0:T(8,128)(2,1)S(1)} %fusion.7), channel_id=1, replica_groups=mesh['pairs'=16,'core'=2,'fac'=4] {'fac'}, dimensions={1}, use_global_device_ids=true | all-gather | bytes 737280 | tf_op jit(solution)/shard_map/all_gather | solution.py:63
  151.6 3.9 %fusion.15 = (bf16[96,768]{1,0:T(8,128)(2,1)}, f32[96,768]{1,0:T(8,128)S(1)}) fusion(bf16[96,3072]{1,0:T(8,128)(2,1)S(1)} %all_gather.22, bf16[3072,768]{1,0:T(8,128)(2,1)} %param.13), kind=kOutput, calls=%fused_computation.42 | convolution fusion | flops 453058560 | bytes 5750784 | tf_op jit(solution)/shard_map/dot_general | solution.py:62
  155.8 6.8 %fusion.4 = bf16[3072,384]{0,1:T(8,128)(2,1)} fusion(bf16[1024,3072]{1,0:T(8,128)(2,1)} %param.7, bf16[1024,768]{1,0:T(8,128)(2,1)S(1)} %copy-done.3), kind=kOutput, calls=%fused_computation.10 | convolution fusion | flops 2417098752 | bytes 9437184 | tf_op jit(solution)/shard_map/dot_general | solution.py:19
  165.9 7.5 %all_to_all.46 = bf16[16,2,96,384]{3,2,0,1:T(8,128)(2,1)S(1)} all-to-all(bf16[16,2,96,384]{3,2,0,1:T(8,128)(2,1)S(1)} %copy.29), channel_id=1, replica_groups=mesh['pairs'=16,'core'=2,'fac'=4] {'core'}, dimensions={1} | all-to-all | bytes 4718592 | tf_op jit(solution)/shard_map/all_to_all | solution.py:30
  175.1 26.9 %all_to_all.47 = bf16[16,96,384]{2,1,0:T(8,128)(2,1)S(1)} all-to-all(bf16[16,96,384]{2,1,0:T(8,128)(2,1)} %reduce_sum.140), channel_id=1, replica_groups=mesh['pairs'=16,'core'=2,'fac'=4] {'pairs'}, dimensions={0} | all-to-all | bytes 2359296 | tf_op jit(solution)/shard_map/all_to_all | solution.py:32
  203.1 10.8 %all_gather.23 = bf16[96,3072]{1,0:T(8,128)(2,1)S(1)} all-gather(bf16[96,768]{1,0:T(8,128)(2,1)S(1)} %pad_maximum_fusion), channel_id=1, replica_groups=mesh['pairs'=16,'core'=2,'fac'=4] {'fac'}, dimensions={1}, use_global_device_ids=true | all-gather | bytes 737280 | tf_op jit(solution)/shard_map/all_gather | solution.py:85
  214.0 4.5 %multiply_reduce_fusion.5 = (f32[]{:T(128)}, f32[]{:T(128)}, bf16[96,768]{1,0:T(8,128)(2,1)}, f32[96,768]{1,0:T(8,128)S(1)}) fusion(f32[96,768]{1,0:T(8,128)S(1)} %get-tuple-element.20, f32[96,768]{1,0:T(8,128)S(1)} %convert_reduce_fusion, bf16[96,3072]{1,0:T(8,128)(2,1)S(1)} %all_gather.23, bf16[3072,768]{1,0:T(8,128)(2,1)} %all-gather.7.cloned.1.call-done), kind=kOutput, calls=%fused_computation.32 | convolution fusion | flops 453574656 | bytes 6340616 | tf_op jit(solution)/shard_map/dot_general | solution.py:15
  220.0 19.8 %all_to_all.48 = f32[128,1,2]{2,1,0:T(1,128)S(1)} all-to-all(f32[128,1,2]{2,1,0:T(1,128)S(1)} %broadcast_in_dim.7), channel_id=1, replica_groups=mesh['pairs'=16,'core'=2,'fac'=4] {'pairs','core','fac'}, dimensions={0} | all-to-all | bytes 2048 | tf_op jit(solution)/shard_map/all_to_all | solution.py:39
  241.8 26.5 %all-gather.9.cloned.1.call-done = bf16[3072,768]{1,0:T(8,128)(2,1)} async-done(((bf16[96,768]{1,0:T(8,128)(2,1)}), bf16[3072,768]{1,0:T(8,128)(2,1)}) %all-gather.9.cloned.1.call-update) | async-done | bytes 4718608 | tf_op jit(solution)/shard_map/all_gather | solution.py:57
  268.3 5.5 %fusion.8 = bf16[96,768]{1,0:T(8,128)(2,1)S(1)} fusion(bf16[96,3072]{1,0:T(8,128)(2,1)S(1)} %copy-done, bf16[3072,768]{1,0:T(8,128)(2,1)} %all-gather.9.cloned.1.call-done, bf16[3072,768]{1,0:T(8,128)(2,1)} %all-gather.5.cloned.1.call-done, f32[]{:T(128)S(6)} %div.17), kind=kOutput, calls=%fused_computation.20 | convolution fusion | flops 464855040 | bytes 10174468 | tf_op jit(solution)/shard_map/dot_general | solution.py:15
  273.8 11.3 %all_gather.26 = bf16[96,3072]{1,0:T(8,128)(2,1)S(1)} all-gather(bf16[96,768]{1,0:T(8,128)(2,1)S(1)} %fusion.8), channel_id=1, replica_groups=mesh['pairs'=16,'core'=2,'fac'=4] {'fac'}, dimensions={1}, use_global_device_ids=true | all-gather | bytes 737280 | tf_op jit(solution)/shard_map/all_gather | solution.py:63
  285.1 3.9 %fusion.16 = (bf16[96,768]{1,0:T(8,128)(2,1)}, f32[96,768]{1,0:T(8,128)S(1)}) fusion(bf16[96,3072]{1,0:T(8,128)(2,1)S(1)} %all_gather.26, bf16[3072,768]{1,0:T(8,128)(2,1)} %param.13), kind=kOutput, calls=%fused_computation.43 | convolution fusion | flops 453058560 | bytes 5750784 | tf_op jit(solution)/shard_map/dot_general | solution.py:62
  289.0 48.5 %all-gather.11.cloned.1.call-done = bf16[3072,768]{1,0:T(8,128)(2,1)} async-done(((bf16[96,768]{1,0:T(8,128)(2,1)}), bf16[3072,768]{1,0:T(8,128)(2,1)}) %all-gather.11.cloned.1.call-update) | async-done | bytes 4718608 | tf_op jit(solution)/shard_map/all_gather | solution.py:57
  337.5 3.9 %multiply_reduce_fusion.3 = (f32[]{:T(128)}, f32[]{:T(128)}, f32[]{:T(128)}, f32[]{:T(128)}, f32[96,768]{1,0:T(8,128)S(1)}) fusion(f32[96,768]{1,0:T(8,128)S(1)} %get-tuple-element.23, f32[96,768]{1,0:T(8,128)S(1)} %get-tuple-element.21, f32[96,768]{1,0:T(8,128)S(1)} %convert_reduce_fusion, f32[]{:T(128)S(6)} %div.17, f32[96,768]{1,0:T(8,128)S(1)} %get-tuple-element.20, ...), kind=kOutput, calls=%fused_computation.29 | convolution fusion | flops 453943296 | bytes 6782996 | tf_op jit(solution)/shard_map/dot_general | solution.py:15
  344.1 16.6 %all_to_all.49 = f32[128,1,4]{2,1,0:T(1,128)S(1)} all-to-all(f32[128,1,4]{2,1,0:T(1,128)S(1)} %broadcast_in_dim.8), channel_id=1, replica_groups=mesh['pairs'=16,'core'=2,'fac'=4] {'pairs','core','fac'}, dimensions={0} | all-to-all | bytes 4096 | tf_op jit(solution)/shard_map/all_to_all | solution.py:39
  (48 shorter events, 29.5 us)
Async XLA Ops:
  7.2 129.3 %copy-start = (bf16[96,3072]{1,0:T(8,128)(2,1)S(1)}, bf16[96,3072]{1,0:T(8,128)(2,1)}, u32[]{:S(2)}) copy-start(bf16[96,3072]{1,0:T(8,128)(2,1)} %param.12) | copy-start | bytes 1769476
  7.2 129.3 %all-gather.5.cloned.1.call-start = ((), (), s32[]{:S(2)}) async-start(), calls=%async_computation.8 | async-start | bytes 4866048 | tf_op jit(solution)/shard_map/all_gather | solution.py:57
  39.8 39.6 %copy-start.5 = (s32[1024]{0:T(1024)S(1)}, s32[1024]{0:T(1024)}, u32[]{:S(2)}) copy-start(s32[1024]{0:T(1024)} %param.9) | copy-start | bytes 12292
  39.8 39.6 %copy-start.1 = (f32[32768]{0:T(1024)S(1)}, f32[32768]{0:T(1024)}, u32[]{:S(2)}) copy-start(f32[32768]{0:T(1024)} %param.11) | copy-start | bytes 393220
  78.3 7.3 %copy-start.4 = (s32[1024]{0:T(1024)S(1)}, s32[1024]{0:T(1024)}, u32[]{:S(2)}) copy-start(s32[1024]{0:T(1024)} %param.10) | copy-start | bytes 12292
  79.3 134.7 %all-gather.7.cloned.1.call-start = ((), (), s32[]{:S(2)}) async-start(), calls=%async_computation.9 | async-start | bytes 4866048 | tf_op jit(solution)/shard_map/all_gather | solution.py:57
  87.3 1.2 copy-start.2
  136.5 19.3 %copy-start.3 = (bf16[1024,768]{1,0:T(8,128)(2,1)S(1)}, bf16[1024,768]{1,0:T(8,128)(2,1)}, u32[]{:S(2)}) copy-start(bf16[1024,768]{1,0:T(8,128)(2,1)} %copy-done.2) | copy-start | bytes 4718596
  155.5 112.8 %all-gather.9.cloned.1.call-start = ((), (), s32[]{:S(2)}) async-start(), calls=%async_computation.10 | async-start | bytes 4866048 | tf_op jit(solution)/shard_map/all_gather | solution.py:57
  218.5 119.0 %all-gather.11.cloned.1.call-start = ((), (), s32[]{:S(2)}) async-start(), calls=%async_computation.11 | async-start | bytes 4866048 | tf_op jit(solution)/shard_map/all_gather | solution.py:57
Sparse Core Ops, SparseCore 0:
  79.4 55.4 all-gather.4
  155.6 52.8 all-gather.6
  218.7 49.5 all-gather.8
  289.1 48.3 all-gather.10

commit v7 on v6

--- a/solution.py
+++ b/solution.py
@@ -22,6 +22,15 @@
 
 
 FSDP = ("pairs", "core")
+
+
+def stacked_product(pieces, right):
+    return lax.dot_general(
+        pieces,
+        right.reshape(pieces.shape[0], pieces.shape[2], right.shape[1]),
+        (((0, 2), (0, 1)), ((), ())),
+        preferred_element_type=jnp.float32,
+    )
 
 
 def scatter_sum(partial):
@@ -59,11 +68,7 @@
     def precondition(gathered):
         mixed = add_columns(in_inverse, gathered)
         mixed_low = mixed.astype(jnp.bfloat16)
-        return jnp.dot(
-            lax.all_gather(mixed_low, "fac", axis=1, tiled=True),
-            out_inverse,
-            preferred_element_type=jnp.float32,
-        )
+        return stacked_product(lax.all_gather(mixed_low, "fac", axis=0), out_inverse)
 
     def inner_part(left, right):
         return jnp.sum(left * right)
@@ -82,10 +87,10 @@
     residual_rows, first_rows = lax.optimization_barrier((residual_rows, scatter_sum(gram_first)))
     precond = precondition(residual_rows)
     gram_own = jnp.concatenate([first_rows, scatter_sum(gram_second)], axis=1)
-    gram_rows = lax.all_gather(gram_own.astype(jnp.bfloat16), "fac", axis=1, tiled=True)
+    gram_rows = lax.all_gather(gram_own.astype(jnp.bfloat16), "fac", axis=0)
 
     def curvature(matrix):
-        return add_columns(gram_rows, gather_rows(matrix)) + damping * matrix
+        return stacked_product(gram_rows, gather_rows(matrix)) + damping * matrix
 
     direction = precond
     image = curvature(direction)

time: 375 us -> 375 us (level)
    dot_general x4 -> x2, matrix products: 17.3 us -> 8.7 us  [add_columns(): return jnp.dot(matrix, piece, preferred_element_type=jnp.float32)]
    dot_general x2 -> x4, matrix products: 7.76 us -> 16.3 us  [stacked_product(): lax.dot_general(pieces, right.reshape(pieces.shape[0], pieces.shape[2], r...]
where the time goes in v7:
time: 375 us; the launch traced here: 373 us
  blocking collectives  188 us (50%)
  waiting for transfers between devices  75.1 us (20%)
  matrix products  48 us (13%)
  local copies, waits for them, and re-layouts  24.5 us (7%)
  between operations  19.8 us (5%)
  other arithmetic  17.5 us (5%)
    all_to_all x3, blocking collectives, scatter_sum(): received = lax.all_to_all(chip_sum, 'pairs', 0, 0, tiled=False)  93.8 us
    all_gather x4, waiting for transfers between devices, gather_rows(): return lax.all_gather(matrix.astype(jnp.bfloat16), FSDP, axis=0, tiled=True)  75 us
    all_to_all x2, blocking collectives, global_sums(): received = lax.all_to_all(stacked, FSDP + ('fac',), 0, 0, tiled=True)  36.4 us
    all_to_all x3, blocking collectives, scatter_sum(): on_chip = lax.all_to_all(blocks, 'core', 1, 1, tiled=False)  24 us
    all_gather x2, blocking collectives, precondition(): lax.all_gather(mixed_low, 'fac', axis=0)  23.2 us
    dot_general x3, matrix products, transposed_term(): lax.dot_general(matrix, right, (((0,), (0,)), ((), ())), preferred_elemen...  23 us
    dot_general x4, matrix products, stacked_product(): lax.dot_general(pieces, right.reshape(pieces.shape[0], pieces.shape[2], r...  16.3 us
    all_gather x1, blocking collectives, body(): gram_rows = lax.all_gather(gram_own.astype(jnp.bfloat16), 'fac', axis=0)  10.8 us
  transfers between devices with their start and end apart: 4, of which 2 were waited for; matrix products, arithmetic and copies ran while one was open for 10% of the time, Pallas kernels for 0%

profile of v7, /device:TPU:1, one launch (start us, length us, event | category | flops | bytes accessed | tf_op | source)
XLA Modules:
  0.0 373.4 jit_solution(18271733732283597670)
XLA Ops:
  8.0 9.3 %fusion.2 = bf16[3072,768]{0,1:T(8,128)(2,1)} fusion(bf16[1024,3072]{1,0:T(8,128)(2,1)} %param.7, bf16[1024,768]{1,0:T(8,128)(2,1)} %param.8, bf16[1024]{0:T(1024)(128)(2,1)S(1)} %convert_element_type.86), kind=kOutput, calls=%fused_computation.6 | convolution fusion | flops 4837343232 | bytes 12584960 | tf_op jit(solution)/shard_map/dot_general | solution.py:19
  17.3 6.7 %copy.24 = bf16[3072,768]{1,0:T(8,128)(2,1)} copy(bf16[3072,768]{0,1:T(8,128)(2,1)} %fusion.2) | data formatting | bytes 9437184 | tf_op jit(solution)/shard_map/convert_element_type | solution.py:62
  26.7 9.7 %all_to_all.42 = bf16[16,2,96,768]{3,2,0,1:T(8,128)(2,1)} all-to-all(bf16[16,2,96,768]{3,2,0,1:T(8,128)(2,1)S(1)} %copy.25), channel_id=1, replica_groups=mesh['pairs'=16,'core'=2,'fac'=4] {'core'}, dimensions={1} | all-to-all | bytes 9437184 | tf_op jit(solution)/shard_map/all_to_all | solution.py:39
  36.3 3.5 reduce_sum.135
  39.8 38.5 %all_to_all.43 = bf16[16,96,768]{2,1,0:T(8,128)(2,1)S(1)} all-to-all(bf16[16,96,768]{2,1,0:T(8,128)(2,1)S(1)} %reduce_sum.135), channel_id=1, replica_groups=mesh['pairs'=16,'core'=2,'fac'=4] {'pairs'}, dimensions={0} | all-to-all | bytes 4718592 | tf_op jit(solution)/shard_map/all_to_all | solution.py:41
  79.4 6.2 %gather_fusion = f32[1024]{0:T(1024)S(1)} fusion(f32[32768]{0:T(1024)S(1)} %copy-done.1, s32[1024]{0:T(1024)S(1)} %fusion.14), kind=kCustom, calls=%fused_computation | custom fusion | bytes 12288 | tf_op jit(solution)/shard_map/gather | solution.py:57
  88.5 6.9 %fusion.3 = bf16[3072,384]{0,1:T(8,128)(2,1)} fusion(bf16[1024,3072]{1,0:T(8,128)(2,1)} %param.7, bf16[1024,768]{1,0:T(8,128)(2,1)S(1)} %multiply_convert_fusion.1), kind=kOutput, calls=%fused_computation.9 | convolution fusion | flops 2417098752 | bytes 9437184 | tf_op jit(solution)/shard_map/dot_general | solution.py:19
  98.6 6.8 %all_to_all.44 = bf16[16,2,96,384]{3,2,0,1:T(8,128)(2,1)S(1)} all-to-all(bf16[16,2,96,384]{3,2,0,1:T(8,128)(2,1)S(1)} %copy.27), channel_id=1, replica_groups=mesh['pairs'=16,'core'=2,'fac'=4] {'core'}, dimensions={1} | all-to-all | bytes 4718592 | tf_op jit(solution)/shard_map/all_to_all | solution.py:39
  107.2 28.5 %all_to_all.45 = bf16[16,96,384]{2,1,0:T(8,128)(2,1)S(1)} all-to-all(bf16[16,96,384]{2,1,0:T(8,128)(2,1)} %reduce_sum.137), channel_id=1, replica_groups=mesh['pairs'=16,'core'=2,'fac'=4] {'pairs'}, dimensions={0} | all-to-all | bytes 2359296 | tf_op jit(solution)/shard_map/all_to_all | solution.py:41
  139.7 11.9 %all-gather = bf16[384,768]{1,0:T(8,128)(2,1)S(1)} all-gather(bf16[96,768]{1,0:T(8,128)(2,1)S(1)} %fusion.9), channel_id=2, replica_groups=mesh['pairs'=16,'core'=2,'fac'=4] {'fac'}, dimensions={0}, use_global_device_ids=true | all-gather | bytes 737280 | tf_op jit(solution)/shard_map/all_gather | solution.py:71
  151.6 3.9 %fusion.17 = (bf16[96,768]{1,0:T(8,128)(2,1)}, f32[96,768]{1,0:T(8,128)S(1)}) fusion(bf16[4,96,768]{2,1,0:T(8,128)(2,1)S(1)} %bitcast.68, bf16[4,768,768]{2,1,0:T(8,128)(2,1)} %bitcast.61), kind=kOutput, calls=%fused_computation.48 | convolution fusion | flops 453058560 | bytes 5750784 | tf_op jit(solution)/shard_map/dot_general | solution.py:28
  155.8 6.8 %fusion.4 = bf16[3072,384]{0,1:T(8,128)(2,1)} fusion(bf16[1024,3072]{1,0:T(8,128)(2,1)} %param.7, bf16[1024,768]{1,0:T(8,128)(2,1)S(1)} %copy-done.3), kind=kOutput, calls=%fused_computation.10 | convolution fusion | flops 2417098752 | bytes 9437184 | tf_op jit(solution)/shard_map/dot_general | solution.py:19
  165.9 7.5 %all_to_all.46 = bf16[16,2,96,384]{3,2,0,1:T(8,128)(2,1)S(1)} all-to-all(bf16[16,2,96,384]{3,2,0,1:T(8,128)(2,1)S(1)} %copy.29), channel_id=1, replica_groups=mesh['pairs'=16,'core'=2,'fac'=4] {'core'}, dimensions={1} | all-to-all | bytes 4718592 | tf_op jit(solution)/shard_map/all_to_all | solution.py:39
  175.2 26.9 %all_to_all.47 = bf16[16,96,384]{2,1,0:T(8,128)(2,1)S(1)} all-to-all(bf16[16,96,384]{2,1,0:T(8,128)(2,1)} %reduce_sum.140), channel_id=1, replica_groups=mesh['pairs'=16,'core'=2,'fac'=4] {'pairs'}, dimensions={0} | all-to-all | bytes 2359296 | tf_op jit(solution)/shard_map/all_to_all | solution.py:41
  203.1 10.8 %all_gather.31 = bf16[4,96,768]{2,1,0:T(8,128)(2,1)S(1)} all-gather(bf16[1,96,768]{2,1,0:T(8,128)(2,1)S(1)} %pad_maximum_fusion), channel_id=1, replica_groups=mesh['pairs'=16,'core'=2,'fac'=4] {'fac'}, dimensions={0}, use_global_device_ids=true | all-gather | bytes 737280 | tf_op jit(solution)/shard_map/all_gather | solution.py:90
  213.9 4.5 %multiply_reduce_fusion.5 = (f32[]{:T(128)}, f32[]{:T(128)}, bf16[96,768]{1,0:T(8,128)(2,1)}, f32[96,768]{1,0:T(8,128)S(1)}) fusion(f32[96,768]{1,0:T(8,128)S(1)} %get-tuple-element.20, f32[96,768]{1,0:T(8,128)S(1)} %convert_reduce_fusion, bf16[4,96,768]{2,1,0:T(8,128)(2,1)S(1)} %all_gather.31, bf16[4,768,768]{2,1,0:T(8,128)(2,1)} %bitcast.67), kind=kOutput, calls=%fused_computation.36 | convolution fusion | flops 453574656 | bytes 6340616 | tf_op jit(solution)/shard_map/dot_general | solution.py:28
  219.9 19.8 %all_to_all.48 = f32[128,1,2]{2,1,0:T(1,128)S(1)} all-to-all(f32[128,1,2]{2,1,0:T(1,128)S(1)} %broadcast_in_dim.7), channel_id=1, replica_groups=mesh['pairs'=16,'core'=2,'fac'=4] {'pairs','core','fac'}, dimensions={0} | all-to-all | bytes 2048 | tf_op jit(solution)/shard_map/all_to_all | solution.py:48
  241.8 26.5 %all-gather.11.cloned.1.call-done = bf16[3072,768]{1,0:T(8,128)(2,1)} async-done(((bf16[96,768]{1,0:T(8,128)(2,1)}), bf16[3072,768]{1,0:T(8,128)(2,1)}) %all-gather.11.cloned.1.call-update) | async-done | bytes 4718608 | tf_op jit(solution)/shard_map/all_gather | solution.py:66
  268.2 5.5 %fusion.10 = bf16[96,768]{1,0:T(8,128)(2,1)S(1)} fusion(bf16[96,3072]{1,0:T(8,128)(2,1)S(1)} %copy-done, bf16[3072,768]{1,0:T(8,128)(2,1)} %all-gather.11.cloned.1.call-done, bf16[3072,768]{1,0:T(8,128)(2,1)} %all-gather.7.cloned.1.call-done, f32[]{:T(128)S(6)} %div.17), kind=kOutput, calls=%fused_computation.24 | convolution fusion | flops 464855040 | bytes 10174468 | tf_op jit(solution)/shard_map/dot_general | solution.py:15
  273.7 11.3 %all-gather.1 = bf16[384,768]{1,0:T(8,128)(2,1)S(1)} all-gather(bf16[96,768]{1,0:T(8,128)(2,1)S(1)} %fusion.10), channel_id=3, replica_groups=mesh['pairs'=16,'core'=2,'fac'=4] {'fac'}, dimensions={0}, use_global_device_ids=true | all-gather | bytes 737280 | tf_op jit(solution)/shard_map/all_gather | solution.py:71
  285.0 3.9 %fusion.18 = (bf16[96,768]{1,0:T(8,128)(2,1)}, f32[96,768]{1,0:T(8,128)S(1)}) fusion(bf16[4,96,768]{2,1,0:T(8,128)(2,1)S(1)} %bitcast.69, bf16[4,768,768]{2,1,0:T(8,128)(2,1)} %bitcast.62), kind=kOutput, calls=%fused_computation.49 | convolution fusion | flops 453058560 | bytes 5750784 | tf_op jit(solution)/shard_map/dot_general | solution.py:28
  288.9 48.6 %all-gather.13.cloned.1.call-done = bf16[3072,768]{1,0:T(8,128)(2,1)} async-done(((bf16[96,768]{1,0:T(8,128)(2,1)}), bf16[3072,768]{1,0:T(8,128)(2,1)}) %all-gather.13.cloned.1.call-update) | async-done | bytes 4718608 | tf_op jit(solution)/shard_map/all_gather | solution.py:66
  337.5 3.9 %multiply_reduce_fusion.3 = (f32[]{:T(128)}, f32[]{:T(128)}, f32[]{:T(128)}, f32[]{:T(128)}, f32[96,768]{1,0:T(8,128)S(1)}) fusion(f32[96,768]{1,0:T(8,128)S(1)} %get-tuple-element.23, f32[96,768]{1,0:T(8,128)S(1)} %get-tuple-element.21, f32[96,768]{1,0:T(8,128)S(1)} %convert_reduce_fusion, f32[]{:T(128)S(6)} %div.17, f32[96,768]{1,0:T(8,128)S(1)} %get-tuple-element.20, ...), kind=kOutput, calls=%fused_computation.33 | convolution fusion | flops 453943296 | bytes 6782996 | tf_op jit(solution)/shard_map/dot_general | solution.py:28
  344.0 16.6 %all_to_all.49 = f32[128,1,4]{2,1,0:T(1,128)S(1)} all-to-all(f32[128,1,4]{2,1,0:T(1,128)S(1)} %broadcast_in_dim.8), channel_id=1, replica_groups=mesh['pairs'=16,'core'=2,'fac'=4] {'pairs','core','fac'}, dimensions={0} | all-to-all | bytes 4096 | tf_op jit(solution)/shard_map/all_to_all | solution.py:48
  (48 shorter events, 29.4 us)
Async XLA Ops:
  7.2 129.3 %copy-start = (bf16[96,3072]{1,0:T(8,128)(2,1)S(1)}, bf16[96,3072]{1,0:T(8,128)(2,1)}, u32[]{:S(2)}) copy-start(bf16[96,3072]{1,0:T(8,128)(2,1)} %param.12) | copy-start | bytes 1769476
  7.2 129.3 %all-gather.7.cloned.1.call-start = ((), (), s32[]{:S(2)}) async-start(), calls=%async_computation.8 | async-start | bytes 4866048 | tf_op jit(solution)/shard_map/all_gather | solution.py:66
  39.8 39.6 %copy-start.5 = (s32[1024]{0:T(1024)S(1)}, s32[1024]{0:T(1024)}, u32[]{:S(2)}) copy-start(s32[1024]{0:T(1024)} %param.9) | copy-start | bytes 12292
  39.8 39.6 %copy-start.1 = (f32[32768]{0:T(1024)S(1)}, f32[32768]{0:T(1024)}, u32[]{:S(2)}) copy-start(f32[32768]{0:T(1024)} %param.11) | copy-start | bytes 393220
  78.3 7.3 %copy-start.4 = (s32[1024]{0:T(1024)S(1)}, s32[1024]{0:T(1024)}, u32[]{:S(2)}) copy-start(s32[1024]{0:T(1024)} %param.10) | copy-start | bytes 12292
  79.3 134.6 %all-gather.9.cloned.1.call-start = ((), (), s32[]{:S(2)}) async-start(), calls=%async_computation.9 | async-start | bytes 4866048 | tf_op jit(solution)/shard_map/all_gather | solution.py:66
  87.3 1.2 copy-start.2
  139.7 16.1 %copy-start.3 = (bf16[1024,768]{1,0:T(8,128)(2,1)S(1)}, bf16[1024,768]{1,0:T(8,128)(2,1)}, u32[]{:S(2)}) copy-start(bf16[1024,768]{1,0:T(8,128)(2,1)} %copy-done.2) | copy-start | bytes 4718596
  155.5 112.7 %all-gather.11.cloned.1.call-start = ((), (), s32[]{:S(2)}) async-start(), calls=%async_computation.10 | async-start | bytes 4866048 | tf_op jit(solution)/shard_map/all_gather | solution.py:66
  218.5 119.0 %all-gather.13.cloned.1.call-start = ((), (), s32[]{:S(2)}) async-start(), calls=%async_computation.11 | async-start | bytes 4866048 | tf_op jit(solution)/shard_map/all_gather | solution.py:66
Sparse Core Ops, SparseCore 0:
  79.4 55.4 all-gather.6
  155.7 52.8 all-gather.8
  218.6 49.6 all-gather.10
  289.0 48.3 all-gather.12

commit v8 on v6

--- a/solution.py
+++ b/solution.py
@@ -68,6 +68,15 @@
     def inner_part(left, right):
         return jnp.sum(left * right)
 
+    d_out_part = out_inverse.shape[1]
+    in_cols = lax.all_gather(
+        lax.dynamic_slice_in_dim(in_inverse, lax.axis_index("fac") * d_out_part, d_out_part, axis=1),
+        FSDP,
+        axis=0,
+        tiled=True,
+    )
+
+    gradient, in_cols = lax.optimization_barrier((gradient, in_cols))
     residual = -gradient
     residual_rows = gather_rows(residual)
 
@@ -91,6 +100,9 @@
     image = curvature(direction)
     image_rows = gather_rows(image)
     inner_now, energy = global_sums(inner_part(residual, precond), inner_part(direction, image))
+    gram_inverse = lax.all_gather(
+        add_columns(gram_rows, in_cols).astype(jnp.bfloat16), "fac", axis=1, tiled=True
+    )
     alpha = inner_now / energy
     newton_step = alpha * direction
     residual = residual - alpha * image
@@ -98,8 +110,14 @@
         residual_rows.astype(jnp.float32) - alpha * image_rows.astype(jnp.float32)
     ).astype(jnp.bfloat16)
 
-    precond = precondition(next_rows)
-    precond_image = curvature(precond)
+    rows = in_inverse.shape[0]
+    left = jnp.concatenate([in_inverse, gram_inverse], axis=0)
+    both = add_columns(left, next_rows).astype(jnp.bfloat16)
+    both_out = jnp.dot(
+        lax.all_gather(both, "fac", axis=1, tiled=True), out_inverse, preferred_element_type=jnp.float32
+    )
+    precond = both_out[:rows]
+    precond_image = both_out[rows:] + damping * precond
     inner_next, z_hz, z_hd, d_hz = global_sums(
         inner_part(residual, precond),
         inner_part(precond, precond_image),

time: 375 us -> 346 us (0.923)
  waiting for transfers between devices: 75.1 us -> 45.1 us
  blocking collectives: 188 us -> 177 us
  starting transfers between devices: 0.34 us -> 11.1 us
    all_gather x4 -> x3, waiting for transfers between devices: 75 us -> 22.7 us  [gather_rows(): return lax.all_gather(matrix.astype(jnp.bfloat16), FSDP, axis=0, tiled=True)]
    all_gather x0 -> x2, waiting for transfers between devices: none -> 22.4 us  [the longest x1 22.4 us: body(): lax.all_gather(both, 'fac', axis=1, tiled=True)]
    all_to_all x2 -> x1, blocking collectives: 36.4 us -> 19.3 us  [global_sums(): received = lax.all_to_all(stacked, FSDP + ('fac',), 0, 0, tiled=True)]
    all_gather x2 -> x1, blocking collectives: 23.1 us -> 11.5 us  [precondition(): lax.all_gather(mixed_low, 'fac', axis=1, tiled=True)]
    all_gather x0 -> x1, blocking collectives: none -> 11.3 us  [body(): lax.all_gather(add_columns(gram_rows, in_cols).astype(jnp.bfloat16), 'fac...]
    all_to_all x0 -> x1, starting transfers between devices: none -> 10.9 us  [global_sums(): received = lax.all_to_all(stacked, FSDP + ('fac',), 0, 0, tiled=True)]
    all_to_all x3, blocking collectives: 93.9 us -> 99.5 us  [scatter_sum(): received = lax.all_to_all(chip_sum, 'pairs', 0, 0, tiled=False)]
    dot_general x2 -> x1, matrix products: 7.76 us -> 3.88 us  [precondition(): jnp.dot(lax.all_gather(mixed_low, 'fac', axis=1, tiled=True), out_inverse...]
  transfers between devices with their start and end apart: 4 -> 6, of which waited for: 2 -> 3; matrix products, arithmetic and copies ran while one was open for 10% -> 18% of each run, Pallas kernels for 0% -> 0%
where the time goes in v8:
time: 346 us; the launch traced here: 344 us
  blocking collectives  177 us (51%)
  matrix products  48.2 us (14%)
  waiting for transfers between devices  45.1 us (13%)
  local copies, waits for them, and re-layouts  26.7 us (8%)
  between operations  19.8 us (6%)
  other arithmetic  16.8 us (5%)
  starting transfers between devices  11.1 us (3%)
    all_to_all x3, blocking collectives, scatter_sum(): received = lax.all_to_all(chip_sum, 'pairs', 0, 0, tiled=False)  99.5 us
    all_to_all x3, blocking collectives, scatter_sum(): on_chip = lax.all_to_all(blocks, 'core', 1, 1, tiled=False)  23.4 us
    dot_general x3, matrix products, transposed_term(): lax.dot_general(matrix, right, (((0,), (0,)), ((), ())), preferred_elemen...  23.2 us
    all_gather x3, waiting for transfers between devices, gather_rows(): return lax.all_gather(matrix.astype(jnp.bfloat16), FSDP, axis=0, tiled=True)  22.7 us
    all_gather x1, waiting for transfers between devices, body(): lax.all_gather(both, 'fac', axis=1, tiled=True)  22.4 us
    all_to_all x1, blocking collectives, global_sums(): received = lax.all_to_all(stacked, FSDP + ('fac',), 0, 0, tiled=True)  19.3 us
    dot_general x4, matrix products, add_columns(): return jnp.dot(matrix, piece, preferred_element_type=jnp.float32)  17.3 us
    all_gather x1, blocking collectives, body(): lax.all_gather(gram_own.astype(jnp.bfloat16), 'fac', axis=1, tiled=True)  11.7 us
  transfers between devices with their start and end apart: 6, of which 3 were waited for; matrix products, arithmetic and copies ran while one was open for 18% of the time, Pallas kernels for 0%

profile of v8, /device:TPU:1, one launch (start us, length us, event | category | flops | bytes accessed | tf_op | source)
XLA Modules:
  0.0 344.4 jit_solution(2328392124073033827)
XLA Ops:
  9.6 9.4 %fusion.2 = bf16[3072,768]{0,1:T(8,128)(2,1)} fusion(bf16[1024,3072]{1,0:T(8,128)(2,1)} %param.7, bf16[1024,768]{1,0:T(8,128)(2,1)} %param.8, bf16[1024]{0:T(1024)(128)(2,1)S(1)} %convert_element_type.76), kind=kOutput, calls=%fused_computation.6 | convolution fusion | flops 4837343232 | bytes 12584960 | tf_op jit(solution)/shard_map/dot_general | solution.py:19
  19.0 6.7 %copy.24 = bf16[3072,768]{1,0:T(8,128)(2,1)} copy(bf16[3072,768]{0,1:T(8,128)(2,1)} %fusion.2) | data formatting | bytes 9437184 | tf_op jit(solution)/shard_map/convert_element_type | solution.py:53
  28.3 9.7 %all_to_all.42 = bf16[16,2,96,768]{3,2,0,1:T(8,128)(2,1)} all-to-all(bf16[16,2,96,768]{3,2,0,1:T(8,128)(2,1)S(1)} %copy.25), channel_id=1, replica_groups=mesh['pairs'=16,'core'=2,'fac'=4] {'core'}, dimensions={1} | all-to-all | bytes 9437184 | tf_op jit(solution)/shard_map/all_to_all | solution.py:30
  38.0 3.5 %reduce_sum.135 = bf16[16,96,768]{2,1,0:T(8,128)(2,1)S(1)} reduce(bf16[16,2,96,768]{3,2,0,1:T(8,128)(2,1)} %all_to_all.42, bf16[]{:T(256)} %constant.5.clone.1), dimensions={1}, to_apply=%region_0.0 | reduce | flops 1179648 | bytes 7077890 | tf_op jit(solution)/shard_map/reduce_sum | solution.py:31
  41.5 43.2 %all_to_all.43 = bf16[16,96,768]{2,1,0:T(8,128)(2,1)S(1)} all-to-all(bf16[16,96,768]{2,1,0:T(8,128)(2,1)S(1)} %reduce_sum.135), channel_id=1, replica_groups=mesh['pairs'=16,'core'=2,'fac'=4] {'pairs'}, dimensions={0} | all-to-all | bytes 4718592 | tf_op jit(solution)/shard_map/all_to_all | solution.py:32
  85.9 6.2 %gather_fusion = f32[1024]{0:T(1024)S(1)} fusion(f32[32768]{0:T(1024)S(1)} %copy-done, s32[1024]{0:T(1024)S(1)} %fusion.14), kind=kCustom, calls=%fused_computation | custom fusion | bytes 12288 | tf_op jit(solution)/shard_map/gather | solution.py:48
  95.0 7.0 %fusion.3 = bf16[3072,384]{0,1:T(8,128)(2,1)} fusion(bf16[1024,3072]{1,0:T(8,128)(2,1)} %param.7, bf16[1024,768]{1,0:T(8,128)(2,1)S(1)} %multiply_convert_fusion.1), kind=kOutput, calls=%fused_computation.9 | convolution fusion | flops 2417098752 | bytes 9437184 | tf_op jit(solution)/shard_map/dot_general | solution.py:19
  105.2 6.1 %all_to_all.44 = bf16[16,2,96,384]{3,2,0,1:T(8,128)(2,1)S(1)} all-to-all(bf16[16,2,96,384]{3,2,0,1:T(8,128)(2,1)S(1)} %copy.27), channel_id=1, replica_groups=mesh['pairs'=16,'core'=2,'fac'=4] {'core'}, dimensions={1} | all-to-all | bytes 4718592 | tf_op jit(solution)/shard_map/all_to_all | solution.py:30
  113.1 30.0 %all_to_all.45 = bf16[16,96,384]{2,1,0:T(8,128)(2,1)S(1)} all-to-all(bf16[16,96,384]{2,1,0:T(8,128)(2,1)} %reduce_sum.137), channel_id=1, replica_groups=mesh['pairs'=16,'core'=2,'fac'=4] {'pairs'}, dimensions={0} | all-to-all | bytes 2359296 | tf_op jit(solution)/shard_map/all_to_all | solution.py:32
  148.5 11.5 %all_gather.26 = bf16[96,3072]{1,0:T(8,128)(2,1)S(1)} all-gather(bf16[96,768]{1,0:T(8,128)(2,1)S(1)} %fusion.10), channel_id=1, replica_groups=mesh['pairs'=16,'core'=2,'fac'=4] {'fac'}, dimensions={1}, use_global_device_ids=true | all-gather | bytes 737280 | tf_op jit(solution)/shard_map/all_gather | solution.py:63
  160.0 3.9 %fusion.18 = (bf16[96,768]{1,0:T(8,128)(2,1)}, f32[96,768]{1,0:T(8,128)S(1)}) fusion(bf16[96,3072]{1,0:T(8,128)(2,1)S(1)} %all_gather.26, bf16[3072,768]{1,0:T(8,128)(2,1)} %param.13), kind=kOutput, calls=%fused_computation.47 | convolution fusion | flops 453058560 | bytes 5750784 | tf_op jit(solution)/shard_map/dot_general | solution.py:62
  163.9 6.8 %fusion.4 = bf16[3072,384]{0,1:T(8,128)(2,1)} fusion(bf16[1024,3072]{1,0:T(8,128)(2,1)} %param.7, bf16[1024,768]{1,0:T(8,128)(2,1)S(1)} %copy-done.3), kind=kOutput, calls=%fused_computation.10 | convolution fusion | flops 2417098752 | bytes 9437184 | tf_op jit(solution)/shard_map/dot_general | solution.py:19
  174.0 7.5 %all_to_all.46 = bf16[16,2,96,384]{3,2,0,1:T(8,128)(2,1)S(1)} all-to-all(bf16[16,2,96,384]{3,2,0,1:T(8,128)(2,1)S(1)} %copy.29), channel_id=1, replica_groups=mesh['pairs'=16,'core'=2,'fac'=4] {'core'}, dimensions={1} | all-to-all | bytes 4718592 | tf_op jit(solution)/shard_map/all_to_all | solution.py:30
  183.3 26.3 %all_to_all.47 = bf16[16,96,384]{2,1,0:T(8,128)(2,1)S(1)} all-to-all(bf16[16,96,384]{2,1,0:T(8,128)(2,1)} %reduce_sum.140), channel_id=1, replica_groups=mesh['pairs'=16,'core'=2,'fac'=4] {'pairs'}, dimensions={0} | all-to-all | bytes 2359296 | tf_op jit(solution)/shard_map/all_to_all | solution.py:32
  209.8 11.7 %all_gather.27 = bf16[96,3072]{1,0:T(8,128)(2,1)S(1)} all-gather(bf16[96,768]{1,0:T(8,128)(2,1)S(1)} %pad_maximum_fusion), channel_id=1, replica_groups=mesh['pairs'=16,'core'=2,'fac'=4] {'fac'}, dimensions={1}, use_global_device_ids=true | all-gather | bytes 737280 | tf_op jit(solution)/shard_map/all_gather | solution.py:94
  221.5 4.5 %multiply_reduce_fusion.5 = (f32[]{:T(128)}, f32[]{:T(128)}, bf16[96,768]{1,0:T(8,128)(2,1)}, f32[96,768]{1,0:T(8,128)S(1)}) fusion(f32[96,768]{1,0:T(8,128)S(1)} %get-tuple-element.26, f32[96,768]{1,0:T(8,128)S(1)} %convert_reduce_fusion, bf16[96,3072]{1,0:T(8,128)(2,1)S(1)} %all_gather.27, bf16[3072,768]{1,0:T(8,128)(2,1)} %all-gather.10.cloned.1.call-done), kind=kOutput, calls=%fused_computation.35 | convolution fusion | flops 453574656 | bytes 6340616 | tf_op jit(solution)/shard_map/dot_general | solution.py:15
  226.0 3.3 convolution_convert_fusion.3
  231.3 10.9 %all-to-all-start.6 = ((f32[128,1,2]{2,1,0:T(1,128)}), f32[128,1,2]{2,1,0:T(1,128)S(1)}, u32[]{:S(2)}, u32[]{:S(2)}) async-start(f32[128,1,2]{2,1,0:T(1,128)} %broadcast_in_dim.7), calls=%async_computation.6 | async-start | bytes 131072 | tf_op jit(solution)/shard_map/all_to_all | solution.py:39
  242.3 11.3 %all_gather.29 = bf16[96,3072]{1,0:T(8,128)(2,1)S(1)} all-gather(bf16[96,768]{1,0:T(8,128)(2,1)S(1)} %convolution_convert_fusion.3), channel_id=1, replica_groups=mesh['pairs'=16,'core'=2,'fac'=4] {'fac'}, dimensions={1}, use_global_device_ids=true | all-gather | bytes 737280 | tf_op jit(solution)/shard_map/all_gather | solution.py:103
  255.6 20.6 %all-gather.12.cloned.1.call-done = bf16[3072,768]{1,0:T(8,128)(2,1)} async-done(((bf16[96,768]{1,0:T(8,128)(2,1)}), bf16[3072,768]{1,0:T(8,128)(2,1)}) %all-gather.12.cloned.1.call-update) | async-done | bytes 4718608 | tf_op jit(solution)/shard_map/all_gather | solution.py:57
  276.3 6.3 %fusion.6 = bf16[192,768]{1,0:T(8,128)(2,1)} fusion(bf16[3072,768]{1,0:T(8,128)(2,1)} %all-gather.12.cloned.1.call-done, bf16[3072,768]{1,0:T(8,128)(2,1)} %all-gather.8.cloned.1.call-done, f32[]{:T(128)S(6)} %div.17, bf16[96,3072]{1,0:T(8,128)(2,1)S(1)} %all_gather.29, bf16[96,3072]{1,0:T(8,128)(2,1)S(1)} %copy-done.5), kind=kOutput, calls=%fused_computation.15 | convolution fusion | flops 920272896 | bytes 10911748 | tf_op jit(solution)/shard_map/dot_general | solution.py:15
  282.6 22.4 %all-gather.14.cloned.1.call-done = bf16[192,3072]{1,0:T(8,128)(2,1)} async-done(((bf16[192,768]{1,0:T(8,128)(2,1)}), bf16[192,3072]{1,0:T(8,128)(2,1)}) %all-gather.14.cloned.1.call-update) | async-done | bytes 1179664 | tf_op jit(solution)/shard_map/all_gather | solution.py:117
  305.0 3.8 %fusion.19 = f32[192,768]{1,0:T(8,128)S(1)} fusion(bf16[192,3072]{1,0:T(8,128)(2,1)} %all-gather.14.cloned.1.call-done, bf16[3072,768]{1,0:T(8,128)(2,1)} %param.13), kind=kOutput, calls=%fused_computation.48 | convolution fusion | flops 905969664 | bytes 6488064 | tf_op jit(solution)/shard_map/dot_general | solution.py:116
  312.2 19.3 %all_to_all.48 = f32[128,1,4]{2,1,0:T(1,128)S(1)} all-to-all(f32[128,1,4]{2,1,0:T(1,128)S(1)} %broadcast_in_dim.8), channel_id=1, replica_groups=mesh['pairs'=16,'core'=2,'fac'=4] {'pairs','core','fac'}, dimensions={0} | all-to-all | bytes 4096 | tf_op jit(solution)/shard_map/all_to_all | solution.py:39
  (58 shorter events, 32.8 us)
Async XLA Ops:
  7.2 78.7 %copy-start = (f32[32768]{0:T(1024)S(1)}, f32[32768]{0:T(1024)}, u32[]{:S(2)}) copy-start(f32[32768]{0:T(1024)} %param.11) | copy-start | bytes 393220
  7.2 77.9 %all-gather.6.cloned.1.call-start = ((), (), s32[]{:S(2)}) async-start(), calls=%async_computation.8 | async-start | bytes 4866048 | tf_op jit(solution)/shard_map/all_gather | solution.py:72
  8.8 136.4 %all-gather.8.cloned.1.call-start = ((), (), s32[]{:S(2)}) async-start(), calls=%async_computation.9 | async-start | bytes 4866048 | tf_op jit(solution)/shard_map/all_gather | solution.py:57
  41.5 44.3 %copy-start.7 = (s32[1024]{0:T(1024)S(1)}, s32[1024]{0:T(1024)}, u32[]{:S(2)}) copy-start(s32[1024]{0:T(1024)} %param.9) | copy-start | bytes 12292
  84.7 7.3 %copy-start.6 = (s32[1024]{0:T(1024)S(1)}, s32[1024]{0:T(1024)}, u32[]{:S(2)}) copy-start(s32[1024]{0:T(1024)} %param.10) | copy-start | bytes 12292
  85.8 135.7 %all-gather.10.cloned.1.call-start = ((), (), s32[]{:S(2)}) async-start(), calls=%async_computation.10 | async-start | bytes 4866048 | tf_op jit(solution)/shard_map/all_gather | solution.py:57
  93.8 1.1 copy-start.2
  111.3 34.0 %copy-start.4 = (bf16[96,3072]{1,0:T(8,128)(2,1)S(1)}, bf16[96,3072]{1,0:T(8,128)(2,1)}, u32[]{:S(2)}) copy-start(bf16[96,3072]{1,0:T(8,128)(2,1)} %param.12) | copy-start | bytes 1769476
  143.2 20.7 %copy-start.3 = (bf16[1024,768]{1,0:T(8,128)(2,1)S(1)}, bf16[1024,768]{1,0:T(8,128)(2,1)}, u32[]{:S(2)}) copy-start(bf16[1024,768]{1,0:T(8,128)(2,1)} %copy-done.2) | copy-start | bytes 4718596
  163.9 112.4 %all-gather.12.cloned.1.call-start = ((), (), s32[]{:S(2)}) async-start(), calls=%async_computation.11 | async-start | bytes 4866048 | tf_op jit(solution)/shard_map/all_gather | solution.py:57
  226.0 50.3 %copy-start.5 = (bf16[96,3072]{1,0:T(8,128)(2,1)S(1)}, bf16[96,3072]{1,0:T(8,128)(2,1)}, u32[]{:S(2)}) copy-start(bf16[96,3072]{1,0:T(8,128)(2,1)} %param.12) | copy-start | bytes 1769476
  231.3 22.3 %all-to-all-start.6 = ((f32[128,1,2]{2,1,0:T(1,128)}), f32[128,1,2]{2,1,0:T(1,128)S(1)}, u32[]{:S(2)}, u32[]{:S(2)}) async-start(f32[128,1,2]{2,1,0:T(1,128)} %broadcast_in_dim.7), calls=%async_computation.6 | async-start | bytes 131072 | tf_op jit(solution)/shard_map/all_to_all | solution.py:39
  242.2 62.7 %all-gather.14.cloned.1.call-start = ((), (), s32[]{:S(2)}) async-start(), calls=%async_computation.12 | async-start | bytes 1474560 | tf_op jit(solution)/shard_map/all_gather | solution.py:117
  282.6 55.2 %copy-start.1 = (f32[32768]{0:T(1024)S(1)}, f32[32768]{0:T(1024)}, u32[]{:S(2)}) copy-start(f32[32768]{0:T(1024)} %param.11) | copy-start | bytes 393220
Sparse Core Ops, SparseCore 0:
  10.8 68.8 all-gather.5
  85.9 59.2 all-gather.7
  164.0 53.3 all-gather.9
  226.1 50.0 all-gather.11
  282.7 22.2 all-gather.13

commit v9 on v8

--- a/solution.py
+++ b/solution.py
@@ -22,6 +22,26 @@
 
 
 FSDP = ("pairs", "core")
+
+
+def ring_product(piece, right):
+    n = lax.axis_size("fac")
+    me = lax.axis_index("fac")
+    width = piece.shape[1]
+
+    def right_block(k):
+        return lax.dynamic_slice_in_dim(right, (k % n) * width, width, axis=0)
+
+    total = add_columns(piece, right_block(me))
+    ahead = piece
+    behind = piece
+    for step in range(1, n // 2 + 1):
+        ahead = lax.ppermute(ahead, "fac", [(j, (j + 1) % n) for j in range(n)])
+        total = total + add_columns(ahead, right_block(me - step))
+        if 2 * step < n:
+            behind = lax.ppermute(behind, "fac", [(j, (j - 1) % n) for j in range(n)])
+            total = total + add_columns(behind, right_block(me + step))
+    return total
 
 
 def scatter_sum(partial):
@@ -113,9 +133,7 @@
     rows = in_inverse.shape[0]
     left = jnp.concatenate([in_inverse, gram_inverse], axis=0)
     both = add_columns(left, next_rows).astype(jnp.bfloat16)
-    both_out = jnp.dot(
-        lax.all_gather(both, "fac", axis=1, tiled=True), out_inverse, preferred_element_type=jnp.float32
-    )
+    both_out = ring_product(both, out_inverse)
     precond = both_out[:rows]
     precond_image = both_out[rows:] + damping * precond
     inner_next, z_hz, z_hd, d_hz = global_sums(

time: 346 us -> 335 us (0.968)
  waiting for transfers between devices: 45.1 us -> 33.1 us
  blocking collectives: 177 us -> 173 us
    all_gather x1 -> x0, waiting for transfers between devices: 22.4 us -> none  [body(): lax.all_gather(both, 'fac', axis=1, tiled=True)]
    ppermute x0 -> x3, waiting for transfers between devices: none -> 10.4 us  [the longest x2 10.4 us: ring_product(): ahead = lax.ppermute(ahead, 'fac', [(j, (j + 1) % n) for j in range(n)])]
    dot_general x4 -> x8, matrix products: 17.3 us -> 23.3 us  [add_columns(): return jnp.dot(matrix, piece, preferred_element_type=jnp.float32)]
    dot_general x1 -> x0, matrix products: 3.78 us -> none  [body(): jnp.dot(lax.all_gather(both, 'fac', axis=1, tiled=True), out_inverse, pre...]
  transfers between devices with their start and end apart: 6 -> 8, of which waited for: 3 -> 4; matrix products, arithmetic and copies ran while one was open for 18% -> 20% of each run, Pallas kernels for 0% -> 0%
where the time goes in v9:
time: 335 us; the launch traced here: 334 us
  blocking collectives  173 us (52%)
  matrix products  50.4 us (15%)
  waiting for transfers between devices  33.1 us (10%)
  local copies, waits for them, and re-layouts  26.6 us (8%)
  between operations  19.9 us (6%)
  other arithmetic  16.8 us (5%)
  starting transfers between devices  13.8 us (4%)
    all_to_all x3, blocking collectives, scatter_sum(): received = lax.all_to_all(chip_sum, 'pairs', 0, 0, tiled=False)  99.5 us
    all_to_all x3, blocking collectives, scatter_sum(): on_chip = lax.all_to_all(blocks, 'core', 1, 1, tiled=False)  23.4 us
    dot_general x8, matrix products, add_columns(): return jnp.dot(matrix, piece, preferred_element_type=jnp.float32)  23.3 us
    dot_general x3, matrix products, transposed_term(): lax.dot_general(matrix, right, (((0,), (0,)), ((), ())), preferred_elemen...  23.2 us
    all_gather x3, waiting for transfers between devices, gather_rows(): return lax.all_gather(matrix.astype(jnp.bfloat16), FSDP, axis=0, tiled=True)  22.6 us
    all_to_all x1, blocking collectives, global_sums(): received = lax.all_to_all(stacked, FSDP + ('fac',), 0, 0, tiled=True)  16 us
    all_gather x1, blocking collectives, body(): lax.all_gather(gram_own.astype(jnp.bfloat16), 'fac', axis=1, tiled=True)  11.7 us
    all_gather x1, blocking collectives, precondition(): lax.all_gather(mixed_low, 'fac', axis=1, tiled=True)  11.5 us
  transfers between devices with their start and end apart: 8, of which 4 were waited for; matrix products, arithmetic and copies ran while one was open for 20% of the time, Pallas kernels for 0%

profile of v9, /device:TPU:1, one launch (start us, length us, event | category | flops | bytes accessed | tf_op | source)
XLA Modules:
  0.0 333.9 jit_solution(15328082240654221681)
XLA Ops:
  9.6 9.4 %fusion.2 = bf16[3072,768]{0,1:T(8,128)(2,1)} fusion(bf16[1024,3072]{1,0:T(8,128)(2,1)} %param.7, bf16[1024,768]{1,0:T(8,128)(2,1)} %param.8, bf16[1024]{0:T(1024)(128)(2,1)S(1)} %convert_element_type.76), kind=kOutput, calls=%fused_computation.6 | convolution fusion | flops 4837343232 | bytes 12584960 | tf_op jit(solution)/shard_map/dot_general | solution.py:19
  19.0 6.7 %copy.24 = bf16[3072,768]{1,0:T(8,128)(2,1)} copy(bf16[3072,768]{0,1:T(8,128)(2,1)} %fusion.2) | data formatting | bytes 9437184 | tf_op jit(solution)/shard_map/convert_element_type | solution.py:73
  28.3 9.7 %all_to_all.42 = bf16[16,2,96,768]{3,2,0,1:T(8,128)(2,1)} all-to-all(bf16[16,2,96,768]{3,2,0,1:T(8,128)(2,1)S(1)} %copy.25), channel_id=1, replica_groups=mesh['pairs'=16,'core'=2,'fac'=4] {'core'}, dimensions={1} | all-to-all | bytes 9437184 | tf_op jit(solution)/shard_map/all_to_all | solution.py:50
  38.0 3.5 %reduce_sum.135 = bf16[16,96,768]{2,1,0:T(8,128)(2,1)S(1)} reduce(bf16[16,2,96,768]{3,2,0,1:T(8,128)(2,1)} %all_to_all.42, bf16[]{:T(256)} %constant.44.clone.1), dimensions={1}, to_apply=%region_0.0 | reduce | flops 1179648 | bytes 7077890 | tf_op jit(solution)/shard_map/reduce_sum | solution.py:51
  41.5 43.2 %all_to_all.43 = bf16[16,96,768]{2,1,0:T(8,128)(2,1)S(1)} all-to-all(bf16[16,96,768]{2,1,0:T(8,128)(2,1)S(1)} %reduce_sum.135), channel_id=1, replica_groups=mesh['pairs'=16,'core'=2,'fac'=4] {'pairs'}, dimensions={0} | all-to-all | bytes 4718592 | tf_op jit(solution)/shard_map/all_to_all | solution.py:52
  85.9 6.2 %gather_fusion = f32[1024]{0:T(1024)S(1)} fusion(f32[32768]{0:T(1024)S(1)} %copy-done, s32[1024]{0:T(1024)S(1)} %fusion.19), kind=kCustom, calls=%fused_computation | custom fusion | bytes 12288 | tf_op jit(solution)/shard_map/gather | solution.py:68
  95.0 7.0 %fusion.3 = bf16[3072,384]{0,1:T(8,128)(2,1)} fusion(bf16[1024,3072]{1,0:T(8,128)(2,1)} %param.7, bf16[1024,768]{1,0:T(8,128)(2,1)S(1)} %multiply_convert_fusion.1), kind=kOutput, calls=%fused_computation.9 | convolution fusion | flops 2417098752 | bytes 9437184 | tf_op jit(solution)/shard_map/dot_general | solution.py:19
  105.2 6.1 %all_to_all.44 = bf16[16,2,96,384]{3,2,0,1:T(8,128)(2,1)S(1)} all-to-all(bf16[16,2,96,384]{3,2,0,1:T(8,128)(2,1)S(1)} %copy.27), channel_id=1, replica_groups=mesh['pairs'=16,'core'=2,'fac'=4] {'core'}, dimensions={1} | all-to-all | bytes 4718592 | tf_op jit(solution)/shard_map/all_to_all | solution.py:50
  113.1 30.0 %all_to_all.45 = bf16[16,96,384]{2,1,0:T(8,128)(2,1)S(1)} all-to-all(bf16[16,96,384]{2,1,0:T(8,128)(2,1)} %reduce_sum.137), channel_id=1, replica_groups=mesh['pairs'=16,'core'=2,'fac'=4] {'pairs'}, dimensions={0} | all-to-all | bytes 2359296 | tf_op jit(solution)/shard_map/all_to_all | solution.py:52
  148.5 11.5 %all_gather.23 = bf16[96,3072]{1,0:T(8,128)(2,1)S(1)} all-gather(bf16[96,768]{1,0:T(8,128)(2,1)S(1)} %fusion.15), channel_id=1, replica_groups=mesh['pairs'=16,'core'=2,'fac'=4] {'fac'}, dimensions={1}, use_global_device_ids=true | all-gather | bytes 737280 | tf_op jit(solution)/shard_map/all_gather | solution.py:83
  160.0 3.9 %fusion.27 = (bf16[96,768]{1,0:T(8,128)(2,1)}, f32[96,768]{1,0:T(8,128)S(1)}) fusion(bf16[96,3072]{1,0:T(8,128)(2,1)S(1)} %all_gather.23, bf16[3072,768]{1,0:T(8,128)(2,1)} %param.13), kind=kOutput, calls=%fused_computation.59 | convolution fusion | flops 453058560 | bytes 5750784 | tf_op jit(solution)/shard_map/dot_general | solution.py:82
  163.9 6.8 %fusion.4 = bf16[3072,384]{0,1:T(8,128)(2,1)} fusion(bf16[1024,3072]{1,0:T(8,128)(2,1)} %param.7, bf16[1024,768]{1,0:T(8,128)(2,1)S(1)} %copy-done.3), kind=kOutput, calls=%fused_computation.10 | convolution fusion | flops 2417098752 | bytes 9437184 | tf_op jit(solution)/shard_map/dot_general | solution.py:19
  174.0 7.5 %all_to_all.46 = bf16[16,2,96,384]{3,2,0,1:T(8,128)(2,1)S(1)} all-to-all(bf16[16,2,96,384]{3,2,0,1:T(8,128)(2,1)S(1)} %copy.29), channel_id=1, replica_groups=mesh['pairs'=16,'core'=2,'fac'=4] {'core'}, dimensions={1} | all-to-all | bytes 4718592 | tf_op jit(solution)/shard_map/all_to_all | solution.py:50
  183.3 26.3 %all_to_all.47 = bf16[16,96,384]{2,1,0:T(8,128)(2,1)S(1)} all-to-all(bf16[16,96,384]{2,1,0:T(8,128)(2,1)} %reduce_sum.140), channel_id=1, replica_groups=mesh['pairs'=16,'core'=2,'fac'=4] {'pairs'}, dimensions={0} | all-to-all | bytes 2359296 | tf_op jit(solution)/shard_map/all_to_all | solution.py:52
  209.8 11.7 %all_gather.24 = bf16[96,3072]{1,0:T(8,128)(2,1)S(1)} all-gather(bf16[96,768]{1,0:T(8,128)(2,1)S(1)} %pad_maximum_fusion), channel_id=1, replica_groups=mesh['pairs'=16,'core'=2,'fac'=4] {'fac'}, dimensions={1}, use_global_device_ids=true | all-gather | bytes 737280 | tf_op jit(solution)/shard_map/all_gather | solution.py:114
  221.5 4.5 %multiply_reduce_fusion.5 = (f32[]{:T(128)}, f32[]{:T(128)}, bf16[96,768]{1,0:T(8,128)(2,1)}, f32[96,768]{1,0:T(8,128)S(1)}) fusion(f32[96,768]{1,0:T(8,128)S(1)} %get-tuple-element.26, f32[96,768]{1,0:T(8,128)S(1)} %convert_reduce_fusion, bf16[96,3072]{1,0:T(8,128)(2,1)S(1)} %all_gather.24, bf16[3072,768]{1,0:T(8,128)(2,1)} %all-gather.9.cloned.1.call-done), kind=kOutput, calls=%fused_computation.43 | convolution fusion | flops 453574656 | bytes 6340616 | tf_op jit(solution)/shard_map/dot_general | solution.py:15
  226.0 3.3 convolution_convert_fusion.3
  231.3 10.9 %all-to-all-start.6 = ((f32[128,1,2]{2,1,0:T(1,128)}), f32[128,1,2]{2,1,0:T(1,128)S(1)}, u32[]{:S(2)}, u32[]{:S(2)}) async-start(f32[128,1,2]{2,1,0:T(1,128)} %broadcast_in_dim.7), calls=%async_computation.6 | async-start | bytes 131072 | tf_op jit(solution)/shard_map/all_to_all | solution.py:59
  242.2 11.3 %all_gather.26 = bf16[96,3072]{1,0:T(8,128)(2,1)S(1)} all-gather(bf16[96,768]{1,0:T(8,128)(2,1)S(1)} %convolution_convert_fusion.3), channel_id=1, replica_groups=mesh['pairs'=16,'core'=2,'fac'=4] {'fac'}, dimensions={1}, use_global_device_ids=true | all-gather | bytes 737280 | tf_op jit(solution)/shard_map/all_gather | solution.py:123
  255.7 20.6 %all-gather.11.cloned.1.call-done = bf16[3072,768]{1,0:T(8,128)(2,1)} async-done(((bf16[96,768]{1,0:T(8,128)(2,1)}), bf16[3072,768]{1,0:T(8,128)(2,1)}) %all-gather.11.cloned.1.call-update) | async-done | bytes 4718608 | tf_op jit(solution)/shard_map/all_gather | solution.py:77
  276.2 5.6 %fusion.6 = bf16[192,768]{1,0:T(8,128)(2,1)S(1)} fusion(bf16[3072,768]{1,0:T(8,128)(2,1)} %all-gather.11.cloned.1.call-done, bf16[3072,768]{1,0:T(8,128)(2,1)} %all-gather.7.cloned.1.call-done, f32[]{:T(128)S(6)} %div.17, bf16[96,3072]{1,0:T(8,128)(2,1)S(1)} %all_gather.26, bf16[96,3072]{1,0:T(8,128)(2,1)S(1)} %copy-done.5), kind=kOutput, calls=%fused_computation.18 | convolution fusion | flops 920272896 | bytes 10911748 | tf_op jit(solution)/shard_map/dot_general | solution.py:15
  286.2 5.2 %collective-permute-done = bf16[192,768]{1,0:T(8,128)(2,1)S(1)} collective-permute-done((bf16[192,768]{1,0:T(8,128)(2,1)S(1)}, bf16[192,768]{1,0:T(8,128)(2,1)S(1)}, u32[]{:S(2)}, u32[]{:S(2)}) %collective-permute-start) | collective-permute-done | bytes 294944 | tf_op jit(solution)/shard_map/ppermute | solution.py:39
  294.9 5.2 %collective-permute-done.2 = bf16[192,768]{1,0:T(8,128)(2,1)S(1)} collective-permute-done((bf16[192,768]{1,0:T(8,128)(2,1)S(1)}, bf16[192,768]{1,0:T(8,128)(2,1)S(1)}, u32[]{:S(2)}, u32[]{:S(2)}) %collective-permute-start.2) | collective-permute-done | bytes 294944 | tf_op jit(solution)/shard_map/ppermute | solution.py:39
  305.2 16.0 %all_to_all.48 = f32[128,1,4]{2,1,0:T(1,128)S(1)} all-to-all(f32[128,1,4]{2,1,0:T(1,128)S(1)} %broadcast_in_dim.8), channel_id=1, replica_groups=mesh['pairs'=16,'core'=2,'fac'=4] {'pairs','core','fac'}, dimensions={0} | all-to-all | bytes 4096 | tf_op jit(solution)/shard_map/all_to_all | solution.py:59
  (64 shorter events, 42.1 us)
Async XLA Ops:
  7.2 78.7 %copy-start = (f32[32768]{0:T(1024)S(1)}, f32[32768]{0:T(1024)}, u32[]{:S(2)}) copy-start(f32[32768]{0:T(1024)} %param.11) | copy-start | bytes 393220
  7.2 77.9 %all-gather.5.cloned.1.call-start = ((), (), s32[]{:S(2)}) async-start(), calls=%async_computation.8 | async-start | bytes 4866048 | tf_op jit(solution)/shard_map/all_gather | solution.py:92
  8.8 136.4 %all-gather.7.cloned.1.call-start = ((), (), s32[]{:S(2)}) async-start(), calls=%async_computation.9 | async-start | bytes 4866048 | tf_op jit(solution)/shard_map/all_gather | solution.py:77
  41.5 44.3 %copy-start.7 = (s32[1024]{0:T(1024)S(1)}, s32[1024]{0:T(1024)}, u32[]{:S(2)}) copy-start(s32[1024]{0:T(1024)} %param.9) | copy-start | bytes 12292
  84.7 7.3 %copy-start.6 = (s32[1024]{0:T(1024)S(1)}, s32[1024]{0:T(1024)}, u32[]{:S(2)}) copy-start(s32[1024]{0:T(1024)} %param.10) | copy-start | bytes 12292
  85.8 135.7 %all-gather.9.cloned.1.call-start = ((), (), s32[]{:S(2)}) async-start(), calls=%async_computation.10 | async-start | bytes 4866048 | tf_op jit(solution)/shard_map/all_gather | solution.py:77
  93.8 1.1 copy-start.2
  111.3 34.0 %copy-start.4 = (bf16[96,3072]{1,0:T(8,128)(2,1)S(1)}, bf16[96,3072]{1,0:T(8,128)(2,1)}, u32[]{:S(2)}) copy-start(bf16[96,3072]{1,0:T(8,128)(2,1)} %param.12) | copy-start | bytes 1769476
  143.2 20.7 %copy-start.3 = (bf16[1024,768]{1,0:T(8,128)(2,1)S(1)}, bf16[1024,768]{1,0:T(8,128)(2,1)}, u32[]{:S(2)}) copy-start(bf16[1024,768]{1,0:T(8,128)(2,1)} %copy-done.2) | copy-start | bytes 4718596
  163.9 112.4 %all-gather.11.cloned.1.call-start = ((), (), s32[]{:S(2)}) async-start(), calls=%async_computation.11 | async-start | bytes 4866048 | tf_op jit(solution)/shard_map/all_gather | solution.py:77
  226.0 50.3 %copy-start.5 = (bf16[96,3072]{1,0:T(8,128)(2,1)S(1)}, bf16[96,3072]{1,0:T(8,128)(2,1)}, u32[]{:S(2)}) copy-start(bf16[96,3072]{1,0:T(8,128)(2,1)} %param.12) | copy-start | bytes 1769476
  231.3 22.2 %all-to-all-start.6 = ((f32[128,1,2]{2,1,0:T(1,128)}), f32[128,1,2]{2,1,0:T(1,128)S(1)}, u32[]{:S(2)}, u32[]{:S(2)}) async-start(f32[128,1,2]{2,1,0:T(1,128)} %broadcast_in_dim.7), calls=%async_computation.6 | async-start | bytes 131072 | tf_op jit(solution)/shard_map/all_to_all | solution.py:59
  281.8 9.6 %collective-permute-start = (bf16[192,768]{1,0:T(8,128)(2,1)S(1)}, bf16[192,768]{1,0:T(8,128)(2,1)S(1)}, u32[]{:S(2)}, u32[]{:S(2)}) collective-permute-start(bf16[192,768]{1,0:T(8,128)(2,1)S(1)} %fusion.6), channel_id=1, source_target_pairs={{0,1},{1,2},{2,3},{3,0},{4,5},{5,6},{6,7},{7,4},{8,9},{9,10},{10,1... | collective-permute-start | bytes 884744 | tf_op jit(solution)/shard_map/ppermute | solution.py:39
  283.1 10.1 %collective-permute-start.1 = (bf16[192,768]{1,0:T(8,128)(2,1)S(1)}, bf16[192,768]{1,0:T(8,128)(2,1)S(1)}, u32[]{:S(2)}, u32[]{:S(2)}) collective-permute-start(bf16[192,768]{1,0:T(8,128)(2,1)S(1)} %fusion.6), channel_id=1, source_target_pairs={{0,3},{1,0},{2,1},{3,2},{4,7},{5,4},{6,5},{7,6},{8,11},{9,8},{10,9... | collective-permute-start | bytes 884744 | tf_op jit(solution)/shard_map/ppermute | solution.py:42
  291.4 8.6 %collective-permute-start.2 = (bf16[192,768]{1,0:T(8,128)(2,1)S(1)}, bf16[192,768]{1,0:T(8,128)(2,1)S(1)}, u32[]{:S(2)}, u32[]{:S(2)}) collective-permute-start(bf16[192,768]{1,0:T(8,128)(2,1)S(1)} %collective-permute-done), channel_id=1, source_target_pairs={{0,1},{1,2},{2,3},{3,0},{4,5},{5,6},{6,7},{7,4},{8,9},{9,10},{10,1... | collective-permute-start | bytes 884744 | tf_op jit(solution)/shard_map/ppermute | solution.py:39
  291.4 35.9 %copy-start.1 = (f32[32768]{0:T(1024)S(1)}, f32[32768]{0:T(1024)}, u32[]{:S(2)}) copy-start(f32[32768]{0:T(1024)} %param.11) | copy-start | bytes 393220
Sparse Core Ops, SparseCore 0:
  10.8 68.8 all-gather.4
  85.9 59.2 all-gather.6
  164.0 53.3 all-gather.8
  226.1 50.0 all-gather.10

commit v10 on v9

--- a/solution.py
+++ b/solution.py
@@ -3,6 +3,7 @@
 import jax
 import jax.numpy as jnp
 from jax import lax
+from jax.experimental import pallas as pl
 from jax.sharding import PartitionSpec as P
 
 ITERS = 2
@@ -44,11 +45,30 @@
     return total
 
 
-def scatter_sum(partial):
+def block_term(acts_t, right, scale):
     pairs, cores = lax.axis_size("pairs"), lax.axis_size("core")
-    blocks = partial.reshape(pairs, cores, partial.shape[0] // (pairs * cores), partial.shape[1])
-    on_chip = lax.all_to_all(blocks, "core", 1, 1, tiled=False)
-    chip_sum = jnp.sum(on_chip.astype(jnp.float32), axis=1).astype(jnp.bfloat16)
+    rows = acts_t.shape[0] // (pairs * cores)
+    tokens, cols = right.shape
+
+    def kernel(a_ref, x_ref, o_ref):
+        product = jnp.dot(a_ref[...], x_ref[...], preferred_element_type=jnp.float32)
+        o_ref[0, 0] = (product * scale).astype(o_ref.dtype)
+
+    return pl.pallas_call(
+        kernel,
+        grid=(cores, pairs),
+        in_specs=[
+            pl.BlockSpec((rows, tokens), lambda k, p: (p * cores + k, 0)),
+            pl.BlockSpec((tokens, cols), lambda k, p: (0, 0)),
+        ],
+        out_specs=pl.BlockSpec((1, 1, rows, cols), lambda k, p: (k, p, 0, 0)),
+        out_shape=jax.ShapeDtypeStruct((cores, pairs, rows, cols), jnp.bfloat16),
+    )(acts_t, right)
+
+
+def scatter_sum(blocks):
+    on_chip = lax.all_to_all(blocks, "core", 0, 0, tiled=False)
+    chip_sum = jnp.sum(on_chip.astype(jnp.float32), axis=0).astype(jnp.bfloat16)
     received = lax.all_to_all(chip_sum, "pairs", 0, 0, tiled=False)
     return lax.optimization_barrier(jnp.sum(received.astype(jnp.float32), axis=0))
 
@@ -69,9 +89,8 @@
     forget_grads = out_grads * forget_mask.astype(jnp.bfloat16)[:, None]
     grad_scale = 1.0 / math.sqrt(total)
 
-    gradient = scatter_sum(
-        (transposed_term(activations, forget_grads) * grad_scale).astype(jnp.bfloat16)
-    )
+    acts_t = activations.T
+    gradient = scatter_sum(block_term(acts_t, forget_grads, grad_scale))
 
     def gather_rows(matrix):
         return lax.all_gather(matrix.astype(jnp.bfloat16), FSDP, axis=0, tiled=True)
@@ -106,8 +125,8 @@
     )
     weighted = (own_cols * weights[:, None]).astype(jnp.bfloat16)
     half = gram_cols // 2
-    gram_first = transposed_term(activations, weighted[:, :half]).astype(jnp.bfloat16)
-    gram_second = transposed_term(activations, weighted[:, half:]).astype(jnp.bfloat16)
+    gram_first = block_term(acts_t, weighted[:, :half], 1.0)
+    gram_second = block_term(acts_t, weighted[:, half:], 1.0)
     residual_rows, first_rows = lax.optimization_barrier((residual_rows, scatter_sum(gram_first)))
     precond = precondition(residual_rows)
     gram_own = jnp.concatenate([first_rows, scatter_sum(gram_second)], axis=1)

time: 335 us -> 368 us (1.099)
  Pallas kernels: 0 us -> 68.9 us
  matrix products: 50.4 us -> 27.2 us
  local copies, waits for them, and re-layouts: 26.6 us -> 19.9 us
  blocking collectives: 173 us -> 169 us
    pallas_call x0 -> x3, Pallas kernels: none -> 68.9 us  [block_term(): pl.pallas_call(kernel, grid=(cores, pairs), in_specs=[pl.BlockSpec((rows,...]
    dot_general x3 -> x0, matrix products: 23.2 us -> none  [transposed_term(): lax.dot_general(matrix, right, (((0,), (0,)), ((), ())), preferred_elemen...]
    all_to_all x3, blocking collectives: 99.5 us -> 85.4 us  [scatter_sum(): received = lax.all_to_all(chip_sum, 'pairs', 0, 0, tiled=False)]
    convert_element_type x3 -> x0, local copies, waits for them, and re-layouts: 12.6 us -> none  [the longest x1 6.65 us: body(): (transposed_term(activations, forget_grads) * grad_scale).astype(jnp.bflo...]
    all_to_all x3, blocking collectives: 23.4 us -> 33.3 us  [scatter_sum(): on_chip = lax.all_to_all(blocks, 'core', 0, 0, tiled=False)]
    unnamed x16 -> x15, local copies, waits for them, and re-layouts: 1.17 us -> 8.82 us
  transfers between devices with their start and end apart: 8 -> 8, of which waited for: 4 -> 3; matrix products, arithmetic and copies ran while one was open for 20% -> 11% of each run, Pallas kernels for 0% -> 19%
where the time goes in v10:
time: 368 us; the launch traced here: 365 us
  blocking collectives  169 us (46%)
  Pallas kernels  68.9 us (19%)
  waiting for transfers between devices  31.2 us (8%)
  matrix products  27.2 us (7%)
  local copies, waits for them, and re-layouts  19.9 us (5%)
  between operations  19.6 us (5%)
  other arithmetic  18.1 us (5%)
  starting transfers between devices  11 us (3%)
    all_to_all x3, blocking collectives, scatter_sum(): received = lax.all_to_all(chip_sum, 'pairs', 0, 0, tiled=False)  85.4 us
    pallas_call x3, Pallas kernels, block_term(): pl.pallas_call(kernel, grid=(cores, pairs), in_specs=[pl.BlockSpec((rows,...  68.9 us
    all_to_all x3, blocking collectives, scatter_sum(): on_chip = lax.all_to_all(blocks, 'core', 0, 0, tiled=False)  33.3 us
    dot_general x8, matrix products, add_columns(): return jnp.dot(matrix, piece, preferred_element_type=jnp.float32)  23.3 us
    all_gather x3, waiting for transfers between devices, gather_rows(): return lax.all_gather(matrix.astype(jnp.bfloat16), FSDP, axis=0, tiled=True)  20.7 us
    all_to_all x1, blocking collectives, global_sums(): received = lax.all_to_all(stacked, FSDP + ('fac',), 0, 0, tiled=True)  15.9 us
    all_gather x1, blocking collectives, precondition(): lax.all_gather(mixed_low, 'fac', axis=1, tiled=True)  11.8 us
    all_gather x1, blocking collectives, body(): lax.all_gather(gram_own.astype(jnp.bfloat16), 'fac', axis=1, tiled=True)  11.5 us
  transfers between devices with their start and end apart: 8, of which 3 were waited for; matrix products, arithmetic and copies ran while one was open for 11% of the time, Pallas kernels for 19%

profile of v10, /device:TPU:1, one launch (start us, length us, event | category | flops | bytes accessed | tf_op | source)
XLA Modules:
  0.0 365.2 jit_solution(6536354368932992721)
XLA Ops:
  9.6 8.8 %copy.12 = bf16[1024,3072]{0,1:T(8,128)(2,1)} copy(bf16[1024,3072]{1,0:T(8,128)(2,1)} %param.7) | data formatting | bytes 12582912 | tf_op args[0]
  19.7 24.4 %shard_map.86 = bf16[2,16,96,768]{3,2,1,0:T(8,128)(2,1)} custom-call(bf16[3072,1024]{1,0:T(8,128)(2,1)} %bitcast.26, bf16[1024,768]{1,0:T(8,128)(2,1)} %broadcast_multiply_fusion.x_ref), custom_call_target="tpu_custom_call" | custom-call | tf_op jit(solution)/shard_map/pallas_call | solution.py:57
  44.1 14.8 %all_to_all.42 = bf16[2,16,96,768]{3,2,1,0:T(8,128)(2,1)} all-to-all(bf16[2,16,96,768]{3,2,1,0:T(8,128)(2,1)} %shard_map.86), channel_id=1, replica_groups=mesh['pairs'=16,'core'=2,'fac'=4] {'core'}, dimensions={0} | all-to-all | bytes 9437184 | tf_op jit(solution)/shard_map/all_to_all | solution.py:70
  59.0 3.5 reduce_sum.135
  62.5 38.2 %all_to_all.43 = bf16[16,96,768]{2,1,0:T(8,128)(2,1)S(1)} all-to-all(bf16[16,96,768]{2,1,0:T(8,128)(2,1)S(1)} %reduce_sum.135), channel_id=1, replica_groups=mesh['pairs'=16,'core'=2,'fac'=4] {'pairs'}, dimensions={0} | all-to-all | bytes 4718592 | tf_op jit(solution)/shard_map/all_to_all | solution.py:72
  101.9 6.2 %gather_fusion = f32[1024]{0:T(1024)S(1)} fusion(f32[32768]{0:T(1024)S(1)} %copy-done, s32[1024]{0:T(1024)S(1)} %fusion.12), kind=kCustom, calls=%fused_computation | custom fusion | bytes 12288 | tf_op jit(solution)/shard_map/gather | solution.py:88
  111.1 22.3 %shard_map.87 = bf16[2,16,96,384]{3,2,1,0:T(8,128)(2,1)} custom-call(bf16[3072,1024]{1,0:T(8,128)(2,1)} %bitcast.27, bf16[1024,384]{1,0:T(8,128)(2,1)} %get-tuple-element.17.x_ref), custom_call_target="tpu_custom_call" | custom-call | tf_op jit(solution)/shard_map/pallas_call | solution.py:57
  133.4 8.5 %all_to_all.44 = bf16[2,16,96,384]{3,2,1,0:T(8,128)(2,1)S(1)} all-to-all(bf16[2,16,96,384]{3,2,1,0:T(8,128)(2,1)} %shard_map.87), channel_id=1, replica_groups=mesh['pairs'=16,'core'=2,'fac'=4] {'core'}, dimensions={0} | all-to-all | bytes 4718592 | tf_op jit(solution)/shard_map/all_to_all | solution.py:70
  143.7 22.0 %all_to_all.45 = bf16[16,96,384]{2,1,0:T(8,128)(2,1)S(1)} all-to-all(bf16[16,96,384]{2,1,0:T(8,128)(2,1)} %reduce_sum.137), channel_id=1, replica_groups=mesh['pairs'=16,'core'=2,'fac'=4] {'pairs'}, dimensions={0} | all-to-all | bytes 2359296 | tf_op jit(solution)/shard_map/all_to_all | solution.py:72
  169.1 11.8 %all_gather.23 = bf16[96,3072]{1,0:T(8,128)(2,1)S(1)} all-gather(bf16[96,768]{1,0:T(8,128)(2,1)S(1)} %fusion.11), channel_id=1, replica_groups=mesh['pairs'=16,'core'=2,'fac'=4] {'fac'}, dimensions={1}, use_global_device_ids=true | all-gather | bytes 737280 | tf_op jit(solution)/shard_map/all_gather | solution.py:102
  180.8 3.9 %fusion.21 = (bf16[96,768]{1,0:T(8,128)(2,1)}, f32[96,768]{1,0:T(8,128)S(1)}) fusion(bf16[96,3072]{1,0:T(8,128)(2,1)S(1)} %all_gather.23, bf16[3072,768]{1,0:T(8,128)(2,1)} %param.13), kind=kOutput, calls=%fused_computation.51 | convolution fusion | flops 453058560 | bytes 5750784 | tf_op jit(solution)/shard_map/dot_general | solution.py:101
  184.8 22.2 %shard_map.88 = bf16[2,16,96,384]{3,2,1,0:T(8,128)(2,1)} custom-call(bf16[3072,1024]{1,0:T(8,128)(2,1)} %bitcast.28, bf16[1024,384]{1,0:T(8,128)(2,1)} %get-tuple-element.16.x_ref), custom_call_target="tpu_custom_call" | custom-call | tf_op jit(solution)/shard_map/pallas_call | solution.py:57
  207.0 10.0 %all_to_all.46 = bf16[2,16,96,384]{3,2,1,0:T(8,128)(2,1)S(1)} all-to-all(bf16[2,16,96,384]{3,2,1,0:T(8,128)(2,1)} %shard_map.88), channel_id=1, replica_groups=mesh['pairs'=16,'core'=2,'fac'=4] {'core'}, dimensions={0} | all-to-all | bytes 4718592 | tf_op jit(solution)/shard_map/all_to_all | solution.py:70
  218.8 25.2 %all_to_all.47 = bf16[16,96,384]{2,1,0:T(8,128)(2,1)S(1)} all-to-all(bf16[16,96,384]{2,1,0:T(8,128)(2,1)} %reduce_sum.140), channel_id=1, replica_groups=mesh['pairs'=16,'core'=2,'fac'=4] {'pairs'}, dimensions={0} | all-to-all | bytes 2359296 | tf_op jit(solution)/shard_map/all_to_all | solution.py:72
  244.1 11.5 %all_gather.24 = bf16[96,3072]{1,0:T(8,128)(2,1)S(1)} all-gather(bf16[96,768]{1,0:T(8,128)(2,1)S(1)} %pad_maximum_fusion), channel_id=1, replica_groups=mesh['pairs'=16,'core'=2,'fac'=4] {'fac'}, dimensions={1}, use_global_device_ids=true | all-gather | bytes 737280 | tf_op jit(solution)/shard_map/all_gather | solution.py:133
  255.6 4.5 %multiply_reduce_fusion.5 = (f32[]{:T(128)}, f32[]{:T(128)}, bf16[96,768]{1,0:T(8,128)(2,1)}, f32[96,768]{1,0:T(8,128)S(1)}) fusion(f32[96,768]{1,0:T(8,128)S(1)} %get-tuple-element.28, f32[96,768]{1,0:T(8,128)S(1)} %convert_reduce_fusion, bf16[96,3072]{1,0:T(8,128)(2,1)S(1)} %all_gather.24, bf16[3072,768]{1,0:T(8,128)(2,1)} %all-gather.9.cloned.1.call-done), kind=kOutput, calls=%fused_computation.34 | convolution fusion | flops 453574656 | bytes 6340616 | tf_op jit(solution)/shard_map/dot_general | solution.py:16
  260.1 3.3 convolution_convert_fusion.1
  265.3 8.1 %all-to-all-start.6 = ((f32[128,1,2]{2,1,0:T(1,128)}), f32[128,1,2]{2,1,0:T(1,128)S(1)}, u32[]{:S(2)}, u32[]{:S(2)}) async-start(f32[128,1,2]{2,1,0:T(1,128)} %broadcast_in_dim.7), calls=%async_computation.6 | async-start | bytes 131072 | tf_op jit(solution)/shard_map/all_to_all | solution.py:79
  273.4 11.5 %all_gather.26 = bf16[96,3072]{1,0:T(8,128)(2,1)S(1)} all-gather(bf16[96,768]{1,0:T(8,128)(2,1)S(1)} %convolution_convert_fusion.1), channel_id=1, replica_groups=mesh['pairs'=16,'core'=2,'fac'=4] {'fac'}, dimensions={1}, use_global_device_ids=true | all-gather | bytes 737280 | tf_op jit(solution)/shard_map/all_gather | solution.py:142
  286.9 20.7 %all-gather.11.cloned.1.call-done = bf16[3072,768]{1,0:T(8,128)(2,1)} async-done(((bf16[96,768]{1,0:T(8,128)(2,1)}), bf16[3072,768]{1,0:T(8,128)(2,1)}) %all-gather.11.cloned.1.call-update) | async-done | bytes 4718608 | tf_op jit(solution)/shard_map/all_gather | solution.py:96
  307.6 5.6 %fusion.2 = bf16[192,768]{1,0:T(8,128)(2,1)S(1)} fusion(bf16[3072,768]{1,0:T(8,128)(2,1)} %all-gather.11.cloned.1.call-done, bf16[3072,768]{1,0:T(8,128)(2,1)} %all-gather.7.cloned.1.call-done, f32[]{:T(128)S(6)} %div.17, bf16[96,3072]{1,0:T(8,128)(2,1)S(1)} %all_gather.26, bf16[96,3072]{1,0:T(8,128)(2,1)S(1)} %copy-done.4), kind=kOutput, calls=%fused_computation.11 | convolution fusion | flops 920272896 | bytes 10911748 | tf_op jit(solution)/shard_map/dot_general | solution.py:16
  317.6 5.2 %collective-permute-done = bf16[192,768]{1,0:T(8,128)(2,1)S(1)} collective-permute-done((bf16[192,768]{1,0:T(8,128)(2,1)S(1)}, bf16[192,768]{1,0:T(8,128)(2,1)S(1)}, u32[]{:S(2)}, u32[]{:S(2)}) %collective-permute-start) | collective-permute-done | bytes 294944 | tf_op jit(solution)/shard_map/ppermute | solution.py:40
  326.2 5.2 %collective-permute-done.2 = bf16[192,768]{1,0:T(8,128)(2,1)S(1)} collective-permute-done((bf16[192,768]{1,0:T(8,128)(2,1)S(1)}, bf16[192,768]{1,0:T(8,128)(2,1)S(1)}, u32[]{:S(2)}, u32[]{:S(2)}) %collective-permute-start.2) | collective-permute-done | bytes 294944 | tf_op jit(solution)/shard_map/ppermute | solution.py:40
  336.6 15.9 %all_to_all.48 = f32[128,1,4]{2,1,0:T(1,128)S(1)} all-to-all(f32[128,1,4]{2,1,0:T(1,128)S(1)} %broadcast_in_dim.8), channel_id=1, replica_groups=mesh['pairs'=16,'core'=2,'fac'=4] {'pairs','core','fac'}, dimensions={0} | all-to-all | bytes 4096 | tf_op jit(solution)/shard_map/all_to_all | solution.py:79
  (59 shorter events, 32.5 us)
Async XLA Ops:
  7.2 94.7 %copy-start = (f32[32768]{0:T(1024)S(1)}, f32[32768]{0:T(1024)}, u32[]{:S(2)}) copy-start(f32[32768]{0:T(1024)} %param.11) | copy-start | bytes 393220
  7.2 93.9 %all-gather.5.cloned.1.call-start = ((), (), s32[]{:S(2)}) async-start(), calls=%async_computation.8 | async-start | bytes 4866048 | tf_op jit(solution)/shard_map/all_gather | solution.py:111
  8.8 157.0 %all-gather.7.cloned.1.call-start = ((), (), s32[]{:S(2)}) async-start(), calls=%async_computation.9 | async-start | bytes 4866048 | tf_op jit(solution)/shard_map/all_gather | solution.py:96
  9.6 8.8 %copy-start.2 = (bf16[1024,768]{1,0:T(8,128)(2,1)S(1)}, bf16[1024,768]{1,0:T(8,128)(2,1)}, u32[]{:S(2)}) copy-start(bf16[1024,768]{1,0:T(8,128)(2,1)} %param.8) | copy-start | bytes 4718596
  62.5 39.3 %copy-start.6 = (s32[1024]{0:T(1024)S(1)}, s32[1024]{0:T(1024)}, u32[]{:S(2)}) copy-start(s32[1024]{0:T(1024)} %param.9) | copy-start | bytes 12292
  100.7 7.3 %copy-start.5 = (s32[1024]{0:T(1024)S(1)}, s32[1024]{0:T(1024)}, u32[]{:S(2)}) copy-start(s32[1024]{0:T(1024)} %param.10) | copy-start | bytes 12292
  101.8 153.8 %all-gather.9.cloned.1.call-start = ((), (), s32[]{:S(2)}) async-start(), calls=%async_computation.10 | async-start | bytes 4866048 | tf_op jit(solution)/shard_map/all_gather | solution.py:96
  141.9 23.9 %copy-start.3 = (bf16[96,3072]{1,0:T(8,128)(2,1)S(1)}, bf16[96,3072]{1,0:T(8,128)(2,1)}, u32[]{:S(2)}) copy-start(bf16[96,3072]{1,0:T(8,128)(2,1)} %param.12) | copy-start | bytes 1769476
  184.7 122.8 %all-gather.11.cloned.1.call-start = ((), (), s32[]{:S(2)}) async-start(), calls=%async_computation.11 | async-start | bytes 4866048 | tf_op jit(solution)/shard_map/all_gather | solution.py:96
  260.1 47.5 %copy-start.4 = (bf16[96,3072]{1,0:T(8,128)(2,1)S(1)}, bf16[96,3072]{1,0:T(8,128)(2,1)}, u32[]{:S(2)}) copy-start(bf16[96,3072]{1,0:T(8,128)(2,1)} %param.12) | copy-start | bytes 1769476
  265.3 19.6 %all-to-all-start.6 = ((f32[128,1,2]{2,1,0:T(1,128)}), f32[128,1,2]{2,1,0:T(1,128)S(1)}, u32[]{:S(2)}, u32[]{:S(2)}) async-start(f32[128,1,2]{2,1,0:T(1,128)} %broadcast_in_dim.7), calls=%async_computation.6 | async-start | bytes 131072 | tf_op jit(solution)/shard_map/all_to_all | solution.py:79
  313.1 9.6 %collective-permute-start = (bf16[192,768]{1,0:T(8,128)(2,1)S(1)}, bf16[192,768]{1,0:T(8,128)(2,1)S(1)}, u32[]{:S(2)}, u32[]{:S(2)}) collective-permute-start(bf16[192,768]{1,0:T(8,128)(2,1)S(1)} %fusion.2), channel_id=1, source_target_pairs={{0,1},{1,2},{2,3},{3,0},{4,5},{5,6},{6,7},{7,4},{8,9},{9,10},{10,1... | collective-permute-start | bytes 884744 | tf_op jit(solution)/shard_map/ppermute | solution.py:40
  314.4 10.1 %collective-permute-start.1 = (bf16[192,768]{1,0:T(8,128)(2,1)S(1)}, bf16[192,768]{1,0:T(8,128)(2,1)S(1)}, u32[]{:S(2)}, u32[]{:S(2)}) collective-permute-start(bf16[192,768]{1,0:T(8,128)(2,1)S(1)} %fusion.2), channel_id=1, source_target_pairs={{0,3},{1,0},{2,1},{3,2},{4,7},{5,4},{6,5},{7,6},{8,11},{9,8},{10,9... | collective-permute-start | bytes 884744 | tf_op jit(solution)/shard_map/ppermute | solution.py:43
  322.8 8.6 %collective-permute-start.2 = (bf16[192,768]{1,0:T(8,128)(2,1)S(1)}, bf16[192,768]{1,0:T(8,128)(2,1)S(1)}, u32[]{:S(2)}, u32[]{:S(2)}) collective-permute-start(bf16[192,768]{1,0:T(8,128)(2,1)S(1)} %collective-permute-done), channel_id=1, source_target_pairs={{0,1},{1,2},{2,3},{3,0},{4,5},{5,6},{6,7},{7,4},{8,9},{9,10},{10,1... | collective-permute-start | bytes 884744 | tf_op jit(solution)/shard_map/ppermute | solution.py:40
  322.8 35.9 %copy-start.1 = (f32[32768]{0:T(1024)S(1)}, f32[32768]{0:T(1024)}, u32[]{:S(2)}) copy-start(f32[32768]{0:T(1024)} %param.11) | copy-start | bytes 393220
Sparse Core Ops, SparseCore 0:
  10.8 50.7 all-gather.4
  101.9 45.7 all-gather.6
  184.9 55.2 all-gather.8
  260.2 47.2 all-gather.10

commit v11 on v10

--- a/solution.py
+++ b/solution.py
@@ -45,25 +45,31 @@
     return total
 
 
-def block_term(acts_t, right, scale):
+def block_term(activations, right, scale):
     pairs, cores = lax.axis_size("pairs"), lax.axis_size("core")
-    rows = acts_t.shape[0] // (pairs * cores)
-    tokens, cols = right.shape
+    tokens, d_in = activations.shape
+    rows = d_in // (pairs * cores)
+    cols = right.shape[1]
+    step = 384 if cols % 384 == 0 else cols
 
     def kernel(a_ref, x_ref, o_ref):
-        product = jnp.dot(a_ref[...], x_ref[...], preferred_element_type=jnp.float32)
-        o_ref[0, 0] = (product * scale).astype(o_ref.dtype)
+        product = lax.dot_general(
+            a_ref[...], x_ref[...], (((0,), (0,)), ((), ())), preferred_element_type=jnp.float32
+        )
+        product = (product * scale).astype(o_ref.dtype)
+        for block in range(pairs * cores):
+            o_ref[block % cores, block // cores] = product[block * rows : (block + 1) * rows]
 
     return pl.pallas_call(
         kernel,
-        grid=(cores, pairs),
+        grid=(cols // step,),
         in_specs=[
-            pl.BlockSpec((rows, tokens), lambda k, p: (p * cores + k, 0)),
-            pl.BlockSpec((tokens, cols), lambda k, p: (0, 0)),
+            pl.BlockSpec((tokens, d_in), lambda j: (0, 0)),
+            pl.BlockSpec((tokens, step), lambda j: (0, j)),
         ],
-        out_specs=pl.BlockSpec((1, 1, rows, cols), lambda k, p: (k, p, 0, 0)),
+        out_specs=pl.BlockSpec((cores, pairs, rows, step), lambda j: (0, 0, 0, j)),
         out_shape=jax.ShapeDtypeStruct((cores, pairs, rows, cols), jnp.bfloat16),
-    )(acts_t, right)
+    )(activations, right)
 
 
 def scatter_sum(blocks):
@@ -89,8 +95,7 @@
     forget_grads = out_grads * forget_mask.astype(jnp.bfloat16)[:, None]
     grad_scale = 1.0 / math.sqrt(total)
 
-    acts_t = activations.T
-    gradient = scatter_sum(block_term(acts_t, forget_grads, grad_scale))
+    gradient = scatter_sum(block_term(activations, forget_grads, grad_scale))
 
     def gather_rows(matrix):
         return lax.all_gather(matrix.astype(jnp.bfloat16), FSDP, axis=0, tiled=True)
@@ -125,8 +130,8 @@
     )
     weighted = (own_cols * weights[:, None]).astype(jnp.bfloat16)
     half = gram_cols // 2
-    gram_first = block_term(acts_t, weighted[:, :half], 1.0)
-    gram_second = block_term(acts_t, weighted[:, half:], 1.0)
+    gram_first = block_term(activations, weighted[:, :half], 1.0)
+    gram_second = block_term(activations, weighted[:, half:], 1.0)
     residual_rows, first_rows = lax.optimization_barrier((residual_rows, scatter_sum(gram_first)))
     precond = precondition(residual_rows)
     gram_own = jnp.concatenate([first_rows, scatter_sum(gram_second)], axis=1)

time: 368 us -> 332 us (0.902)
  Pallas kernels: 68.9 us -> 27.2 us
  blocking collectives: 169 us -> 179 us
  local copies, waits for them, and re-layouts: 19.9 us -> 11 us
    pallas_call x3, Pallas kernels: 68.9 us -> 27.2 us  [block_term(): pl.pallas_call(kernel, grid=(cols // step,), in_specs=[pl.BlockSpec((toke...]
    all_to_all x3, blocking collectives: 85.4 us -> 98.6 us  [scatter_sum(): received = lax.all_to_all(chip_sum, 'pairs', 0, 0, tiled=False)]
    unnamed x15 -> x12, local copies, waits for them, and re-layouts: 8.82 us -> 0.04 us
  transfers between devices with their start and end apart: 8 -> 8, of which waited for: 3 -> 4; matrix products, arithmetic and copies ran while one was open for 11% -> 10% of each run, Pallas kernels for 19% -> 8%
where the time goes in v11:
time: 332 us; the launch traced here: 331 us
  blocking collectives  179 us (54%)
  waiting for transfers between devices  33.5 us (10%)
  Pallas kernels  27.2 us (8%)
  matrix products  27.2 us (8%)
  between operations  19.8 us (6%)
  other arithmetic  19.6 us (6%)
  starting transfers between devices  13.7 us (4%)
  local copies, waits for them, and re-layouts  11 us (3%)
    all_to_all x3, blocking collectives, scatter_sum(): received = lax.all_to_all(chip_sum, 'pairs', 0, 0, tiled=False)  98.6 us
    all_to_all x3, blocking collectives, scatter_sum(): on_chip = lax.all_to_all(blocks, 'core', 0, 0, tiled=False)  30 us
    pallas_call x3, Pallas kernels, block_term(): pl.pallas_call(kernel, grid=(cols // step,), in_specs=[pl.BlockSpec((toke...  27.2 us
    dot_general x8, matrix products, add_columns(): return jnp.dot(matrix, piece, preferred_element_type=jnp.float32)  23.3 us
    all_gather x3, waiting for transfers between devices, gather_rows(): return lax.all_gather(matrix.astype(jnp.bfloat16), FSDP, axis=0, tiled=True)  22.9 us
    all_to_all x1, blocking collectives, global_sums(): received = lax.all_to_all(stacked, FSDP + ('fac',), 0, 0, tiled=True)  15.9 us
    all_gather x1, blocking collectives, body(): lax.all_gather(gram_own.astype(jnp.bfloat16), 'fac', axis=1, tiled=True)  11.6 us
    all_gather x1, blocking collectives, precondition(): lax.all_gather(mixed_low, 'fac', axis=1, tiled=True)  11.4 us
  transfers between devices with their start and end apart: 8, of which 4 were waited for; matrix products, arithmetic and copies ran while one was open for 10% of the time, Pallas kernels for 8%

profile of v11, /device:TPU:1, one launch (start us, length us, event | category | flops | bytes accessed | tf_op | source)
XLA Modules:
  0.0 330.8 jit_solution(16016968158624077435)
XLA Ops:
  12.4 11.5 %shard_map.86 = bf16[2,16,96,768]{3,2,1,0:T(8,128)(2,1)} custom-call(bf16[1024,3072]{1,0:T(8,128)(2,1)} %a_ref.5, bf16[1024,768]{1,0:T(8,128)(2,1)} %broadcast_multiply_fusion.x_ref), custom_call_target="tpu_custom_call" | custom-call | tf_op jit(solution)/shard_map/pallas_call | solution.py:63
  23.8 13.8 %all_to_all.42 = bf16[2,16,96,768]{3,2,1,0:T(8,128)(2,1)} all-to-all(bf16[2,16,96,768]{3,2,1,0:T(8,128)(2,1)} %shard_map.86), channel_id=1, replica_groups=mesh['pairs'=16,'core'=2,'fac'=4] {'core'}, dimensions={0} | all-to-all | bytes 9437184 | tf_op jit(solution)/shard_map/all_to_all | solution.py:76
  37.6 3.5 %reduce_sum.135 = bf16[16,96,768]{2,1,0:T(8,128)(2,1)S(1)} reduce(bf16[2,16,96,768]{3,2,1,0:T(8,128)(2,1)} %all_to_all.42, bf16[]{:T(256)} %constant.42.clone.1), dimensions={0}, to_apply=%region_0.0 | reduce | flops 1179648 | bytes 7077890 | tf_op jit(solution)/shard_map/reduce_sum | solution.py:77
  41.1 43.5 %all_to_all.43 = bf16[16,96,768]{2,1,0:T(8,128)(2,1)S(1)} all-to-all(bf16[16,96,768]{2,1,0:T(8,128)(2,1)S(1)} %reduce_sum.135), channel_id=1, replica_groups=mesh['pairs'=16,'core'=2,'fac'=4] {'pairs'}, dimensions={0} | all-to-all | bytes 4718592 | tf_op jit(solution)/shard_map/all_to_all | solution.py:78
  85.8 6.2 %gather_fusion = f32[1024]{0:T(1024)S(1)} fusion(f32[32768]{0:T(1024)S(1)} %copy-done, s32[1024]{0:T(1024)S(1)} %fusion.12), kind=kCustom, calls=%fused_computation | custom fusion | bytes 12288 | tf_op jit(solution)/shard_map/gather | solution.py:94
  95.0 7.9 %shard_map.87 = bf16[2,16,96,384]{3,2,1,0:T(8,128)(2,1)} custom-call(bf16[1024,3072]{1,0:T(8,128)(2,1)} %a_ref.5, bf16[1024,384]{1,0:T(8,128)(2,1)} %get-tuple-element.17.x_ref), custom_call_target="tpu_custom_call" | custom-call | tf_op jit(solution)/shard_map/pallas_call | solution.py:63
  102.9 7.5 %all_to_all.44 = bf16[2,16,96,384]{3,2,1,0:T(8,128)(2,1)S(1)} all-to-all(bf16[2,16,96,384]{3,2,1,0:T(8,128)(2,1)} %shard_map.87), channel_id=1, replica_groups=mesh['pairs'=16,'core'=2,'fac'=4] {'core'}, dimensions={0} | all-to-all | bytes 4718592 | tf_op jit(solution)/shard_map/all_to_all | solution.py:76
  112.2 29.7 %all_to_all.45 = bf16[16,96,384]{2,1,0:T(8,128)(2,1)S(1)} all-to-all(bf16[16,96,384]{2,1,0:T(8,128)(2,1)} %reduce_sum.137), channel_id=1, replica_groups=mesh['pairs'=16,'core'=2,'fac'=4] {'pairs'}, dimensions={0} | all-to-all | bytes 2359296 | tf_op jit(solution)/shard_map/all_to_all | solution.py:78
  144.4 3.2 fusion.11
  147.6 11.4 %all_gather.23 = bf16[96,3072]{1,0:T(8,128)(2,1)S(1)} all-gather(bf16[96,768]{1,0:T(8,128)(2,1)S(1)} %fusion.11), channel_id=1, replica_groups=mesh['pairs'=16,'core'=2,'fac'=4] {'fac'}, dimensions={1}, use_global_device_ids=true | all-gather | bytes 737280 | tf_op jit(solution)/shard_map/all_gather | solution.py:107
  159.0 3.9 %fusion.21 = (bf16[96,768]{1,0:T(8,128)(2,1)}, f32[96,768]{1,0:T(8,128)S(1)}) fusion(bf16[96,3072]{1,0:T(8,128)(2,1)S(1)} %all_gather.23, bf16[3072,768]{1,0:T(8,128)(2,1)} %param.13), kind=kOutput, calls=%fused_computation.51 | convolution fusion | flops 453058560 | bytes 5750784 | tf_op jit(solution)/shard_map/dot_general | solution.py:106
  163.0 7.8 %shard_map.88 = bf16[2,16,96,384]{3,2,1,0:T(8,128)(2,1)} custom-call(bf16[1024,3072]{1,0:T(8,128)(2,1)} %a_ref.5, bf16[1024,384]{1,0:T(8,128)(2,1)} %get-tuple-element.16.x_ref), custom_call_target="tpu_custom_call" | custom-call | tf_op jit(solution)/shard_map/pallas_call | solution.py:63
  170.8 8.7 %all_to_all.46 = bf16[2,16,96,384]{3,2,1,0:T(8,128)(2,1)S(1)} all-to-all(bf16[2,16,96,384]{3,2,1,0:T(8,128)(2,1)} %shard_map.88), channel_id=1, replica_groups=mesh['pairs'=16,'core'=2,'fac'=4] {'core'}, dimensions={0} | all-to-all | bytes 4718592 | tf_op jit(solution)/shard_map/all_to_all | solution.py:76
  181.3 25.4 %all_to_all.47 = bf16[16,96,384]{2,1,0:T(8,128)(2,1)S(1)} all-to-all(bf16[16,96,384]{2,1,0:T(8,128)(2,1)} %reduce_sum.140), channel_id=1, replica_groups=mesh['pairs'=16,'core'=2,'fac'=4] {'pairs'}, dimensions={0} | all-to-all | bytes 2359296 | tf_op jit(solution)/shard_map/all_to_all | solution.py:78
  206.9 11.6 %all_gather.24 = bf16[96,3072]{1,0:T(8,128)(2,1)S(1)} all-gather(bf16[96,768]{1,0:T(8,128)(2,1)S(1)} %pad_maximum_fusion), channel_id=1, replica_groups=mesh['pairs'=16,'core'=2,'fac'=4] {'fac'}, dimensions={1}, use_global_device_ids=true | all-gather | bytes 737280 | tf_op jit(solution)/shard_map/all_gather | solution.py:138
  218.5 4.5 %multiply_reduce_fusion.5 = (f32[]{:T(128)}, f32[]{:T(128)}, bf16[96,768]{1,0:T(8,128)(2,1)}, f32[96,768]{1,0:T(8,128)S(1)}) fusion(f32[96,768]{1,0:T(8,128)S(1)} %get-tuple-element.28, f32[96,768]{1,0:T(8,128)S(1)} %convert_reduce_fusion, bf16[96,3072]{1,0:T(8,128)(2,1)S(1)} %all_gather.24, bf16[3072,768]{1,0:T(8,128)(2,1)} %all-gather.9.cloned.1.call-done), kind=kOutput, calls=%fused_computation.34 | convolution fusion | flops 453574656 | bytes 6340616 | tf_op jit(solution)/shard_map/dot_general | solution.py:16
  223.0 3.3 convolution_convert_fusion.1
  228.3 10.7 %all-to-all-start.6 = ((f32[128,1,2]{2,1,0:T(1,128)}), f32[128,1,2]{2,1,0:T(1,128)S(1)}, u32[]{:S(2)}, u32[]{:S(2)}) async-start(f32[128,1,2]{2,1,0:T(1,128)} %broadcast_in_dim.7), calls=%async_computation.6 | async-start | bytes 131072 | tf_op jit(solution)/shard_map/all_to_all | solution.py:85
  239.1 11.3 %all_gather.26 = bf16[96,3072]{1,0:T(8,128)(2,1)S(1)} all-gather(bf16[96,768]{1,0:T(8,128)(2,1)S(1)} %convolution_convert_fusion.1), channel_id=1, replica_groups=mesh['pairs'=16,'core'=2,'fac'=4] {'fac'}, dimensions={1}, use_global_device_ids=true | all-gather | bytes 737280 | tf_op jit(solution)/shard_map/all_gather | solution.py:147
  252.5 20.6 %all-gather.11.cloned.1.call-done = bf16[3072,768]{1,0:T(8,128)(2,1)} async-done(((bf16[96,768]{1,0:T(8,128)(2,1)}), bf16[3072,768]{1,0:T(8,128)(2,1)}) %all-gather.11.cloned.1.call-update) | async-done | bytes 4718608 | tf_op jit(solution)/shard_map/all_gather | solution.py:101
  273.1 5.6 %fusion.2 = bf16[192,768]{1,0:T(8,128)(2,1)S(1)} fusion(bf16[3072,768]{1,0:T(8,128)(2,1)} %all-gather.11.cloned.1.call-done, bf16[3072,768]{1,0:T(8,128)(2,1)} %all-gather.7.cloned.1.call-done, f32[]{:T(128)S(6)} %div.17, bf16[96,3072]{1,0:T(8,128)(2,1)S(1)} %all_gather.26, bf16[96,3072]{1,0:T(8,128)(2,1)S(1)} %copy-done.3), kind=kOutput, calls=%fused_computation.11 | convolution fusion | flops 920272896 | bytes 10911748 | tf_op jit(solution)/shard_map/dot_general | solution.py:16
  283.1 5.2 %collective-permute-done = bf16[192,768]{1,0:T(8,128)(2,1)S(1)} collective-permute-done((bf16[192,768]{1,0:T(8,128)(2,1)S(1)}, bf16[192,768]{1,0:T(8,128)(2,1)S(1)}, u32[]{:S(2)}, u32[]{:S(2)}) %collective-permute-start) | collective-permute-done | bytes 294944 | tf_op jit(solution)/shard_map/ppermute | solution.py:40
  291.8 5.2 %collective-permute-done.2 = bf16[192,768]{1,0:T(8,128)(2,1)S(1)} collective-permute-done((bf16[192,768]{1,0:T(8,128)(2,1)S(1)}, bf16[192,768]{1,0:T(8,128)(2,1)S(1)}, u32[]{:S(2)}, u32[]{:S(2)}) %collective-permute-start.2) | collective-permute-done | bytes 294944 | tf_op jit(solution)/shard_map/ppermute | solution.py:40
  302.1 15.9 %all_to_all.48 = f32[128,1,4]{2,1,0:T(1,128)S(1)} all-to-all(f32[128,1,4]{2,1,0:T(1,128)S(1)} %broadcast_in_dim.8), channel_id=1, replica_groups=mesh['pairs'=16,'core'=2,'fac'=4] {'pairs','core','fac'}, dimensions={0} | all-to-all | bytes 4096 | tf_op jit(solution)/shard_map/all_to_all | solution.py:85
  (56 shorter events, 33.0 us)
Async XLA Ops:
  7.2 78.6 %copy-start = (f32[32768]{0:T(1024)S(1)}, f32[32768]{0:T(1024)}, u32[]{:S(2)}) copy-start(f32[32768]{0:T(1024)} %param.11) | copy-start | bytes 393220
  7.2 77.8 %all-gather.5.cloned.1.call-start = ((), (), s32[]{:S(2)}) async-start(), calls=%async_computation.8 | async-start | bytes 4866048 | tf_op jit(solution)/shard_map/all_gather | solution.py:116
  8.8 135.5 %all-gather.7.cloned.1.call-start = ((), (), s32[]{:S(2)}) async-start(), calls=%async_computation.9 | async-start | bytes 4866048 | tf_op jit(solution)/shard_map/all_gather | solution.py:101
  41.1 44.7 %copy-start.5 = (s32[1024]{0:T(1024)S(1)}, s32[1024]{0:T(1024)}, u32[]{:S(2)}) copy-start(s32[1024]{0:T(1024)} %param.9) | copy-start | bytes 12292
  84.6 7.3 %copy-start.4 = (s32[1024]{0:T(1024)S(1)}, s32[1024]{0:T(1024)}, u32[]{:S(2)}) copy-start(s32[1024]{0:T(1024)} %param.10) | copy-start | bytes 12292
  85.7 132.8 %all-gather.9.cloned.1.call-start = ((), (), s32[]{:S(2)}) async-start(), calls=%async_computation.10 | async-start | bytes 4866048 | tf_op jit(solution)/shard_map/all_gather | solution.py:101
  110.4 34.0 %copy-start.2 = (bf16[96,3072]{1,0:T(8,128)(2,1)S(1)}, bf16[96,3072]{1,0:T(8,128)(2,1)}, u32[]{:S(2)}) copy-start(bf16[96,3072]{1,0:T(8,128)(2,1)} %param.12) | copy-start | bytes 1769476
  162.9 110.2 %all-gather.11.cloned.1.call-start = ((), (), s32[]{:S(2)}) async-start(), calls=%async_computation.11 | async-start | bytes 4866048 | tf_op jit(solution)/shard_map/all_gather | solution.py:101
  223.0 50.1 %copy-start.3 = (bf16[96,3072]{1,0:T(8,128)(2,1)S(1)}, bf16[96,3072]{1,0:T(8,128)(2,1)}, u32[]{:S(2)}) copy-start(bf16[96,3072]{1,0:T(8,128)(2,1)} %param.12) | copy-start | bytes 1769476
  228.3 22.0 %all-to-all-start.6 = ((f32[128,1,2]{2,1,0:T(1,128)}), f32[128,1,2]{2,1,0:T(1,128)S(1)}, u32[]{:S(2)}, u32[]{:S(2)}) async-start(f32[128,1,2]{2,1,0:T(1,128)} %broadcast_in_dim.7), calls=%async_computation.6 | async-start | bytes 131072 | tf_op jit(solution)/shard_map/all_to_all | solution.py:85
  278.7 9.6 %collective-permute-start = (bf16[192,768]{1,0:T(8,128)(2,1)S(1)}, bf16[192,768]{1,0:T(8,128)(2,1)S(1)}, u32[]{:S(2)}, u32[]{:S(2)}) collective-permute-start(bf16[192,768]{1,0:T(8,128)(2,1)S(1)} %fusion.2), channel_id=1, source_target_pairs={{0,1},{1,2},{2,3},{3,0},{4,5},{5,6},{6,7},{7,4},{8,9},{9,10},{10,1... | collective-permute-start | bytes 884744 | tf_op jit(solution)/shard_map/ppermute | solution.py:40
  280.0 10.1 %collective-permute-start.1 = (bf16[192,768]{1,0:T(8,128)(2,1)S(1)}, bf16[192,768]{1,0:T(8,128)(2,1)S(1)}, u32[]{:S(2)}, u32[]{:S(2)}) collective-permute-start(bf16[192,768]{1,0:T(8,128)(2,1)S(1)} %fusion.2), channel_id=1, source_target_pairs={{0,3},{1,0},{2,1},{3,2},{4,7},{5,4},{6,5},{7,6},{8,11},{9,8},{10,9... | collective-permute-start | bytes 884744 | tf_op jit(solution)/shard_map/ppermute | solution.py:43
  288.3 8.6 %collective-permute-start.2 = (bf16[192,768]{1,0:T(8,128)(2,1)S(1)}, bf16[192,768]{1,0:T(8,128)(2,1)S(1)}, u32[]{:S(2)}, u32[]{:S(2)}) collective-permute-start(bf16[192,768]{1,0:T(8,128)(2,1)S(1)} %collective-permute-done), channel_id=1, source_target_pairs={{0,1},{1,2},{2,3},{3,0},{4,5},{5,6},{6,7},{7,4},{8,9},{9,10},{10,1... | collective-permute-start | bytes 884744 | tf_op jit(solution)/shard_map/ppermute | solution.py:40
  290.0 34.2 %copy-start.1 = (f32[32768]{0:T(1024)S(1)}, f32[32768]{0:T(1024)}, u32[]{:S(2)}) copy-start(f32[32768]{0:T(1024)} %param.11) | copy-start | bytes 393220
Sparse Core Ops, SparseCore 0:
  10.8 68.0 all-gather.4
  85.8 58.4 all-gather.6
  163.0 52.1 all-gather.8
  223.1 49.9 all-gather.10

commit v12 on v11

--- a/solution.py
+++ b/solution.py
@@ -91,7 +91,13 @@
     tok_rows, d_in = activations.shape
     total = tok_rows * lax.axis_size("pairs") * lax.axis_size("core")
     keep = 1.0 - forget_mask.astype(jnp.float32)
-    weights = importance[token_ids] * keep / total
+    lanes = 128
+    table_rows = importance.reshape(importance.shape[0] // lanes, lanes)[token_ids // lanes]
+    lane_ids = lax.broadcasted_iota(jnp.int32, table_rows.shape, 1)
+    picked = jnp.sum(
+        jnp.where(lane_ids == (token_ids % lanes)[:, None], table_rows, 0.0), axis=1
+    )
+    weights = picked * keep / total
     forget_grads = out_grads * forget_mask.astype(jnp.bfloat16)[:, None]
     grad_scale = 1.0 / math.sqrt(total)
 
@@ -102,12 +108,7 @@
 
     def precondition(gathered):
         mixed = add_columns(in_inverse, gathered)
-        mixed_low = mixed.astype(jnp.bfloat16)
-        return jnp.dot(
-            lax.all_gather(mixed_low, "fac", axis=1, tiled=True),
-            out_inverse,
-            preferred_element_type=jnp.float32,
-        )
+        return ring_product(mixed.astype(jnp.bfloat16), out_inverse)
 
     def inner_part(left, right):
         return jnp.sum(left * right)
@@ -134,18 +135,16 @@
     gram_second = block_term(activations, weighted[:, half:], 1.0)
     residual_rows, first_rows = lax.optimization_barrier((residual_rows, scatter_sum(gram_first)))
     precond = precondition(residual_rows)
-    gram_own = jnp.concatenate([first_rows, scatter_sum(gram_second)], axis=1)
-    gram_rows = lax.all_gather(gram_own.astype(jnp.bfloat16), "fac", axis=1, tiled=True)
-
-    def curvature(matrix):
-        return add_columns(gram_rows, gather_rows(matrix)) + damping * matrix
+    gram_own = jnp.concatenate([first_rows, scatter_sum(gram_second)], axis=1).astype(jnp.bfloat16)
 
     direction = precond
-    image = curvature(direction)
+    d_out_part = out_inverse.shape[1]
+    gram_both = ring_product(gram_own, jnp.concatenate([gather_rows(direction), in_cols], axis=1))
+    image = gram_both[:, :d_out_part] + damping * direction
     image_rows = gather_rows(image)
     inner_now, energy = global_sums(inner_part(residual, precond), inner_part(direction, image))
     gram_inverse = lax.all_gather(
-        add_columns(gram_rows, in_cols).astype(jnp.bfloat16), "fac", axis=1, tiled=True
+        gram_both[:, d_out_part:].astype(jnp.bfloat16), "fac", axis=1, tiled=True
     )
     alpha = inner_now / energy
     newton_step = alpha * direction

time: 332 us -> 333 us (level)
  blocking collectives: 179 us -> 129 us
  waiting for transfers between devices: 33.5 us -> 73.9 us
  starting transfers between devices: 13.7 us -> 22.6 us
    all_to_all x3 -> x2, blocking collectives: 98.6 us -> 71.2 us  [scatter_sum(): received = lax.all_to_all(chip_sum, 'pairs', 0, 0, tiled=False)]
    all_to_all x0 -> x1, waiting for transfers between devices: none -> 23.3 us  [scatter_sum(): received = lax.all_to_all(chip_sum, 'pairs', 0, 0, tiled=False)]
    all_gather x3 -> x1, blocking collectives: 34.3 us -> 11.5 us  [body(): lax.all_gather(gram_both[:, d_out_part:].astype(jnp.bfloat16), 'fac', axi...]
    ppermute x2 -> x6, waiting for transfers between devices: 10.4 us -> 19.4 us  [ring_product(): ahead = lax.ppermute(ahead, 'fac', [(j, (j + 1) % n) for j in range(n)])]
    all_gather x3, waiting for transfers between devices: 22.9 us -> 31.1 us  [gather_rows(): return lax.all_gather(matrix.astype(jnp.bfloat16), FSDP, axis=0, tiled=True)]
    ppermute x1 -> x3, starting transfers between devices: 1.49 us -> 6.63 us  [ring_product(): behind = lax.ppermute(behind, 'fac', [(j, (j - 1) % n) for j in range(n)])]
    dot_general x1 -> x0, matrix products: 3.88 us -> none  [precondition(): jnp.dot(lax.all_gather(mixed_low, 'fac', axis=1, tiled=True), out_inverse...]
    all_to_all x0 -> x1, starting transfers between devices: none -> 3.7 us  [scatter_sum(): received = lax.all_to_all(chip_sum, 'pairs', 0, 0, tiled=False)]
  transfers between devices with their start and end apart: 8 -> 15, of which waited for: 4 -> 9; matrix products, arithmetic and copies ran while one was open for 10% -> 11% of each run, Pallas kernels for 8% -> 8%
where the time goes in v12:
time: 333 us; the launch traced here: 332 us
  blocking collectives  129 us (39%)
  waiting for transfers between devices  73.9 us (22%)
  Pallas kernels  27.1 us (8%)
  matrix products  24.7 us (7%)
  starting transfers between devices  22.6 us (7%)
  other arithmetic  21.4 us (6%)
  between operations  19.9 us (6%)
  local copies, waits for them, and re-layouts  13.1 us (4%)
    all_to_all x2, blocking collectives, scatter_sum(): received = lax.all_to_all(chip_sum, 'pairs', 0, 0, tiled=False)  71.2 us
    all_gather x3, waiting for transfers between devices, gather_rows(): return lax.all_gather(matrix.astype(jnp.bfloat16), FSDP, axis=0, tiled=True)  31.1 us
    all_to_all x3, blocking collectives, scatter_sum(): on_chip = lax.all_to_all(blocks, 'core', 0, 0, tiled=False)  30.3 us
    pallas_call x3, Pallas kernels, block_term(): pl.pallas_call(kernel, grid=(cols // step,), in_specs=[pl.BlockSpec((toke...  27.1 us
    dot_general x14, matrix products, add_columns(): return jnp.dot(matrix, piece, preferred_element_type=jnp.float32)  24.7 us
    all_to_all x1, waiting for transfers between devices, scatter_sum(): received = lax.all_to_all(chip_sum, 'pairs', 0, 0, tiled=False)  23.3 us
    ppermute x6, waiting for transfers between devices, ring_product(): ahead = lax.ppermute(ahead, 'fac', [(j, (j + 1) % n) for j in range(n)])  19.4 us
    all_to_all x1, blocking collectives, global_sums(): received = lax.all_to_all(stacked, FSDP + ('fac',), 0, 0, tiled=True)  15.9 us
  transfers between devices with their start and end apart: 15, of which 9 were waited for; matrix products, arithmetic and copies ran while one was open for 11% of the time, Pallas kernels for 8%

profile of v12, /device:TPU:1, one launch (start us, length us, event | category | flops | bytes accessed | tf_op | source)
XLA Modules:
  0.0 331.8 jit_solution(3337812153813986391)
XLA Ops:
  9.6 2.8 broadcast_multiply_fusion.x_ref
  12.4 11.5 %shard_map.86 = bf16[2,16,96,768]{3,2,1,0:T(8,128)(2,1)} custom-call(bf16[1024,3072]{1,0:T(8,128)(2,1)} %a_ref.5, bf16[1024,768]{1,0:T(8,128)(2,1)} %broadcast_multiply_fusion.x_ref), custom_call_target="tpu_custom_call" | custom-call | tf_op jit(solution)/shard_map/pallas_call | solution.py:63
  23.8 13.8 %all_to_all.42 = bf16[2,16,96,768]{3,2,1,0:T(8,128)(2,1)} all-to-all(bf16[2,16,96,768]{3,2,1,0:T(8,128)(2,1)} %shard_map.86), channel_id=1, replica_groups=mesh['pairs'=16,'core'=2,'fac'=4] {'core'}, dimensions={0} | all-to-all | bytes 9437184 | tf_op jit(solution)/shard_map/all_to_all | solution.py:76
  37.6 3.5 %reduce_sum.144 = bf16[16,96,768]{2,1,0:T(8,128)(2,1)S(1)} reduce(bf16[2,16,96,768]{3,2,1,0:T(8,128)(2,1)} %all_to_all.42, bf16[]{:T(256)} %constant.80.clone.1), dimensions={0}, to_apply=%region_0.1 | reduce | flops 1179648 | bytes 7077890 | tf_op jit(solution)/shard_map/reduce_sum | solution.py:77
  41.1 43.5 %all_to_all.43 = bf16[16,96,768]{2,1,0:T(8,128)(2,1)S(1)} all-to-all(bf16[16,96,768]{2,1,0:T(8,128)(2,1)S(1)} %reduce_sum.144), channel_id=1, replica_groups=mesh['pairs'=16,'core'=2,'fac'=4] {'pairs'}, dimensions={0} | all-to-all | bytes 4718592 | tf_op jit(solution)/shard_map/all_to_all | solution.py:78
  85.7 2.8 gather_fusion
  92.0 7.8 %shard_map.87 = bf16[2,16,96,384]{3,2,1,0:T(8,128)(2,1)} custom-call(bf16[1024,3072]{1,0:T(8,128)(2,1)} %a_ref.5, bf16[1024,384]{1,0:T(8,128)(2,1)} %get-tuple-element.18.x_ref), custom_call_target="tpu_custom_call" | custom-call | tf_op jit(solution)/shard_map/pallas_call | solution.py:63
  99.8 7.5 %all_to_all.44 = bf16[2,16,96,384]{3,2,1,0:T(8,128)(2,1)S(1)} all-to-all(bf16[2,16,96,384]{3,2,1,0:T(8,128)(2,1)} %shard_map.87), channel_id=1, replica_groups=mesh['pairs'=16,'core'=2,'fac'=4] {'core'}, dimensions={0} | all-to-all | bytes 4718592 | tf_op jit(solution)/shard_map/all_to_all | solution.py:76
  109.1 3.7 %all-to-all-start.3 = ((bf16[16,96,384]{2,1,0:T(8,128)(2,1)}), bf16[16,96,384]{2,1,0:T(8,128)(2,1)S(1)}, u32[]{:S(2)}, u32[]{:S(2)}) async-start(bf16[16,96,384]{2,1,0:T(8,128)(2,1)} %reduce_sum.147), calls=%async_computation.3 | async-start | bytes 2359296 | tf_op jit(solution)/shard_map/all_to_all | solution.py:78
  113.1 23.3 %all-to-all-done.3 = bf16[16,96,384]{2,1,0:T(8,128)(2,1)S(1)} async-done(((bf16[16,96,384]{2,1,0:T(8,128)(2,1)}), bf16[16,96,384]{2,1,0:T(8,128)(2,1)S(1)}, u32[]{:S(2)}, u32[]{:S(2)}) %all-to-all-start.3) | async-done | bytes 1179680 | tf_op jit(solution)/shard_map/all_to_all | solution.py:78
  136.6 6.3 %all-gather.7.cloned.1.call-done = bf16[3072,768]{1,0:T(8,128)(2,1)} async-done(((bf16[96,768]{1,0:T(8,128)(2,1)}), bf16[3072,768]{1,0:T(8,128)(2,1)}) %all-gather.7.cloned.1.call-update) | async-done | bytes 4718608 | tf_op jit(solution)/shard_map/all_gather | solution.py:107
  142.9 3.2 convolution_convert_fusion
  150.2 4.5 %collective-permute-done = bf16[96,768]{1,0:T(8,128)(2,1)S(1)} collective-permute-done((bf16[96,768]{1,0:T(8,128)(2,1)S(1)}, bf16[96,768]{1,0:T(8,128)(2,1)S(1)}, u32[]{:S(2)}, u32[]{:S(2)}) %collective-permute-start) | collective-permute-done | bytes 147488 | tf_op jit(solution)/shard_map/ppermute | solution.py:40
  162.2 7.8 %shard_map.88 = bf16[2,16,96,384]{3,2,1,0:T(8,128)(2,1)} custom-call(bf16[1024,3072]{1,0:T(8,128)(2,1)} %a_ref.5, bf16[1024,384]{1,0:T(8,128)(2,1)} %get-tuple-element.17.x_ref), custom_call_target="tpu_custom_call" | custom-call | tf_op jit(solution)/shard_map/pallas_call | solution.py:63
  170.0 9.0 %all_to_all.45 = bf16[2,16,96,384]{3,2,1,0:T(8,128)(2,1)S(1)} all-to-all(bf16[2,16,96,384]{3,2,1,0:T(8,128)(2,1)} %shard_map.88), channel_id=1, replica_groups=mesh['pairs'=16,'core'=2,'fac'=4] {'core'}, dimensions={0} | all-to-all | bytes 4718592 | tf_op jit(solution)/shard_map/all_to_all | solution.py:76
  180.8 27.7 %all_to_all.46 = bf16[16,96,384]{2,1,0:T(8,128)(2,1)S(1)} all-to-all(bf16[16,96,384]{2,1,0:T(8,128)(2,1)} %reduce_sum.150), channel_id=1, replica_groups=mesh['pairs'=16,'core'=2,'fac'=4] {'pairs'}, dimensions={0} | all-to-all | bytes 2359296 | tf_op jit(solution)/shard_map/all_to_all | solution.py:78
  217.4 2.7 constant_dynamic-update-slice_fusion
  225.7 10.6 %all-to-all-start.6 = ((f32[128,1,2]{2,1,0:T(1,128)}), f32[128,1,2]{2,1,0:T(1,128)S(1)}, u32[]{:S(2)}, u32[]{:S(2)}) async-start(f32[128,1,2]{2,1,0:T(1,128)} %broadcast_in_dim.12), calls=%async_computation.6 | async-start | bytes 131072 | tf_op jit(solution)/shard_map/all_to_all | solution.py:85
  236.3 11.5 %all_gather.18 = bf16[96,3072]{1,0:T(8,128)(2,1)S(1)} all-gather(bf16[96,768]{1,0:T(8,128)(2,1)S(1)} %slice.77), channel_id=1, replica_groups=mesh['pairs'=16,'core'=2,'fac'=4] {'fac'}, dimensions={1}, use_global_device_ids=true | all-gather | bytes 737280 | tf_op jit(solution)/shard_map/all_gather | solution.py:146
  249.9 24.1 %all-gather.11.cloned.1.call-done = bf16[3072,768]{1,0:T(8,128)(2,1)} async-done(((bf16[96,768]{1,0:T(8,128)(2,1)}), bf16[3072,768]{1,0:T(8,128)(2,1)}) %all-gather.11.cloned.1.call-update) | async-done | bytes 4718608 | tf_op jit(solution)/shard_map/all_gather | solution.py:107
  274.0 5.6 %fusion.7 = bf16[192,768]{1,0:T(8,128)(2,1)S(1)} fusion(bf16[3072,768]{1,0:T(8,128)(2,1)} %all-gather.11.cloned.1.call-done, bf16[3072,768]{1,0:T(8,128)(2,1)} %all-gather.7.cloned.1.call-done, f32[]{:T(128)S(6)} %div.33, bf16[96,3072]{1,0:T(8,128)(2,1)S(1)} %all_gather.18, bf16[96,3072]{1,0:T(8,128)(2,1)S(1)} %copy-done.3), kind=kOutput, calls=%fused_computation.19 | convolution fusion | flops 920272896 | bytes 10911748 | tf_op jit(solution)/shard_map/dot_general | solution.py:16
  284.0 5.2 %collective-permute-done.6 = bf16[192,768]{1,0:T(8,128)(2,1)S(1)} collective-permute-done((bf16[192,768]{1,0:T(8,128)(2,1)S(1)}, bf16[192,768]{1,0:T(8,128)(2,1)S(1)}, u32[]{:S(2)}, u32[]{:S(2)}) %collective-permute-start.6) | collective-permute-done | bytes 294944 | tf_op jit(solution)/shard_map/ppermute | solution.py:40
  292.7 5.2 %collective-permute-done.8 = bf16[192,768]{1,0:T(8,128)(2,1)S(1)} collective-permute-done((bf16[192,768]{1,0:T(8,128)(2,1)S(1)}, bf16[192,768]{1,0:T(8,128)(2,1)S(1)}, u32[]{:S(2)}, u32[]{:S(2)}) %collective-permute-start.8) | collective-permute-done | bytes 294944 | tf_op jit(solution)/shard_map/ppermute | solution.py:40
  303.1 15.9 %all_to_all.47 = f32[128,1,4]{2,1,0:T(1,128)S(1)} all-to-all(f32[128,1,4]{2,1,0:T(1,128)S(1)} %broadcast_in_dim.13), channel_id=1, replica_groups=mesh['pairs'=16,'core'=2,'fac'=4] {'pairs','core','fac'}, dimensions={0} | all-to-all | bytes 4096 | tf_op jit(solution)/shard_map/all_to_all | solution.py:85
  (78 shorter events, 52.3 us)
Async XLA Ops:
  7.2 78.6 %copy-start = (f32[32768]{0:T(1024)S(1)}, f32[32768]{0:T(1024)}, u32[]{:S(2)}) copy-start(f32[32768]{0:T(1024)} %param.11) | copy-start | bytes 393220
  7.2 77.8 %all-gather.5.cloned.1.call-start = ((), (), s32[]{:S(2)}) async-start(), calls=%async_computation.8 | async-start | bytes 4866048 | tf_op jit(solution)/shard_map/all_gather | solution.py:117
  8.8 134.1 %all-gather.7.cloned.1.call-start = ((), (), s32[]{:S(2)}) async-start(), calls=%async_computation.9 | async-start | bytes 4866048 | tf_op jit(solution)/shard_map/all_gather | solution.py:107
  41.1 44.6 %copy-start.5 = (s32[1024]{0:T(1024)S(1)}, s32[1024]{0:T(1024)}, u32[]{:S(2)}) copy-start(s32[1024]{0:T(1024)} %param.9) | copy-start | bytes 12292
  85.0 4.0 %copy-start.4 = (s32[1024]{0:T(1024)S(1)}, s32[1024]{0:T(1024)}, u32[]{:S(2)}) copy-start(s32[1024]{0:T(1024)} %param.10) | copy-start | bytes 12292
  107.4 35.5 %copy-start.2 = (bf16[96,3072]{1,0:T(8,128)(2,1)S(1)}, bf16[96,3072]{1,0:T(8,128)(2,1)}, u32[]{:S(2)}) copy-start(bf16[96,3072]{1,0:T(8,128)(2,1)} %param.12) | copy-start | bytes 1769476
  109.1 27.3 %all-to-all-start.3 = ((bf16[16,96,384]{2,1,0:T(8,128)(2,1)}), bf16[16,96,384]{2,1,0:T(8,128)(2,1)S(1)}, u32[]{:S(2)}, u32[]{:S(2)}) async-start(bf16[16,96,384]{2,1,0:T(8,128)(2,1)} %reduce_sum.147), calls=%async_computation.3 | async-start | bytes 2359296 | tf_op jit(solution)/shard_map/all_to_all | solution.py:78
  112.8 101.8 %all-gather.9.cloned.1.call-start = ((), (), s32[]{:S(2)}) async-start(), calls=%async_computation.10 | async-start | bytes 4866048 | tf_op jit(solution)/shard_map/all_gather | solution.py:107
  146.1 10.2 %collective-permute-start.1 = (bf16[96,768]{1,0:T(8,128)(2,1)S(1)}, bf16[96,768]{1,0:T(8,128)(2,1)S(1)}, u32[]{:S(2)}, u32[]{:S(2)}) collective-permute-start(bf16[96,768]{1,0:T(8,128)(2,1)S(1)} %bitcast.27), channel_id=1, source_target_pairs={{0,3},{1,0},{2,1},{3,2},{4,7},{5,4},{6,5},{7,6},{8,11},{9,8},{10,9... | collective-permute-start | bytes 442376 | tf_op jit(solution)/shard_map/ppermute | solution.py:43
  148.6 6.1 %collective-permute-start = (bf16[96,768]{1,0:T(8,128)(2,1)S(1)}, bf16[96,768]{1,0:T(8,128)(2,1)S(1)}, u32[]{:S(2)}, u32[]{:S(2)}) collective-permute-start(bf16[96,768]{1,0:T(8,128)(2,1)S(1)} %bitcast.28), channel_id=1, source_target_pairs={{0,1},{1,2},{2,3},{3,0},{4,5},{5,6},{6,7},{7,4},{8,9},{9,10},{10,1... | collective-permute-start | bytes 442376 | tf_op jit(solution)/shard_map/ppermute | solution.py:40
  154.7 5.2 %collective-permute-start.2 = (bf16[96,768]{1,0:T(8,128)(2,1)S(1)}, bf16[96,768]{1,0:T(8,128)(2,1)S(1)}, u32[]{:S(2)}, u32[]{:S(2)}) collective-permute-start(bf16[96,768]{1,0:T(8,128)(2,1)S(1)} %collective-permute-done), channel_id=1, source_target_pairs={{0,1},{1,2},{2,3},{3,0},{4,5},{5,6},{6,7},{7,4},{8,9},{9,10},{10,1... | collective-permute-start | bytes 442376 | tf_op jit(solution)/shard_map/ppermute | solution.py:40
  162.2 111.8 %all-gather.11.cloned.1.call-start = ((), (), s32[]{:S(2)}) async-start(), calls=%async_computation.11 | async-start | bytes 4866048 | tf_op jit(solution)/shard_map/all_gather | solution.py:107
  208.7 5.3 %collective-permute-start.3 = (bf16[96,768]{1,0:T(8,128)(2,1)S(1)}, bf16[96,768]{1,0:T(8,128)(2,1)S(1)}, u32[]{:S(2)}, u32[]{:S(2)}) collective-permute-start(bf16[96,768]{1,0:T(8,128)(2,1)S(1)} %pad_maximum_fusion), channel_id=1, source_target_pairs={{0,1},{1,2},{2,3},{3,0},{4,5},{5,6},{6,7},{7,4},{8,9},{9,10},{10,1... | collective-permute-start | bytes 442376 | tf_op jit(solution)/shard_map/ppermute | solution.py:40
  208.8 12.3 %collective-permute-start.4 = (bf16[96,768]{1,0:T(8,128)(2,1)S(1)}, bf16[96,768]{1,0:T(8,128)(2,1)S(1)}, u32[]{:S(2)}, u32[]{:S(2)}) collective-permute-start(bf16[96,768]{1,0:T(8,128)(2,1)S(1)} %pad_maximum_fusion), channel_id=1, source_target_pairs={{0,3},{1,0},{2,1},{3,2},{4,7},{5,4},{6,5},{7,6},{8,11},{9,8},{10,9... | collective-permute-start | bytes 442376 | tf_op jit(solution)/shard_map/ppermute | solution.py:43
  214.0 7.7 %collective-permute-start.5 = (bf16[96,768]{1,0:T(8,128)(2,1)S(1)}, bf16[96,768]{1,0:T(8,128)(2,1)S(1)}, u32[]{:S(2)}, u32[]{:S(2)}) collective-permute-start(bf16[96,768]{1,0:T(8,128)(2,1)S(1)} %collective-permute-done.3), channel_id=1, source_target_pairs={{0,1},{1,2},{2,3},{3,0},{4,5},{5,6},{6,7},{7,4},{8,9},{9,10},{10,1... | collective-permute-start | bytes 442376 | tf_op jit(solution)/shard_map/ppermute | solution.py:40
  221.7 52.3 %copy-start.3 = (bf16[96,3072]{1,0:T(8,128)(2,1)S(1)}, bf16[96,3072]{1,0:T(8,128)(2,1)}, u32[]{:S(2)}) copy-start(bf16[96,3072]{1,0:T(8,128)(2,1)} %param.12) | copy-start | bytes 1769476
  225.7 22.1 %all-to-all-start.6 = ((f32[128,1,2]{2,1,0:T(1,128)}), f32[128,1,2]{2,1,0:T(1,128)S(1)}, u32[]{:S(2)}, u32[]{:S(2)}) async-start(f32[128,1,2]{2,1,0:T(1,128)} %broadcast_in_dim.12), calls=%async_computation.6 | async-start | bytes 131072 | tf_op jit(solution)/shard_map/all_to_all | solution.py:85
  279.6 9.6 %collective-permute-start.6 = (bf16[192,768]{1,0:T(8,128)(2,1)S(1)}, bf16[192,768]{1,0:T(8,128)(2,1)S(1)}, u32[]{:S(2)}, u32[]{:S(2)}) collective-permute-start(bf16[192,768]{1,0:T(8,128)(2,1)S(1)} %fusion.7), channel_id=1, source_target_pairs={{0,1},{1,2},{2,3},{3,0},{4,5},{5,6},{6,7},{7,4},{8,9},{9,10},{10,1... | collective-permute-start | bytes 884744 | tf_op jit(solution)/shard_map/ppermute | solution.py:40
  280.9 10.1 %collective-permute-start.7 = (bf16[192,768]{1,0:T(8,128)(2,1)S(1)}, bf16[192,768]{1,0:T(8,128)(2,1)S(1)}, u32[]{:S(2)}, u32[]{:S(2)}) collective-permute-start(bf16[192,768]{1,0:T(8,128)(2,1)S(1)} %fusion.7), channel_id=1, source_target_pairs={{0,3},{1,0},{2,1},{3,2},{4,7},{5,4},{6,5},{7,6},{8,11},{9,8},{10,9... | collective-permute-start | bytes 884744 | tf_op jit(solution)/shard_map/ppermute | solution.py:43
  289.2 8.6 %collective-permute-start.8 = (bf16[192,768]{1,0:T(8,128)(2,1)S(1)}, bf16[192,768]{1,0:T(8,128)(2,1)S(1)}, u32[]{:S(2)}, u32[]{:S(2)}) collective-permute-start(bf16[192,768]{1,0:T(8,128)(2,1)S(1)} %collective-permute-done.6), channel_id=1, source_target_pairs={{0,1},{1,2},{2,3},{3,0},{4,5},{5,6},{6,7},{7,4},{8,9},{9,10},{10,1... | collective-permute-start | bytes 884744 | tf_op jit(solution)/shard_map/ppermute | solution.py:40
  290.9 34.3 %copy-start.1 = (f32[32768]{0:T(1024)S(1)}, f32[32768]{0:T(1024)}, u32[]{:S(2)}) copy-start(f32[32768]{0:T(1024)} %param.11) | copy-start | bytes 393220
Sparse Core Ops, SparseCore 0:
  10.8 68.0 all-gather.4
  85.8 57.0 all-gather.6
  162.3 52.3 all-gather.8
  223.8 50.1 all-gather.10

commit v13 on v11

--- a/solution.py
+++ b/solution.py
@@ -73,8 +73,12 @@
 
 
 def scatter_sum(blocks):
-    on_chip = lax.all_to_all(blocks, "core", 0, 0, tiled=False)
-    chip_sum = jnp.sum(on_chip.astype(jnp.float32), axis=0).astype(jnp.bfloat16)
+    cores = lax.axis_size("core")
+    me = lax.axis_index("core")
+    sibling = [(j, (j + 1) % cores) for j in range(cores)]
+    sent = lax.ppermute(lax.dynamic_index_in_dim(blocks, 1 - me, 0, keepdims=False), "core", sibling)
+    own = lax.dynamic_index_in_dim(blocks, me, 0, keepdims=False)
+    chip_sum = (own.astype(jnp.float32) + sent.astype(jnp.float32)).astype(jnp.bfloat16)
     received = lax.all_to_all(chip_sum, "pairs", 0, 0, tiled=False)
     return lax.optimization_barrier(jnp.sum(received.astype(jnp.float32), axis=0))
 
@@ -91,7 +95,13 @@
     tok_rows, d_in = activations.shape
     total = tok_rows * lax.axis_size("pairs") * lax.axis_size("core")
     keep = 1.0 - forget_mask.astype(jnp.float32)
-    weights = importance[token_ids] * keep / total
+    lanes = 128
+    table_rows = importance.reshape(importance.shape[0] // lanes, lanes)[token_ids // lanes]
+    lane_ids = lax.broadcasted_iota(jnp.int32, table_rows.shape, 1)
+    picked = jnp.sum(
+        jnp.where(lane_ids == (token_ids % lanes)[:, None], table_rows, 0.0), axis=1
+    )
+    weights = picked * keep / total
     forget_grads = out_grads * forget_mask.astype(jnp.bfloat16)[:, None]
     grad_scale = 1.0 / math.sqrt(total)
 

time: 332 us -> 319 us (0.961)
  blocking collectives: 179 us -> 147 us
  waiting for transfers between devices: 33.5 us -> 52.2 us
  other arithmetic: 19.6 us -> 15.9 us
    all_to_all x3 -> x0, blocking collectives: 30 us -> none  [scatter_sum(): on_chip = lax.all_to_all(blocks, 'core', 0, 0, tiled=False)]
    all_gather x3, waiting for transfers between devices: 22.9 us -> 32.3 us  [gather_rows(): return lax.all_gather(matrix.astype(jnp.bfloat16), FSDP, axis=0, tiled=True)]
    ppermute x0 -> x3, waiting for transfers between devices: none -> 9.32 us  [scatter_sum(): lax.ppermute(lax.dynamic_index_in_dim(blocks, 1 - me, 0, keepdims=False),...]
    reduce_sum x3 -> x1, other arithmetic: 7.03 us -> 0.36 us  [body(): jnp.sum(jnp.where(lane_ids == (token_ids % lanes)[:, None], table_rows, 0...]
    squeeze x0 -> x3, local copies, waits for them, and re-layouts: none -> 6.36 us  [scatter_sum(): lax.dynamic_index_in_dim(blocks, 1 - me, 0, keepdims=False)]
    ppermute x0 -> x3, starting transfers between devices: none -> 5.2 us  [scatter_sum(): lax.ppermute(lax.dynamic_index_in_dim(blocks, 1 - me, 0, keepdims=False),...]
    all_to_all x1, starting transfers between devices: 10.7 us -> 7.11 us  [global_sums(): received = lax.all_to_all(stacked, FSDP + ('fac',), 0, 0, tiled=True)]
    gather x1, local copies, waits for them, and re-layouts: 6.15 us -> 2.81 us  [body(): importance.reshape(importance.shape[0] // lanes, lanes)[token_ids // lanes]]
  transfers between devices with their start and end apart: 8 -> 11, of which waited for: 4 -> 8; matrix products, arithmetic and copies ran while one was open for 10% -> 10% of each run, Pallas kernels for 8% -> 9%
where the time goes in v13:
time: 319 us; the launch traced here: 318 us
  blocking collectives  147 us (46%)
  waiting for transfers between devices  52.2 us (16%)
  Pallas kernels  27.1 us (8%)
  matrix products  27.1 us (8%)
  between operations  19.9 us (6%)
  other arithmetic  15.9 us (5%)
  starting transfers between devices  15.2 us (5%)
  local copies, waits for them, and re-layouts  14 us (4%)
    all_to_all x3, blocking collectives, scatter_sum(): received = lax.all_to_all(chip_sum, 'pairs', 0, 0, tiled=False)  95.7 us
    all_gather x3, waiting for transfers between devices, gather_rows(): return lax.all_gather(matrix.astype(jnp.bfloat16), FSDP, axis=0, tiled=True)  32.3 us
    pallas_call x3, Pallas kernels, block_term(): pl.pallas_call(kernel, grid=(cols // step,), in_specs=[pl.BlockSpec((toke...  27.1 us
    dot_general x8, matrix products, add_columns(): return jnp.dot(matrix, piece, preferred_element_type=jnp.float32)  23.2 us
    all_to_all x1, blocking collectives, global_sums(): received = lax.all_to_all(stacked, FSDP + ('fac',), 0, 0, tiled=True)  16 us
    all_gather x1, blocking collectives, body(): lax.all_gather(gram_own.astype(jnp.bfloat16), 'fac', axis=1, tiled=True)  11.9 us
    all_gather x1, blocking collectives, precondition(): lax.all_gather(mixed_low, 'fac', axis=1, tiled=True)  11.7 us
    all_gather x1, blocking collectives, body(): lax.all_gather(add_columns(gram_rows, in_cols).astype(jnp.bfloat16), 'fac...  11.3 us
  transfers between devices with their start and end apart: 11, of which 8 were waited for; matrix products, arithmetic and copies ran while one was open for 10% of the time, Pallas kernels for 9%

profile of v13, /device:TPU:1, one launch (start us, length us, event | category | flops | bytes accessed | tf_op | source)
XLA Modules:
  0.0 318.0 jit_solution(16547956694087706120)
XLA Ops:
  12.4 11.5 %shard_map.86 = bf16[2,16,96,768]{3,2,1,0:T(8,128)(2,1)} custom-call(bf16[1024,3072]{1,0:T(8,128)(2,1)} %a_ref.5, bf16[1024,768]{1,0:T(8,128)(2,1)} %broadcast_multiply_fusion.x_ref), custom_call_target="tpu_custom_call" | custom-call | tf_op jit(solution)/shard_map/pallas_call | solution.py:63
  23.9 3.3 %dynamic-slice_bitcast_fusion = bf16[16,96,768]{2,1,0:T(8,128)(2,1)} fusion(bf16[2,16,96,768]{3,2,1,0:T(8,128)(2,1)} %shard_map.86, s32[]{:T(128)S(6)} %select_n.66), kind=kLoop, calls=%fused_computation.14 | loop fusion | bytes 4718596 | tf_op jit(solution)/shard_map/jit(dynamic_index_in_dim)/squeeze | solution.py:79
  28.5 4.4 %collective-permute-done = bf16[16,96,768]{2,1,0:T(8,128)(2,1)S(1)} collective-permute-done((bf16[16,96,768]{2,1,0:T(8,128)(2,1)}, bf16[16,96,768]{2,1,0:T(8,128)(2,1)S(1)}, u32[]{:S(2)}, u32[]{:S(2)}) %collective-permute-start) | collective-permute-done | bytes 2359328 | tf_op jit(solution)/shard_map/ppermute | solution.py:79
  35.2 47.9 %all_to_all.27 = bf16[16,96,768]{2,1,0:T(8,128)(2,1)S(1)} all-to-all(bf16[16,96,768]{2,1,0:T(8,128)(2,1)S(1)} %fusion.1), channel_id=1, replica_groups=mesh['pairs'=16,'core'=2,'fac'=4] {'pairs'}, dimensions={0} | all-to-all | bytes 4718592 | tf_op jit(solution)/shard_map/all_to_all | solution.py:82
  84.3 2.8 gather_fusion
  90.5 7.8 %shard_map.87 = bf16[2,16,96,384]{3,2,1,0:T(8,128)(2,1)} custom-call(bf16[1024,3072]{1,0:T(8,128)(2,1)} %a_ref.5, bf16[1024,384]{1,0:T(8,128)(2,1)} %get-tuple-element.17.x_ref), custom_call_target="tpu_custom_call" | custom-call | tf_op jit(solution)/shard_map/pallas_call | solution.py:63
  104.2 25.1 %all_to_all.28 = bf16[16,96,384]{2,1,0:T(8,128)(2,1)S(1)} all-to-all(bf16[16,96,384]{2,1,0:T(8,128)(2,1)S(1)} %fusion.4), channel_id=1, replica_groups=mesh['pairs'=16,'core'=2,'fac'=4] {'pairs'}, dimensions={0} | all-to-all | bytes 2359296 | tf_op jit(solution)/shard_map/all_to_all | solution.py:82
  129.5 7.5 %all-gather.7.cloned.1.call-done = bf16[3072,768]{1,0:T(8,128)(2,1)} async-done(((bf16[96,768]{1,0:T(8,128)(2,1)}), bf16[3072,768]{1,0:T(8,128)(2,1)}) %all-gather.7.cloned.1.call-update) | async-done | bytes 4718608 | tf_op jit(solution)/shard_map/all_gather | solution.py:111
  137.0 3.2 %fusion.14 = bf16[96,768]{1,0:T(8,128)(2,1)S(1)} fusion(bf16[96,3072]{1,0:T(8,128)(2,1)S(1)} %copy-done.4, bf16[3072,768]{1,0:T(8,128)(2,1)} %all-gather.7.cloned.1.call-done), kind=kOutput, calls=%fused_computation.32 | convolution fusion | flops 453058560 | bytes 5455872 | tf_op jit(solution)/shard_map/dot_general | solution.py:16
  140.3 11.7 %all_gather.23 = bf16[96,3072]{1,0:T(8,128)(2,1)S(1)} all-gather(bf16[96,768]{1,0:T(8,128)(2,1)S(1)} %fusion.14), channel_id=1, replica_groups=mesh['pairs'=16,'core'=2,'fac'=4] {'fac'}, dimensions={1}, use_global_device_ids=true | all-gather | bytes 737280 | tf_op jit(solution)/shard_map/all_gather | solution.py:117
  151.9 3.9 %fusion.26 = (bf16[96,768]{1,0:T(8,128)(2,1)}, f32[96,768]{1,0:T(8,128)S(1)}) fusion(bf16[96,3072]{1,0:T(8,128)(2,1)S(1)} %all_gather.23, bf16[3072,768]{1,0:T(8,128)(2,1)} %param.13), kind=kOutput, calls=%fused_computation.70 | convolution fusion | flops 453058560 | bytes 5750784 | tf_op jit(solution)/shard_map/dot_general | solution.py:116
  155.9 7.8 %shard_map.88 = bf16[2,16,96,384]{3,2,1,0:T(8,128)(2,1)} custom-call(bf16[1024,3072]{1,0:T(8,128)(2,1)} %a_ref.5, bf16[1024,384]{1,0:T(8,128)(2,1)} %get-tuple-element.16.x_ref), custom_call_target="tpu_custom_call" | custom-call | tf_op jit(solution)/shard_map/pallas_call | solution.py:63
  170.4 22.7 %all_to_all.29 = bf16[16,96,384]{2,1,0:T(8,128)(2,1)S(1)} all-to-all(bf16[16,96,384]{2,1,0:T(8,128)(2,1)S(1)} %fusion.3), channel_id=1, replica_groups=mesh['pairs'=16,'core'=2,'fac'=4] {'pairs'}, dimensions={0} | all-to-all | bytes 2359296 | tf_op jit(solution)/shard_map/all_to_all | solution.py:82
  193.2 11.9 %all_gather.24 = bf16[96,3072]{1,0:T(8,128)(2,1)S(1)} all-gather(bf16[96,768]{1,0:T(8,128)(2,1)S(1)} %pad_maximum_fusion), channel_id=1, replica_groups=mesh['pairs'=16,'core'=2,'fac'=4] {'fac'}, dimensions={1}, use_global_device_ids=true | all-gather | bytes 737280 | tf_op jit(solution)/shard_map/all_gather | solution.py:148
  205.1 4.2 %all-gather.9.cloned.1.call-done = bf16[3072,768]{1,0:T(8,128)(2,1)} async-done(((bf16[96,768]{1,0:T(8,128)(2,1)}), bf16[3072,768]{1,0:T(8,128)(2,1)}) %all-gather.9.cloned.1.call-update) | async-done | bytes 4718608 | tf_op jit(solution)/shard_map/all_gather | solution.py:111
  209.3 4.5 %multiply_reduce_fusion.5 = (f32[]{:T(128)}, f32[]{:T(128)}, bf16[96,768]{1,0:T(8,128)(2,1)}, f32[96,768]{1,0:T(8,128)S(1)}) fusion(f32[96,768]{1,0:T(8,128)S(1)} %get-tuple-element.30, f32[96,768]{1,0:T(8,128)S(1)} %convert_reduce_fusion, bf16[96,3072]{1,0:T(8,128)(2,1)S(1)} %all_gather.24, bf16[3072,768]{1,0:T(8,128)(2,1)} %all-gather.9.cloned.1.call-done), kind=kOutput, calls=%fused_computation.45 | convolution fusion | flops 453574656 | bytes 6340616 | tf_op jit(solution)/shard_map/dot_general | solution.py:16
  213.8 3.2 %convolution_convert_fusion.1 = bf16[96,768]{1,0:T(8,128)(2,1)S(1)} fusion(bf16[96,3072]{1,0:T(8,128)(2,1)S(1)} %all_gather.24, bf16[3072,768]{1,0:T(8,128)(2,1)} %all-gather.5.cloned.1.call-done), kind=kOutput, calls=%fused_computation.31 | convolution fusion | flops 453058560 | bytes 5455872 | tf_op jit(solution)/shard_map/dot_general | solution.py:16
  219.1 7.1 %all-to-all-start.3 = ((f32[128,1,2]{2,1,0:T(1,128)}), f32[128,1,2]{2,1,0:T(1,128)S(1)}, u32[]{:S(2)}, u32[]{:S(2)}) async-start(f32[128,1,2]{2,1,0:T(1,128)} %broadcast_in_dim.12), calls=%async_computation.3 | async-start | bytes 131072 | tf_op jit(solution)/shard_map/all_to_all | solution.py:89
  226.2 11.3 %all_gather.26 = bf16[96,3072]{1,0:T(8,128)(2,1)S(1)} all-gather(bf16[96,768]{1,0:T(8,128)(2,1)S(1)} %convolution_convert_fusion.1), channel_id=1, replica_groups=mesh['pairs'=16,'core'=2,'fac'=4] {'fac'}, dimensions={1}, use_global_device_ids=true | all-gather | bytes 737280 | tf_op jit(solution)/shard_map/all_gather | solution.py:157
  239.6 20.7 %all-gather.11.cloned.1.call-done = bf16[3072,768]{1,0:T(8,128)(2,1)} async-done(((bf16[96,768]{1,0:T(8,128)(2,1)}), bf16[3072,768]{1,0:T(8,128)(2,1)}) %all-gather.11.cloned.1.call-update) | async-done | bytes 4718608 | tf_op jit(solution)/shard_map/all_gather | solution.py:111
  260.3 5.6 %fusion.5 = bf16[192,768]{1,0:T(8,128)(2,1)S(1)} fusion(bf16[3072,768]{1,0:T(8,128)(2,1)} %all-gather.11.cloned.1.call-done, bf16[3072,768]{1,0:T(8,128)(2,1)} %all-gather.7.cloned.1.call-done, f32[]{:T(128)S(6)} %div.33, bf16[96,3072]{1,0:T(8,128)(2,1)S(1)} %all_gather.26, bf16[96,3072]{1,0:T(8,128)(2,1)S(1)} %copy-done.4), kind=kOutput, calls=%fused_computation.18 | convolution fusion | flops 920272896 | bytes 10911748 | tf_op jit(solution)/shard_map/dot_general | solution.py:16
  270.3 5.2 %collective-permute-done.3 = bf16[192,768]{1,0:T(8,128)(2,1)S(1)} collective-permute-done((bf16[192,768]{1,0:T(8,128)(2,1)S(1)}, bf16[192,768]{1,0:T(8,128)(2,1)S(1)}, u32[]{:S(2)}, u32[]{:S(2)}) %collective-permute-start.3) | collective-permute-done | bytes 294944 | tf_op jit(solution)/shard_map/ppermute | solution.py:40
  278.9 5.3 %collective-permute-done.5 = bf16[192,768]{1,0:T(8,128)(2,1)S(1)} collective-permute-done((bf16[192,768]{1,0:T(8,128)(2,1)S(1)}, bf16[192,768]{1,0:T(8,128)(2,1)S(1)}, u32[]{:S(2)}, u32[]{:S(2)}) %collective-permute-start.5) | collective-permute-done | bytes 294944 | tf_op jit(solution)/shard_map/ppermute | solution.py:40
  289.3 16.0 %all_to_all.30 = f32[128,1,4]{2,1,0:T(1,128)S(1)} all-to-all(f32[128,1,4]{2,1,0:T(1,128)S(1)} %broadcast_in_dim.13), channel_id=1, replica_groups=mesh['pairs'=16,'core'=2,'fac'=4] {'pairs','core','fac'}, dimensions={0} | all-to-all | bytes 4096 | tf_op jit(solution)/shard_map/all_to_all | solution.py:89
  (65 shorter events, 43.7 us)
Async XLA Ops:
  7.2 77.1 %copy-start = (f32[32768]{0:T(1024)S(1)}, f32[32768]{0:T(1024)}, u32[]{:S(2)}) copy-start(f32[32768]{0:T(1024)} %param.11) | copy-start | bytes 393220
  7.2 76.3 %all-gather.5.cloned.1.call-start = ((), (), s32[]{:S(2)}) async-start(), calls=%async_computation.5 | async-start | bytes 4866048 | tf_op jit(solution)/shard_map/all_gather | solution.py:126
  8.8 128.2 %all-gather.7.cloned.1.call-start = ((), (), s32[]{:S(2)}) async-start(), calls=%async_computation.6 | async-start | bytes 4866048 | tf_op jit(solution)/shard_map/all_gather | solution.py:111
  27.1 5.7 %collective-permute-start = (bf16[16,96,768]{2,1,0:T(8,128)(2,1)}, bf16[16,96,768]{2,1,0:T(8,128)(2,1)S(1)}, u32[]{:S(2)}, u32[]{:S(2)}) collective-permute-start(bf16[16,96,768]{2,1,0:T(8,128)(2,1)} %dynamic-slice_bitcast_fusion), channel_id=1, source_target_pairs={{0,4},{4,0},{1,5},{5,1},{2,6},{6,2},{3,7},{7,3},{8,12},{12,8},{9,1... | collective-permute-start | bytes 7077896 | tf_op jit(solution)/shard_map/ppermute | solution.py:79
  83.1 1.1 copy-start.6
  84.2 125.1 %all-gather.9.cloned.1.call-start = ((), (), s32[]{:S(2)}) async-start(), calls=%async_computation.7 | async-start | bytes 4866048 | tf_op jit(solution)/shard_map/all_gather | solution.py:111
  84.3 3.2 %copy-start.5 = (s32[1024]{0:T(1024)S(1)}, s32[1024]{0:T(1024)}, u32[]{:S(2)}) copy-start(s32[1024]{0:T(1024)} %param.10) | copy-start | bytes 12292
  98.3 5.6 %copy-start.3 = (bf16[2,16,96,384]{3,2,1,0:T(8,128)(2,1)S(1)}, bf16[2,16,96,384]{3,2,1,0:T(8,128)(2,1)}, u32[]{:S(2)}) copy-start(bf16[2,16,96,384]{3,2,1,0:T(8,128)(2,1)} %shard_map.87) | copy-start | bytes 7077892
  99.9 4.0 %collective-permute-start.1 = (bf16[16,96,384]{2,1,0:T(8,128)(2,1)S(1)}, bf16[16,96,384]{2,1,0:T(8,128)(2,1)S(1)}, u32[]{:S(2)}, u32[]{:S(2)}) collective-permute-start(bf16[16,96,384]{2,1,0:T(8,128)(2,1)S(1)} %dynamic-slice_bitcast_fusion.2), channel_id=1, source_target_pairs={{0,4},{4,0},{1,5},{5,1},{2,6},{6,2},{3,7},{7,3},{8,12},{12,8},{9,1... | collective-permute-start | bytes 3538952 | tf_op jit(solution)/shard_map/ppermute | solution.py:79
  104.2 32.8 %copy-start.4 = (bf16[96,3072]{1,0:T(8,128)(2,1)S(1)}, bf16[96,3072]{1,0:T(8,128)(2,1)}, u32[]{:S(2)}) copy-start(bf16[96,3072]{1,0:T(8,128)(2,1)} %param.12) | copy-start | bytes 1769476
  155.8 104.5 %all-gather.11.cloned.1.call-start = ((), (), s32[]{:S(2)}) async-start(), calls=%async_computation.8 | async-start | bytes 4866048 | tf_op jit(solution)/shard_map/all_gather | solution.py:111
  163.7 6.3 %copy-start.2 = (bf16[2,16,96,384]{3,2,1,0:T(8,128)(2,1)S(1)}, bf16[2,16,96,384]{3,2,1,0:T(8,128)(2,1)}, u32[]{:S(2)}) copy-start(bf16[2,16,96,384]{3,2,1,0:T(8,128)(2,1)} %shard_map.88) | copy-start | bytes 7077892
  165.2 4.8 %collective-permute-start.2 = (bf16[16,96,384]{2,1,0:T(8,128)(2,1)S(1)}, bf16[16,96,384]{2,1,0:T(8,128)(2,1)S(1)}, u32[]{:S(2)}, u32[]{:S(2)}) collective-permute-start(bf16[16,96,384]{2,1,0:T(8,128)(2,1)S(1)} %dynamic-slice_bitcast_fusion.1), channel_id=1, source_target_pairs={{0,4},{4,0},{1,5},{5,1},{2,6},{6,2},{3,7},{7,3},{8,12},{12,8},{9,1... | collective-permute-start | bytes 3538952 | tf_op jit(solution)/shard_map/ppermute | solution.py:79
  219.1 18.4 %all-to-all-start.3 = ((f32[128,1,2]{2,1,0:T(1,128)}), f32[128,1,2]{2,1,0:T(1,128)S(1)}, u32[]{:S(2)}, u32[]{:S(2)}) async-start(f32[128,1,2]{2,1,0:T(1,128)} %broadcast_in_dim.12), calls=%async_computation.3 | async-start | bytes 131072 | tf_op jit(solution)/shard_map/all_to_all | solution.py:89
  265.9 9.6 %collective-permute-start.3 = (bf16[192,768]{1,0:T(8,128)(2,1)S(1)}, bf16[192,768]{1,0:T(8,128)(2,1)S(1)}, u32[]{:S(2)}, u32[]{:S(2)}) collective-permute-start(bf16[192,768]{1,0:T(8,128)(2,1)S(1)} %fusion.5), channel_id=1, source_target_pairs={{0,1},{1,2},{2,3},{3,0},{4,5},{5,6},{6,7},{7,4},{8,9},{9,10},{10,1... | collective-permute-start | bytes 884744 | tf_op jit(solution)/shard_map/ppermute | solution.py:40
  267.1 10.1 %collective-permute-start.4 = (bf16[192,768]{1,0:T(8,128)(2,1)S(1)}, bf16[192,768]{1,0:T(8,128)(2,1)S(1)}, u32[]{:S(2)}, u32[]{:S(2)}) collective-permute-start(bf16[192,768]{1,0:T(8,128)(2,1)S(1)} %fusion.5), channel_id=1, source_target_pairs={{0,3},{1,0},{2,1},{3,2},{4,7},{5,4},{6,5},{7,6},{8,11},{9,8},{10,9... | collective-permute-start | bytes 884744 | tf_op jit(solution)/shard_map/ppermute | solution.py:43
  275.5 8.6 %collective-permute-start.5 = (bf16[192,768]{1,0:T(8,128)(2,1)S(1)}, bf16[192,768]{1,0:T(8,128)(2,1)S(1)}, u32[]{:S(2)}, u32[]{:S(2)}) collective-permute-start(bf16[192,768]{1,0:T(8,128)(2,1)S(1)} %collective-permute-done.3), channel_id=1, source_target_pairs={{0,1},{1,2},{2,3},{3,0},{4,5},{5,6},{6,7},{7,4},{8,9},{9,10},{10,1... | collective-permute-start | bytes 884744 | tf_op jit(solution)/shard_map/ppermute | solution.py:40
  284.1 27.3 %copy-start.1 = (f32[32768]{0:T(1024)S(1)}, f32[32768]{0:T(1024)}, u32[]{:S(2)}) copy-start(f32[32768]{0:T(1024)} %param.11) | copy-start | bytes 393220
Sparse Core Ops, SparseCore 0:
  10.8 71.9 all-gather.4
  85.7 51.2 all-gather.6
  155.9 53.3 all-gather.8
  214.0 46.2 all-gather.10

commit v14 on v13

--- a/solution.py
+++ b/solution.py
@@ -45,16 +45,17 @@
     return total
 
 
-def block_term(activations, right, scale):
+def block_term(activations, right, factor, scale):
     pairs, cores = lax.axis_size("pairs"), lax.axis_size("core")
     tokens, d_in = activations.shape
     rows = d_in // (pairs * cores)
     cols = right.shape[1]
     step = 384 if cols % 384 == 0 else cols
 
-    def kernel(a_ref, x_ref, o_ref):
+    def kernel(a_ref, x_ref, f_ref, o_ref):
+        scaled = (x_ref[...].astype(jnp.float32) * f_ref[...]).astype(jnp.bfloat16)
         product = lax.dot_general(
-            a_ref[...], x_ref[...], (((0,), (0,)), ((), ())), preferred_element_type=jnp.float32
+            a_ref[...], scaled, (((0,), (0,)), ((), ())), preferred_element_type=jnp.float32
         )
         product = (product * scale).astype(o_ref.dtype)
         for block in range(pairs * cores):
@@ -66,10 +67,11 @@
         in_specs=[
             pl.BlockSpec((tokens, d_in), lambda j: (0, 0)),
             pl.BlockSpec((tokens, step), lambda j: (0, j)),
+            pl.BlockSpec((tokens, 1), lambda j: (0, 0)),
         ],
         out_specs=pl.BlockSpec((cores, pairs, rows, step), lambda j: (0, 0, 0, j)),
         out_shape=jax.ShapeDtypeStruct((cores, pairs, rows, cols), jnp.bfloat16),
-    )(activations, right)
+    )(activations, right, factor.reshape(tokens, 1))
 
 
 def scatter_sum(blocks):
@@ -102,10 +104,11 @@
         jnp.where(lane_ids == (token_ids % lanes)[:, None], table_rows, 0.0), axis=1
     )
     weights = picked * keep / total
-    forget_grads = out_grads * forget_mask.astype(jnp.bfloat16)[:, None]
     grad_scale = 1.0 / math.sqrt(total)
 
-    gradient = scatter_sum(block_term(activations, forget_grads, grad_scale))
+    gradient = scatter_sum(
+        block_term(activations, out_grads, forget_mask.astype(jnp.float32), grad_scale)
+    )
 
     def gather_rows(matrix):
         return lax.all_gather(matrix.astype(jnp.bfloat16), FSDP, axis=0, tiled=True)
@@ -138,10 +141,9 @@
     own_cols = lax.dynamic_slice_in_dim(
         activations, lax.axis_index("fac") * gram_cols, gram_cols, axis=1
     )
-    weighted = (own_cols * weights[:, None]).astype(jnp.bfloat16)
     half = gram_cols // 2
-    gram_first = block_term(activations, weighted[:, :half], 1.0)
-    gram_second = block_term(activations, weighted[:, half:], 1.0)
+    gram_first = block_term(activations, own_cols[:, :half], weights, 1.0)
+    gram_second = block_term(activations, own_cols[:, half:], weights, 1.0)
     residual_rows, first_rows = lax.optimization_barrier((residual_rows, scatter_sum(gram_first)))
     precond = precondition(residual_rows)
     gram_own = jnp.concatenate([first_rows, scatter_sum(gram_second)], axis=1)

time: 319 us -> 318 us (level)
  other arithmetic: 15.9 us -> 11.4 us
  local copies, waits for them, and re-layouts: 14 us -> 17.5 us
  transfers between devices with their start and end apart: 11 -> 11, of which waited for: 8 -> 8; matrix products, arithmetic and copies ran while one was open for 10% -> 9% of each run, Pallas kernels for 9% -> 9%
where the time goes in v14:
time: 318 us
  blocking collectives  147 us (46%)
  waiting for transfers between devices  51.7 us (16%)
  Pallas kernels  27.8 us (9%)
  matrix products  27.1 us (9%)
  between operations  19.8 us (6%)
  local copies, waits for them, and re-layouts  17.5 us (6%)
  starting transfers between devices  15.4 us (5%)
  other arithmetic  11.4 us (4%)
    all_to_all x3, blocking collectives, scatter_sum(): received = lax.all_to_all(chip_sum, 'pairs', 0, 0, tiled=False)  96.6 us
    all_gather x3, waiting for transfers between devices, gather_rows(): return lax.all_gather(matrix.astype(jnp.bfloat16), FSDP, axis=0, tiled=True)  31.8 us
    pallas_call x3, Pallas kernels, block_term(): pl.pallas_call(kernel, grid=(cols // step,), in_specs=[pl.BlockSpec((toke...  27.8 us
    dot_general x8, matrix products, add_columns(): return jnp.dot(matrix, piece, preferred_element_type=jnp.float32)  23.2 us
    all_to_all x1, blocking collectives, global_sums(): received = lax.all_to_all(stacked, FSDP + ('fac',), 0, 0, tiled=True)  16 us
    all_gather x1, blocking collectives, body(): lax.all_gather(gram_own.astype(jnp.bfloat16), 'fac', axis=1, tiled=True)  11.5 us
    all_gather x1, blocking collectives, precondition(): lax.all_gather(mixed_low, 'fac', axis=1, tiled=True)  11.5 us
    all_gather x1, blocking collectives, body(): lax.all_gather(add_columns(gram_rows, in_cols).astype(jnp.bfloat16), 'fac...  11.3 us
  transfers between devices with their start and end apart: 11, of which 8 were waited for; matrix products, arithmetic and copies ran while one was open for 9% of the time, Pallas kernels for 9%

profile of v14, /device:TPU:1, one launch (start us, length us, event | category | flops | bytes accessed | tf_op | source)
XLA Modules:
  0.0 317.6 jit_solution(10143034153554127746)
XLA Ops:
  10.6 11.8 %shard_map.86 = bf16[2,16,96,768]{3,2,1,0:T(8,128)(2,1)} custom-call(bf16[1024,3072]{1,0:T(8,128)(2,1)} %a_ref.5, bf16[1024,768]{1,0:T(8,128)(2,1)} %x_ref.1, f32[1024,1]{1,0:T(8,128)} %copy.15.f_ref), custom_call_target="tpu_custom_call" | custom-call | tf_op jit(solution)/shard_map/pallas_call | solution.py:64
  22.4 3.3 %dynamic-slice_bitcast_fusion = bf16[16,96,768]{2,1,0:T(8,128)(2,1)} fusion(bf16[2,16,96,768]{3,2,1,0:T(8,128)(2,1)} %shard_map.86, s32[]{:T(128)S(6)} %select_n.66), kind=kLoop, calls=%fused_computation.13 | loop fusion | bytes 4718596 | tf_op jit(solution)/shard_map/jit(dynamic_index_in_dim)/squeeze | solution.py:81
  27.1 4.4 %collective-permute-done = bf16[16,96,768]{2,1,0:T(8,128)(2,1)S(1)} collective-permute-done((bf16[16,96,768]{2,1,0:T(8,128)(2,1)}, bf16[16,96,768]{2,1,0:T(8,128)(2,1)S(1)}, u32[]{:S(2)}, u32[]{:S(2)}) %collective-permute-start) | collective-permute-done | bytes 2359328 | tf_op jit(solution)/shard_map/ppermute | solution.py:81
  33.8 47.8 %all_to_all.27 = bf16[16,96,768]{2,1,0:T(8,128)(2,1)S(1)} all-to-all(bf16[16,96,768]{2,1,0:T(8,128)(2,1)S(1)} %fusion.1), channel_id=1, replica_groups=mesh['pairs'=16,'core'=2,'fac'=4] {'pairs'}, dimensions={0} | all-to-all | bytes 4718592 | tf_op jit(solution)/shard_map/all_to_all | solution.py:84
  82.7 2.8 gather_fusion
  89.7 8.0 %shard_map.87 = bf16[2,16,96,384]{3,2,1,0:T(8,128)(2,1)} custom-call(bf16[1024,3072]{1,0:T(8,128)(2,1)} %a_ref.5, bf16[1024,384]{1,0:T(8,128)(2,1)} %get-tuple-element.17.x_ref, f32[1024,1]{1,0:T(8,128)} %copy.16.f_ref), custom_call_target="tpu_custom_call" | custom-call | tf_op jit(solution)/shard_map/pallas_call | solution.py:64
  103.7 25.8 %all_to_all.28 = bf16[16,96,384]{2,1,0:T(8,128)(2,1)S(1)} all-to-all(bf16[16,96,384]{2,1,0:T(8,128)(2,1)S(1)} %fusion.4), channel_id=1, replica_groups=mesh['pairs'=16,'core'=2,'fac'=4] {'pairs'}, dimensions={0} | all-to-all | bytes 2359296 | tf_op jit(solution)/shard_map/all_to_all | solution.py:84
  129.6 6.5 %all-gather.7.cloned.1.call-done = bf16[3072,768]{1,0:T(8,128)(2,1)} async-done(((bf16[96,768]{1,0:T(8,128)(2,1)}), bf16[3072,768]{1,0:T(8,128)(2,1)}) %all-gather.7.cloned.1.call-update) | async-done | bytes 4718608 | tf_op jit(solution)/shard_map/all_gather | solution.py:114
  136.1 3.2 %fusion.14 = bf16[96,768]{1,0:T(8,128)(2,1)S(1)} fusion(bf16[96,3072]{1,0:T(8,128)(2,1)S(1)} %copy-done.4, bf16[3072,768]{1,0:T(8,128)(2,1)} %all-gather.7.cloned.1.call-done), kind=kOutput, calls=%fused_computation.31 | convolution fusion | flops 453058560 | bytes 5455872 | tf_op jit(solution)/shard_map/dot_general | solution.py:16
  139.3 11.5 %all_gather.23 = bf16[96,3072]{1,0:T(8,128)(2,1)S(1)} all-gather(bf16[96,768]{1,0:T(8,128)(2,1)S(1)} %fusion.14), channel_id=1, replica_groups=mesh['pairs'=16,'core'=2,'fac'=4] {'fac'}, dimensions={1}, use_global_device_ids=true | all-gather | bytes 737280 | tf_op jit(solution)/shard_map/all_gather | solution.py:120
  150.8 3.9 %fusion.25 = (bf16[96,768]{1,0:T(8,128)(2,1)}, f32[96,768]{1,0:T(8,128)S(1)}) fusion(bf16[96,3072]{1,0:T(8,128)(2,1)S(1)} %all_gather.23, bf16[3072,768]{1,0:T(8,128)(2,1)} %param.13), kind=kOutput, calls=%fused_computation.69 | convolution fusion | flops 453058560 | bytes 5750784 | tf_op jit(solution)/shard_map/dot_general | solution.py:119
  154.8 8.0 %shard_map.88 = bf16[2,16,96,384]{3,2,1,0:T(8,128)(2,1)} custom-call(bf16[1024,3072]{1,0:T(8,128)(2,1)} %a_ref.5, bf16[1024,384]{1,0:T(8,128)(2,1)} %get-tuple-element.16.x_ref, f32[1024,1]{1,0:T(8,128)} %copy.16.f_ref), custom_call_target="tpu_custom_call" | custom-call | tf_op jit(solution)/shard_map/pallas_call | solution.py:64
  169.4 23.0 %all_to_all.29 = bf16[16,96,384]{2,1,0:T(8,128)(2,1)S(1)} all-to-all(bf16[16,96,384]{2,1,0:T(8,128)(2,1)S(1)} %fusion.3), channel_id=1, replica_groups=mesh['pairs'=16,'core'=2,'fac'=4] {'pairs'}, dimensions={0} | all-to-all | bytes 2359296 | tf_op jit(solution)/shard_map/all_to_all | solution.py:84
  192.7 11.5 %all_gather.24 = bf16[96,3072]{1,0:T(8,128)(2,1)S(1)} all-gather(bf16[96,768]{1,0:T(8,128)(2,1)S(1)} %pad_maximum_fusion), channel_id=1, replica_groups=mesh['pairs'=16,'core'=2,'fac'=4] {'fac'}, dimensions={1}, use_global_device_ids=true | all-gather | bytes 737280 | tf_op jit(solution)/shard_map/all_gather | solution.py:150
  204.2 4.7 %all-gather.9.cloned.1.call-done = bf16[3072,768]{1,0:T(8,128)(2,1)} async-done(((bf16[96,768]{1,0:T(8,128)(2,1)}), bf16[3072,768]{1,0:T(8,128)(2,1)}) %all-gather.9.cloned.1.call-update) | async-done | bytes 4718608 | tf_op jit(solution)/shard_map/all_gather | solution.py:114
  208.9 4.5 %multiply_reduce_fusion.5 = (f32[]{:T(128)}, f32[]{:T(128)}, bf16[96,768]{1,0:T(8,128)(2,1)}, f32[96,768]{1,0:T(8,128)S(1)}) fusion(f32[96,768]{1,0:T(8,128)S(1)} %get-tuple-element.30, f32[96,768]{1,0:T(8,128)S(1)} %convert_reduce_fusion, bf16[96,3072]{1,0:T(8,128)(2,1)S(1)} %all_gather.24, bf16[3072,768]{1,0:T(8,128)(2,1)} %all-gather.9.cloned.1.call-done), kind=kOutput, calls=%fused_computation.43 | convolution fusion | flops 453574656 | bytes 6340616 | tf_op jit(solution)/shard_map/dot_general | solution.py:16
  213.4 3.2 %convolution_convert_fusion.1 = bf16[96,768]{1,0:T(8,128)(2,1)S(1)} fusion(bf16[96,3072]{1,0:T(8,128)(2,1)S(1)} %all_gather.24, bf16[3072,768]{1,0:T(8,128)(2,1)} %all-gather.5.cloned.1.call-done), kind=kOutput, calls=%fused_computation.30 | convolution fusion | flops 453058560 | bytes 5455872 | tf_op jit(solution)/shard_map/dot_general | solution.py:16
  218.7 7.1 %all-to-all-start.3 = ((f32[128,1,2]{2,1,0:T(1,128)}), f32[128,1,2]{2,1,0:T(1,128)S(1)}, u32[]{:S(2)}, u32[]{:S(2)}) async-start(f32[128,1,2]{2,1,0:T(1,128)} %broadcast_in_dim.22), calls=%async_computation.3 | async-start | bytes 131072 | tf_op jit(solution)/shard_map/all_to_all | solution.py:91
  225.8 11.3 %all_gather.26 = bf16[96,3072]{1,0:T(8,128)(2,1)S(1)} all-gather(bf16[96,768]{1,0:T(8,128)(2,1)S(1)} %convolution_convert_fusion.1), channel_id=1, replica_groups=mesh['pairs'=16,'core'=2,'fac'=4] {'fac'}, dimensions={1}, use_global_device_ids=true | all-gather | bytes 737280 | tf_op jit(solution)/shard_map/all_gather | solution.py:159
  239.2 20.7 %all-gather.11.cloned.1.call-done = bf16[3072,768]{1,0:T(8,128)(2,1)} async-done(((bf16[96,768]{1,0:T(8,128)(2,1)}), bf16[3072,768]{1,0:T(8,128)(2,1)}) %all-gather.11.cloned.1.call-update) | async-done | bytes 4718608 | tf_op jit(solution)/shard_map/all_gather | solution.py:114
  259.9 5.6 %fusion.5 = bf16[192,768]{1,0:T(8,128)(2,1)S(1)} fusion(bf16[3072,768]{1,0:T(8,128)(2,1)} %all-gather.11.cloned.1.call-done, bf16[3072,768]{1,0:T(8,128)(2,1)} %all-gather.7.cloned.1.call-done, f32[]{:T(128)S(6)} %div.33, bf16[96,3072]{1,0:T(8,128)(2,1)S(1)} %all_gather.26, bf16[96,3072]{1,0:T(8,128)(2,1)S(1)} %copy-done.4), kind=kOutput, calls=%fused_computation.17 | convolution fusion | flops 920272896 | bytes 10911748 | tf_op jit(solution)/shard_map/dot_general | solution.py:16
  269.9 5.2 %collective-permute-done.3 = bf16[192,768]{1,0:T(8,128)(2,1)S(1)} collective-permute-done((bf16[192,768]{1,0:T(8,128)(2,1)S(1)}, bf16[192,768]{1,0:T(8,128)(2,1)S(1)}, u32[]{:S(2)}, u32[]{:S(2)}) %collective-permute-start.3) | collective-permute-done | bytes 294944 | tf_op jit(solution)/shard_map/ppermute | solution.py:40
  278.4 5.3 %collective-permute-done.5 = bf16[192,768]{1,0:T(8,128)(2,1)S(1)} collective-permute-done((bf16[192,768]{1,0:T(8,128)(2,1)S(1)}, bf16[192,768]{1,0:T(8,128)(2,1)S(1)}, u32[]{:S(2)}, u32[]{:S(2)}) %collective-permute-start.5) | collective-permute-done | bytes 294944 | tf_op jit(solution)/shard_map/ppermute | solution.py:40
  288.8 16.0 %all_to_all.30 = f32[128,1,4]{2,1,0:T(1,128)S(1)} all-to-all(f32[128,1,4]{2,1,0:T(1,128)S(1)} %broadcast_in_dim.23), channel_id=1, replica_groups=mesh['pairs'=16,'core'=2,'fac'=4] {'pairs','core','fac'}, dimensions={0} | all-to-all | bytes 4096 | tf_op jit(solution)/shard_map/all_to_all | solution.py:91
  (65 shorter events, 42.8 us)
Async XLA Ops:
  7.2 75.5 %copy-start = (f32[32768]{0:T(1024)S(1)}, f32[32768]{0:T(1024)}, u32[]{:S(2)}) copy-start(f32[32768]{0:T(1024)} %param.11) | copy-start | bytes 393220
  7.2 74.7 %all-gather.5.cloned.1.call-start = ((), (), s32[]{:S(2)}) async-start(), calls=%async_computation.5 | async-start | bytes 4866048 | tf_op jit(solution)/shard_map/all_gather | solution.py:129
  8.8 127.3 %all-gather.7.cloned.1.call-start = ((), (), s32[]{:S(2)}) async-start(), calls=%async_computation.6 | async-start | bytes 4866048 | tf_op jit(solution)/shard_map/all_gather | solution.py:114
  25.7 5.8 %collective-permute-start = (bf16[16,96,768]{2,1,0:T(8,128)(2,1)}, bf16[16,96,768]{2,1,0:T(8,128)(2,1)S(1)}, u32[]{:S(2)}, u32[]{:S(2)}) collective-permute-start(bf16[16,96,768]{2,1,0:T(8,128)(2,1)} %dynamic-slice_bitcast_fusion), channel_id=1, source_target_pairs={{0,4},{4,0},{1,5},{5,1},{2,6},{6,2},{3,7},{7,3},{8,12},{12,8},{9,1... | collective-permute-start | bytes 7077896 | tf_op jit(solution)/shard_map/ppermute | solution.py:81
  81.6 1.1 copy-start.6
  82.6 126.2 %all-gather.9.cloned.1.call-start = ((), (), s32[]{:S(2)}) async-start(), calls=%async_computation.7 | async-start | bytes 4866048 | tf_op jit(solution)/shard_map/all_gather | solution.py:114
  82.7 3.2 %copy-start.5 = (s32[1024]{0:T(1024)S(1)}, s32[1024]{0:T(1024)}, u32[]{:S(2)}) copy-start(s32[1024]{0:T(1024)} %param.10) | copy-start | bytes 12292
  97.7 5.7 %copy-start.3 = (bf16[2,16,96,384]{3,2,1,0:T(8,128)(2,1)S(1)}, bf16[2,16,96,384]{3,2,1,0:T(8,128)(2,1)}, u32[]{:S(2)}) copy-start(bf16[2,16,96,384]{3,2,1,0:T(8,128)(2,1)} %shard_map.87) | copy-start | bytes 7077892
  99.3 4.1 %collective-permute-start.1 = (bf16[16,96,384]{2,1,0:T(8,128)(2,1)S(1)}, bf16[16,96,384]{2,1,0:T(8,128)(2,1)S(1)}, u32[]{:S(2)}, u32[]{:S(2)}) collective-permute-start(bf16[16,96,384]{2,1,0:T(8,128)(2,1)S(1)} %dynamic-slice_bitcast_fusion.2), channel_id=1, source_target_pairs={{0,4},{4,0},{1,5},{5,1},{2,6},{6,2},{3,7},{7,3},{8,12},{12,8},{9,1... | collective-permute-start | bytes 3538952 | tf_op jit(solution)/shard_map/ppermute | solution.py:81
  103.7 32.4 %copy-start.4 = (bf16[96,3072]{1,0:T(8,128)(2,1)S(1)}, bf16[96,3072]{1,0:T(8,128)(2,1)}, u32[]{:S(2)}) copy-start(bf16[96,3072]{1,0:T(8,128)(2,1)} %param.12) | copy-start | bytes 1769476
  154.7 105.1 %all-gather.11.cloned.1.call-start = ((), (), s32[]{:S(2)}) async-start(), calls=%async_computation.8 | async-start | bytes 4866048 | tf_op jit(solution)/shard_map/all_gather | solution.py:114
  162.8 6.3 %copy-start.2 = (bf16[2,16,96,384]{3,2,1,0:T(8,128)(2,1)S(1)}, bf16[2,16,96,384]{3,2,1,0:T(8,128)(2,1)}, u32[]{:S(2)}) copy-start(bf16[2,16,96,384]{3,2,1,0:T(8,128)(2,1)} %shard_map.88) | copy-start | bytes 7077892
  164.3 4.8 %collective-permute-start.2 = (bf16[16,96,384]{2,1,0:T(8,128)(2,1)S(1)}, bf16[16,96,384]{2,1,0:T(8,128)(2,1)S(1)}, u32[]{:S(2)}, u32[]{:S(2)}) collective-permute-start(bf16[16,96,384]{2,1,0:T(8,128)(2,1)S(1)} %dynamic-slice_bitcast_fusion.1), channel_id=1, source_target_pairs={{0,4},{4,0},{1,5},{5,1},{2,6},{6,2},{3,7},{7,3},{8,12},{12,8},{9,1... | collective-permute-start | bytes 3538952 | tf_op jit(solution)/shard_map/ppermute | solution.py:81
  218.7 18.4 %all-to-all-start.3 = ((f32[128,1,2]{2,1,0:T(1,128)}), f32[128,1,2]{2,1,0:T(1,128)S(1)}, u32[]{:S(2)}, u32[]{:S(2)}) async-start(f32[128,1,2]{2,1,0:T(1,128)} %broadcast_in_dim.22), calls=%async_computation.3 | async-start | bytes 131072 | tf_op jit(solution)/shard_map/all_to_all | solution.py:91
  265.4 9.6 %collective-permute-start.3 = (bf16[192,768]{1,0:T(8,128)(2,1)S(1)}, bf16[192,768]{1,0:T(8,128)(2,1)S(1)}, u32[]{:S(2)}, u32[]{:S(2)}) collective-permute-start(bf16[192,768]{1,0:T(8,128)(2,1)S(1)} %fusion.5), channel_id=1, source_target_pairs={{0,1},{1,2},{2,3},{3,0},{4,5},{5,6},{6,7},{7,4},{8,9},{9,10},{10,1... | collective-permute-start | bytes 884744 | tf_op jit(solution)/shard_map/ppermute | solution.py:40
  266.7 10.1 %collective-permute-start.4 = (bf16[192,768]{1,0:T(8,128)(2,1)S(1)}, bf16[192,768]{1,0:T(8,128)(2,1)S(1)}, u32[]{:S(2)}, u32[]{:S(2)}) collective-permute-start(bf16[192,768]{1,0:T(8,128)(2,1)S(1)} %fusion.5), channel_id=1, source_target_pairs={{0,3},{1,0},{2,1},{3,2},{4,7},{5,4},{6,5},{7,6},{8,11},{9,8},{10,9... | collective-permute-start | bytes 884744 | tf_op jit(solution)/shard_map/ppermute | solution.py:43
  275.1 8.6 %collective-permute-start.5 = (bf16[192,768]{1,0:T(8,128)(2,1)S(1)}, bf16[192,768]{1,0:T(8,128)(2,1)S(1)}, u32[]{:S(2)}, u32[]{:S(2)}) collective-permute-start(bf16[192,768]{1,0:T(8,128)(2,1)S(1)} %collective-permute-done.3), channel_id=1, source_target_pairs={{0,1},{1,2},{2,3},{3,0},{4,5},{5,6},{6,7},{7,4},{8,9},{9,10},{10,1... | collective-permute-start | bytes 884744 | tf_op jit(solution)/shard_map/ppermute | solution.py:40
  283.7 27.3 %copy-start.1 = (f32[32768]{0:T(1024)S(1)}, f32[32768]{0:T(1024)}, u32[]{:S(2)}) copy-start(f32[32768]{0:T(1024)} %param.11) | copy-start | bytes 393220
Sparse Core Ops, SparseCore 0:
  10.8 70.6 all-gather.4
  84.4 51.6 all-gather.6
  154.9 53.9 all-gather.8
  213.5 46.2 all-gather.10

commit v15 on v14

--- a/solution.py
+++ b/solution.py
@@ -4,6 +4,7 @@
 import jax.numpy as jnp
 from jax import lax
 from jax.experimental import pallas as pl
+from jax.experimental.pallas import tpu as pltpu
 from jax.sharding import PartitionSpec as P
 
 ITERS = 2
@@ -52,15 +53,20 @@
     cols = right.shape[1]
     step = 384 if cols % 384 == 0 else cols
 
-    def kernel(a_ref, x_ref, f_ref, o_ref):
+    def kernel(a_ref, x_ref, f_ref, own_ref, other_ref, product_ref):
         scaled = (x_ref[...].astype(jnp.float32) * f_ref[...]).astype(jnp.bfloat16)
         product = lax.dot_general(
             a_ref[...], scaled, (((0,), (0,)), ((), ())), preferred_element_type=jnp.float32
         )
-        product = (product * scale).astype(o_ref.dtype)
-        for block in range(pairs * cores):
-            o_ref[block % cores, block // cores] = product[block * rows : (block + 1) * rows]
-
+        product_ref[...] = (product * scale).astype(product_ref.dtype)
+        me = lax.axis_index("core")
+        for pair in range(pairs):
+            mine = pl.multiple_of((pair * cores + me) * rows, rows)
+            theirs = pl.multiple_of((pair * cores + (cores - 1 - me)) * rows, rows)
+            own_ref[pair] = product_ref[pl.ds(mine, rows), :]
+            other_ref[pair] = product_ref[pl.ds(theirs, rows), :]
+
+    half = jax.ShapeDtypeStruct((pairs, rows, cols), jnp.bfloat16)
     return pl.pallas_call(
         kernel,
         grid=(cols // step,),
@@ -69,17 +75,20 @@
             pl.BlockSpec((tokens, step), lambda j: (0, j)),
             pl.BlockSpec((tokens, 1), lambda j: (0, 0)),
         ],
-        out_specs=pl.BlockSpec((cores, pairs, rows, step), lambda j: (0, 0, 0, j)),
-        out_shape=jax.ShapeDtypeStruct((cores, pairs, rows, cols), jnp.bfloat16),
+        out_specs=[
+            pl.BlockSpec((pairs, rows, step), lambda j: (0, 0, j)),
+            pl.BlockSpec((pairs, rows, step), lambda j: (0, 0, j)),
+        ],
+        out_shape=[half, half],
+        scratch_shapes=[pltpu.VMEM((d_in, step), jnp.bfloat16)],
     )(activations, right, factor.reshape(tokens, 1))
 
 
-def scatter_sum(blocks):
+def scatter_sum(halves):
     cores = lax.axis_size("core")
-    me = lax.axis_index("core")
+    own, other = halves
     sibling = [(j, (j + 1) % cores) for j in range(cores)]
-    sent = lax.ppermute(lax.dynamic_index_in_dim(blocks, 1 - me, 0, keepdims=False), "core", sibling)
-    own = lax.dynamic_index_in_dim(blocks, me, 0, keepdims=False)
+    sent = lax.ppermute(other, "core", sibling)
     chip_sum = (own.astype(jnp.float32) + sent.astype(jnp.float32)).astype(jnp.bfloat16)
     received = lax.all_to_all(chip_sum, "pairs", 0, 0, tiled=False)
     return lax.optimization_barrier(jnp.sum(received.astype(jnp.float32), axis=0))

time: 318 us -> 318 us (level)
  local copies, waits for them, and re-layouts: 17.5 us -> 11.1 us
  Pallas kernels: 27.8 us -> 32.7 us
    squeeze x3 -> x0, local copies, waits for them, and re-layouts: 6.35 us -> none  [scatter_sum(): lax.dynamic_index_in_dim(blocks, 1 - me, 0, keepdims=False)]
    pallas_call x3, Pallas kernels: 27.8 us -> 32.7 us  [block_term(): pl.pallas_call(kernel, grid=(cols // step,), in_specs=[pl.BlockSpec((toke...]
  transfers between devices with their start and end apart: 11 -> 11, of which waited for: 8 -> 8; matrix products, arithmetic and copies ran while one was open for 9% -> 8% of each run, Pallas kernels for 9% -> 10%
where the time goes in v15:
time: 318 us; the launch traced here: 317 us
  blocking collectives  147 us (46%)
  waiting for transfers between devices  50.3 us (16%)
  Pallas kernels  32.7 us (10%)
  matrix products  27.2 us (9%)
  between operations  19.6 us (6%)
  starting transfers between devices  15.5 us (5%)
  other arithmetic  13.9 us (4%)
  local copies, waits for them, and re-layouts  11.1 us (3%)
    all_to_all x3, blocking collectives, scatter_sum(): received = lax.all_to_all(chip_sum, 'pairs', 0, 0, tiled=False)  96.4 us
    pallas_call x3, Pallas kernels, block_term(): pl.pallas_call(kernel, grid=(cols // step,), in_specs=[pl.BlockSpec((toke...  32.7 us
    all_gather x3, waiting for transfers between devices, gather_rows(): return lax.all_gather(matrix.astype(jnp.bfloat16), FSDP, axis=0, tiled=True)  30 us
    dot_general x8, matrix products, add_columns(): return jnp.dot(matrix, piece, preferred_element_type=jnp.float32)  23.3 us
    all_to_all x1, blocking collectives, global_sums(): received = lax.all_to_all(stacked, FSDP + ('fac',), 0, 0, tiled=True)  15.9 us
    all_gather x1, blocking collectives, body(): lax.all_gather(gram_own.astype(jnp.bfloat16), 'fac', axis=1, tiled=True)  12 us
    all_gather x1, blocking collectives, precondition(): lax.all_gather(mixed_low, 'fac', axis=1, tiled=True)  11.4 us
    all_gather x1, blocking collectives, body(): lax.all_gather(add_columns(gram_rows, in_cols).astype(jnp.bfloat16), 'fac...  11.3 us
  transfers between devices with their start and end apart: 11, of which 8 were waited for; matrix products, arithmetic and copies ran while one was open for 8% of the time, Pallas kernels for 10%

profile of v15, /device:TPU:1, one launch (start us, length us, event | category | flops | bytes accessed | tf_op | source)
XLA Modules:
  0.0 317.3 jit_solution(11339947517386083514)
XLA Ops:
  10.6 14.4 %shard_map.86 = (bf16[16,96,768]{2,1,0:T(8,128)(2,1)}, bf16[16,96,768]{2,1,0:T(8,128)(2,1)}) custom-call(bf16[1024,3072]{1,0:T(8,128)(2,1)} %a_ref.5, bf16[1024,768]{1,0:T(8,128)(2,1)} %x_ref.1, f32[1024,1]{1,0:T(8,128)} %copy.15.f_ref), custom_call_target="tpu_custom_call" | custom-call | tf_op jit(solution)/shard_map/pallas_call | solution.py:70
  26.5 4.4 %collective-permute-done = bf16[16,96,768]{2,1,0:T(8,128)(2,1)S(1)} collective-permute-done((bf16[16,96,768]{2,1,0:T(8,128)(2,1)}, bf16[16,96,768]{2,1,0:T(8,128)(2,1)S(1)}, u32[]{:S(2)}, u32[]{:S(2)}) %collective-permute-start) | collective-permute-done | bytes 2359328 | tf_op jit(solution)/shard_map/ppermute | solution.py:91
  33.2 47.8 %all_to_all.27 = bf16[16,96,768]{2,1,0:T(8,128)(2,1)S(1)} all-to-all(bf16[16,96,768]{2,1,0:T(8,128)(2,1)S(1)} %add_convert_fusion), channel_id=1, replica_groups=mesh['pairs'=16,'core'=2,'fac'=4] {'pairs'}, dimensions={0} | all-to-all | bytes 4718592 | tf_op jit(solution)/shard_map/all_to_all | solution.py:93
  82.2 2.8 gather_fusion
  86.4 2.7 constant_dynamic-slice_fusion.1
  89.1 9.1 %shard_map.87 = (bf16[16,96,384]{2,1,0:T(8,128)(2,1)}, bf16[16,96,384]{2,1,0:T(8,128)(2,1)}) custom-call(bf16[1024,3072]{1,0:T(8,128)(2,1)} %a_ref.5, bf16[1024,384]{1,0:T(8,128)(2,1)} %get-tuple-element.29.x_ref, f32[1024,1]{1,0:T(8,128)} %copy.16.f_ref), custom_call_target="tpu_custom_call" | custom-call | tf_op jit(solution)/shard_map/pallas_call | solution.py:70
  104.1 26.6 %all_to_all.28 = bf16[16,96,384]{2,1,0:T(8,128)(2,1)S(1)} all-to-all(bf16[16,96,384]{2,1,0:T(8,128)(2,1)S(1)} %add_convert_fusion.2), channel_id=1, replica_groups=mesh['pairs'=16,'core'=2,'fac'=4] {'pairs'}, dimensions={0} | all-to-all | bytes 2359296 | tf_op jit(solution)/shard_map/all_to_all | solution.py:93
  130.8 5.5 %all-gather.7.cloned.1.call-done = bf16[3072,768]{1,0:T(8,128)(2,1)} async-done(((bf16[96,768]{1,0:T(8,128)(2,1)}), bf16[3072,768]{1,0:T(8,128)(2,1)}) %all-gather.7.cloned.1.call-update) | async-done | bytes 4718608 | tf_op jit(solution)/shard_map/all_gather | solution.py:123
  136.4 3.2 %fusion.11 = bf16[96,768]{1,0:T(8,128)(2,1)S(1)} fusion(bf16[96,3072]{1,0:T(8,128)(2,1)S(1)} %copy-done.2, bf16[3072,768]{1,0:T(8,128)(2,1)} %all-gather.7.cloned.1.call-done), kind=kOutput, calls=%fused_computation.25 | convolution fusion | flops 453058560 | bytes 5455872 | tf_op jit(solution)/shard_map/dot_general | solution.py:17
  139.6 11.4 %all_gather.23 = bf16[96,3072]{1,0:T(8,128)(2,1)S(1)} all-gather(bf16[96,768]{1,0:T(8,128)(2,1)S(1)} %fusion.11), channel_id=1, replica_groups=mesh['pairs'=16,'core'=2,'fac'=4] {'fac'}, dimensions={1}, use_global_device_ids=true | all-gather | bytes 737280 | tf_op jit(solution)/shard_map/all_gather | solution.py:129
  150.9 3.9 %fusion.22 = (bf16[96,768]{1,0:T(8,128)(2,1)}, f32[96,768]{1,0:T(8,128)S(1)}) fusion(bf16[96,3072]{1,0:T(8,128)(2,1)S(1)} %all_gather.23, bf16[3072,768]{1,0:T(8,128)(2,1)} %param.13), kind=kOutput, calls=%fused_computation.63 | convolution fusion | flops 453058560 | bytes 5750784 | tf_op jit(solution)/shard_map/dot_general | solution.py:128
  154.9 9.1 %shard_map.88 = (bf16[16,96,384]{2,1,0:T(8,128)(2,1)}, bf16[16,96,384]{2,1,0:T(8,128)(2,1)}) custom-call(bf16[1024,3072]{1,0:T(8,128)(2,1)} %a_ref.5, bf16[1024,384]{1,0:T(8,128)(2,1)} %get-tuple-element.28.x_ref, f32[1024,1]{1,0:T(8,128)} %copy.16.f_ref), custom_call_target="tpu_custom_call" | custom-call | tf_op jit(solution)/shard_map/pallas_call | solution.py:70
  170.5 22.1 %all_to_all.29 = bf16[16,96,384]{2,1,0:T(8,128)(2,1)S(1)} all-to-all(bf16[16,96,384]{2,1,0:T(8,128)(2,1)S(1)} %add_convert_fusion.1), channel_id=1, replica_groups=mesh['pairs'=16,'core'=2,'fac'=4] {'pairs'}, dimensions={0} | all-to-all | bytes 2359296 | tf_op jit(solution)/shard_map/all_to_all | solution.py:93
  192.8 12.0 %all_gather.24 = bf16[96,3072]{1,0:T(8,128)(2,1)S(1)} all-gather(bf16[96,768]{1,0:T(8,128)(2,1)S(1)} %pad_maximum_fusion), channel_id=1, replica_groups=mesh['pairs'=16,'core'=2,'fac'=4] {'fac'}, dimensions={1}, use_global_device_ids=true | all-gather | bytes 737280 | tf_op jit(solution)/shard_map/all_gather | solution.py:159
  204.8 3.6 %all-gather.9.cloned.1.call-done = bf16[3072,768]{1,0:T(8,128)(2,1)} async-done(((bf16[96,768]{1,0:T(8,128)(2,1)}), bf16[3072,768]{1,0:T(8,128)(2,1)}) %all-gather.9.cloned.1.call-update) | async-done | bytes 4718608 | tf_op jit(solution)/shard_map/all_gather | solution.py:123
  208.4 4.5 %multiply_reduce_fusion.5 = (f32[]{:T(128)}, f32[]{:T(128)}, bf16[96,768]{1,0:T(8,128)(2,1)}, f32[96,768]{1,0:T(8,128)S(1)}) fusion(f32[96,768]{1,0:T(8,128)S(1)} %get-tuple-element.42, f32[96,768]{1,0:T(8,128)S(1)} %convert_reduce_fusion, bf16[96,3072]{1,0:T(8,128)(2,1)S(1)} %all_gather.24, bf16[3072,768]{1,0:T(8,128)(2,1)} %all-gather.9.cloned.1.call-done), kind=kOutput, calls=%fused_computation.37 | convolution fusion | flops 453574656 | bytes 6340616 | tf_op jit(solution)/shard_map/dot_general | solution.py:17
  213.0 3.2 %convolution_convert_fusion.1 = bf16[96,768]{1,0:T(8,128)(2,1)S(1)} fusion(bf16[96,3072]{1,0:T(8,128)(2,1)S(1)} %all_gather.24, bf16[3072,768]{1,0:T(8,128)(2,1)} %all-gather.5.cloned.1.call-done), kind=kOutput, calls=%fused_computation.24 | convolution fusion | flops 453058560 | bytes 5455872 | tf_op jit(solution)/shard_map/dot_general | solution.py:17
  218.2 7.1 %all-to-all-start.3 = ((f32[128,1,2]{2,1,0:T(1,128)}), f32[128,1,2]{2,1,0:T(1,128)S(1)}, u32[]{:S(2)}, u32[]{:S(2)}) async-start(f32[128,1,2]{2,1,0:T(1,128)} %broadcast_in_dim.22), calls=%async_computation.3 | async-start | bytes 131072 | tf_op jit(solution)/shard_map/all_to_all | solution.py:100
  225.3 11.3 %all_gather.26 = bf16[96,3072]{1,0:T(8,128)(2,1)S(1)} all-gather(bf16[96,768]{1,0:T(8,128)(2,1)S(1)} %convolution_convert_fusion.1), channel_id=1, replica_groups=mesh['pairs'=16,'core'=2,'fac'=4] {'fac'}, dimensions={1}, use_global_device_ids=true | all-gather | bytes 737280 | tf_op jit(solution)/shard_map/all_gather | solution.py:168
  238.6 20.8 %all-gather.11.cloned.1.call-done = bf16[3072,768]{1,0:T(8,128)(2,1)} async-done(((bf16[96,768]{1,0:T(8,128)(2,1)}), bf16[3072,768]{1,0:T(8,128)(2,1)}) %all-gather.11.cloned.1.call-update) | async-done | bytes 4718608 | tf_op jit(solution)/shard_map/all_gather | solution.py:123
  259.4 5.6 %fusion.2 = bf16[192,768]{1,0:T(8,128)(2,1)S(1)} fusion(bf16[3072,768]{1,0:T(8,128)(2,1)} %all-gather.11.cloned.1.call-done, bf16[3072,768]{1,0:T(8,128)(2,1)} %all-gather.7.cloned.1.call-done, f32[]{:T(128)S(6)} %div.33, bf16[96,3072]{1,0:T(8,128)(2,1)S(1)} %all_gather.26, bf16[96,3072]{1,0:T(8,128)(2,1)S(1)} %copy-done.2), kind=kOutput, calls=%fused_computation.13 | convolution fusion | flops 920272896 | bytes 10911748 | tf_op jit(solution)/shard_map/dot_general | solution.py:17
  269.6 5.2 %collective-permute-done.3 = bf16[192,768]{1,0:T(8,128)(2,1)S(1)} collective-permute-done((bf16[192,768]{1,0:T(8,128)(2,1)S(1)}, bf16[192,768]{1,0:T(8,128)(2,1)S(1)}, u32[]{:S(2)}, u32[]{:S(2)}) %collective-permute-start.3) | collective-permute-done | bytes 294944 | tf_op jit(solution)/shard_map/ppermute | solution.py:41
  278.2 5.3 %collective-permute-done.5 = bf16[192,768]{1,0:T(8,128)(2,1)S(1)} collective-permute-done((bf16[192,768]{1,0:T(8,128)(2,1)S(1)}, bf16[192,768]{1,0:T(8,128)(2,1)S(1)}, u32[]{:S(2)}, u32[]{:S(2)}) %collective-permute-start.5) | collective-permute-done | bytes 294944 | tf_op jit(solution)/shard_map/ppermute | solution.py:41
  288.7 15.9 %all_to_all.30 = f32[128,1,4]{2,1,0:T(1,128)S(1)} all-to-all(f32[128,1,4]{2,1,0:T(1,128)S(1)} %broadcast_in_dim.23), channel_id=1, replica_groups=mesh['pairs'=16,'core'=2,'fac'=4] {'pairs','core','fac'}, dimensions={0} | all-to-all | bytes 4096 | tf_op jit(solution)/shard_map/all_to_all | solution.py:100
  (58 shorter events, 40.1 us)
Async XLA Ops:
  7.2 75.0 %copy-start = (f32[32768]{0:T(1024)S(1)}, f32[32768]{0:T(1024)}, u32[]{:S(2)}) copy-start(f32[32768]{0:T(1024)} %param.11) | copy-start | bytes 393220
  7.2 74.2 %all-gather.5.cloned.1.call-start = ((), (), s32[]{:S(2)}) async-start(), calls=%async_computation.5 | async-start | bytes 4866048 | tf_op jit(solution)/shard_map/all_gather | solution.py:138
  8.8 127.5 %all-gather.7.cloned.1.call-start = ((), (), s32[]{:S(2)}) async-start(), calls=%async_computation.6 | async-start | bytes 4866048 | tf_op jit(solution)/shard_map/all_gather | solution.py:123
  25.1 5.8 %collective-permute-start = (bf16[16,96,768]{2,1,0:T(8,128)(2,1)}, bf16[16,96,768]{2,1,0:T(8,128)(2,1)S(1)}, u32[]{:S(2)}, u32[]{:S(2)}) collective-permute-start(bf16[16,96,768]{2,1,0:T(8,128)(2,1)} %get-tuple-element.13), channel_id=1, source_target_pairs={{0,4},{4,0},{1,5},{5,1},{2,6},{6,2},{3,7},{7,3},{8,12},{12,8},{9,1... | collective-permute-start | bytes 7077896 | tf_op jit(solution)/shard_map/ppermute | solution.py:91
  81.0 1.1 copy-start.4
  82.1 126.3 %all-gather.9.cloned.1.call-start = ((), (), s32[]{:S(2)}) async-start(), calls=%async_computation.7 | async-start | bytes 4866048 | tf_op jit(solution)/shard_map/all_gather | solution.py:123
  82.2 3.2 %copy-start.3 = (s32[1024]{0:T(1024)S(1)}, s32[1024]{0:T(1024)}, u32[]{:S(2)}) copy-start(s32[1024]{0:T(1024)} %param.10) | copy-start | bytes 12292
  98.3 4.2 %collective-permute-start.1 = (bf16[16,96,384]{2,1,0:T(8,128)(2,1)}, bf16[16,96,384]{2,1,0:T(8,128)(2,1)S(1)}, u32[]{:S(2)}, u32[]{:S(2)}) collective-permute-start(bf16[16,96,384]{2,1,0:T(8,128)(2,1)} %get-tuple-element.16), channel_id=1, source_target_pairs={{0,4},{4,0},{1,5},{5,1},{2,6},{6,2},{3,7},{7,3},{8,12},{12,8},{9,1... | collective-permute-start | bytes 3538952 | tf_op jit(solution)/shard_map/ppermute | solution.py:91
  104.1 32.3 %copy-start.2 = (bf16[96,3072]{1,0:T(8,128)(2,1)S(1)}, bf16[96,3072]{1,0:T(8,128)(2,1)}, u32[]{:S(2)}) copy-start(bf16[96,3072]{1,0:T(8,128)(2,1)} %param.12) | copy-start | bytes 1769476
  154.9 104.5 %all-gather.11.cloned.1.call-start = ((), (), s32[]{:S(2)}) async-start(), calls=%async_computation.8 | async-start | bytes 4866048 | tf_op jit(solution)/shard_map/all_gather | solution.py:123
  164.0 5.0 %collective-permute-start.2 = (bf16[16,96,384]{2,1,0:T(8,128)(2,1)}, bf16[16,96,384]{2,1,0:T(8,128)(2,1)S(1)}, u32[]{:S(2)}, u32[]{:S(2)}) collective-permute-start(bf16[16,96,384]{2,1,0:T(8,128)(2,1)} %get-tuple-element.20), channel_id=1, source_target_pairs={{0,4},{4,0},{1,5},{5,1},{2,6},{6,2},{3,7},{7,3},{8,12},{12,8},{9,1... | collective-permute-start | bytes 3538952 | tf_op jit(solution)/shard_map/ppermute | solution.py:91
  218.2 18.4 %all-to-all-start.3 = ((f32[128,1,2]{2,1,0:T(1,128)}), f32[128,1,2]{2,1,0:T(1,128)S(1)}, u32[]{:S(2)}, u32[]{:S(2)}) async-start(f32[128,1,2]{2,1,0:T(1,128)} %broadcast_in_dim.22), calls=%async_computation.3 | async-start | bytes 131072 | tf_op jit(solution)/shard_map/all_to_all | solution.py:100
  265.0 9.9 %collective-permute-start.3 = (bf16[192,768]{1,0:T(8,128)(2,1)S(1)}, bf16[192,768]{1,0:T(8,128)(2,1)S(1)}, u32[]{:S(2)}, u32[]{:S(2)}) collective-permute-start(bf16[192,768]{1,0:T(8,128)(2,1)S(1)} %fusion.2), channel_id=1, source_target_pairs={{0,1},{1,2},{2,3},{3,0},{4,5},{5,6},{6,7},{7,4},{8,9},{9,10},{10,1... | collective-permute-start | bytes 884744 | tf_op jit(solution)/shard_map/ppermute | solution.py:41
  266.5 10.1 %collective-permute-start.4 = (bf16[192,768]{1,0:T(8,128)(2,1)S(1)}, bf16[192,768]{1,0:T(8,128)(2,1)S(1)}, u32[]{:S(2)}, u32[]{:S(2)}) collective-permute-start(bf16[192,768]{1,0:T(8,128)(2,1)S(1)} %fusion.2), channel_id=1, source_target_pairs={{0,3},{1,0},{2,1},{3,2},{4,7},{5,4},{6,5},{7,6},{8,11},{9,8},{10,9... | collective-permute-start | bytes 884744 | tf_op jit(solution)/shard_map/ppermute | solution.py:44
  274.8 8.6 %collective-permute-start.5 = (bf16[192,768]{1,0:T(8,128)(2,1)S(1)}, bf16[192,768]{1,0:T(8,128)(2,1)S(1)}, u32[]{:S(2)}, u32[]{:S(2)}) collective-permute-start(bf16[192,768]{1,0:T(8,128)(2,1)S(1)} %collective-permute-done.3), channel_id=1, source_target_pairs={{0,1},{1,2},{2,3},{3,0},{4,5},{5,6},{6,7},{7,4},{8,9},{9,10},{10,1... | collective-permute-start | bytes 884744 | tf_op jit(solution)/shard_map/ppermute | solution.py:41
  283.5 27.3 %copy-start.1 = (f32[32768]{0:T(1024)S(1)}, f32[32768]{0:T(1024)}, u32[]{:S(2)}) copy-start(f32[32768]{0:T(1024)} %param.11) | copy-start | bytes 393220
Sparse Core Ops, SparseCore 0:
  10.8 70.3 all-gather.4
  84.0 52.2 all-gather.6
  155.0 53.3 all-gather.8
  213.1 46.2 all-gather.10

commit v16 on v14

--- a/solution.py
+++ b/solution.py
@@ -166,12 +166,11 @@
         residual_rows.astype(jnp.float32) - alpha * image_rows.astype(jnp.float32)
     ).astype(jnp.bfloat16)
 
-    rows = in_inverse.shape[0]
-    left = jnp.concatenate([in_inverse, gram_inverse], axis=0)
-    both = add_columns(left, next_rows).astype(jnp.bfloat16)
-    both_out = ring_product(both, out_inverse)
-    precond = both_out[:rows]
-    precond_image = both_out[rows:] + damping * precond
+    precond = ring_product(add_columns(in_inverse, next_rows).astype(jnp.bfloat16), out_inverse)
+    precond_image = (
+        ring_product(add_columns(gram_inverse, next_rows).astype(jnp.bfloat16), out_inverse)
+        + damping * precond
+    )
     inner_next, z_hz, z_hd, d_hz = global_sums(
         inner_part(residual, precond),
         inner_part(precond, precond_image),

time: 318 us -> 322 us (1.013)
    ppermute x1 -> x2, starting transfers between devices: 1.48 us -> 5.44 us  [ring_product(): behind = lax.ppermute(behind, 'fac', [(j, (j - 1) % n) for j in range(n)])]
    ppermute x2 -> x4, waiting for transfers between devices: 10.5 us -> 8.99 us  [ring_product(): ahead = lax.ppermute(ahead, 'fac', [(j, (j + 1) % n) for j in range(n)])]
    dot_general x8 -> x13, matrix products: 23.2 us -> 24.1 us  [add_columns(): return jnp.dot(matrix, piece, preferred_element_type=jnp.float32)]
  transfers between devices with their start and end apart: 11 -> 14, of which waited for: 8 -> 9; matrix products, arithmetic and copies ran while one was open for 9% -> 10% of each run, Pallas kernels for 9% -> 9%
where the time goes in v16:
time: 322 us; the launch traced here: 321 us
  blocking collectives  149 us (46%)
  waiting for transfers between devices  48.5 us (15%)
  matrix products  27.9 us (9%)
  Pallas kernels  27.8 us (9%)
  between operations  19.8 us (6%)
  starting transfers between devices  18.2 us (6%)
  local copies, waits for them, and re-layouts  17.3 us (5%)
  other arithmetic  13 us (4%)
    all_to_all x3, blocking collectives, scatter_sum(): received = lax.all_to_all(chip_sum, 'pairs', 0, 0, tiled=False)  96.4 us
    all_gather x3, waiting for transfers between devices, gather_rows(): return lax.all_gather(matrix.astype(jnp.bfloat16), FSDP, axis=0, tiled=True)  30.1 us
    pallas_call x3, Pallas kernels, block_term(): pl.pallas_call(kernel, grid=(cols // step,), in_specs=[pl.BlockSpec((toke...  27.8 us
    dot_general x13, matrix products, add_columns(): return jnp.dot(matrix, piece, preferred_element_type=jnp.float32)  24.1 us
    all_to_all x1, blocking collectives, global_sums(): received = lax.all_to_all(stacked, FSDP + ('fac',), 0, 0, tiled=True)  17.8 us
    all_gather x1, blocking collectives, body(): lax.all_gather(gram_own.astype(jnp.bfloat16), 'fac', axis=1, tiled=True)  12 us
    all_gather x1, blocking collectives, precondition(): lax.all_gather(mixed_low, 'fac', axis=1, tiled=True)  11.6 us
    all_gather x1, blocking collectives, body(): lax.all_gather(add_columns(gram_rows, in_cols).astype(jnp.bfloat16), 'fac...  11.3 us
  transfers between devices with their start and end apart: 14, of which 9 were waited for; matrix products, arithmetic and copies ran while one was open for 10% of the time, Pallas kernels for 9%

profile of v16, /device:TPU:1, one launch (start us, length us, event | category | flops | bytes accessed | tf_op | source)
XLA Modules:
  0.0 321.5 jit_solution(514935237550055875)
XLA Ops:
  10.7 11.8 %shard_map.86 = bf16[2,16,96,768]{3,2,1,0:T(8,128)(2,1)} custom-call(bf16[1024,3072]{1,0:T(8,128)(2,1)} %a_ref.5, bf16[1024,768]{1,0:T(8,128)(2,1)} %x_ref.1, f32[1024,1]{1,0:T(8,128)} %copy.15.f_ref), custom_call_target="tpu_custom_call" | custom-call | tf_op jit(solution)/shard_map/pallas_call | solution.py:64
  22.5 3.3 %dynamic-slice_bitcast_fusion = bf16[16,96,768]{2,1,0:T(8,128)(2,1)} fusion(bf16[2,16,96,768]{3,2,1,0:T(8,128)(2,1)} %shard_map.86, s32[]{:T(128)S(6)} %select_n.78), kind=kLoop, calls=%fused_computation.11 | loop fusion | bytes 4718596 | tf_op jit(solution)/shard_map/jit(dynamic_index_in_dim)/squeeze | solution.py:81
  27.2 4.4 %collective-permute-done = bf16[16,96,768]{2,1,0:T(8,128)(2,1)S(1)} collective-permute-done((bf16[16,96,768]{2,1,0:T(8,128)(2,1)}, bf16[16,96,768]{2,1,0:T(8,128)(2,1)S(1)}, u32[]{:S(2)}, u32[]{:S(2)}) %collective-permute-start) | collective-permute-done | bytes 2359328 | tf_op jit(solution)/shard_map/ppermute | solution.py:81
  33.9 47.9 %all_to_all.27 = bf16[16,96,768]{2,1,0:T(8,128)(2,1)S(1)} all-to-all(bf16[16,96,768]{2,1,0:T(8,128)(2,1)S(1)} %fusion), channel_id=1, replica_groups=mesh['pairs'=16,'core'=2,'fac'=4] {'pairs'}, dimensions={0} | all-to-all | bytes 4718592 | tf_op jit(solution)/shard_map/all_to_all | solution.py:84
  89.9 8.0 %shard_map.87 = bf16[2,16,96,384]{3,2,1,0:T(8,128)(2,1)} custom-call(bf16[1024,3072]{1,0:T(8,128)(2,1)} %a_ref.5, bf16[1024,384]{1,0:T(8,128)(2,1)} %get-tuple-element.16.x_ref, f32[1024,1]{1,0:T(8,128)} %copy.16.f_ref), custom_call_target="tpu_custom_call" | custom-call | tf_op jit(solution)/shard_map/pallas_call | solution.py:64
  105.0 26.4 %all_to_all.28 = bf16[16,96,384]{2,1,0:T(8,128)(2,1)S(1)} all-to-all(bf16[16,96,384]{2,1,0:T(8,128)(2,1)S(1)} %fusion.2), channel_id=1, replica_groups=mesh['pairs'=16,'core'=2,'fac'=4] {'pairs'}, dimensions={0} | all-to-all | bytes 2359296 | tf_op jit(solution)/shard_map/all_to_all | solution.py:84
  131.6 5.5 %all-gather.7.cloned.1.call-done = bf16[3072,768]{1,0:T(8,128)(2,1)} async-done(((bf16[96,768]{1,0:T(8,128)(2,1)}), bf16[3072,768]{1,0:T(8,128)(2,1)}) %all-gather.7.cloned.1.call-update) | async-done | bytes 4718608 | tf_op jit(solution)/shard_map/all_gather | solution.py:114
  137.2 3.2 fusion.8
  140.4 11.6 %all_gather.23 = bf16[96,3072]{1,0:T(8,128)(2,1)S(1)} all-gather(bf16[96,768]{1,0:T(8,128)(2,1)S(1)} %fusion.8), channel_id=1, replica_groups=mesh['pairs'=16,'core'=2,'fac'=4] {'fac'}, dimensions={1}, use_global_device_ids=true | all-gather | bytes 737280 | tf_op jit(solution)/shard_map/all_gather | solution.py:120
  151.9 3.9 %fusion.32 = (bf16[96,768]{1,0:T(8,128)(2,1)}, f32[96,768]{1,0:T(8,128)S(1)}) fusion(bf16[96,3072]{1,0:T(8,128)(2,1)S(1)} %all_gather.23, bf16[3072,768]{1,0:T(8,128)(2,1)} %param.13), kind=kOutput, calls=%fused_computation.78 | convolution fusion | flops 453058560 | bytes 5750784 | tf_op jit(solution)/shard_map/dot_general | solution.py:119
  155.9 8.0 %shard_map.88 = bf16[2,16,96,384]{3,2,1,0:T(8,128)(2,1)} custom-call(bf16[1024,3072]{1,0:T(8,128)(2,1)} %a_ref.5, bf16[1024,384]{1,0:T(8,128)(2,1)} %get-tuple-element.17.x_ref, f32[1024,1]{1,0:T(8,128)} %copy.16.f_ref), custom_call_target="tpu_custom_call" | custom-call | tf_op jit(solution)/shard_map/pallas_call | solution.py:64
  171.7 22.1 %all_to_all.29 = bf16[16,96,384]{2,1,0:T(8,128)(2,1)S(1)} all-to-all(bf16[16,96,384]{2,1,0:T(8,128)(2,1)S(1)} %fusion.1), channel_id=1, replica_groups=mesh['pairs'=16,'core'=2,'fac'=4] {'pairs'}, dimensions={0} | all-to-all | bytes 2359296 | tf_op jit(solution)/shard_map/all_to_all | solution.py:84
  193.9 12.0 %all_gather.24 = bf16[96,3072]{1,0:T(8,128)(2,1)S(1)} all-gather(bf16[96,768]{1,0:T(8,128)(2,1)S(1)} %pad_maximum_fusion), channel_id=1, replica_groups=mesh['pairs'=16,'core'=2,'fac'=4] {'fac'}, dimensions={1}, use_global_device_ids=true | all-gather | bytes 737280 | tf_op jit(solution)/shard_map/all_gather | solution.py:150
  205.9 3.8 %all-gather.9.cloned.1.call-done = bf16[3072,768]{1,0:T(8,128)(2,1)} async-done(((bf16[96,768]{1,0:T(8,128)(2,1)}), bf16[3072,768]{1,0:T(8,128)(2,1)}) %all-gather.9.cloned.1.call-update) | async-done | bytes 4718608 | tf_op jit(solution)/shard_map/all_gather | solution.py:114
  209.7 4.5 %multiply_reduce_fusion.5 = (f32[]{:T(128)}, f32[]{:T(128)}, bf16[96,768]{1,0:T(8,128)(2,1)}, f32[96,768]{1,0:T(8,128)S(1)}) fusion(f32[96,768]{1,0:T(8,128)S(1)} %get-tuple-element.28, f32[96,768]{1,0:T(8,128)S(1)} %convert_reduce_fusion, bf16[96,3072]{1,0:T(8,128)(2,1)S(1)} %all_gather.24, bf16[3072,768]{1,0:T(8,128)(2,1)} %all-gather.9.cloned.1.call-done), kind=kOutput, calls=%fused_computation.49 | convolution fusion | flops 453574656 | bytes 6340616 | tf_op jit(solution)/shard_map/dot_general | solution.py:16
  214.3 3.2 convolution_convert_fusion.1
  219.5 7.1 %all-to-all-start.3 = ((f32[128,1,2]{2,1,0:T(1,128)}), f32[128,1,2]{2,1,0:T(1,128)S(1)}, u32[]{:S(2)}, u32[]{:S(2)}) async-start(f32[128,1,2]{2,1,0:T(1,128)} %broadcast_in_dim.22), calls=%async_computation.3 | async-start | bytes 131072 | tf_op jit(solution)/shard_map/all_to_all | solution.py:91
  226.6 11.3 %all_gather.27 = bf16[96,3072]{1,0:T(8,128)(2,1)S(1)} all-gather(bf16[96,768]{1,0:T(8,128)(2,1)S(1)} %convolution_convert_fusion.1), channel_id=1, replica_groups=mesh['pairs'=16,'core'=2,'fac'=4] {'fac'}, dimensions={1}, use_global_device_ids=true | all-gather | bytes 737280 | tf_op jit(solution)/shard_map/all_gather | solution.py:159
  239.9 20.7 %all-gather.11.cloned.1.call-done = bf16[3072,768]{1,0:T(8,128)(2,1)} async-done(((bf16[96,768]{1,0:T(8,128)(2,1)}), bf16[3072,768]{1,0:T(8,128)(2,1)}) %all-gather.11.cloned.1.call-update) | async-done | bytes 4718608 | tf_op jit(solution)/shard_map/all_gather | solution.py:114
  260.7 5.6 %fusion.6 = bf16[768,96]{0,1:T(8,128)(2,1)S(1)} fusion(bf16[96,3072]{1,0:T(8,128)(2,1)S(1)} %copy-done, bf16[3072,768]{1,0:T(8,128)(2,1)} %all-gather.11.cloned.1.call-done, bf16[3072,768]{1,0:T(8,128)(2,1)} %all-gather.7.cloned.1.call-done, f32[]{:T(128)S(6)} %div.33), kind=kOutput, calls=%fused_computation.26 | convolution fusion | flops 464855040 | bytes 10174468 | tf_op jit(solution)/shard_map/dot_general | solution.py:16
  268.8 4.1 %fusion.7 = bf16[96,768]{1,0:T(8,128)(2,1)S(1)} fusion(bf16[96,3072]{1,0:T(8,128)(2,1)S(1)} %all_gather.27, bf16[3072,768]{1,0:T(8,128)(2,1)S(1)} %copy-done.4, bf16[3072,768]{1,0:T(8,128)(2,1)} %all-gather.7.cloned.1.call-done, f32[]{:T(128)S(6)} %div.33), kind=kOutput, calls=%fused_computation.27 | convolution fusion | flops 464855040 | bytes 10174468 | tf_op jit(solution)/shard_map/dot_general | solution.py:16
  272.9 3.0 collective-permute-start.7
  276.7 4.4 %collective-permute-done.6 = bf16[96,768]{1,0:T(8,128)(2,1)S(1)} collective-permute-done((bf16[96,768]{1,0:T(8,128)(2,1)S(1)}, bf16[96,768]{1,0:T(8,128)(2,1)S(1)}, u32[]{:S(2)}, u32[]{:S(2)}) %collective-permute-start.6) | collective-permute-done | bytes 147488 | tf_op jit(solution)/shard_map/ppermute | solution.py:40
  291.0 17.8 %all_to_all.30 = f32[128,1,4]{2,1,0:T(1,128)S(1)} all-to-all(f32[128,1,4]{2,1,0:T(1,128)S(1)} %broadcast_in_dim.23), channel_id=1, replica_groups=mesh['pairs'=16,'core'=2,'fac'=4] {'pairs','core','fac'}, dimensions={0} | all-to-all | bytes 4096 | tf_op jit(solution)/shard_map/all_to_all | solution.py:91
  (76 shorter events, 48.1 us)
Async XLA Ops:
  7.2 1.1 copy-start
  7.2 75.0 %all-gather.5.cloned.1.call-start = ((), (), s32[]{:S(2)}) async-start(), calls=%async_computation.5 | async-start | bytes 4866048 | tf_op jit(solution)/shard_map/all_gather | solution.py:129
  8.9 128.2 %all-gather.7.cloned.1.call-start = ((), (), s32[]{:S(2)}) async-start(), calls=%async_computation.6 | async-start | bytes 4866048 | tf_op jit(solution)/shard_map/all_gather | solution.py:114
  25.8 5.8 %collective-permute-start = (bf16[16,96,768]{2,1,0:T(8,128)(2,1)}, bf16[16,96,768]{2,1,0:T(8,128)(2,1)S(1)}, u32[]{:S(2)}, u32[]{:S(2)}) collective-permute-start(bf16[16,96,768]{2,1,0:T(8,128)(2,1)} %dynamic-slice_bitcast_fusion), channel_id=1, source_target_pairs={{0,4},{4,0},{1,5},{5,1},{2,6},{6,2},{3,7},{7,3},{8,12},{12,8},{9,1... | collective-permute-start | bytes 7077896 | tf_op jit(solution)/shard_map/ppermute | solution.py:81
  33.9 49.0 %copy-start.3 = (s32[1024]{0:T(1024)S(1)}, s32[1024]{0:T(1024)}, u32[]{:S(2)}) copy-start(s32[1024]{0:T(1024)} %param.9) | copy-start | bytes 12292
  33.9 49.0 %copy-start.1 = (f32[32768]{0:T(1024)S(1)}, f32[32768]{0:T(1024)}, u32[]{:S(2)}) copy-start(f32[32768]{0:T(1024)} %param.11) | copy-start | bytes 393220
  81.8 4.3 %copy-start.2 = (s32[1024]{0:T(1024)S(1)}, s32[1024]{0:T(1024)}, u32[]{:S(2)}) copy-start(s32[1024]{0:T(1024)} %param.10) | copy-start | bytes 12292
  82.9 126.8 %all-gather.9.cloned.1.call-start = ((), (), s32[]{:S(2)}) async-start(), calls=%async_computation.7 | async-start | bytes 4866048 | tf_op jit(solution)/shard_map/all_gather | solution.py:114
  99.3 4.1 %collective-permute-start.1 = (bf16[16,96,384]{2,1,0:T(8,128)(2,1)S(1)}, bf16[16,96,384]{2,1,0:T(8,128)(2,1)S(1)}, u32[]{:S(2)}, u32[]{:S(2)}) collective-permute-start(bf16[16,96,384]{2,1,0:T(8,128)(2,1)S(1)} %dynamic-slice_bitcast_fusion.2), channel_id=1, source_target_pairs={{0,4},{4,0},{1,5},{5,1},{2,6},{6,2},{3,7},{7,3},{8,12},{12,8},{9,1... | collective-permute-start | bytes 3538952 | tf_op jit(solution)/shard_map/ppermute | solution.py:81
  155.8 104.8 %all-gather.11.cloned.1.call-start = ((), (), s32[]{:S(2)}) async-start(), calls=%async_computation.8 | async-start | bytes 4866048 | tf_op jit(solution)/shard_map/all_gather | solution.py:114
  165.3 4.8 %collective-permute-start.2 = (bf16[16,96,384]{2,1,0:T(8,128)(2,1)S(1)}, bf16[16,96,384]{2,1,0:T(8,128)(2,1)S(1)}, u32[]{:S(2)}, u32[]{:S(2)}) collective-permute-start(bf16[16,96,384]{2,1,0:T(8,128)(2,1)S(1)} %dynamic-slice_bitcast_fusion.1), channel_id=1, source_target_pairs={{0,4},{4,0},{1,5},{5,1},{2,6},{6,2},{3,7},{7,3},{8,12},{12,8},{9,1... | collective-permute-start | bytes 3538952 | tf_op jit(solution)/shard_map/ppermute | solution.py:81
  219.5 18.4 %all-to-all-start.3 = ((f32[128,1,2]{2,1,0:T(1,128)}), f32[128,1,2]{2,1,0:T(1,128)S(1)}, u32[]{:S(2)}, u32[]{:S(2)}) async-start(f32[128,1,2]{2,1,0:T(1,128)} %broadcast_in_dim.22), calls=%async_computation.3 | async-start | bytes 131072 | tf_op jit(solution)/shard_map/all_to_all | solution.py:91
  260.7 8.1 %copy-start.4 = (bf16[3072,768]{1,0:T(8,128)(2,1)S(1)}, bf16[3072,768]{1,0:T(8,128)(2,1)}, u32[]{:S(2)}) copy-start(bf16[3072,768]{1,0:T(8,128)(2,1)} %all-gather.11.cloned.1.call-done) | copy-start | bytes 14155780
  266.3 9.6 %slice-start = ((s8[4718592]{0:T(1024)(128)(4,1)}), s8[4194304]{0:T(1024)(128)(4,1)S(1)}, s32[]{:S(2)}) async-start(s8[4718592]{0:T(1024)(128)(4,1)} %bitcast.51), calls=%async_computation.9 | async-start | bytes 8388608
  266.3 9.6 %slice-start.1 = ((s8[4718592]{0:T(1024)(128)(4,1)}), s8[524288]{0:T(1024)(128)(4,1)S(1)}, s32[]{:S(2)}) async-start(s8[4718592]{0:T(1024)(128)(4,1)} %bitcast.51), calls=%async_computation.10 | async-start | bytes 1048576
  266.3 15.5 %collective-permute-start.4 = (bf16[96,768]{1,0:T(8,128)(2,1)S(1)}, bf16[96,768]{1,0:T(8,128)(2,1)S(1)}, u32[]{:S(2)}, u32[]{:S(2)}) collective-permute-start(bf16[96,768]{1,0:T(8,128)(2,1)S(1)} %bitcast.53), channel_id=1, source_target_pairs={{0,3},{1,0},{2,1},{3,2},{4,7},{5,4},{6,5},{7,6},{8,11},{9,8},{10,9... | collective-permute-start | bytes 442376 | tf_op jit(solution)/shard_map/ppermute | solution.py:43
  268.8 7.8 %collective-permute-start.3 = (bf16[96,768]{1,0:T(8,128)(2,1)S(1)}, bf16[96,768]{1,0:T(8,128)(2,1)S(1)}, u32[]{:S(2)}, u32[]{:S(2)}) collective-permute-start(bf16[96,768]{1,0:T(8,128)(2,1)S(1)} %bitcast.54), channel_id=1, source_target_pairs={{0,1},{1,2},{2,3},{3,0},{4,5},{5,6},{6,7},{7,4},{8,9},{9,10},{10,1... | collective-permute-start | bytes 442376 | tf_op jit(solution)/shard_map/ppermute | solution.py:40
  272.9 9.2 %collective-permute-start.7 = (bf16[96,768]{1,0:T(8,128)(2,1)S(1)}, bf16[96,768]{1,0:T(8,128)(2,1)S(1)}, u32[]{:S(2)}, u32[]{:S(2)}) collective-permute-start(bf16[96,768]{1,0:T(8,128)(2,1)S(1)} %fusion.7), channel_id=1, source_target_pairs={{0,3},{1,0},{2,1},{3,2},{4,7},{5,4},{6,5},{7,6},{8,11},{9,8},{10,9... | collective-permute-start | bytes 442376 | tf_op jit(solution)/shard_map/ppermute | solution.py:43
  275.9 5.2 %collective-permute-start.6 = (bf16[96,768]{1,0:T(8,128)(2,1)S(1)}, bf16[96,768]{1,0:T(8,128)(2,1)S(1)}, u32[]{:S(2)}, u32[]{:S(2)}) collective-permute-start(bf16[96,768]{1,0:T(8,128)(2,1)S(1)} %fusion.7), channel_id=1, source_target_pairs={{0,1},{1,2},{2,3},{3,0},{4,5},{5,6},{6,7},{7,4},{8,9},{9,10},{10,1... | collective-permute-start | bytes 442376 | tf_op jit(solution)/shard_map/ppermute | solution.py:40
  276.6 7.9 %collective-permute-start.5 = (bf16[96,768]{1,0:T(8,128)(2,1)S(1)}, bf16[96,768]{1,0:T(8,128)(2,1)S(1)}, u32[]{:S(2)}, u32[]{:S(2)}) collective-permute-start(bf16[96,768]{1,0:T(8,128)(2,1)S(1)} %collective-permute-done.3), channel_id=1, source_target_pairs={{0,1},{1,2},{2,3},{3,0},{4,5},{5,6},{6,7},{7,4},{8,9},{9,10},{10,1... | collective-permute-start | bytes 442376 | tf_op jit(solution)/shard_map/ppermute | solution.py:40
  281.1 6.3 %collective-permute-start.8 = (bf16[96,768]{1,0:T(8,128)(2,1)S(1)}, bf16[96,768]{1,0:T(8,128)(2,1)S(1)}, u32[]{:S(2)}, u32[]{:S(2)}) collective-permute-start(bf16[96,768]{1,0:T(8,128)(2,1)S(1)} %collective-permute-done.6), channel_id=1, source_target_pairs={{0,1},{1,2},{2,3},{3,0},{4,5},{5,6},{6,7},{7,4},{8,9},{9,10},{10,1... | collective-permute-start | bytes 442376 | tf_op jit(solution)/shard_map/ppermute | solution.py:40
Sparse Core Ops, SparseCore 0:
  10.8 71.0 all-gather.4
  84.8 52.3 all-gather.6
  156.0 53.7 all-gather.8
  214.4 46.2 all-gather.10

commit v17 on v14

--- a/solution.py
+++ b/solution.py
@@ -45,15 +45,20 @@
     return total
 
 
-def block_term(activations, right, factor, scale):
+def block_term(activations, right, factor, scale, own_half=None):
     pairs, cores = lax.axis_size("pairs"), lax.axis_size("core")
     tokens, d_in = activations.shape
     rows = d_in // (pairs * cores)
-    cols = right.shape[1]
+    cols = right.shape[1] if own_half is None else own_half[1]
     step = 384 if cols % 384 == 0 else cols
 
     def kernel(a_ref, x_ref, f_ref, o_ref):
-        scaled = (x_ref[...].astype(jnp.float32) * f_ref[...]).astype(jnp.bfloat16)
+        if own_half is None:
+            x = x_ref[...]
+        else:
+            start = (lax.axis_index("fac") * 2 + own_half[0]) * cols + pl.program_id(0) * step
+            x = a_ref[:, pl.ds(pl.multiple_of(start, 128), step)]
+        scaled = (x.astype(jnp.float32) * f_ref[...]).astype(jnp.bfloat16)
         product = lax.dot_general(
             a_ref[...], scaled, (((0,), (0,)), ((), ())), preferred_element_type=jnp.float32
         )
@@ -66,7 +71,7 @@
         grid=(cols // step,),
         in_specs=[
             pl.BlockSpec((tokens, d_in), lambda j: (0, 0)),
-            pl.BlockSpec((tokens, step), lambda j: (0, j)),
+            pl.BlockSpec((tokens, step), lambda j: (0, j if own_half is None else 0)),
             pl.BlockSpec((tokens, 1), lambda j: (0, 0)),
         ],
         out_specs=pl.BlockSpec((cores, pairs, rows, step), lambda j: (0, 0, 0, j)),
@@ -138,12 +143,9 @@
     residual_rows = gather_rows(residual)
 
     gram_cols = d_in // lax.axis_size("fac")
-    own_cols = lax.dynamic_slice_in_dim(
-        activations, lax.axis_index("fac") * gram_cols, gram_cols, axis=1
-    )
     half = gram_cols // 2
-    gram_first = block_term(activations, own_cols[:, :half], weights, 1.0)
-    gram_second = block_term(activations, own_cols[:, half:], weights, 1.0)
+    gram_first = block_term(activations, activations, weights, 1.0, own_half=(0, half))
+    gram_second = block_term(activations, activations, weights, 1.0, own_half=(1, half))
     residual_rows, first_rows = lax.optimization_barrier((residual_rows, scatter_sum(gram_first)))
     precond = precondition(residual_rows)
     gram_own = jnp.concatenate([first_rows, scatter_sum(gram_second)], axis=1)

time: 318 us -> 316 us (level)
  no operation moved by 1% of the time
where the time goes in v17:
time: 316 us; the launch traced here: 315 us
  blocking collectives  145 us (46%)
  waiting for transfers between devices  54 us (17%)
  Pallas kernels  27.8 us (9%)
  matrix products  27.1 us (9%)
  between operations  19.8 us (6%)
  starting transfers between devices  15.3 us (5%)
  local copies, waits for them, and re-layouts  14.8 us (5%)
  other arithmetic  11.4 us (4%)
    all_to_all x3, blocking collectives, scatter_sum(): received = lax.all_to_all(chip_sum, 'pairs', 0, 0, tiled=False)  94.3 us
    all_gather x3, waiting for transfers between devices, gather_rows(): return lax.all_gather(matrix.astype(jnp.bfloat16), FSDP, axis=0, tiled=True)  34.1 us
    pallas_call x3, Pallas kernels, block_term(): pl.pallas_call(kernel, grid=(cols // step,), in_specs=[pl.BlockSpec((toke...  27.8 us
    dot_general x8, matrix products, add_columns(): return jnp.dot(matrix, piece, preferred_element_type=jnp.float32)  23.2 us
    all_to_all x1, blocking collectives, global_sums(): received = lax.all_to_all(stacked, FSDP + ('fac',), 0, 0, tiled=True)  16 us
    all_gather x1, blocking collectives, body(): lax.all_gather(gram_own.astype(jnp.bfloat16), 'fac', axis=1, tiled=True)  11.7 us
    all_gather x1, blocking collectives, precondition(): lax.all_gather(mixed_low, 'fac', axis=1, tiled=True)  11.6 us
    all_gather x1, blocking collectives, body(): lax.all_gather(add_columns(gram_rows, in_cols).astype(jnp.bfloat16), 'fac...  11.3 us
  transfers between devices with their start and end apart: 11, of which 8 were waited for; matrix products, arithmetic and copies ran while one was open for 9% of the time, Pallas kernels for 9%

profile of v17, /device:TPU:1, one launch (start us, length us, event | category | flops | bytes accessed | tf_op | source)
XLA Modules:
  0.0 315.1 jit_solution(12040805838267755677)
XLA Ops:
  10.6 11.8 %shard_map.86 = bf16[2,16,96,768]{3,2,1,0:T(8,128)(2,1)} custom-call(bf16[1024,3072]{1,0:T(8,128)(2,1)} %x_ref.5, bf16[1024,768]{1,0:T(8,128)(2,1)} %x_ref.3, f32[1024,1]{1,0:T(8,128)} %copy.15.f_ref), custom_call_target="tpu_custom_call" | custom-call | tf_op jit(solution)/shard_map/pallas_call | solution.py:69
  22.4 3.3 %dynamic-slice_bitcast_fusion = bf16[16,96,768]{2,1,0:T(8,128)(2,1)} fusion(bf16[2,16,96,768]{3,2,1,0:T(8,128)(2,1)} %shard_map.86, s32[]{:T(128)S(6)} %select_n.65), kind=kLoop, calls=%fused_computation.13 | loop fusion | bytes 4718596 | tf_op jit(solution)/shard_map/jit(dynamic_index_in_dim)/squeeze | solution.py:86
  27.1 4.4 %collective-permute-done = bf16[16,96,768]{2,1,0:T(8,128)(2,1)S(1)} collective-permute-done((bf16[16,96,768]{2,1,0:T(8,128)(2,1)}, bf16[16,96,768]{2,1,0:T(8,128)(2,1)S(1)}, u32[]{:S(2)}, u32[]{:S(2)}) %collective-permute-start) | collective-permute-done | bytes 2359328 | tf_op jit(solution)/shard_map/ppermute | solution.py:86
  33.8 47.8 %all_to_all.27 = bf16[16,96,768]{2,1,0:T(8,128)(2,1)S(1)} all-to-all(bf16[16,96,768]{2,1,0:T(8,128)(2,1)S(1)} %fusion.1), channel_id=1, replica_groups=mesh['pairs'=16,'core'=2,'fac'=4] {'pairs'}, dimensions={0} | all-to-all | bytes 4718592 | tf_op jit(solution)/shard_map/all_to_all | solution.py:89
  82.7 2.8 gather_fusion
  87.0 8.0 %shard_map.87 = bf16[2,16,96,384]{3,2,1,0:T(8,128)(2,1)} custom-call(bf16[1024,3072]{1,0:T(8,128)(2,1)} %x_ref.5, bf16[1024,3072]{1,0:T(8,128)(2,1)} %x_ref.5, f32[1024,1]{1,0:T(8,128)} %copy.16.f_ref), custom_call_target="tpu_custom_call" | custom-call | tf_op jit(solution)/shard_map/pallas_call | solution.py:69
  100.9 23.8 %all_to_all.28 = bf16[16,96,384]{2,1,0:T(8,128)(2,1)S(1)} all-to-all(bf16[16,96,384]{2,1,0:T(8,128)(2,1)S(1)} %fusion.4), channel_id=1, replica_groups=mesh['pairs'=16,'core'=2,'fac'=4] {'pairs'}, dimensions={0} | all-to-all | bytes 2359296 | tf_op jit(solution)/shard_map/all_to_all | solution.py:89
  124.8 8.8 %all-gather.7.cloned.1.call-done = bf16[3072,768]{1,0:T(8,128)(2,1)} async-done(((bf16[96,768]{1,0:T(8,128)(2,1)}), bf16[3072,768]{1,0:T(8,128)(2,1)}) %all-gather.7.cloned.1.call-update) | async-done | bytes 4718608 | tf_op jit(solution)/shard_map/all_gather | solution.py:119
  133.7 3.2 %fusion.14 = bf16[96,768]{1,0:T(8,128)(2,1)S(1)} fusion(bf16[96,3072]{1,0:T(8,128)(2,1)S(1)} %copy-done.4, bf16[3072,768]{1,0:T(8,128)(2,1)} %all-gather.7.cloned.1.call-done), kind=kOutput, calls=%fused_computation.31 | convolution fusion | flops 453058560 | bytes 5455872 | tf_op jit(solution)/shard_map/dot_general | solution.py:16
  136.9 11.6 %all_gather.23 = bf16[96,3072]{1,0:T(8,128)(2,1)S(1)} all-gather(bf16[96,768]{1,0:T(8,128)(2,1)S(1)} %fusion.14), channel_id=1, replica_groups=mesh['pairs'=16,'core'=2,'fac'=4] {'fac'}, dimensions={1}, use_global_device_ids=true | all-gather | bytes 737280 | tf_op jit(solution)/shard_map/all_gather | solution.py:125
  148.5 3.9 %fusion.25 = (bf16[96,768]{1,0:T(8,128)(2,1)}, f32[96,768]{1,0:T(8,128)S(1)}) fusion(bf16[96,3072]{1,0:T(8,128)(2,1)S(1)} %all_gather.23, bf16[3072,768]{1,0:T(8,128)(2,1)} %param.13), kind=kOutput, calls=%fused_computation.67 | convolution fusion | flops 453058560 | bytes 5750784 | tf_op jit(solution)/shard_map/dot_general | solution.py:124
  152.5 8.0 %shard_map.88 = bf16[2,16,96,384]{3,2,1,0:T(8,128)(2,1)} custom-call(bf16[1024,3072]{1,0:T(8,128)(2,1)} %x_ref.5, bf16[1024,3072]{1,0:T(8,128)(2,1)} %x_ref.5, f32[1024,1]{1,0:T(8,128)} %copy.16.f_ref), custom_call_target="tpu_custom_call" | custom-call | tf_op jit(solution)/shard_map/pallas_call | solution.py:69
  167.1 22.8 %all_to_all.29 = bf16[16,96,384]{2,1,0:T(8,128)(2,1)S(1)} all-to-all(bf16[16,96,384]{2,1,0:T(8,128)(2,1)S(1)} %fusion.3), channel_id=1, replica_groups=mesh['pairs'=16,'core'=2,'fac'=4] {'pairs'}, dimensions={0} | all-to-all | bytes 2359296 | tf_op jit(solution)/shard_map/all_to_all | solution.py:89
  190.1 11.7 %all_gather.24 = bf16[96,3072]{1,0:T(8,128)(2,1)S(1)} all-gather(bf16[96,768]{1,0:T(8,128)(2,1)S(1)} %pad_maximum_fusion), channel_id=1, replica_groups=mesh['pairs'=16,'core'=2,'fac'=4] {'fac'}, dimensions={1}, use_global_device_ids=true | all-gather | bytes 737280 | tf_op jit(solution)/shard_map/all_gather | solution.py:152
  201.8 4.6 %all-gather.9.cloned.1.call-done = bf16[3072,768]{1,0:T(8,128)(2,1)} async-done(((bf16[96,768]{1,0:T(8,128)(2,1)}), bf16[3072,768]{1,0:T(8,128)(2,1)}) %all-gather.9.cloned.1.call-update) | async-done | bytes 4718608 | tf_op jit(solution)/shard_map/all_gather | solution.py:119
  206.4 4.5 %multiply_reduce_fusion.5 = (f32[]{:T(128)}, f32[]{:T(128)}, bf16[96,768]{1,0:T(8,128)(2,1)}, f32[96,768]{1,0:T(8,128)S(1)}) fusion(f32[96,768]{1,0:T(8,128)S(1)} %get-tuple-element.28, f32[96,768]{1,0:T(8,128)S(1)} %convert_reduce_fusion, bf16[96,3072]{1,0:T(8,128)(2,1)S(1)} %all_gather.24, bf16[3072,768]{1,0:T(8,128)(2,1)} %all-gather.9.cloned.1.call-done), kind=kOutput, calls=%fused_computation.43 | convolution fusion | flops 453574656 | bytes 6340616 | tf_op jit(solution)/shard_map/dot_general | solution.py:16
  210.9 3.2 %convolution_convert_fusion.1 = bf16[96,768]{1,0:T(8,128)(2,1)S(1)} fusion(bf16[96,3072]{1,0:T(8,128)(2,1)S(1)} %all_gather.24, bf16[3072,768]{1,0:T(8,128)(2,1)} %all-gather.5.cloned.1.call-done), kind=kOutput, calls=%fused_computation.30 | convolution fusion | flops 453058560 | bytes 5455872 | tf_op jit(solution)/shard_map/dot_general | solution.py:16
  216.2 7.1 %all-to-all-start.3 = ((f32[128,1,2]{2,1,0:T(1,128)}), f32[128,1,2]{2,1,0:T(1,128)S(1)}, u32[]{:S(2)}, u32[]{:S(2)}) async-start(f32[128,1,2]{2,1,0:T(1,128)} %broadcast_in_dim.22), calls=%async_computation.3 | async-start | bytes 131072 | tf_op jit(solution)/shard_map/all_to_all | solution.py:96
  223.3 11.3 %all_gather.26 = bf16[96,3072]{1,0:T(8,128)(2,1)S(1)} all-gather(bf16[96,768]{1,0:T(8,128)(2,1)S(1)} %convolution_convert_fusion.1), channel_id=1, replica_groups=mesh['pairs'=16,'core'=2,'fac'=4] {'fac'}, dimensions={1}, use_global_device_ids=true | all-gather | bytes 737280 | tf_op jit(solution)/shard_map/all_gather | solution.py:161
  236.7 20.7 %all-gather.11.cloned.1.call-done = bf16[3072,768]{1,0:T(8,128)(2,1)} async-done(((bf16[96,768]{1,0:T(8,128)(2,1)}), bf16[3072,768]{1,0:T(8,128)(2,1)}) %all-gather.11.cloned.1.call-update) | async-done | bytes 4718608 | tf_op jit(solution)/shard_map/all_gather | solution.py:119
  257.4 5.6 %fusion.5 = bf16[192,768]{1,0:T(8,128)(2,1)S(1)} fusion(bf16[3072,768]{1,0:T(8,128)(2,1)} %all-gather.11.cloned.1.call-done, bf16[3072,768]{1,0:T(8,128)(2,1)} %all-gather.7.cloned.1.call-done, f32[]{:T(128)S(6)} %div.33, bf16[96,3072]{1,0:T(8,128)(2,1)S(1)} %all_gather.26, bf16[96,3072]{1,0:T(8,128)(2,1)S(1)} %copy-done.4), kind=kOutput, calls=%fused_computation.17 | convolution fusion | flops 920272896 | bytes 10911748 | tf_op jit(solution)/shard_map/dot_general | solution.py:16
  267.4 5.2 %collective-permute-done.3 = bf16[192,768]{1,0:T(8,128)(2,1)S(1)} collective-permute-done((bf16[192,768]{1,0:T(8,128)(2,1)S(1)}, bf16[192,768]{1,0:T(8,128)(2,1)S(1)}, u32[]{:S(2)}, u32[]{:S(2)}) %collective-permute-start.3) | collective-permute-done | bytes 294944 | tf_op jit(solution)/shard_map/ppermute | solution.py:40
  276.0 5.3 %collective-permute-done.5 = bf16[192,768]{1,0:T(8,128)(2,1)S(1)} collective-permute-done((bf16[192,768]{1,0:T(8,128)(2,1)S(1)}, bf16[192,768]{1,0:T(8,128)(2,1)S(1)}, u32[]{:S(2)}, u32[]{:S(2)}) %collective-permute-start.5) | collective-permute-done | bytes 294944 | tf_op jit(solution)/shard_map/ppermute | solution.py:40
  286.4 16.0 %all_to_all.30 = f32[128,1,4]{2,1,0:T(1,128)S(1)} all-to-all(f32[128,1,4]{2,1,0:T(1,128)S(1)} %broadcast_in_dim.23), channel_id=1, replica_groups=mesh['pairs'=16,'core'=2,'fac'=4] {'pairs','core','fac'}, dimensions={0} | all-to-all | bytes 4096 | tf_op jit(solution)/shard_map/all_to_all | solution.py:96
  (64 shorter events, 40.1 us)
Async XLA Ops:
  7.2 75.5 %copy-start = (f32[32768]{0:T(1024)S(1)}, f32[32768]{0:T(1024)}, u32[]{:S(2)}) copy-start(f32[32768]{0:T(1024)} %param.11) | copy-start | bytes 393220
  7.2 74.7 %all-gather.5.cloned.1.call-start = ((), (), s32[]{:S(2)}) async-start(), calls=%async_computation.5 | async-start | bytes 4866048 | tf_op jit(solution)/shard_map/all_gather | solution.py:134
  8.8 124.8 %all-gather.7.cloned.1.call-start = ((), (), s32[]{:S(2)}) async-start(), calls=%async_computation.6 | async-start | bytes 4866048 | tf_op jit(solution)/shard_map/all_gather | solution.py:119
  25.6 5.8 %collective-permute-start = (bf16[16,96,768]{2,1,0:T(8,128)(2,1)}, bf16[16,96,768]{2,1,0:T(8,128)(2,1)S(1)}, u32[]{:S(2)}, u32[]{:S(2)}) collective-permute-start(bf16[16,96,768]{2,1,0:T(8,128)(2,1)} %dynamic-slice_bitcast_fusion), channel_id=1, source_target_pairs={{0,4},{4,0},{1,5},{5,1},{2,6},{6,2},{3,7},{7,3},{8,12},{12,8},{9,1... | collective-permute-start | bytes 7077896 | tf_op jit(solution)/shard_map/ppermute | solution.py:86
  81.6 1.1 copy-start.6
  82.6 123.8 %all-gather.9.cloned.1.call-start = ((), (), s32[]{:S(2)}) async-start(), calls=%async_computation.7 | async-start | bytes 4866048 | tf_op jit(solution)/shard_map/all_gather | solution.py:119
  82.7 3.2 %copy-start.5 = (s32[1024]{0:T(1024)S(1)}, s32[1024]{0:T(1024)}, u32[]{:S(2)}) copy-start(s32[1024]{0:T(1024)} %param.10) | copy-start | bytes 12292
  95.0 5.6 %copy-start.3 = (bf16[2,16,96,384]{3,2,1,0:T(8,128)(2,1)S(1)}, bf16[2,16,96,384]{3,2,1,0:T(8,128)(2,1)}, u32[]{:S(2)}) copy-start(bf16[2,16,96,384]{3,2,1,0:T(8,128)(2,1)} %shard_map.87) | copy-start | bytes 7077892
  96.6 4.0 %collective-permute-start.1 = (bf16[16,96,384]{2,1,0:T(8,128)(2,1)S(1)}, bf16[16,96,384]{2,1,0:T(8,128)(2,1)S(1)}, u32[]{:S(2)}, u32[]{:S(2)}) collective-permute-start(bf16[16,96,384]{2,1,0:T(8,128)(2,1)S(1)} %dynamic-slice_bitcast_fusion.2), channel_id=1, source_target_pairs={{0,4},{4,0},{1,5},{5,1},{2,6},{6,2},{3,7},{7,3},{8,12},{12,8},{9,1... | collective-permute-start | bytes 3538952 | tf_op jit(solution)/shard_map/ppermute | solution.py:86
  100.9 32.8 %copy-start.4 = (bf16[96,3072]{1,0:T(8,128)(2,1)S(1)}, bf16[96,3072]{1,0:T(8,128)(2,1)}, u32[]{:S(2)}) copy-start(bf16[96,3072]{1,0:T(8,128)(2,1)} %param.12) | copy-start | bytes 1769476
  152.4 105.0 %all-gather.11.cloned.1.call-start = ((), (), s32[]{:S(2)}) async-start(), calls=%async_computation.8 | async-start | bytes 4866048 | tf_op jit(solution)/shard_map/all_gather | solution.py:119
  160.5 6.3 %copy-start.2 = (bf16[2,16,96,384]{3,2,1,0:T(8,128)(2,1)S(1)}, bf16[2,16,96,384]{3,2,1,0:T(8,128)(2,1)}, u32[]{:S(2)}) copy-start(bf16[2,16,96,384]{3,2,1,0:T(8,128)(2,1)} %shard_map.88) | copy-start | bytes 7077892
  162.1 4.7 %collective-permute-start.2 = (bf16[16,96,384]{2,1,0:T(8,128)(2,1)S(1)}, bf16[16,96,384]{2,1,0:T(8,128)(2,1)S(1)}, u32[]{:S(2)}, u32[]{:S(2)}) collective-permute-start(bf16[16,96,384]{2,1,0:T(8,128)(2,1)S(1)} %dynamic-slice_bitcast_fusion.1), channel_id=1, source_target_pairs={{0,4},{4,0},{1,5},{5,1},{2,6},{6,2},{3,7},{7,3},{8,12},{12,8},{9,1... | collective-permute-start | bytes 3538952 | tf_op jit(solution)/shard_map/ppermute | solution.py:86
  216.2 18.4 %all-to-all-start.3 = ((f32[128,1,2]{2,1,0:T(1,128)}), f32[128,1,2]{2,1,0:T(1,128)S(1)}, u32[]{:S(2)}, u32[]{:S(2)}) async-start(f32[128,1,2]{2,1,0:T(1,128)} %broadcast_in_dim.22), calls=%async_computation.3 | async-start | bytes 131072 | tf_op jit(solution)/shard_map/all_to_all | solution.py:96
  263.0 9.6 %collective-permute-start.3 = (bf16[192,768]{1,0:T(8,128)(2,1)S(1)}, bf16[192,768]{1,0:T(8,128)(2,1)S(1)}, u32[]{:S(2)}, u32[]{:S(2)}) collective-permute-start(bf16[192,768]{1,0:T(8,128)(2,1)S(1)} %fusion.5), channel_id=1, source_target_pairs={{0,1},{1,2},{2,3},{3,0},{4,5},{5,6},{6,7},{7,4},{8,9},{9,10},{10,1... | collective-permute-start | bytes 884744 | tf_op jit(solution)/shard_map/ppermute | solution.py:40
  264.2 10.1 %collective-permute-start.4 = (bf16[192,768]{1,0:T(8,128)(2,1)S(1)}, bf16[192,768]{1,0:T(8,128)(2,1)S(1)}, u32[]{:S(2)}, u32[]{:S(2)}) collective-permute-start(bf16[192,768]{1,0:T(8,128)(2,1)S(1)} %fusion.5), channel_id=1, source_target_pairs={{0,3},{1,0},{2,1},{3,2},{4,7},{5,4},{6,5},{7,6},{8,11},{9,8},{10,9... | collective-permute-start | bytes 884744 | tf_op jit(solution)/shard_map/ppermute | solution.py:43
  272.6 8.6 %collective-permute-start.5 = (bf16[192,768]{1,0:T(8,128)(2,1)S(1)}, bf16[192,768]{1,0:T(8,128)(2,1)S(1)}, u32[]{:S(2)}, u32[]{:S(2)}) collective-permute-start(bf16[192,768]{1,0:T(8,128)(2,1)S(1)} %collective-permute-done.3), channel_id=1, source_target_pairs={{0,1},{1,2},{2,3},{3,0},{4,5},{5,6},{6,7},{7,4},{8,9},{9,10},{10,1... | collective-permute-start | bytes 884744 | tf_op jit(solution)/shard_map/ppermute | solution.py:40
  281.2 27.3 %copy-start.1 = (f32[32768]{0:T(1024)S(1)}, f32[32768]{0:T(1024)}, u32[]{:S(2)}) copy-start(f32[32768]{0:T(1024)} %param.11) | copy-start | bytes 393220
Sparse Core Ops, SparseCore 0:
  10.8 70.6 all-gather.4
  84.4 49.2 all-gather.6
  152.5 53.8 all-gather.8
  211.1 46.2 all-gather.10

commit v18 on v17

--- a/solution.py
+++ b/solution.py
@@ -58,7 +58,7 @@
         else:
             start = (lax.axis_index("fac") * 2 + own_half[0]) * cols + pl.program_id(0) * step
             x = a_ref[:, pl.ds(pl.multiple_of(start, 128), step)]
-        scaled = (x.astype(jnp.float32) * f_ref[...]).astype(jnp.bfloat16)
+        scaled = (x.astype(jnp.float32) * f_ref[...].reshape(tokens, 1)).astype(jnp.bfloat16)
         product = lax.dot_general(
             a_ref[...], scaled, (((0,), (0,)), ((), ())), preferred_element_type=jnp.float32
         )
@@ -72,11 +72,11 @@
         in_specs=[
             pl.BlockSpec((tokens, d_in), lambda j: (0, 0)),
             pl.BlockSpec((tokens, step), lambda j: (0, j if own_half is None else 0)),
-            pl.BlockSpec((tokens, 1), lambda j: (0, 0)),
+            pl.BlockSpec((tokens,), lambda j: (0,)),
         ],
         out_specs=pl.BlockSpec((cores, pairs, rows, step), lambda j: (0, 0, 0, j)),
         out_shape=jax.ShapeDtypeStruct((cores, pairs, rows, cols), jnp.bfloat16),
-    )(activations, right, factor.reshape(tokens, 1))
+    )(activations, right, factor)
 
 
 def scatter_sum(blocks):

time: 316 us -> 315 us (level)
  transfers between devices with their start and end apart: 11 -> 11, of which waited for: 8 -> 8; matrix products, arithmetic and copies ran while one was open for 9% -> 8% of each run, Pallas kernels for 9% -> 9%
where the time goes in v18:
time: 315 us; the launch traced here: 314 us
  blocking collectives  144 us (46%)
  waiting for transfers between devices  54.5 us (17%)
  Pallas kernels  27.6 us (9%)
  matrix products  27.1 us (9%)
  between operations  19.8 us (6%)
  starting transfers between devices  15.3 us (5%)
  local copies, waits for them, and re-layouts  12.6 us (4%)
  other arithmetic  12.6 us (4%)
    all_to_all x3, blocking collectives, scatter_sum(): received = lax.all_to_all(chip_sum, 'pairs', 0, 0, tiled=False)  93.9 us
    all_gather x3, waiting for transfers between devices, gather_rows(): return lax.all_gather(matrix.astype(jnp.bfloat16), FSDP, axis=0, tiled=True)  34.7 us
    pallas_call x3, Pallas kernels, block_term(): pl.pallas_call(kernel, grid=(cols // step,), in_specs=[pl.BlockSpec((toke...  27.6 us
    dot_general x8, matrix products, add_columns(): return jnp.dot(matrix, piece, preferred_element_type=jnp.float32)  23.3 us
    all_to_all x1, blocking collectives, global_sums(): received = lax.all_to_all(stacked, FSDP + ('fac',), 0, 0, tiled=True)  16 us
    all_gather x1, blocking collectives, body(): lax.all_gather(gram_own.astype(jnp.bfloat16), 'fac', axis=1, tiled=True)  11.7 us
    all_gather x1, blocking collectives, precondition(): lax.all_gather(mixed_low, 'fac', axis=1, tiled=True)  11.6 us
    all_gather x1, blocking collectives, body(): lax.all_gather(add_columns(gram_rows, in_cols).astype(jnp.bfloat16), 'fac...  11.3 us
  transfers between devices with their start and end apart: 11, of which 8 were waited for; matrix products, arithmetic and copies ran while one was open for 8% of the time, Pallas kernels for 9%

profile of v18, /device:TPU:1, one launch (start us, length us, event | category | flops | bytes accessed | tf_op | source)
XLA Modules:
  0.0 314.1 jit_solution(585858692820812629)
XLA Ops:
  10.2 11.6 %shard_map.86 = bf16[2,16,96,768]{3,2,1,0:T(8,128)(2,1)} custom-call(bf16[1024,3072]{1,0:T(8,128)(2,1)} %x_ref.5, bf16[1024,768]{1,0:T(8,128)(2,1)} %x_ref.3, f32[1024]{0:T(1024)} %convert_element_type.80.f_ref), custom_call_target="tpu_custom_call" | custom-call | tf_op jit(solution)/shard_map/pallas_call | solution.py:69
  21.8 3.2 %dynamic-slice_bitcast_fusion = bf16[16,96,768]{2,1,0:T(8,128)(2,1)} fusion(bf16[2,16,96,768]{3,2,1,0:T(8,128)(2,1)} %shard_map.86, s32[]{:T(128)S(6)} %select_n.65), kind=kLoop, calls=%fused_computation.13 | loop fusion | bytes 4718596 | tf_op jit(solution)/shard_map/jit(dynamic_index_in_dim)/squeeze | solution.py:86
  26.5 4.4 %collective-permute-done = bf16[16,96,768]{2,1,0:T(8,128)(2,1)S(1)} collective-permute-done((bf16[16,96,768]{2,1,0:T(8,128)(2,1)}, bf16[16,96,768]{2,1,0:T(8,128)(2,1)S(1)}, u32[]{:S(2)}, u32[]{:S(2)}) %collective-permute-start) | collective-permute-done | bytes 2359328 | tf_op jit(solution)/shard_map/ppermute | solution.py:86
  33.2 47.8 %all_to_all.27 = bf16[16,96,768]{2,1,0:T(8,128)(2,1)S(1)} all-to-all(bf16[16,96,768]{2,1,0:T(8,128)(2,1)S(1)} %fusion.1), channel_id=1, replica_groups=mesh['pairs'=16,'core'=2,'fac'=4] {'pairs'}, dimensions={0} | all-to-all | bytes 4718592 | tf_op jit(solution)/shard_map/all_to_all | solution.py:89
  82.2 2.8 gather_fusion
  86.0 8.0 %shard_map.87 = bf16[2,16,96,384]{3,2,1,0:T(8,128)(2,1)} custom-call(bf16[1024,3072]{1,0:T(8,128)(2,1)} %x_ref.5, bf16[1024,3072]{1,0:T(8,128)(2,1)} %x_ref.5, f32[1024]{0:T(1024)} %multiply_multiply_fusion.f_ref), custom_call_target="tpu_custom_call" | custom-call | tf_op jit(solution)/shard_map/pallas_call | solution.py:69
  99.9 23.3 %all_to_all.28 = bf16[16,96,384]{2,1,0:T(8,128)(2,1)S(1)} all-to-all(bf16[16,96,384]{2,1,0:T(8,128)(2,1)S(1)} %fusion.4), channel_id=1, replica_groups=mesh['pairs'=16,'core'=2,'fac'=4] {'pairs'}, dimensions={0} | all-to-all | bytes 2359296 | tf_op jit(solution)/shard_map/all_to_all | solution.py:89
  123.3 9.4 %all-gather.7.cloned.1.call-done = bf16[3072,768]{1,0:T(8,128)(2,1)} async-done(((bf16[96,768]{1,0:T(8,128)(2,1)}), bf16[3072,768]{1,0:T(8,128)(2,1)}) %all-gather.7.cloned.1.call-update) | async-done | bytes 4718608 | tf_op jit(solution)/shard_map/all_gather | solution.py:119
  132.7 3.2 %fusion.14 = bf16[96,768]{1,0:T(8,128)(2,1)S(1)} fusion(bf16[96,3072]{1,0:T(8,128)(2,1)S(1)} %copy-done.4, bf16[3072,768]{1,0:T(8,128)(2,1)} %all-gather.7.cloned.1.call-done), kind=kOutput, calls=%fused_computation.31 | convolution fusion | flops 453058560 | bytes 5455872 | tf_op jit(solution)/shard_map/dot_general | solution.py:16
  135.9 11.6 %all_gather.23 = bf16[96,3072]{1,0:T(8,128)(2,1)S(1)} all-gather(bf16[96,768]{1,0:T(8,128)(2,1)S(1)} %fusion.14), channel_id=1, replica_groups=mesh['pairs'=16,'core'=2,'fac'=4] {'fac'}, dimensions={1}, use_global_device_ids=true | all-gather | bytes 737280 | tf_op jit(solution)/shard_map/all_gather | solution.py:125
  147.5 3.9 %fusion.25 = (bf16[96,768]{1,0:T(8,128)(2,1)}, f32[96,768]{1,0:T(8,128)S(1)}) fusion(bf16[96,3072]{1,0:T(8,128)(2,1)S(1)} %all_gather.23, bf16[3072,768]{1,0:T(8,128)(2,1)} %param.13), kind=kOutput, calls=%fused_computation.67 | convolution fusion | flops 453058560 | bytes 5750784 | tf_op jit(solution)/shard_map/dot_general | solution.py:124
  151.5 8.0 %shard_map.88 = bf16[2,16,96,384]{3,2,1,0:T(8,128)(2,1)} custom-call(bf16[1024,3072]{1,0:T(8,128)(2,1)} %x_ref.5, bf16[1024,3072]{1,0:T(8,128)(2,1)} %x_ref.5, f32[1024]{0:T(1024)} %multiply_multiply_fusion.f_ref), custom_call_target="tpu_custom_call" | custom-call | tf_op jit(solution)/shard_map/pallas_call | solution.py:69
  166.1 22.8 %all_to_all.29 = bf16[16,96,384]{2,1,0:T(8,128)(2,1)S(1)} all-to-all(bf16[16,96,384]{2,1,0:T(8,128)(2,1)S(1)} %fusion.3), channel_id=1, replica_groups=mesh['pairs'=16,'core'=2,'fac'=4] {'pairs'}, dimensions={0} | all-to-all | bytes 2359296 | tf_op jit(solution)/shard_map/all_to_all | solution.py:89
  189.1 11.7 %all_gather.24 = bf16[96,3072]{1,0:T(8,128)(2,1)S(1)} all-gather(bf16[96,768]{1,0:T(8,128)(2,1)S(1)} %pad_maximum_fusion), channel_id=1, replica_groups=mesh['pairs'=16,'core'=2,'fac'=4] {'fac'}, dimensions={1}, use_global_device_ids=true | all-gather | bytes 737280 | tf_op jit(solution)/shard_map/all_gather | solution.py:152
  200.8 4.6 %all-gather.9.cloned.1.call-done = bf16[3072,768]{1,0:T(8,128)(2,1)} async-done(((bf16[96,768]{1,0:T(8,128)(2,1)}), bf16[3072,768]{1,0:T(8,128)(2,1)}) %all-gather.9.cloned.1.call-update) | async-done | bytes 4718608 | tf_op jit(solution)/shard_map/all_gather | solution.py:119
  205.4 4.5 %multiply_reduce_fusion.5 = (f32[]{:T(128)}, f32[]{:T(128)}, bf16[96,768]{1,0:T(8,128)(2,1)}, f32[96,768]{1,0:T(8,128)S(1)}) fusion(f32[96,768]{1,0:T(8,128)S(1)} %get-tuple-element.28, f32[96,768]{1,0:T(8,128)S(1)} %convert_reduce_fusion, bf16[96,3072]{1,0:T(8,128)(2,1)S(1)} %all_gather.24, bf16[3072,768]{1,0:T(8,128)(2,1)} %all-gather.9.cloned.1.call-done), kind=kOutput, calls=%fused_computation.43 | convolution fusion | flops 453574656 | bytes 6340616 | tf_op jit(solution)/shard_map/dot_general | solution.py:16
  209.9 3.2 %convolution_convert_fusion.1 = bf16[96,768]{1,0:T(8,128)(2,1)S(1)} fusion(bf16[96,3072]{1,0:T(8,128)(2,1)S(1)} %all_gather.24, bf16[3072,768]{1,0:T(8,128)(2,1)} %all-gather.5.cloned.1.call-done), kind=kOutput, calls=%fused_computation.30 | convolution fusion | flops 453058560 | bytes 5455872 | tf_op jit(solution)/shard_map/dot_general | solution.py:16
  215.2 7.1 %all-to-all-start.3 = ((f32[128,1,2]{2,1,0:T(1,128)}), f32[128,1,2]{2,1,0:T(1,128)S(1)}, u32[]{:S(2)}, u32[]{:S(2)}) async-start(f32[128,1,2]{2,1,0:T(1,128)} %broadcast_in_dim.22), calls=%async_computation.3 | async-start | bytes 131072 | tf_op jit(solution)/shard_map/all_to_all | solution.py:96
  222.3 11.3 %all_gather.26 = bf16[96,3072]{1,0:T(8,128)(2,1)S(1)} all-gather(bf16[96,768]{1,0:T(8,128)(2,1)S(1)} %convolution_convert_fusion.1), channel_id=1, replica_groups=mesh['pairs'=16,'core'=2,'fac'=4] {'fac'}, dimensions={1}, use_global_device_ids=true | all-gather | bytes 737280 | tf_op jit(solution)/shard_map/all_gather | solution.py:161
  235.7 20.7 %all-gather.11.cloned.1.call-done = bf16[3072,768]{1,0:T(8,128)(2,1)} async-done(((bf16[96,768]{1,0:T(8,128)(2,1)}), bf16[3072,768]{1,0:T(8,128)(2,1)}) %all-gather.11.cloned.1.call-update) | async-done | bytes 4718608 | tf_op jit(solution)/shard_map/all_gather | solution.py:119
  256.4 5.6 %fusion.5 = bf16[192,768]{1,0:T(8,128)(2,1)S(1)} fusion(bf16[3072,768]{1,0:T(8,128)(2,1)} %all-gather.11.cloned.1.call-done, bf16[3072,768]{1,0:T(8,128)(2,1)} %all-gather.7.cloned.1.call-done, f32[]{:T(128)S(6)} %div.33, bf16[96,3072]{1,0:T(8,128)(2,1)S(1)} %all_gather.26, bf16[96,3072]{1,0:T(8,128)(2,1)S(1)} %copy-done.4), kind=kOutput, calls=%fused_computation.17 | convolution fusion | flops 920272896 | bytes 10911748 | tf_op jit(solution)/shard_map/dot_general | solution.py:16
  266.4 5.2 %collective-permute-done.3 = bf16[192,768]{1,0:T(8,128)(2,1)S(1)} collective-permute-done((bf16[192,768]{1,0:T(8,128)(2,1)S(1)}, bf16[192,768]{1,0:T(8,128)(2,1)S(1)}, u32[]{:S(2)}, u32[]{:S(2)}) %collective-permute-start.3) | collective-permute-done | bytes 294944 | tf_op jit(solution)/shard_map/ppermute | solution.py:40
  275.0 5.3 %collective-permute-done.5 = bf16[192,768]{1,0:T(8,128)(2,1)S(1)} collective-permute-done((bf16[192,768]{1,0:T(8,128)(2,1)S(1)}, bf16[192,768]{1,0:T(8,128)(2,1)S(1)}, u32[]{:S(2)}, u32[]{:S(2)}) %collective-permute-start.5) | collective-permute-done | bytes 294944 | tf_op jit(solution)/shard_map/ppermute | solution.py:40
  285.4 16.0 %all_to_all.30 = f32[128,1,4]{2,1,0:T(1,128)S(1)} all-to-all(f32[128,1,4]{2,1,0:T(1,128)S(1)} %broadcast_in_dim.23), channel_id=1, replica_groups=mesh['pairs'=16,'core'=2,'fac'=4] {'pairs','core','fac'}, dimensions={0} | all-to-all | bytes 4096 | tf_op jit(solution)/shard_map/all_to_all | solution.py:96
  (62 shorter events, 39.2 us)
Async XLA Ops:
  7.2 75.0 %copy-start = (f32[32768]{0:T(1024)S(1)}, f32[32768]{0:T(1024)}, u32[]{:S(2)}) copy-start(f32[32768]{0:T(1024)} %param.11) | copy-start | bytes 393220
  7.2 74.2 %all-gather.5.cloned.1.call-start = ((), (), s32[]{:S(2)}) async-start(), calls=%async_computation.5 | async-start | bytes 4866048 | tf_op jit(solution)/shard_map/all_gather | solution.py:134
  8.8 123.8 %all-gather.7.cloned.1.call-start = ((), (), s32[]{:S(2)}) async-start(), calls=%async_computation.6 | async-start | bytes 4866048 | tf_op jit(solution)/shard_map/all_gather | solution.py:119
  25.0 5.8 %collective-permute-start = (bf16[16,96,768]{2,1,0:T(8,128)(2,1)}, bf16[16,96,768]{2,1,0:T(8,128)(2,1)S(1)}, u32[]{:S(2)}, u32[]{:S(2)}) collective-permute-start(bf16[16,96,768]{2,1,0:T(8,128)(2,1)} %dynamic-slice_bitcast_fusion), channel_id=1, source_target_pairs={{0,4},{4,0},{1,5},{5,1},{2,6},{6,2},{3,7},{7,3},{8,12},{12,8},{9,1... | collective-permute-start | bytes 7077896 | tf_op jit(solution)/shard_map/ppermute | solution.py:86
  81.0 1.1 copy-start.6
  82.1 123.3 %all-gather.9.cloned.1.call-start = ((), (), s32[]{:S(2)}) async-start(), calls=%async_computation.7 | async-start | bytes 4866048 | tf_op jit(solution)/shard_map/all_gather | solution.py:119
  82.2 3.2 %copy-start.5 = (s32[1024]{0:T(1024)S(1)}, s32[1024]{0:T(1024)}, u32[]{:S(2)}) copy-start(s32[1024]{0:T(1024)} %param.10) | copy-start | bytes 12292
  93.9 5.6 %copy-start.3 = (bf16[2,16,96,384]{3,2,1,0:T(8,128)(2,1)S(1)}, bf16[2,16,96,384]{3,2,1,0:T(8,128)(2,1)}, u32[]{:S(2)}) copy-start(bf16[2,16,96,384]{3,2,1,0:T(8,128)(2,1)} %shard_map.87) | copy-start | bytes 7077892
  95.5 4.0 %collective-permute-start.1 = (bf16[16,96,384]{2,1,0:T(8,128)(2,1)S(1)}, bf16[16,96,384]{2,1,0:T(8,128)(2,1)S(1)}, u32[]{:S(2)}, u32[]{:S(2)}) collective-permute-start(bf16[16,96,384]{2,1,0:T(8,128)(2,1)S(1)} %dynamic-slice_bitcast_fusion.2), channel_id=1, source_target_pairs={{0,4},{4,0},{1,5},{5,1},{2,6},{6,2},{3,7},{7,3},{8,12},{12,8},{9,1... | collective-permute-start | bytes 3538952 | tf_op jit(solution)/shard_map/ppermute | solution.py:86
  99.9 32.8 %copy-start.4 = (bf16[96,3072]{1,0:T(8,128)(2,1)S(1)}, bf16[96,3072]{1,0:T(8,128)(2,1)}, u32[]{:S(2)}) copy-start(bf16[96,3072]{1,0:T(8,128)(2,1)} %param.12) | copy-start | bytes 1769476
  151.4 105.0 %all-gather.11.cloned.1.call-start = ((), (), s32[]{:S(2)}) async-start(), calls=%async_computation.8 | async-start | bytes 4866048 | tf_op jit(solution)/shard_map/all_gather | solution.py:119
  159.5 6.3 %copy-start.2 = (bf16[2,16,96,384]{3,2,1,0:T(8,128)(2,1)S(1)}, bf16[2,16,96,384]{3,2,1,0:T(8,128)(2,1)}, u32[]{:S(2)}) copy-start(bf16[2,16,96,384]{3,2,1,0:T(8,128)(2,1)} %shard_map.88) | copy-start | bytes 7077892
  161.0 4.8 %collective-permute-start.2 = (bf16[16,96,384]{2,1,0:T(8,128)(2,1)S(1)}, bf16[16,96,384]{2,1,0:T(8,128)(2,1)S(1)}, u32[]{:S(2)}, u32[]{:S(2)}) collective-permute-start(bf16[16,96,384]{2,1,0:T(8,128)(2,1)S(1)} %dynamic-slice_bitcast_fusion.1), channel_id=1, source_target_pairs={{0,4},{4,0},{1,5},{5,1},{2,6},{6,2},{3,7},{7,3},{8,12},{12,8},{9,1... | collective-permute-start | bytes 3538952 | tf_op jit(solution)/shard_map/ppermute | solution.py:86
  215.2 18.4 %all-to-all-start.3 = ((f32[128,1,2]{2,1,0:T(1,128)}), f32[128,1,2]{2,1,0:T(1,128)S(1)}, u32[]{:S(2)}, u32[]{:S(2)}) async-start(f32[128,1,2]{2,1,0:T(1,128)} %broadcast_in_dim.22), calls=%async_computation.3 | async-start | bytes 131072 | tf_op jit(solution)/shard_map/all_to_all | solution.py:96
  262.0 9.6 %collective-permute-start.3 = (bf16[192,768]{1,0:T(8,128)(2,1)S(1)}, bf16[192,768]{1,0:T(8,128)(2,1)S(1)}, u32[]{:S(2)}, u32[]{:S(2)}) collective-permute-start(bf16[192,768]{1,0:T(8,128)(2,1)S(1)} %fusion.5), channel_id=1, source_target_pairs={{0,1},{1,2},{2,3},{3,0},{4,5},{5,6},{6,7},{7,4},{8,9},{9,10},{10,1... | collective-permute-start | bytes 884744 | tf_op jit(solution)/shard_map/ppermute | solution.py:40
  263.2 10.1 %collective-permute-start.4 = (bf16[192,768]{1,0:T(8,128)(2,1)S(1)}, bf16[192,768]{1,0:T(8,128)(2,1)S(1)}, u32[]{:S(2)}, u32[]{:S(2)}) collective-permute-start(bf16[192,768]{1,0:T(8,128)(2,1)S(1)} %fusion.5), channel_id=1, source_target_pairs={{0,3},{1,0},{2,1},{3,2},{4,7},{5,4},{6,5},{7,6},{8,11},{9,8},{10,9... | collective-permute-start | bytes 884744 | tf_op jit(solution)/shard_map/ppermute | solution.py:43
  271.6 8.6 %collective-permute-start.5 = (bf16[192,768]{1,0:T(8,128)(2,1)S(1)}, bf16[192,768]{1,0:T(8,128)(2,1)S(1)}, u32[]{:S(2)}, u32[]{:S(2)}) collective-permute-start(bf16[192,768]{1,0:T(8,128)(2,1)S(1)} %collective-permute-done.3), channel_id=1, source_target_pairs={{0,1},{1,2},{2,3},{3,0},{4,5},{5,6},{6,7},{7,4},{8,9},{9,10},{10,1... | collective-permute-start | bytes 884744 | tf_op jit(solution)/shard_map/ppermute | solution.py:40
  280.2 27.3 %copy-start.1 = (f32[32768]{0:T(1024)S(1)}, f32[32768]{0:T(1024)}, u32[]{:S(2)}) copy-start(f32[32768]{0:T(1024)} %param.11) | copy-start | bytes 393220
Sparse Core Ops, SparseCore 0:
  10.8 70.3 all-gather.4
  84.0 48.6 all-gather.6
  151.5 53.8 all-gather.8
  210.1 46.2 all-gather.10

commit v19 on v18

--- a/solution.py
+++ b/solution.py
@@ -50,7 +50,7 @@
     tokens, d_in = activations.shape
     rows = d_in // (pairs * cores)
     cols = right.shape[1] if own_half is None else own_half[1]
-    step = 384 if cols % 384 == 0 else cols
+    step = cols
 
     def kernel(a_ref, x_ref, f_ref, o_ref):
         if own_half is None:

time: 315 us -> 314 us (level)
  no operation moved by 1% of the time
where the time goes in v19:
time: 314 us; the launch traced here: 313 us
  blocking collectives  144 us (46%)
  waiting for transfers between devices  54.3 us (17%)
  matrix products  27.1 us (9%)
  Pallas kernels  26.8 us (9%)
  between operations  19.8 us (6%)
  starting transfers between devices  15.6 us (5%)
  local copies, waits for them, and re-layouts  12.6 us (4%)
  other arithmetic  12.6 us (4%)
    all_to_all x3, blocking collectives, scatter_sum(): received = lax.all_to_all(chip_sum, 'pairs', 0, 0, tiled=False)  93.9 us
    all_gather x3, waiting for transfers between devices, gather_rows(): return lax.all_gather(matrix.astype(jnp.bfloat16), FSDP, axis=0, tiled=True)  34.5 us
    pallas_call x3, Pallas kernels, block_term(): pl.pallas_call(kernel, grid=(cols // step,), in_specs=[pl.BlockSpec((toke...  26.8 us
    dot_general x8, matrix products, add_columns(): return jnp.dot(matrix, piece, preferred_element_type=jnp.float32)  23.3 us
    all_to_all x1, blocking collectives, global_sums(): received = lax.all_to_all(stacked, FSDP + ('fac',), 0, 0, tiled=True)  16 us
    all_gather x1, blocking collectives, body(): lax.all_gather(gram_own.astype(jnp.bfloat16), 'fac', axis=1, tiled=True)  11.6 us
    all_gather x1, blocking collectives, precondition(): lax.all_gather(mixed_low, 'fac', axis=1, tiled=True)  11.4 us
    all_gather x1, blocking collectives, body(): lax.all_gather(add_columns(gram_rows, in_cols).astype(jnp.bfloat16), 'fac...  11.3 us
  transfers between devices with their start and end apart: 11, of which 8 were waited for; matrix products, arithmetic and copies ran while one was open for 8% of the time, Pallas kernels for 9%

profile of v19, /device:TPU:1, one launch (start us, length us, event | category | flops | bytes accessed | tf_op | source)
XLA Modules:
  0.0 313.1 jit_solution(8060566414533530616)
XLA Ops:
  10.2 10.8 %shard_map.86 = bf16[2,16,96,768]{3,2,1,0:T(8,128)(2,1)} custom-call(bf16[1024,3072]{1,0:T(8,128)(2,1)} %x_ref.5, bf16[1024,768]{1,0:T(8,128)(2,1)} %x_ref.3, f32[1024]{0:T(1024)} %convert_element_type.80.f_ref), custom_call_target="tpu_custom_call" | custom-call | tf_op jit(solution)/shard_map/pallas_call | solution.py:69
  21.0 3.2 %dynamic-slice_bitcast_fusion = bf16[16,96,768]{2,1,0:T(8,128)(2,1)} fusion(bf16[2,16,96,768]{3,2,1,0:T(8,128)(2,1)} %shard_map.86, s32[]{:T(128)S(6)} %select_n.65), kind=kLoop, calls=%fused_computation.13 | loop fusion | bytes 4718596 | tf_op jit(solution)/shard_map/jit(dynamic_index_in_dim)/squeeze | solution.py:86
  25.7 4.4 %collective-permute-done = bf16[16,96,768]{2,1,0:T(8,128)(2,1)S(1)} collective-permute-done((bf16[16,96,768]{2,1,0:T(8,128)(2,1)}, bf16[16,96,768]{2,1,0:T(8,128)(2,1)S(1)}, u32[]{:S(2)}, u32[]{:S(2)}) %collective-permute-start) | collective-permute-done | bytes 2359328 | tf_op jit(solution)/shard_map/ppermute | solution.py:86
  32.4 47.8 %all_to_all.27 = bf16[16,96,768]{2,1,0:T(8,128)(2,1)S(1)} all-to-all(bf16[16,96,768]{2,1,0:T(8,128)(2,1)S(1)} %fusion.1), channel_id=1, replica_groups=mesh['pairs'=16,'core'=2,'fac'=4] {'pairs'}, dimensions={0} | all-to-all | bytes 4718592 | tf_op jit(solution)/shard_map/all_to_all | solution.py:89
  81.3 2.8 gather_fusion
  85.1 8.0 %shard_map.87 = bf16[2,16,96,384]{3,2,1,0:T(8,128)(2,1)} custom-call(bf16[1024,3072]{1,0:T(8,128)(2,1)} %x_ref.5, bf16[1024,3072]{1,0:T(8,128)(2,1)} %x_ref.5, f32[1024]{0:T(1024)} %multiply_multiply_fusion.f_ref), custom_call_target="tpu_custom_call" | custom-call | tf_op jit(solution)/shard_map/pallas_call | solution.py:69
  99.3 23.4 %all_to_all.28 = bf16[16,96,384]{2,1,0:T(8,128)(2,1)S(1)} all-to-all(bf16[16,96,384]{2,1,0:T(8,128)(2,1)S(1)} %fusion.4), channel_id=1, replica_groups=mesh['pairs'=16,'core'=2,'fac'=4] {'pairs'}, dimensions={0} | all-to-all | bytes 2359296 | tf_op jit(solution)/shard_map/all_to_all | solution.py:89
  122.9 9.2 %all-gather.7.cloned.1.call-done = bf16[3072,768]{1,0:T(8,128)(2,1)} async-done(((bf16[96,768]{1,0:T(8,128)(2,1)}), bf16[3072,768]{1,0:T(8,128)(2,1)}) %all-gather.7.cloned.1.call-update) | async-done | bytes 4718608 | tf_op jit(solution)/shard_map/all_gather | solution.py:119
  132.1 3.2 %fusion.14 = bf16[96,768]{1,0:T(8,128)(2,1)S(1)} fusion(bf16[96,3072]{1,0:T(8,128)(2,1)S(1)} %copy-done.4, bf16[3072,768]{1,0:T(8,128)(2,1)} %all-gather.7.cloned.1.call-done), kind=kOutput, calls=%fused_computation.31 | convolution fusion | flops 453058560 | bytes 5455872 | tf_op jit(solution)/shard_map/dot_general | solution.py:16
  135.3 11.4 %all_gather.23 = bf16[96,3072]{1,0:T(8,128)(2,1)S(1)} all-gather(bf16[96,768]{1,0:T(8,128)(2,1)S(1)} %fusion.14), channel_id=1, replica_groups=mesh['pairs'=16,'core'=2,'fac'=4] {'fac'}, dimensions={1}, use_global_device_ids=true | all-gather | bytes 737280 | tf_op jit(solution)/shard_map/all_gather | solution.py:125
  146.7 3.9 %fusion.25 = (bf16[96,768]{1,0:T(8,128)(2,1)}, f32[96,768]{1,0:T(8,128)S(1)}) fusion(bf16[96,3072]{1,0:T(8,128)(2,1)S(1)} %all_gather.23, bf16[3072,768]{1,0:T(8,128)(2,1)} %param.13), kind=kOutput, calls=%fused_computation.67 | convolution fusion | flops 453058560 | bytes 5750784 | tf_op jit(solution)/shard_map/dot_general | solution.py:124
  150.6 8.0 %shard_map.88 = bf16[2,16,96,384]{3,2,1,0:T(8,128)(2,1)} custom-call(bf16[1024,3072]{1,0:T(8,128)(2,1)} %x_ref.5, bf16[1024,3072]{1,0:T(8,128)(2,1)} %x_ref.5, f32[1024]{0:T(1024)} %multiply_multiply_fusion.f_ref), custom_call_target="tpu_custom_call" | custom-call | tf_op jit(solution)/shard_map/pallas_call | solution.py:69
  165.3 22.7 %all_to_all.29 = bf16[16,96,384]{2,1,0:T(8,128)(2,1)S(1)} all-to-all(bf16[16,96,384]{2,1,0:T(8,128)(2,1)S(1)} %fusion.3), channel_id=1, replica_groups=mesh['pairs'=16,'core'=2,'fac'=4] {'pairs'}, dimensions={0} | all-to-all | bytes 2359296 | tf_op jit(solution)/shard_map/all_to_all | solution.py:89
  188.1 11.6 %all_gather.24 = bf16[96,3072]{1,0:T(8,128)(2,1)S(1)} all-gather(bf16[96,768]{1,0:T(8,128)(2,1)S(1)} %pad_maximum_fusion), channel_id=1, replica_groups=mesh['pairs'=16,'core'=2,'fac'=4] {'fac'}, dimensions={1}, use_global_device_ids=true | all-gather | bytes 737280 | tf_op jit(solution)/shard_map/all_gather | solution.py:152
  199.8 4.7 %all-gather.9.cloned.1.call-done = bf16[3072,768]{1,0:T(8,128)(2,1)} async-done(((bf16[96,768]{1,0:T(8,128)(2,1)}), bf16[3072,768]{1,0:T(8,128)(2,1)}) %all-gather.9.cloned.1.call-update) | async-done | bytes 4718608 | tf_op jit(solution)/shard_map/all_gather | solution.py:119
  204.5 4.5 %multiply_reduce_fusion.5 = (f32[]{:T(128)}, f32[]{:T(128)}, bf16[96,768]{1,0:T(8,128)(2,1)}, f32[96,768]{1,0:T(8,128)S(1)}) fusion(f32[96,768]{1,0:T(8,128)S(1)} %get-tuple-element.28, f32[96,768]{1,0:T(8,128)S(1)} %convert_reduce_fusion, bf16[96,3072]{1,0:T(8,128)(2,1)S(1)} %all_gather.24, bf16[3072,768]{1,0:T(8,128)(2,1)} %all-gather.9.cloned.1.call-done), kind=kOutput, calls=%fused_computation.43 | convolution fusion | flops 453574656 | bytes 6340616 | tf_op jit(solution)/shard_map/dot_general | solution.py:16
  209.0 3.2 %convolution_convert_fusion.1 = bf16[96,768]{1,0:T(8,128)(2,1)S(1)} fusion(bf16[96,3072]{1,0:T(8,128)(2,1)S(1)} %all_gather.24, bf16[3072,768]{1,0:T(8,128)(2,1)} %all-gather.5.cloned.1.call-done), kind=kOutput, calls=%fused_computation.30 | convolution fusion | flops 453058560 | bytes 5455872 | tf_op jit(solution)/shard_map/dot_general | solution.py:16
  214.2 7.1 %all-to-all-start.3 = ((f32[128,1,2]{2,1,0:T(1,128)}), f32[128,1,2]{2,1,0:T(1,128)S(1)}, u32[]{:S(2)}, u32[]{:S(2)}) async-start(f32[128,1,2]{2,1,0:T(1,128)} %broadcast_in_dim.22), calls=%async_computation.3 | async-start | bytes 131072 | tf_op jit(solution)/shard_map/all_to_all | solution.py:96
  221.3 11.3 %all_gather.26 = bf16[96,3072]{1,0:T(8,128)(2,1)S(1)} all-gather(bf16[96,768]{1,0:T(8,128)(2,1)S(1)} %convolution_convert_fusion.1), channel_id=1, replica_groups=mesh['pairs'=16,'core'=2,'fac'=4] {'fac'}, dimensions={1}, use_global_device_ids=true | all-gather | bytes 737280 | tf_op jit(solution)/shard_map/all_gather | solution.py:161
  234.8 20.7 %all-gather.11.cloned.1.call-done = bf16[3072,768]{1,0:T(8,128)(2,1)} async-done(((bf16[96,768]{1,0:T(8,128)(2,1)}), bf16[3072,768]{1,0:T(8,128)(2,1)}) %all-gather.11.cloned.1.call-update) | async-done | bytes 4718608 | tf_op jit(solution)/shard_map/all_gather | solution.py:119
  255.4 5.6 %fusion.5 = bf16[192,768]{1,0:T(8,128)(2,1)S(1)} fusion(bf16[3072,768]{1,0:T(8,128)(2,1)} %all-gather.11.cloned.1.call-done, bf16[3072,768]{1,0:T(8,128)(2,1)} %all-gather.7.cloned.1.call-done, f32[]{:T(128)S(6)} %div.33, bf16[96,3072]{1,0:T(8,128)(2,1)S(1)} %all_gather.26, bf16[96,3072]{1,0:T(8,128)(2,1)S(1)} %copy-done.4), kind=kOutput, calls=%fused_computation.17 | convolution fusion | flops 920272896 | bytes 10911748 | tf_op jit(solution)/shard_map/dot_general | solution.py:16
  265.5 5.1 %collective-permute-done.3 = bf16[192,768]{1,0:T(8,128)(2,1)S(1)} collective-permute-done((bf16[192,768]{1,0:T(8,128)(2,1)S(1)}, bf16[192,768]{1,0:T(8,128)(2,1)S(1)}, u32[]{:S(2)}, u32[]{:S(2)}) %collective-permute-start.3) | collective-permute-done | bytes 294944 | tf_op jit(solution)/shard_map/ppermute | solution.py:40
  274.0 5.3 %collective-permute-done.5 = bf16[192,768]{1,0:T(8,128)(2,1)S(1)} collective-permute-done((bf16[192,768]{1,0:T(8,128)(2,1)S(1)}, bf16[192,768]{1,0:T(8,128)(2,1)S(1)}, u32[]{:S(2)}, u32[]{:S(2)}) %collective-permute-start.5) | collective-permute-done | bytes 294944 | tf_op jit(solution)/shard_map/ppermute | solution.py:40
  284.4 16.0 %all_to_all.30 = f32[128,1,4]{2,1,0:T(1,128)S(1)} all-to-all(f32[128,1,4]{2,1,0:T(1,128)S(1)} %broadcast_in_dim.23), channel_id=1, replica_groups=mesh['pairs'=16,'core'=2,'fac'=4] {'pairs','core','fac'}, dimensions={0} | all-to-all | bytes 4096 | tf_op jit(solution)/shard_map/all_to_all | solution.py:96
  (62 shorter events, 39.5 us)
Async XLA Ops:
  7.2 74.2 %copy-start = (f32[32768]{0:T(1024)S(1)}, f32[32768]{0:T(1024)}, u32[]{:S(2)}) copy-start(f32[32768]{0:T(1024)} %param.11) | copy-start | bytes 393220
  7.2 73.3 %all-gather.5.cloned.1.call-start = ((), (), s32[]{:S(2)}) async-start(), calls=%async_computation.5 | async-start | bytes 4866048 | tf_op jit(solution)/shard_map/all_gather | solution.py:134
  8.8 123.2 %all-gather.7.cloned.1.call-start = ((), (), s32[]{:S(2)}) async-start(), calls=%async_computation.6 | async-start | bytes 4866048 | tf_op jit(solution)/shard_map/all_gather | solution.py:119
  24.2 5.8 %collective-permute-start = (bf16[16,96,768]{2,1,0:T(8,128)(2,1)}, bf16[16,96,768]{2,1,0:T(8,128)(2,1)S(1)}, u32[]{:S(2)}, u32[]{:S(2)}) collective-permute-start(bf16[16,96,768]{2,1,0:T(8,128)(2,1)} %dynamic-slice_bitcast_fusion), channel_id=1, source_target_pairs={{0,4},{4,0},{1,5},{5,1},{2,6},{6,2},{3,7},{7,3},{8,12},{12,8},{9,1... | collective-permute-start | bytes 7077896 | tf_op jit(solution)/shard_map/ppermute | solution.py:86
  80.2 1.1 copy-start.6
  81.2 123.2 %all-gather.9.cloned.1.call-start = ((), (), s32[]{:S(2)}) async-start(), calls=%async_computation.7 | async-start | bytes 4866048 | tf_op jit(solution)/shard_map/all_gather | solution.py:119
  81.3 3.2 %copy-start.5 = (s32[1024]{0:T(1024)S(1)}, s32[1024]{0:T(1024)}, u32[]{:S(2)}) copy-start(s32[1024]{0:T(1024)} %param.10) | copy-start | bytes 12292
  93.1 5.8 %copy-start.3 = (bf16[2,16,96,384]{3,2,1,0:T(8,128)(2,1)S(1)}, bf16[2,16,96,384]{3,2,1,0:T(8,128)(2,1)}, u32[]{:S(2)}) copy-start(bf16[2,16,96,384]{3,2,1,0:T(8,128)(2,1)} %shard_map.87) | copy-start | bytes 7077892
  94.7 4.3 %collective-permute-start.1 = (bf16[16,96,384]{2,1,0:T(8,128)(2,1)S(1)}, bf16[16,96,384]{2,1,0:T(8,128)(2,1)S(1)}, u32[]{:S(2)}, u32[]{:S(2)}) collective-permute-start(bf16[16,96,384]{2,1,0:T(8,128)(2,1)S(1)} %dynamic-slice_bitcast_fusion.2), channel_id=1, source_target_pairs={{0,4},{4,0},{1,5},{5,1},{2,6},{6,2},{3,7},{7,3},{8,12},{12,8},{9,1... | collective-permute-start | bytes 3538952 | tf_op jit(solution)/shard_map/ppermute | solution.py:86
  99.3 32.8 %copy-start.4 = (bf16[96,3072]{1,0:T(8,128)(2,1)S(1)}, bf16[96,3072]{1,0:T(8,128)(2,1)}, u32[]{:S(2)}) copy-start(bf16[96,3072]{1,0:T(8,128)(2,1)} %param.12) | copy-start | bytes 1769476
  150.6 104.9 %all-gather.11.cloned.1.call-start = ((), (), s32[]{:S(2)}) async-start(), calls=%async_computation.8 | async-start | bytes 4866048 | tf_op jit(solution)/shard_map/all_gather | solution.py:119
  158.6 6.3 %copy-start.2 = (bf16[2,16,96,384]{3,2,1,0:T(8,128)(2,1)S(1)}, bf16[2,16,96,384]{3,2,1,0:T(8,128)(2,1)}, u32[]{:S(2)}) copy-start(bf16[2,16,96,384]{3,2,1,0:T(8,128)(2,1)} %shard_map.88) | copy-start | bytes 7077892
  160.2 4.8 %collective-permute-start.2 = (bf16[16,96,384]{2,1,0:T(8,128)(2,1)S(1)}, bf16[16,96,384]{2,1,0:T(8,128)(2,1)S(1)}, u32[]{:S(2)}, u32[]{:S(2)}) collective-permute-start(bf16[16,96,384]{2,1,0:T(8,128)(2,1)S(1)} %dynamic-slice_bitcast_fusion.1), channel_id=1, source_target_pairs={{0,4},{4,0},{1,5},{5,1},{2,6},{6,2},{3,7},{7,3},{8,12},{12,8},{9,1... | collective-permute-start | bytes 3538952 | tf_op jit(solution)/shard_map/ppermute | solution.py:86
  214.2 18.4 %all-to-all-start.3 = ((f32[128,1,2]{2,1,0:T(1,128)}), f32[128,1,2]{2,1,0:T(1,128)S(1)}, u32[]{:S(2)}, u32[]{:S(2)}) async-start(f32[128,1,2]{2,1,0:T(1,128)} %broadcast_in_dim.22), calls=%async_computation.3 | async-start | bytes 131072 | tf_op jit(solution)/shard_map/all_to_all | solution.py:96
  261.0 9.6 %collective-permute-start.3 = (bf16[192,768]{1,0:T(8,128)(2,1)S(1)}, bf16[192,768]{1,0:T(8,128)(2,1)S(1)}, u32[]{:S(2)}, u32[]{:S(2)}) collective-permute-start(bf16[192,768]{1,0:T(8,128)(2,1)S(1)} %fusion.5), channel_id=1, source_target_pairs={{0,1},{1,2},{2,3},{3,0},{4,5},{5,6},{6,7},{7,4},{8,9},{9,10},{10,1... | collective-permute-start | bytes 884744 | tf_op jit(solution)/shard_map/ppermute | solution.py:40
  262.3 10.1 %collective-permute-start.4 = (bf16[192,768]{1,0:T(8,128)(2,1)S(1)}, bf16[192,768]{1,0:T(8,128)(2,1)S(1)}, u32[]{:S(2)}, u32[]{:S(2)}) collective-permute-start(bf16[192,768]{1,0:T(8,128)(2,1)S(1)} %fusion.5), channel_id=1, source_target_pairs={{0,3},{1,0},{2,1},{3,2},{4,7},{5,4},{6,5},{7,6},{8,11},{9,8},{10,9... | collective-permute-start | bytes 884744 | tf_op jit(solution)/shard_map/ppermute | solution.py:43
  270.6 8.6 %collective-permute-start.5 = (bf16[192,768]{1,0:T(8,128)(2,1)S(1)}, bf16[192,768]{1,0:T(8,128)(2,1)S(1)}, u32[]{:S(2)}, u32[]{:S(2)}) collective-permute-start(bf16[192,768]{1,0:T(8,128)(2,1)S(1)} %collective-permute-done.3), channel_id=1, source_target_pairs={{0,1},{1,2},{2,3},{3,0},{4,5},{5,6},{6,7},{7,4},{8,9},{9,10},{10,1... | collective-permute-start | bytes 884744 | tf_op jit(solution)/shard_map/ppermute | solution.py:40
  279.3 27.3 %copy-start.1 = (f32[32768]{0:T(1024)S(1)}, f32[32768]{0:T(1024)}, u32[]{:S(2)}) copy-start(f32[32768]{0:T(1024)} %param.11) | copy-start | bytes 393220
Sparse Core Ops, SparseCore 0:
  10.8 69.5 all-gather.4
  83.2 48.7 all-gather.6
  150.7 53.7 all-gather.8
  209.1 46.2 all-gather.10
